TPU v7x, 32 devices: a whole 2x2x4 slice. The times are simulated.
32 devices in a mesh: seq: 4 (over y, x), shard: 8 (over z, core).
Axes of the slice: x: 2, y: 2, z: 4, core: 2. Of those that a mesh axis runs over, the one named last changes fastest.
Arguments:
- layer_in: bfloat16 [32, 1024, 768], P('shard', 'seq'), may hold values from -6 to 6
- layer_cotangent: bfloat16 [32, 1024, 768], P('shard', 'seq'), may hold values from -6 to 6
- doc_starts: int32 [32, 17], P('shard'), may hold values from 0 to 1024, as said below
- query_weight: float32 [768, 768], P(('seq', 'shard')), may hold values from -0.21875 to 0.21875
- key_weight: float32 [768, 768], P(('seq', 'shard')), may hold values from -0.21875 to 0.21875
- value_weight: float32 [768, 768], P(('seq', 'shard')), may hold values from -0.21875 to 0.21875
- out_weight: float32 [768, 768], P(('seq', 'shard')), may hold values from -3.5 to 3.5
- up_weight: float32 [768, 3072], P(('seq', 'shard')), may hold values from -0.21875 to 0.21875
- down_weight: float32 [3072, 768], P(('seq', 'shard')), may hold values from -0.109375 to 0.109375
- query_bias: float32 [768], P(('seq', 'shard')), may hold values from -0.625 to 0.625
- value_bias: float32 [768], P(('seq', 'shard')), may hold values from -0.1875 to 0.1875
- out_bias: float32 [768], P(('seq', 'shard')), may hold values from -0.625 to 0.625
- up_bias: float32 [3072], P(('seq', 'shard')), may hold values from -0.625 to 0.625
- down_bias: float32 [768], P(('seq', 'shard')), may hold values from -0.625 to 0.625
- mixer_gain: float32 [768], P(('seq', 'shard')), may hold values from 0.5 to 1.5
- mixer_shift: float32 [768], P(('seq', 'shard')), may hold values from -0.625 to 0.625
- final_gain: float32 [768], P(('seq', 'shard')), may hold values from 0.5 to 1.5
- final_shift: float32 [768], P(('seq', 'shard')), may hold values from -0.625 to 0.625
Outputs:
- layer_out: bfloat16 [32, 1024, 768], P('shard', 'seq')
- input_grad: float32 [32, 1024, 768], P('shard', 'seq')
- grad_query_weight: float32 [768, 768], P(('seq', 'shard'))
- grad_key_weight: float32 [768, 768], P(('seq', 'shard'))
- grad_value_weight: float32 [768, 768], P(('seq', 'shard'))
- grad_out_weight: float32 [768, 768], P(('seq', 'shard'))
- grad_up_weight: float32 [768, 3072], P(('seq', 'shard'))
- grad_down_weight: float32 [3072, 768], P(('seq', 'shard'))
- grad_query_bias: float32 [768], P(('seq', 'shard'))
- grad_value_bias: float32 [768], P(('seq', 'shard'))
- grad_out_bias: float32 [768], P(('seq', 'shard'))
- grad_up_bias: float32 [3072], P(('seq', 'shard'))
- grad_down_bias: float32 [768], P(('seq', 'shard'))
- grad_mixer_gain: float32 [768], P(('seq', 'shard'))
- grad_mixer_shift: float32 [768], P(('seq', 'shard'))
- grad_final_gain: float32 [768], P(('seq', 'shard'))
- grad_final_shift: float32 [768], P(('seq', 'shard'))
Inputs may be any that keep to these rules, and one draw needn't show every extreme that they name: `doc_starts`: each row lists the first positions of the documents of its stream in rising order; it begins with 0, entries equal to 1024 mark unused slots, and the last entry is always 1024. A document spans at most 512 positions, some document of every stream exactly that; every document but the last of a stream spans at least 64.
All inputs are finite; a program needn't handle non-finite values.
Results may differ from a plain program's by a relative error of at most 0.017.
Values may be sent and summed in bfloat16 or wider, within the bound.
No kernel may reach another device: no remote copies, remote signals or barrier semaphores. Data moves between devices by JAX's collectives and lax.ppermute only.
A program may use at most 192 MiB of HBM per device.

v0:
```python
import jax
import jax.numpy as jnp
from jax import lax
from jax.sharding import PartitionSpec as P

DH = 64
LEN = 1024


EPS = 1e-06
NEG = -1e30
ROOT_HALF = 0.7071067811865476
INV_ROOT_TWO_PI = 0.3989422804014327


def contract_rows(left, right):
    return lax.dot_general(
        left, right, (((0,), (0,)), ((), ())), preferred_element_type=jnp.float32
    )


def times_transpose(left, right):
    return lax.dot_general(
        left, right, (((1,), (1,)), ((), ())), preferred_element_type=jnp.float32
    )


def segment_ids(starts, length):
    places = lax.broadcasted_iota(jnp.int32, (1, length, 1), 1)
    return jnp.sum((starts[:, None, :] <= places).astype(jnp.int32), axis=2)


def norm_forward(rows, gain, shift):
    middle = jnp.mean(rows, axis=-1, keepdims=True)
    centred = rows - middle
    spread = jnp.mean(centred * centred, axis=-1, keepdims=True)
    inverse = lax.rsqrt(spread + EPS)
    normed = centred * inverse
    return (normed * gain + shift, normed, inverse)


def norm_backward(upstream, gain, normed, inverse):
    scaled = upstream * gain
    inner = jnp.mean(scaled, axis=-1, keepdims=True)
    along = jnp.mean(scaled * normed, axis=-1, keepdims=True)
    return inverse * (scaled - inner - normed * along)


def gelu_value(value):
    return 0.5 * value * (1.0 + lax.erf(value * ROOT_HALF))


def gelu_slope(value):
    return (
        0.5 * (1.0 + lax.erf(value * ROOT_HALF))
        + value * jnp.exp(-0.5 * value * value) * INV_ROOT_TWO_PI
    )


def masked_scores(queries, keys, seg_rows, seg_all, scale):
    scores = jnp.einsum("qhd,khd->hqk", queries, keys, preferred_element_type=jnp.float32) * scale
    allowed = seg_rows[:, None] == seg_all[None, :]
    return jnp.where(allowed[None], scores, NEG)


def attend_forward(item):
    queries, keys, values, segment = item
    length, heads, depth = queries.shape
    rows = min(512, length)
    blocks = length // rows
    scale = depth ** (-0.5)

    def one(piece):
        block_q, block_seg = piece
        scores = masked_scores(block_q, keys, block_seg, segment, scale)
        highest = jnp.max(scores, axis=-1, keepdims=True)
        raised = jnp.exp(scores - highest)
        total = jnp.sum(raised, axis=-1, keepdims=True)
        weights = (raised / total).astype(jnp.bfloat16)
        context = jnp.einsum("hqk,khd->qhd", weights, values, preferred_element_type=jnp.float32)
        return (context.astype(jnp.bfloat16), (highest + jnp.log(total))[..., 0])

    context, logsum = lax.map(
        one, (queries.reshape(blocks, rows, heads, depth), segment.reshape(blocks, rows))
    )
    return (context.reshape(length, heads, depth), logsum)


def attend_backward(item):
    queries, keys, values, segment, logsum, upstream = item
    length, heads, depth = queries.shape
    rows = min(512, length)
    blocks = length // rows
    scale = depth ** (-0.5)

    def one(carry, piece):
        key_acc, value_acc = carry
        block_q, block_seg, block_sum, block_up = piece
        scores = masked_scores(block_q, keys, block_seg, segment, scale)
        weights = jnp.exp(scores - block_sum[..., None])
        value_acc = value_acc + jnp.einsum(
            "hqk,qhd->khd",
            weights.astype(jnp.bfloat16),
            block_up,
            preferred_element_type=jnp.float32,
        )
        slope = jnp.einsum("qhd,khd->hqk", block_up, values, preferred_element_type=jnp.float32)
        inner = jnp.sum(weights * slope, axis=-1, keepdims=True)
        score_grad = (weights * (slope - inner)).astype(jnp.bfloat16)
        query_grad = (
            jnp.einsum("hqk,khd->qhd", score_grad, keys, preferred_element_type=jnp.float32) * scale
        )
        key_acc = (
            key_acc
            + jnp.einsum("hqk,qhd->khd", score_grad, block_q, preferred_element_type=jnp.float32)
            * scale
        )
        return ((key_acc, value_acc), query_grad.astype(jnp.bfloat16))

    empty = jnp.zeros((length, heads, depth), jnp.float32)
    pieces = (
        queries.reshape(blocks, rows, heads, depth),
        segment.reshape(blocks, rows),
        logsum,
        upstream.reshape(blocks, rows, heads, depth),
    )
    (key_grad, value_grad), query_grad = lax.scan(one, (empty, empty), pieces)
    return (
        query_grad.reshape(length, heads, depth),
        key_grad.astype(jnp.bfloat16),
        value_grad.astype(jnp.bfloat16),
    )


def per_device(
    layer_in,
    layer_cotangent,
    doc_starts,
    query_weight,
    key_weight,
    value_weight,
    out_weight,
    up_weight,
    down_weight,
    query_bias,
    value_bias,
    out_bias,
    up_bias,
    down_bias,
    mixer_gain,
    mixer_shift,
    final_gain,
    final_shift,
):
    (
        full_query,
        full_key,
        full_value,
        full_out,
        full_up,
        full_down,
        bias_query,
        bias_value,
        bias_out,
        bias_up,
        bias_down,
        gain_mixer,
        shift_mixer,
        gain_final,
        shift_final,
    ) = (
        lax.all_gather(query_weight.astype(jnp.bfloat16), ("seq", "shard"), axis=0, tiled=True),
        lax.all_gather(key_weight.astype(jnp.bfloat16), ("seq", "shard"), axis=0, tiled=True),
        lax.all_gather(value_weight.astype(jnp.bfloat16), ("seq", "shard"), axis=0, tiled=True),
        lax.all_gather(out_weight.astype(jnp.bfloat16), ("seq", "shard"), axis=0, tiled=True),
        lax.all_gather(up_weight.astype(jnp.bfloat16), ("seq", "shard"), axis=0, tiled=True),
        lax.all_gather(down_weight.astype(jnp.bfloat16), ("seq", "shard"), axis=0, tiled=True),
        lax.all_gather(query_bias.astype(jnp.bfloat16), ("seq", "shard"), axis=0, tiled=True),
        lax.all_gather(value_bias.astype(jnp.bfloat16), ("seq", "shard"), axis=0, tiled=True),
        lax.all_gather(out_bias.astype(jnp.bfloat16), ("seq", "shard"), axis=0, tiled=True),
        lax.all_gather(up_bias.astype(jnp.bfloat16), ("seq", "shard"), axis=0, tiled=True),
        lax.all_gather(down_bias.astype(jnp.bfloat16), ("seq", "shard"), axis=0, tiled=True),
        lax.all_gather(mixer_gain.astype(jnp.bfloat16), ("seq", "shard"), axis=0, tiled=True),
        lax.all_gather(mixer_shift.astype(jnp.bfloat16), ("seq", "shard"), axis=0, tiled=True),
        lax.all_gather(final_gain.astype(jnp.bfloat16), ("seq", "shard"), axis=0, tiled=True),
        lax.all_gather(final_shift.astype(jnp.bfloat16), ("seq", "shard"), axis=0, tiled=True),
    )
    local_in, local_up = (layer_in, layer_cotangent)
    streams, part_len, width = local_in.shape
    row_count = streams * part_len
    heads = width // DH
    flat = local_in.reshape(row_count, width)
    split_shape = (streams, part_len, heads, DH)
    queries = (
        jnp.dot(flat, full_query, preferred_element_type=jnp.float32)
        + bias_query.astype(jnp.float32)
    ).astype(jnp.bfloat16)
    keys = jnp.dot(flat, full_key, preferred_element_type=jnp.float32).astype(jnp.bfloat16)
    values = (
        jnp.dot(flat, full_value, preferred_element_type=jnp.float32)
        + bias_value.astype(jnp.float32)
    ).astype(jnp.bfloat16)
    head_queries, head_keys, head_values = (
        lax.all_to_all(
            queries.reshape(split_shape), "seq", split_axis=2, concat_axis=1, tiled=True
        ),
        lax.all_to_all(keys.reshape(split_shape), "seq", split_axis=2, concat_axis=1, tiled=True),
        lax.all_to_all(values.reshape(split_shape), "seq", split_axis=2, concat_axis=1, tiled=True),
    )
    segment = segment_ids(doc_starts, LEN)
    context, logsum = lax.map(attend_forward, (head_queries, head_keys, head_values, segment))
    context_rows = lax.all_to_all(context, "seq", split_axis=1, concat_axis=2, tiled=True).reshape(
        row_count, width
    )
    attn = jnp.dot(context_rows, full_out, preferred_element_type=jnp.float32) + bias_out.astype(
        jnp.float32
    )
    mixed, normed_mixer, inverse_mixer = norm_forward(
        flat.astype(jnp.float32) + attn,
        gain_mixer.astype(jnp.float32),
        shift_mixer.astype(jnp.float32),
    )
    upper = mixed.astype(jnp.bfloat16)
    preact = jnp.dot(upper, full_up, preferred_element_type=jnp.float32) + bias_up.astype(
        jnp.float32
    )
    hidden = gelu_value(preact).astype(jnp.bfloat16)
    ffout = jnp.dot(hidden, full_down, preferred_element_type=jnp.float32) + bias_down.astype(
        jnp.float32
    )
    result, normed_final, inverse_final = norm_forward(
        mixed + ffout, gain_final.astype(jnp.float32), shift_final.astype(jnp.float32)
    )
    layer_out = result.astype(jnp.bfloat16).reshape(streams, part_len, width)
    upstream = local_up.reshape(row_count, width).astype(jnp.float32)
    grad_final_gain = jnp.sum(upstream * normed_final, axis=0)
    grad_final_shift = jnp.sum(upstream, axis=0)
    back_final = norm_backward(
        upstream, gain_final.astype(jnp.float32), normed_final, inverse_final
    )
    back_ffout = back_final.astype(jnp.bfloat16)
    grad_down_weight = contract_rows(hidden, back_ffout)
    grad_down_bias = jnp.sum(back_ffout.astype(jnp.float32), axis=0)
    back_preact = (times_transpose(back_ffout, full_down) * gelu_slope(preact)).astype(jnp.bfloat16)
    grad_up_weight = contract_rows(upper, back_preact)
    grad_up_bias = jnp.sum(back_preact.astype(jnp.float32), axis=0)
    back_mixed = back_final + times_transpose(back_preact, full_up)
    grad_mixer_gain = jnp.sum(back_mixed * normed_mixer, axis=0)
    grad_mixer_shift = jnp.sum(back_mixed, axis=0)
    back_first = norm_backward(
        back_mixed, gain_mixer.astype(jnp.float32), normed_mixer, inverse_mixer
    )
    back_attn = back_first.astype(jnp.bfloat16)
    grad_out_weight = contract_rows(context_rows, back_attn)
    grad_out_bias = jnp.sum(back_attn.astype(jnp.float32), axis=0)
    back_context = times_transpose(back_attn, full_out).astype(jnp.bfloat16)
    head_back = lax.all_to_all(
        back_context.reshape(split_shape), "seq", split_axis=2, concat_axis=1, tiled=True
    )
    query_back, key_back, value_back = lax.map(
        attend_backward, (head_queries, head_keys, head_values, segment, logsum, head_back)
    )
    query_rows, key_rows, value_rows = (
        lax.all_to_all(query_back, "seq", split_axis=1, concat_axis=2, tiled=True),
        lax.all_to_all(key_back, "seq", split_axis=1, concat_axis=2, tiled=True),
        lax.all_to_all(value_back, "seq", split_axis=1, concat_axis=2, tiled=True),
    )
    query_rows = query_rows.reshape(row_count, width)
    key_rows = key_rows.reshape(row_count, width)
    value_rows = value_rows.reshape(row_count, width)
    grad_query_weight = contract_rows(flat, query_rows)
    grad_key_weight = contract_rows(flat, key_rows)
    grad_value_weight = contract_rows(flat, value_rows)
    grad_query_bias = jnp.sum(query_rows.astype(jnp.float32), axis=0)
    grad_value_bias = jnp.sum(value_rows.astype(jnp.float32), axis=0)
    input_grad = (
        back_first
        + times_transpose(query_rows, full_query)
        + times_transpose(key_rows, full_key)
        + times_transpose(value_rows, full_value)
    ).reshape(streams, part_len, width)
    (
        sum_query_weight,
        sum_key_weight,
        sum_value_weight,
        sum_out_weight,
        sum_up_weight,
        sum_down_weight,
        sum_query_bias,
        sum_value_bias,
        sum_out_bias,
        sum_up_bias,
        sum_down_bias,
        sum_mixer_gain,
        sum_mixer_shift,
        sum_final_gain,
        sum_final_shift,
    ) = (
        lax.psum_scatter(grad_query_weight, ("seq", "shard"), scatter_dimension=0, tiled=True),
        lax.psum_scatter(grad_key_weight, ("seq", "shard"), scatter_dimension=0, tiled=True),
        lax.psum_scatter(grad_value_weight, ("seq", "shard"), scatter_dimension=0, tiled=True),
        lax.psum_scatter(grad_out_weight, ("seq", "shard"), scatter_dimension=0, tiled=True),
        lax.psum_scatter(grad_up_weight, ("seq", "shard"), scatter_dimension=0, tiled=True),
        lax.psum_scatter(grad_down_weight, ("seq", "shard"), scatter_dimension=0, tiled=True),
        lax.psum_scatter(grad_query_bias, ("seq", "shard"), scatter_dimension=0, tiled=True),
        lax.psum_scatter(grad_value_bias, ("seq", "shard"), scatter_dimension=0, tiled=True),
        lax.psum_scatter(grad_out_bias, ("seq", "shard"), scatter_dimension=0, tiled=True),
        lax.psum_scatter(grad_up_bias, ("seq", "shard"), scatter_dimension=0, tiled=True),
        lax.psum_scatter(grad_down_bias, ("seq", "shard"), scatter_dimension=0, tiled=True),
        lax.psum_scatter(grad_mixer_gain, ("seq", "shard"), scatter_dimension=0, tiled=True),
        lax.psum_scatter(grad_mixer_shift, ("seq", "shard"), scatter_dimension=0, tiled=True),
        lax.psum_scatter(grad_final_gain, ("seq", "shard"), scatter_dimension=0, tiled=True),
        lax.psum_scatter(grad_final_shift, ("seq", "shard"), scatter_dimension=0, tiled=True),
    )
    return (
        layer_out,
        input_grad,
        sum_query_weight,
        sum_key_weight,
        sum_value_weight,
        sum_out_weight,
        sum_up_weight,
        sum_down_weight,
        sum_query_bias,
        sum_value_bias,
        sum_out_bias,
        sum_up_bias,
        sum_down_bias,
        sum_mixer_gain,
        sum_mixer_shift,
        sum_final_gain,
        sum_final_shift,
    )


def solution(mesh):
    in_specs = (
        P("shard", "seq", None),
        P("shard", "seq", None),
        P("shard", None),
        P(("seq", "shard"), None),
        P(("seq", "shard"), None),
        P(("seq", "shard"), None),
        P(("seq", "shard"), None),
        P(("seq", "shard"), None),
        P(("seq", "shard"), None),
        P(("seq", "shard")),
        P(("seq", "shard")),
        P(("seq", "shard")),
        P(("seq", "shard")),
        P(("seq", "shard")),
        P(("seq", "shard")),
        P(("seq", "shard")),
        P(("seq", "shard")),
        P(("seq", "shard")),
    )
    out_specs = (
        P("shard", "seq", None),
        P("shard", "seq", None),
        P(("seq", "shard"), None),
        P(("seq", "shard"), None),
        P(("seq", "shard"), None),
        P(("seq", "shard"), None),
        P(("seq", "shard"), None),
        P(("seq", "shard"), None),
        P(("seq", "shard")),
        P(("seq", "shard")),
        P(("seq", "shard")),
        P(("seq", "shard")),
        P(("seq", "shard")),
        P(("seq", "shard")),
        P(("seq", "shard")),
        P(("seq", "shard")),
        P(("seq", "shard")),
    )
    return jax.shard_map(
        per_device, mesh=mesh, in_specs=in_specs, out_specs=out_specs, check_vma=False
    )
```

profile of v0, /device:TPU:0, one launch (start us, length us, event | category | flops | bytes accessed | tf_op | source)
XLA Modules:
  0.0 1251.9 jit_solution(2350865984096955184)
XLA Ops:
  23.0 42.7 %all-reduce.19 = (bf16[768]{0:T(1024)(128)(2,1)S(1)}, bf16[768]{0:T(1024)(128)(2,1)S(1)}, bf16[768]{0:T(1024)(128)(2,1)}, bf16[768]{0:T(1024)(128)(2,1)}, bf16[7...) all-reduce(bf16[768]{0:T(1024)(128)(2,1)S(1)} %dynamic-update-slice, ...), channel_id=1, replica_groups=mesh['seq'=4,'shard'=8] {'seq','shard'}, use_global_device_ids=true, to_apply=%add | all-reduce | flops 9216 | bytes 36864
  68.5 3.1 add_convert_fusion.1
  74.7 3.6 all-to-all-start.2
  78.3 52.2 %all-gather.7.cloned.1.call-done = bf16[768,768]{1,0:T(8,128)(2,1)} async-done(((bf16[24,768]{1,0:T(8,128)(2,1)}), bf16[768,768]{1,0:T(8,128)(2,1)}) %all-gather.7.cloned.1.call-update) | async-done | bytes 1179664 | tf_op jit(solution)/shard_map/all_gather | solution.py:172
  130.6 4.3 add_convert_fusion.2
  138.9 3.6 all-to-all-start
  142.5 49.7 %all-gather.9.cloned.1.call-done = bf16[768,768]{1,0:T(8,128)(2,1)} async-done(((bf16[24,768]{1,0:T(8,128)(2,1)}), bf16[768,768]{1,0:T(8,128)(2,1)}) %all-gather.9.cloned.1.call-update) | async-done | bytes 1179664 | tf_op jit(solution)/shard_map/all_gather | solution.py:173
  192.2 4.3 convolution_convert_fusion.1
  199.1 3.9 reshape.248
  203.0 4.3 all-to-all-start.1
  211.6 16.8 %all-to-all-done.1 = bf16[4,256,12,64]{1,0,3,2:T(4,128)(2,1)} async-done(((bf16[4,256,12,64]{1,0,3,2:T(4,128)(2,1)}), bf16[4,256,12,64]{1,0,3,2:T(4,128)(2,1)}, u32[]{:S(2)}, u32[]{:S(2)}) %all-to-all-start.1) | async-done | bytes 1572896 | tf_op jit(solution)/shard_map/all_to_all | solution.py:207
  231.4 3.1 broadcast.164.clone.1
  234.5 70.0 %while.54 = (s32[]{:T(128)}, bf16[4,1024,3,64]{3,2,1,0:T(4,128)(2,1)}, f32[4,2,3,512]{3,2,1,0:T(4,128)}, bf16[4,1024,3,64]{1,3,2,0:T(8,128)(2,1)S(1)}, s32[4,102...) while((s32[]{:T(128)}, ...), condition=%wide.region_6.7_spmd, body=%wide.region_1.6_spmd.sunk | while | flops 422148608 | bytes 28430672 | solution.py:211
  238.0 11.3 while.57
  255.5 11.3 while.57
  273.0 11.3 while.57
  290.5 11.3 while.57
  304.5 8.5 copy.203
  313.1 5.2 reshape.300
  318.2 4.6 all-to-all-start.3
  324.4 18.5 %all-to-all-done.3 = bf16[4,2,98304]{2,1,0:T(2,128)(2,1)} async-done(((bf16[4,2,98304]{2,1,0:T(2,128)(2,1)}), bf16[4,2,98304]{2,1,0:T(2,128)(2,1)}, u32[]{:S(2)}, u32[]{:S(2)}) %all-to-all-start.3) | async-done | bytes 1572896 | tf_op jit(solution)/shard_map/all_to_all | solution.py:212
  342.9 3.8 reshape.301
  346.7 3.8 copy.170
  353.5 3.9 fusion.70
  357.9 12.8 %multiply_convert_fusion.1 = (bf16[1024,3072]{1,0:T(8,128)(2,1)}, f32[1024,3072]{1,0:T(8,128)}) fusion(f32[3072]{0:T(1024)S(1)} %convert_element_type.186, bf16[768,3072]{1,0:T(8,128)(2,1)} %all-gather.15.cloned.1.call-done, f32[1024,768]{1,0:T(8,128)S(1)} %get-tuple-element.625, f32[768]{0:T(1024)S(1)} %convert_element_type.182, ...), kind=kOutput, calls=%fused_computation.75 | convolution fusion | flops 4854644736 | bytes 26765312 | tf_op jit(solution)/shard_map/dot_general | solution.py:224
  370.6 14.2 %all-gather.17.cloned.1.call-done = bf16[3072,768]{1,0:T(8,128)(2,1)} async-done(((bf16[96,768]{1,0:T(8,128)(2,1)}), bf16[3072,768]{1,0:T(8,128)(2,1)}) %all-gather.17.cloned.1.call-update) | async-done | bytes 4718608 | tf_op jit(solution)/shard_map/all_gather | solution.py:177
  384.8 8.8 fusion.71
  399.8 13.9 %convert_reduce_fusion = (f32[3072]{0:T(1024)}, bf16[1024,3072]{1,0:T(8,128)(2,1)S(1)}) fusion(f32[1024,3072]{1,0:T(8,128)} %get-tuple-element.627, f32[3072]{0:T(1024)S(1)} %convert_element_type.186, bf16[3072,768]{1,0:T(8,128)(2,1)S(1)} %copy-done.46, f32[1024,768]{1,0:T(8,128)S(1)} %get-tuple-element.612), kind=kOutput, calls=%fused_computation.74 | convolution fusion | flops 4873516032 | bytes 26763264 | tf_op jit(solution)/shard_map/dot_general | solution.py:23
  413.7 6.5 multiply_reduce_fusion.1
  426.8 4.0 reshape.252
  430.8 4.4 all-to-all-start.4
  435.2 4.2 fusion.57
  439.6 15.6 %all-to-all-done.4 = bf16[4,256,12,64]{1,0,3,2:T(4,128)(2,1)} async-done(((bf16[4,256,12,64]{1,0,3,2:T(4,128)(2,1)}), bf16[4,256,12,64]{1,0,3,2:T(4,128)(2,1)}, u32[]{:S(2)}, u32[]{:S(2)}) %all-to-all-start.4) | async-done | bytes 1572896 | tf_op jit(solution)/shard_map/all_to_all | solution.py:257
  461.3 142.4 %while.56 = (s32[]{:T(128)}, bf16[4,1024,3,64]{3,2,1,0:T(4,128)(2,1)}, bf16[4,1024,3,64]{1,3,2,0:T(8,128)(2,1)}, bf16[4,1024,3,64]{1,3,2,0:T(8,128)(2,1)}, bf16[...) while((s32[]{:T(128)}, ...), condition=%wide.region_19.20_spmd, body=%wide.region_15.19_spmd.sunk | while | flops 1032321536 | bytes 67146216 | solution.py:260
  470.3 22.2 %while.58 = (s32[]{:T(128)}, f32[1024,3,64]{0,2,1:T(8,128)S(1)}, f32[1024,3,64]{0,2,1:T(8,128)S(1)}, bf16[2,512,3,64]{1,3,2,0:T(8,128)(2,1)S(1)}, bf16[2,512,3,6...) while((s32[]{:T(128)}, f32[1024,3,64]{0,2,1:T(8,128)S(1)}, ...), condition=%wide.region_18.18_spmd.clone, body=%wide.region_16.17_spmd.clone.sunk | while | flops 1031928320 | bytes 54649000 | solution.py:127
  505.9 22.2 %while.58 = (s32[]{:T(128)}, f32[1024,3,64]{0,2,1:T(8,128)S(1)}, f32[1024,3,64]{0,2,1:T(8,128)S(1)}, bf16[2,512,3,64]{1,3,2,0:T(8,128)(2,1)S(1)}, bf16[2,512,3,6...) while((s32[]{:T(128)}, f32[1024,3,64]{0,2,1:T(8,128)S(1)}, ...), condition=%wide.region_18.18_spmd.clone, body=%wide.region_16.17_spmd.clone.sunk | while | flops 1031928320 | bytes 54649000 | solution.py:127
  541.3 22.2 %while.58 = (s32[]{:T(128)}, f32[1024,3,64]{0,2,1:T(8,128)S(1)}, f32[1024,3,64]{0,2,1:T(8,128)S(1)}, bf16[2,512,3,64]{1,3,2,0:T(8,128)(2,1)S(1)}, bf16[2,512,3,6...) while((s32[]{:T(128)}, f32[1024,3,64]{0,2,1:T(8,128)S(1)}, ...), condition=%wide.region_18.18_spmd.clone, body=%wide.region_16.17_spmd.clone.sunk | while | flops 1031928320 | bytes 54649000 | solution.py:127
  576.9 22.2 %while.58 = (s32[]{:T(128)}, f32[1024,3,64]{0,2,1:T(8,128)S(1)}, f32[1024,3,64]{0,2,1:T(8,128)S(1)}, bf16[2,512,3,64]{1,3,2,0:T(8,128)(2,1)S(1)}, bf16[2,512,3,6...) while((s32[]{:T(128)}, f32[1024,3,64]{0,2,1:T(8,128)S(1)}, ...), condition=%wide.region_18.18_spmd.clone, body=%wide.region_16.17_spmd.clone.sunk | while | flops 1031928320 | bytes 54649000 | solution.py:127
  603.7 4.7 copy.180
  608.4 3.3 reshape.306
  611.7 23.3 %all_to_all.132 = bf16[4,2,98304]{2,1,0:T(2,128)(2,1)S(1)} all-to-all(bf16[4,2,98304]{2,1,0:T(2,128)(2,1)} %reshape.306), channel_id=1, replica_groups=mesh['seq'=4,'shard'=8] {'seq'}, dimensions={0} | all-to-all | bytes 3145728 | tf_op jit(solution)/shard_map/all_to_all | solution.py:266
  635.0 3.3 reshape.307
  638.3 4.9 copy.181
  647.7 3.2 copy.189
  650.9 6.2 copy.202
  657.2 3.3 reshape.304
  660.5 21.9 %all_to_all.133 = bf16[4,2,98304]{2,1,0:T(2,128)(2,1)S(1)} all-to-all(bf16[4,2,98304]{2,1,0:T(2,128)(2,1)} %reshape.304), channel_id=1, replica_groups=mesh['seq'=4,'shard'=8] {'seq'}, dimensions={0} | all-to-all | bytes 3145728 | tf_op jit(solution)/shard_map/all_to_all | solution.py:264
  682.4 3.3 reshape.305
  685.7 4.9 copy.177
  698.3 4.7 copy.178
  703.0 3.3 reshape.302
  706.3 23.4 %all_to_all.134 = bf16[4,2,98304]{2,1,0:T(2,128)(2,1)} all-to-all(bf16[4,2,98304]{2,1,0:T(2,128)(2,1)} %reshape.302), channel_id=1, replica_groups=mesh['seq'=4,'shard'=8] {'seq'}, dimensions={0} | all-to-all | bytes 3145728 | tf_op jit(solution)/shard_map/all_to_all | solution.py:265
  729.7 3.8 reshape.303
  733.5 3.9 copy.179
  743.2 3.2 copy.187
  746.6 10.7 fusion.63
  759.1 10.2 fusion.60
  774.5 40.5 %all-reduce.18 = (f32[768]{0:T(1024)S(1)}, f32[768]{0:T(1024)S(1)}, f32[768]{0:T(1024)S(1)}, f32[3072]{0:T(1024)S(1)}, f32[768]{0:T(1024)S(1)}, /*index=5*/f32[7...) all-reduce(f32[768]{0:T(1024)S(1)} %reduce_sum.194, ...), channel_id=8, replica_groups=mesh['seq'=4,'shard'=8] {'seq','shard'}, use_global_device_ids=true, to_apply=%region_27.28.clone | all-reduce | flops 9216 | bytes 73728
  820.3 3.4 fusion.72
  826.5 3.2 add_add_fusion
  829.7 27.3 %reduce-scatter.19.cloned.1.call-done = f32[24,768]{1,0:T(8,128)} async-done(((f32[768,768]{1,0:T(8,128)}), f32[24,768]{1,0:T(8,128)}) %reduce-scatter.19.cloned.1.call-update) | async-done | bytes 73744
  856.9 104.4 %reduce-scatter.21.cloned.1.call-done = f32[24,768]{1,0:T(8,128)} async-done(((f32[768,768]{1,0:T(8,128)}), f32[24,768]{1,0:T(8,128)}) %reduce-scatter.21.cloned.1.call-update) | async-done | bytes 73744
  961.3 141.8 %reduce-scatter.15.cloned.1.call-done = f32[24,3072]{1,0:T(8,128)} async-done(((f32[768,3072]{1,0:T(8,128)}), f32[24,3072]{1,0:T(8,128)}) %reduce-scatter.15.cloned.1.call-update) | async-done | bytes 294928 | tf_op jit(solution)/shard_map/reduce_scatter | solution.py:303
  1103.1 141.5 %reduce-scatter.17.cloned.1.call-done = f32[96,768]{1,0:T(8,128)} async-done(((f32[3072,768]{1,0:T(8,128)}), f32[96,768]{1,0:T(8,128)}) %reduce-scatter.17.cloned.1.call-update) | async-done | bytes 294928 | tf_op jit(solution)/shard_map/reduce_scatter | solution.py:304
  (485 shorter events, 303.0 us)
Async XLA Ops:
  7.2 61.3 %all-gather.11.cloned.1.call-start = ((), (), s32[]{:S(2)}) async-start(), calls=%async_computation.16 | async-start | bytes 1216512 | tf_op jit(solution)/shard_map/all_gather | solution.py:174
  8.8 121.8 %all-gather.7.cloned.1.call-start = ((), (), s32[]{:S(2)}) async-start(), calls=%async_computation.14 | async-start | bytes 1216512 | tf_op jit(solution)/shard_map/all_gather | solution.py:172
  10.3 181.8 %all-gather.9.cloned.1.call-start = ((), (), s32[]{:S(2)}) async-start(), calls=%async_computation.15 | async-start | bytes 1216512 | tf_op jit(solution)/shard_map/all_gather | solution.py:173
  11.9 341.5 %all-gather.13.cloned.1.call-start = ((), (), s32[]{:S(2)}) async-start(), calls=%async_computation.17 | async-start | bytes 1216512 | tf_op jit(solution)/shard_map/all_gather | solution.py:175
  13.5 344.4 %all-gather.15.cloned.1.call-start = ((), (), s32[]{:S(2)}) async-start(), calls=%async_computation.18 | async-start | bytes 4866048 | tf_op jit(solution)/shard_map/all_gather | solution.py:176
  74.7 64.2 %all-to-all-start.2 = ((bf16[4,256,12,64]{1,0,3,2:T(4,128)(2,1)}), bf16[4,256,12,64]{1,0,3,2:T(4,128)(2,1)S(1)}, u32[]{:S(2)}, u32[]{:S(2)}) async-start(bf16[4,256,12,64]{1,0,3,2:T(4,128)(2,1)} %reshape.249), calls=%async_computation.2 | async-start | bytes 3145728 | tf_op jit(solution)/shard_map/all_to_all | solution.py:208
  138.9 64.1 %all-to-all-start = ((bf16[4,256,12,64]{1,0,3,2:T(4,128)(2,1)}), bf16[4,256,12,64]{1,0,3,2:T(4,128)(2,1)S(1)}, u32[]{:S(2)}, u32[]{:S(2)}) async-start(bf16[4,256,12,64]{1,0,3,2:T(4,128)(2,1)} %reshape.247), calls=%async_computation | async-start | bytes 3145728 | tf_op jit(solution)/shard_map/all_to_all | solution.py:204
  199.1 8.8 copy-start.24
  199.1 9.5 copy-start.39
  203.0 25.4 %all-to-all-start.1 = ((bf16[4,256,12,64]{1,0,3,2:T(4,128)(2,1)}), bf16[4,256,12,64]{1,0,3,2:T(4,128)(2,1)}, u32[]{:S(2)}, u32[]{:S(2)}) async-start(bf16[4,256,12,64]{1,0,3,2:T(4,128)(2,1)} %reshape.248), calls=%async_computation.1 | async-start | bytes 3145728 | tf_op jit(solution)/shard_map/all_to_all | solution.py:207
  207.3 177.5 %all-gather.17.cloned.1.call-start = ((), (), s32[]{:S(2)}) async-start(), calls=%async_computation.19 | async-start | bytes 4866048 | tf_op jit(solution)/shard_map/all_gather | solution.py:177
  304.5 8.5 copy-start.2
  313.0 9.9 copy-start.45
  313.0 9.9 copy-start.44
  313.0 9.9 copy-start.43
  313.0 10.0 copy-start.42
  313.0 10.0 copy-start.41
  313.0 10.0 copy-start.40
  313.1 10.0 copy-start.3
  318.2 6.1 copy-start.36
  318.2 24.6 %all-to-all-start.3 = ((bf16[4,2,98304]{2,1,0:T(2,128)(2,1)}), bf16[4,2,98304]{2,1,0:T(2,128)(2,1)}, u32[]{:S(2)}, u32[]{:S(2)}) async-start(bf16[4,2,98304]{2,1,0:T(2,128)(2,1)} %reshape.300), calls=%async_computation.3 | async-start | bytes 3145728 | tf_op jit(solution)/shard_map/all_to_all | solution.py:212
  322.9 97.3 %copy-start.27 = (f32[768]{0:T(1024)}, f32[768]{0:T(1024)S(1)}, u32[]{:S(2)}) copy-start(f32[768]{0:T(1024)S(1)} %convert_element_type.180) | copy-start | bytes 9220
  322.9 61.9 %copy-start.29 = (f32[768]{0:T(1024)}, f32[768]{0:T(1024)S(1)}, u32[]{:S(2)}) copy-start(f32[768]{0:T(1024)S(1)} %convert_element_type.182) | copy-start | bytes 9220
  357.3 62.9 %copy-start = (f32[1024,768]{1,0:T(8,128)}, f32[1024,768]{1,0:T(8,128)S(1)}, u32[]{:S(2)}) copy-start(f32[1024,768]{1,0:T(8,128)S(1)} %get-tuple-element.625) | copy-start | bytes 9437188
  357.3 62.9 %copy-start.22 = (f32[1024]{0:T(1024)}, f32[1024]{0:T(1024)S(1)}, u32[]{:S(2)}) copy-start(f32[1024]{0:T(1024)S(1)} %broadcast_multiply_fusion.4) | copy-start | bytes 12292
  357.8 62.4 %copy-start.25 = (f32[1024]{0:T(1024)}, f32[1024]{0:T(1024)S(1)}, u32[]{:S(2)}) copy-start(f32[1024]{0:T(1024)S(1)} %add_rsqrt_fusion.1) | copy-start | bytes 12292
  396.9 2.9 copy-start.46
  396.9 16.8 %slice-start = ((s8[4718592]{0:T(1024)(128)(4,1)}), s8[4194304]{0:T(1024)(128)(4,1)S(1)}, s32[]{:S(2)}) async-start(s8[4718592]{0:T(1024)(128)(4,1)} %bitcast.311), calls=%async_computation.26 | async-start | bytes 8388608
  399.7 13.9 %copy-start.16 = (f32[1024,768]{1,0:T(8,128)}, f32[1024,768]{1,0:T(8,128)S(1)}, u32[]{:S(2)}) copy-start(f32[1024,768]{1,0:T(8,128)S(1)} %get-tuple-element.612) | copy-start | bytes 9437188
  399.8 13.9 %slice-start.1 = ((s8[4718592]{0:T(1024)(128)(4,1)}), s8[524288]{0:T(1024)(128)(4,1)S(1)}, s32[]{:S(2)}) async-start(s8[4718592]{0:T(1024)(128)(4,1)} %bitcast.311), calls=%async_computation.27 | async-start | bytes 1048576
  413.7 6.5 copy-start.13
  420.3 3.4 copy-start.51
  426.8 8.5 copy-start.10
  430.8 24.4 %all-to-all-start.4 = ((bf16[4,256,12,64]{1,0,3,2:T(4,128)(2,1)}), bf16[4,256,12,64]{1,0,3,2:T(4,128)(2,1)}, u32[]{:S(2)}, u32[]{:S(2)}) async-start(bf16[4,256,12,64]{1,0,3,2:T(4,128)(2,1)} %reshape.252), calls=%async_computation.4 | async-start | bytes 3145728 | tf_op jit(solution)/shard_map/all_to_all | solution.py:257
  435.2 394.5 %reduce-scatter.13.cloned.1.call-start = ((), (), s32[]{:S(2)}) async-start(), calls=%async_computation.20 | async-start | bytes 2433024 | tf_op jit(solution)/shard_map/reduce_scatter | solution.py:302
  439.5 390.1 %reduce-scatter.23.cloned.1.call-start = ((), (), s32[]{:S(2)}) async-start(), calls=%async_computation.25 | async-start | bytes 2433024
  638.3 6.6 copy-start.47
  643.2 4.5 copy-start.5
  650.9 206.0 %reduce-scatter.19.cloned.1.call-start = ((), (), s32[]{:S(2)}) async-start(), calls=%async_computation.23 | async-start | bytes 2433024
  685.7 6.6 copy-start.48
  690.6 4.5 copy-start.7
  698.2 263.1 %reduce-scatter.21.cloned.1.call-start = ((), (), s32[]{:S(2)}) async-start(), calls=%async_computation.24 | async-start | bytes 2433024
  737.3 3.0 copy-start.49
  743.2 3.3 copy-start.1
  743.2 3.3 copy-start.23
  743.2 3.3 copy-start.26
  743.2 3.3 copy-start.28
  743.2 3.3 copy-start.30
  746.5 356.7 %reduce-scatter.15.cloned.1.call-start = ((), (), s32[]{:S(2)}) async-start(), calls=%async_computation.21 | async-start | bytes 9732096 | tf_op jit(solution)/shard_map/reduce_scatter | solution.py:303
  757.3 1.9 copy-start.17
  757.3 487.4 %reduce-scatter.17.cloned.1.call-start = ((), (), s32[]{:S(2)}) async-start(), calls=%async_computation.22 | async-start | bytes 9732096 | tf_op jit(solution)/shard_map/reduce_scatter | solution.py:304
  769.3 3.3 copy-start.8
  769.3 5.1 copy-start.31
  769.3 5.1 copy-start.32
  769.4 5.1 copy-start.33
  769.4 5.1 copy-start.34
  769.4 5.1 copy-start.35
  769.4 5.1 copy-start.37
  769.4 5.1 copy-start.38
  820.3 3.4 copy-start.20
  820.3 3.4 copy-start.50
  823.6 1.9 copy-start.11
  823.7 2.4 copy-start.15
  823.7 2.8 copy-start.21
  (10 other events, 11.5 us)
Sparse Core Ops, SparseCore 0:
  11.6 56.8 all-gather.10
  72.0 58.4 all-gather.6
  134.2 57.9 all-gather.8
  195.6 53.8 all-gather.12
  252.9 62.5 all-gather.14
  319.0 65.8 all-gather.16
  441.8 99.3 reduce-scatter.12
  651.0 101.0 reduce-scatter.22
  758.0 98.8 reduce-scatter.18
  862.6 98.6 reduce-scatter.20
  967.8 135.3 reduce-scatter.14
  1109.5 135.1 reduce-scatter.16
where the time goes:
time: 1260 us; the launch traced here: 1250 us
  waiting for transfers between devices  585 us (46%)
  local copies, waits for them, and re-layouts  217 us (17%)
  matrix products  188 us (15%)
  blocking collectives  152 us (12%)
  other arithmetic  71.6 us (6%)
  starting transfers between devices  21.5 us (2%)
  between operations  15.5 us (1%)
    reduce_scatter x1, waiting for transfers between devices, per_device(): lax.psum_scatter(grad_up_weight, ('seq', 'shard'), scatter_dimension=0, t...  142 us
    reduce_scatter x1, waiting for transfers between devices, per_device(): lax.psum_scatter(grad_down_weight, ('seq', 'shard'), scatter_dimension=0,...  142 us
    unnamed x15, waiting for transfers between devices  132 us
    unnamed x2, blocking collectives  83.2 us
    unnamed x150, local copies, waits for them, and re-layouts  62.4 us
    all_gather x1, waiting for transfers between devices, per_device(): lax.all_gather(query_weight.astype(jnp.bfloat16), ('seq', 'shard'), axis=...  52.2 us
    all_gather x1, waiting for transfers between devices, per_device(): lax.all_gather(key_weight.astype(jnp.bfloat16), ('seq', 'shard'), axis=0,...  49.7 us
    dot_general x6, matrix products, contract_rows(): lax.dot_general(left, right, (((0,), (0,)), ((), ())), preferred_element_...  33.5 us
  transfers between devices with their start and end apart: 17, of which 11 were waited for; matrix products, arithmetic and copies ran while one was open for 33% of the time, Pallas kernels for 0%

commit v1 on v0

v1 whole, which is shorter than its diff:
```python
import jax
import jax.numpy as jnp
from jax import lax
from jax.experimental.layout import Layout, with_layout_constraint
from jax.sharding import PartitionSpec as P


DH = 64
LEN = 1024


EPS = 1e-06
NEG = -1e30
ROOT_HALF = 0.7071067811865476
INV_ROOT_TWO_PI = 0.3989422804014327


def contract_rows(left, right):
    return lax.dot_general(
        left, right, (((0,), (0,)), ((), ())), preferred_element_type=jnp.float32
    )


def times_transpose(left, right):
    return lax.dot_general(
        left, right, (((1,), (1,)), ((), ())), preferred_element_type=jnp.float32
    )


def segment_ids(starts, length):
    places = lax.broadcasted_iota(jnp.int32, (1, length, 1), 1)
    return jnp.sum((starts[:, None, :] <= places).astype(jnp.int32), axis=2)


def norm_forward(rows, gain, shift):
    middle = jnp.mean(rows, axis=-1, keepdims=True)
    centred = rows - middle
    spread = jnp.mean(centred * centred, axis=-1, keepdims=True)
    inverse = lax.rsqrt(spread + EPS)
    normed = centred * inverse
    return (normed * gain + shift, normed, inverse)


def norm_backward(upstream, gain, normed, inverse):
    scaled = upstream * gain
    inner = jnp.mean(scaled, axis=-1, keepdims=True)
    along = jnp.mean(scaled * normed, axis=-1, keepdims=True)
    return inverse * (scaled - inner - normed * along)


def gelu_value(value):
    return 0.5 * value * (1.0 + lax.erf(value * ROOT_HALF))


def gelu_slope(value):
    return (
        0.5 * (1.0 + lax.erf(value * ROOT_HALF))
        + value * jnp.exp(-0.5 * value * value) * INV_ROOT_TWO_PI
    )


def masked_scores(queries, keys, seg_rows, seg_all, scale):
    scores = jnp.einsum("qhd,khd->hqk", queries, keys, preferred_element_type=jnp.float32) * scale
    allowed = seg_rows[:, None] == seg_all[None, :]
    return jnp.where(allowed[None], scores, NEG)


def attend_forward(item):
    qkv, segment = item
    queries, keys, values = qkv[:, 0], qkv[:, 1], qkv[:, 2]
    length, heads, depth = queries.shape
    rows = min(512, length)
    blocks = length // rows
    scale = depth ** (-0.5)

    def one(piece):
        block_q, block_seg = piece
        scores = masked_scores(block_q, keys, block_seg, segment, scale)
        highest = jnp.max(scores, axis=-1, keepdims=True)
        raised = jnp.exp(scores - highest)
        total = jnp.sum(raised, axis=-1, keepdims=True)
        weights = (raised / total).astype(jnp.bfloat16)
        context = jnp.einsum("hqk,khd->qhd", weights, values, preferred_element_type=jnp.float32)
        return (context.astype(jnp.bfloat16), (highest + jnp.log(total))[..., 0])

    context, logsum = lax.map(
        one, (queries.reshape(blocks, rows, heads, depth), segment.reshape(blocks, rows))
    )
    return (context.reshape(length, heads, depth), logsum)


def attend_backward(item):
    qkv, segment, logsum, upstream = item
    queries, keys, values = qkv[:, 0], qkv[:, 1], qkv[:, 2]
    length, heads, depth = queries.shape
    rows = min(512, length)
    blocks = length // rows
    scale = depth ** (-0.5)

    def one(carry, piece):
        key_acc, value_acc = carry
        block_q, block_seg, block_sum, block_up = piece
        scores = masked_scores(block_q, keys, block_seg, segment, scale)
        weights = jnp.exp(scores - block_sum[..., None])
        value_acc = value_acc + jnp.einsum(
            "hqk,qhd->khd",
            weights.astype(jnp.bfloat16),
            block_up,
            preferred_element_type=jnp.float32,
        )
        slope = jnp.einsum("qhd,khd->hqk", block_up, values, preferred_element_type=jnp.float32)
        inner = jnp.sum(weights * slope, axis=-1, keepdims=True)
        score_grad = (weights * (slope - inner)).astype(jnp.bfloat16)
        query_grad = (
            jnp.einsum("hqk,khd->qhd", score_grad, keys, preferred_element_type=jnp.float32) * scale
        )
        key_acc = (
            key_acc
            + jnp.einsum("hqk,qhd->khd", score_grad, block_q, preferred_element_type=jnp.float32)
            * scale
        )
        return ((key_acc, value_acc), query_grad.astype(jnp.bfloat16))

    empty = jnp.zeros((length, heads, depth), jnp.float32)
    pieces = (
        queries.reshape(blocks, rows, heads, depth),
        segment.reshape(blocks, rows),
        logsum,
        upstream.reshape(blocks, rows, heads, depth),
    )
    (key_grad, value_grad), query_grad = lax.scan(one, (empty, empty), pieces)
    return jnp.stack(
        [
            query_grad.reshape(length, heads, depth),
            key_grad.astype(jnp.bfloat16),
            value_grad.astype(jnp.bfloat16),
        ],
        axis=1,
    )


def lane_pick(block, index):
    lanes = lax.broadcasted_iota(jnp.int32, block.shape, 1)
    return jnp.sum(jnp.where(lanes == index, block, 0.0), axis=1)


def pad_lanes(block):
    extra = -block.shape[1] % 256
    block = jnp.pad(block, ((0, 0), (0, extra))) if extra else block
    return with_layout_constraint(block, Layout(major_to_minor=(0, 1)))


def per_device(
    layer_in,
    layer_cotangent,
    doc_starts,
    query_weight,
    key_weight,
    value_weight,
    out_weight,
    up_weight,
    down_weight,
    query_bias,
    value_bias,
    out_bias,
    up_bias,
    down_bias,
    mixer_gain,
    mixer_shift,
    final_gain,
    final_shift,
):
    axes = ("seq", "shard")
    rows, width = query_weight.shape
    ff = up_weight.shape[1]

    def column(vector):
        return vector.reshape(rows, -1)

    packed = jnp.concatenate(
        [
            query_weight,
            key_weight,
            value_weight,
            out_weight,
            up_weight,
            down_weight.reshape(rows, -1),
            column(query_bias),
            column(value_bias),
            column(out_bias),
            column(down_bias),
            column(mixer_gain),
            column(mixer_shift),
            column(final_gain),
            column(final_shift),
            column(up_bias),
        ],
        axis=1,
    ).astype(jnp.bfloat16)
    full = lax.all_gather(packed, axes, axis=0, tiled=True)
    model = full.shape[0]
    full_qkv = full[:, : 3 * width]
    full_out = full[:, 3 * width : 4 * width]
    full_up = full[:, 4 * width : 4 * width + ff]
    full_down = full[:, 4 * width + ff : 4 * width + 2 * ff].reshape(ff, width)
    base = 4 * width + 2 * ff
    bias_query, bias_value, bias_out, bias_down, gain_mixer, shift_mixer, gain_final, shift_final = (
        full[:, base + i].astype(jnp.float32) for i in range(8)
    )
    bias_up = full[:, base + 8 :].reshape(ff).astype(jnp.float32)

    streams, part_len, _ = layer_in.shape
    row_count = streams * part_len
    heads = width // DH
    flat = layer_in.reshape(row_count, width)
    qkv_bias = jnp.concatenate([bias_query, jnp.zeros_like(bias_query), bias_value])
    qkv = (jnp.dot(flat, full_qkv, preferred_element_type=jnp.float32) + qkv_bias).astype(
        jnp.bfloat16
    )
    head_qkv = lax.all_to_all(
        qkv.reshape(streams, part_len, 3, heads, DH), "seq", split_axis=3, concat_axis=1, tiled=True
    )
    segment = segment_ids(doc_starts, LEN)
    context, logsum = lax.map(attend_forward, (head_qkv, segment))
    context_rows = lax.all_to_all(context, "seq", split_axis=1, concat_axis=2, tiled=True).reshape(
        row_count, width
    )
    attn = jnp.dot(context_rows, full_out, preferred_element_type=jnp.float32) + bias_out
    mixed, normed_mixer, inverse_mixer = norm_forward(
        flat.astype(jnp.float32) + attn, gain_mixer, shift_mixer
    )
    upper = mixed.astype(jnp.bfloat16)
    preact = jnp.dot(upper, full_up, preferred_element_type=jnp.float32) + bias_up
    hidden = gelu_value(preact).astype(jnp.bfloat16)
    ffout = jnp.dot(hidden, full_down, preferred_element_type=jnp.float32) + bias_down
    result, normed_final, inverse_final = norm_forward(mixed + ffout, gain_final, shift_final)
    layer_out = result.astype(jnp.bfloat16).reshape(streams, part_len, width)

    upstream = layer_cotangent.reshape(row_count, width).astype(jnp.float32)
    grad_final_gain = jnp.sum(upstream * normed_final, axis=0)
    grad_final_shift = jnp.sum(upstream, axis=0)
    back_final = norm_backward(upstream, gain_final, normed_final, inverse_final)
    back_ffout = back_final.astype(jnp.bfloat16)
    grad_down_weight = contract_rows(hidden, back_ffout)
    grad_down_bias = jnp.sum(back_ffout.astype(jnp.float32), axis=0)
    back_preact = (times_transpose(back_ffout, full_down) * gelu_slope(preact)).astype(jnp.bfloat16)
    grad_up_weight = contract_rows(upper, back_preact)
    grad_up_bias = jnp.sum(back_preact.astype(jnp.float32), axis=0)
    back_mixed = back_final + times_transpose(back_preact, full_up)
    grad_mixer_gain = jnp.sum(back_mixed * normed_mixer, axis=0)
    grad_mixer_shift = jnp.sum(back_mixed, axis=0)
    back_first = norm_backward(back_mixed, gain_mixer, normed_mixer, inverse_mixer)
    back_attn = back_first.astype(jnp.bfloat16)
    grad_out_weight = contract_rows(context_rows, back_attn)
    grad_out_bias = jnp.sum(back_attn.astype(jnp.float32), axis=0)

    early = jnp.concatenate(
        [
            grad_out_weight,
            grad_up_weight,
            grad_down_weight.reshape(model, -1),
            grad_out_bias[:, None],
            grad_down_bias[:, None],
            grad_mixer_gain[:, None],
            grad_mixer_shift[:, None],
            grad_final_gain[:, None],
            grad_final_shift[:, None],
            grad_up_bias.reshape(model, -1),
        ],
        axis=1,
    )
    early = pad_lanes(early)
    early, back_attn = lax.optimization_barrier((early, back_attn))
    early_sum = lax.psum_scatter(early, axes, scatter_dimension=0, tiled=True)

    back_context = times_transpose(back_attn, full_out).astype(jnp.bfloat16)
    head_back = lax.all_to_all(
        back_context.reshape(streams, part_len, heads, DH), "seq", split_axis=2, concat_axis=1, tiled=True
    )
    qkv_back = lax.map(attend_backward, (head_qkv, segment, logsum, head_back))
    rows_back = lax.all_to_all(qkv_back, "seq", split_axis=1, concat_axis=3, tiled=True).reshape(
        row_count, 3 * width
    )
    grad_qkv_weight = contract_rows(flat, rows_back)
    grad_query_bias = jnp.sum(rows_back[:, :width].astype(jnp.float32), axis=0)
    grad_value_bias = jnp.sum(rows_back[:, 2 * width :].astype(jnp.float32), axis=0)
    input_grad = (back_first + times_transpose(rows_back, full_qkv)).reshape(
        streams, part_len, width
    )
    late = pad_lanes(
        jnp.concatenate([grad_qkv_weight, grad_query_bias[:, None], grad_value_bias[:, None]], axis=1)
    )
    late_sum = lax.psum_scatter(late, axes, scatter_dimension=0, tiled=True)

    base = width + 2 * ff
    late_tail = late_sum[:, 3 * width :]
    early_tail = early_sum[:, base:]
    return (
        layer_out,
        input_grad,
        late_sum[:, :width],
        late_sum[:, width : 2 * width],
        late_sum[:, 2 * width : 3 * width],
        early_sum[:, :width],
        early_sum[:, width : width + ff],
        early_sum[:, width + ff : width + 2 * ff].reshape(-1, width),
        lane_pick(late_tail, 0),
        lane_pick(late_tail, 1),
        lane_pick(early_tail, 0),
        jnp.stack([lane_pick(early_tail, 6 + i) for i in range(ff // width)], axis=1).reshape(-1),
        lane_pick(early_tail, 1),
        lane_pick(early_tail, 2),
        lane_pick(early_tail, 3),
        lane_pick(early_tail, 4),
        lane_pick(early_tail, 5),
    )


def solution(mesh):
    in_specs = (
        P("shard", "seq", None),
        P("shard", "seq", None),
        P("shard", None),
        P(("seq", "shard"), None),
        P(("seq", "shard"), None),
        P(("seq", "shard"), None),
        P(("seq", "shard"), None),
        P(("seq", "shard"), None),
        P(("seq", "shard"), None),
        P(("seq", "shard")),
        P(("seq", "shard")),
        P(("seq", "shard")),
        P(("seq", "shard")),
        P(("seq", "shard")),
        P(("seq", "shard")),
        P(("seq", "shard")),
        P(("seq", "shard")),
        P(("seq", "shard")),
    )
    out_specs = (
        P("shard", "seq", None),
        P("shard", "seq", None),
        P(("seq", "shard"), None),
        P(("seq", "shard"), None),
        P(("seq", "shard"), None),
        P(("seq", "shard"), None),
        P(("seq", "shard"), None),
        P(("seq", "shard"), None),
        P(("seq", "shard")),
        P(("seq", "shard")),
        P(("seq", "shard")),
        P(("seq", "shard")),
        P(("seq", "shard")),
        P(("seq", "shard")),
        P(("seq", "shard")),
        P(("seq", "shard")),
        P(("seq", "shard")),
    )

    return jax.shard_map(per_device, mesh=mesh, in_specs=in_specs, out_specs=out_specs, check_vma=False)
```

time: 1260 us -> 1170 us (0.929)
  blocking collectives: 152 us -> 59.1 us
  waiting for transfers between devices: 585 us -> 520 us
  local copies, waits for them, and re-layouts: 217 us -> 259 us
  matrix products: 188 us -> 213 us
    unnamed x15 -> x3, waiting for transfers between devices: 132 us -> 0.71 us
    unnamed x2 -> x0, blocking collectives: 83.2 us -> none
    reduce_scatter x3 -> x2, waiting for transfers between devices: 283 us -> 338 us  [the longest x1 228 us: per_device(): early_sum = lax.psum_scatter(early, axes, scatter_dimension=0, tiled=True)]
    all_to_all x4 -> x2, waiting for transfers between devices: 32.4 us -> 72.1 us  [the longest x1 53.4 us: per_device(): lax.all_to_all(qkv.reshape(streams, part_len, 3, heads, DH), 'seq', split...]
    concatenate x0 -> x3, local copies, waits for them, and re-layouts: none -> 32.4 us  [the longest x1 23.2 us: per_device(): jnp.concatenate([grad_out_weight, grad_up_weight, grad_down_weight.reshap...]
    reshape x12 -> x22, local copies, waits for them, and re-layouts: 14.9 us -> 44.1 us  [the longest x2 16.3 us: per_device(): qkv.reshape(streams, part_len, 3, heads, DH)]
    unnamed x150 -> x66, local copies, waits for them, and re-layouts: 62.4 us -> 39.2 us
    pad x0 -> x2, local copies, waits for them, and re-layouts: none -> 23 us  [pad_lanes(): block = jnp.pad(block, ((0, 0), (0, extra))) if extra else block]
  transfers between devices with their start and end apart: 17 -> 6, of which waited for: 11 -> 6; matrix products, arithmetic and copies ran while one was open for 33% -> 2% of each run, Pallas kernels for 0% -> 0%
where the time goes in v1:
time: 1170 us; the launch traced here: 1160 us
  waiting for transfers between devices  520 us (44%)
  local copies, waits for them, and re-layouts  259 us (22%)
  matrix products  213 us (18%)
  other arithmetic  73.2 us (6%)
  blocking collectives  59.1 us (5%)
  between operations  14.5 us (1%)
  starting transfers between devices  13.3 us (1%)
    reduce_scatter x1, waiting for transfers between devices, per_device(): early_sum = lax.psum_scatter(early, axes, scatter_dimension=0, tiled=True)  228 us
    reduce_scatter x1, waiting for transfers between devices, per_device(): late_sum = lax.psum_scatter(late, axes, scatter_dimension=0, tiled=True)  110 us
    all_gather x1, waiting for transfers between devices, per_device(): full = lax.all_gather(packed, axes, axis=0, tiled=True)  106 us
    all_to_all x1, blocking collectives, per_device(): lax.all_to_all(qkv_back, 'seq', split_axis=1, concat_axis=3, tiled=True)  59.1 us
    all_to_all x1, waiting for transfers between devices, per_device(): lax.all_to_all(qkv.reshape(streams, part_len, 3, heads, DH), 'seq', split...  53.4 us
    unnamed x66, local copies, waits for them, and re-layouts  39.2 us
    dot_general x4, matrix products, times_transpose(): lax.dot_general(left, right, (((1,), (1,)), ((), ())), preferred_element_...  35.1 us
    dot_general x8, matrix products, one(): jnp.einsum('hqk,qhd->khd', weights.astype(jnp.bfloat16), block_up, prefer...  32.2 us
  transfers between devices with their start and end apart: 6, of which 6 were waited for; matrix products, arithmetic and copies ran while one was open for 2% of the time, Pallas kernels for 0%

profile of v1, /device:TPU:0, one launch (start us, length us, event | category | flops | bytes accessed | tf_op | source)
XLA Modules:
  0.0 1155.1 jit_solution(6364122120303369105)
XLA Ops:
  20.7 106.2 %all-gather.2.cloned.1.call-done = bf16[768,9228]{1,0:T(8,128)(2,1)} async-done(((bf16[24,9228]{1,0:T(8,128)(2,1)}), bf16[768,9228]{1,0:T(8,128)(2,1)}) %all-gather.2.cloned.1.call-update) | async-done | bytes 14174224 | tf_op jit(solution)/shard_map/all_gather | solution.py:200
  126.9 3.6 convert_reduce_fusion.7
  130.5 8.2 fusion.50
  138.7 8.9 reshape.336
  147.6 7.5 copy.188
  155.0 5.2 all-to-all-start
  160.5 53.4 %all-to-all-done = bf16[4,256,3,12,64]{1,0,4,2,3:T(4,128)(2,1)} async-done(((bf16[4,256,3,12,64]{1,0,4,2,3:T(4,128)(2,1)}), bf16[4,256,3,12,64]{1,0,4,2,3:T(4,128)(2,1)}, u32[]{:S(2)}, u32[]{:S(2)}) %all-to-all-start) | async-done | bytes 4718624 | tf_op jit(solution)/shard_map/all_to_all | solution.py:220
  214.0 8.6 copy.189
  222.6 8.7 all_to_all.51
  231.3 67.2 %while.50 = (s32[]{:T(128)}, bf16[4,1024,3,64]{3,2,1,0:T(4,128)(2,1)}, f32[4,2,3,512]{3,2,1,0:T(4,128)S(1)}, bf16[4,1024,3,3,64]{1,4,3,2,0:T(8,128)(2,1)}, s32[4...) while((s32[]{:T(128)}, bf16[4,1024,3,64]{3,2,1,0:T(4,128)(2,1)}, f32[4,2,3,512]{3,2,1,0:T(4,128)S(1)}, ...), condition=%wide.region_6.7_spmd, body=%wide.region_1.6_spmd.sunk | while | flops 422148608 | bytes 30794536 | solution.py:224
  234.4 11.6 %while.53 = (s32[]{:T(128)}, bf16[2,512,3,64]{1,3,2,0:T(8,128)(2,1)S(1)}, f32[2,3,512]{2,1,0:T(4,128)S(1)}, s32[2,512]{1,0:T(2,128)S(1)}, s32[1024]{0:T(1024)S(1...) while((s32[]{:T(128)}, ...), condition=%wide.region_5.5_spmd, body=%wide.region_2.4_spmd.sunk | while | flops 422148608 | bytes 22220908 | solution.py:86
  251.1 11.6 %while.53 = (s32[]{:T(128)}, bf16[2,512,3,64]{1,3,2,0:T(8,128)(2,1)S(1)}, f32[2,3,512]{2,1,0:T(4,128)S(1)}, s32[2,512]{1,0:T(2,128)S(1)}, s32[1024]{0:T(1024)S(1...) while((s32[]{:T(128)}, ...), condition=%wide.region_5.5_spmd, body=%wide.region_2.4_spmd.sunk | while | flops 422148608 | bytes 22220908 | solution.py:86
  267.8 11.6 %while.53 = (s32[]{:T(128)}, bf16[2,512,3,64]{1,3,2,0:T(8,128)(2,1)S(1)}, f32[2,3,512]{2,1,0:T(4,128)S(1)}, s32[2,512]{1,0:T(2,128)S(1)}, s32[1024]{0:T(1024)S(1...) while((s32[]{:T(128)}, ...), condition=%wide.region_5.5_spmd, body=%wide.region_2.4_spmd.sunk | while | flops 422148608 | bytes 22220908 | solution.py:86
  284.5 11.6 %while.53 = (s32[]{:T(128)}, bf16[2,512,3,64]{1,3,2,0:T(8,128)(2,1)S(1)}, f32[2,3,512]{2,1,0:T(4,128)S(1)}, s32[2,512]{1,0:T(2,128)S(1)}, s32[1024]{0:T(1024)S(1...) while((s32[]{:T(128)}, ...), condition=%wide.region_5.5_spmd, body=%wide.region_2.4_spmd.sunk | while | flops 422148608 | bytes 22220908 | solution.py:86
  299.8 6.2 copy.216
  306.0 3.3 reshape.383
  309.3 4.3 all-to-all-start.1
  315.5 4.8 slice.125
  320.3 8.6 reshape.338
  332.8 3.8 reshape.384
  336.6 3.8 copy.192
  342.4 3.5 fusion.85
  346.6 11.3 multiply_convert_fusion.1
  358.0 5.4 fusion.86
  366.6 2.9 convert_reduce_fusion.4
  371.2 7.8 fusion.74
  379.0 11.5 reshape.340
  390.4 14.8 %convert_reduce_fusion = (f32[3072]{0:T(1024)}, bf16[1024,3072]{1,0:T(8,128)(2,1)S(1)}) fusion(f32[1024,3072]{1,0:T(8,128)} %get-tuple-element.440, f32[3072]{0:T(1024)} %reshape.352, bf16[3072,768]{1,0:T(8,128)(2,1)} %reshape.338, f32[1024,768]{1,0:T(8,128)} %copy-done.17), kind=kOutput, calls=%fused_computation.75 | convolution fusion | flops 4873516032 | bytes 26763264 | tf_op jit(solution)/shard_map/dot_general | solution.py:25
  405.3 8.5 fusion.77
  413.8 8.4 multiply_reduce_fusion.1
  430.9 23.2 %concatenate.15 = f32[768,6922]{1,0:T(8,128)} concatenate(f32[768,768]{1,0:T(8,128)S(1)} %fusion.87, f32[768,3072]{1,0:T(8,128)} %fusion.77, f32[768,3072]{1,0:T(8,128)} %reshape.340, f32[768,1]{1,0:T(8,128)S(1)} %broadcast_in_dim.137, f32[768,1]{1,0:T(8,128)} %broadcast_in_dim.138, f32[768,1]{1,0:T(8,128)S(1)} %broadcast_in_dim.139, f32[768,1]{1,0:T(8,128)} %broadcast_in_dim.140, ...), dimensions={1} | concatenate | bytes 42528768 | tf_op jit(solution)/shard_map/concatenate | solution.py:257
  454.1 15.7 %pad.8 = f32[768,7168]{1,0:T(8,128)} pad(f32[768,6922]{1,0:T(8,128)} %concatenate.15, f32[]{:T(128)} %constant.73.clone.1), padding=0_0x0_246 | pad | bytes 43284484 | tf_op jit(solution)/shard_map/jit(_pad)/pad | solution.py:149
  475.7 3.6 all-to-all-start.2
  479.3 18.7 %all-to-all-done.2 = bf16[4,256,12,64]{1,0,3,2:T(4,128)(2,1)S(1)} async-done(((bf16[4,256,12,64]{1,0,3,2:T(4,128)(2,1)}), bf16[4,256,12,64]{1,0,3,2:T(4,128)(2,1)S(1)}, u32[]{:S(2)}, u32[]{:S(2)}) %all-to-all-start.2) | async-done | bytes 1572896 | tf_op jit(solution)/shard_map/all_to_all | solution.py:277
  498.4 156.6 %while.52 = (s32[]{:T(128)}, bf16[4,1024,3,3,64]{1,4,3,2,0:T(8,128)(2,1)}, bf16[4,1024,3,3,64]{1,4,3,2,0:T(8,128)(2,1)}, s32[4,1024]{1,0:T(4,128)}, f32[4,2,3,51...) while((s32[]{:T(128)}, ...), condition=%wide.region_26.27_spmd, body=%wide.region_22.26_spmd.sunk | while | flops 1035860480 | bytes 146281280 | solution.py:280
  504.3 29.2 %while.54 = (s32[]{:T(128)}, f32[1024,3,64]{0,2,1:T(8,128)}, f32[1024,3,64]{0,2,1:T(8,128)}, bf16[2,512,3,64]{1,3,2,0:T(8,128)(2,1)}, bf16[2,512,3,64]{1,3,2,0:T...) while((s32[]{:T(128)}, f32[1024,3,64]{0,2,1:T(8,128)}, ...), condition=%wide.region_25.25_spmd.clone, body=%wide.region_23.24_spmd.clone.sunk | while | flops 1031928320 | bytes 118710280 | solution.py:131
  514.7 3.9 fusion.144
  524.5 3.0 fusion.143
  529.3 4.2 fusion.144
  543.3 29.2 %while.54 = (s32[]{:T(128)}, f32[1024,3,64]{0,2,1:T(8,128)}, f32[1024,3,64]{0,2,1:T(8,128)}, bf16[2,512,3,64]{1,3,2,0:T(8,128)(2,1)}, bf16[2,512,3,64]{1,3,2,0:T...) while((s32[]{:T(128)}, f32[1024,3,64]{0,2,1:T(8,128)}, ...), condition=%wide.region_25.25_spmd.clone, body=%wide.region_23.24_spmd.clone.sunk | while | flops 1031928320 | bytes 118710280 | solution.py:131
  549.2 2.7 fusion.143
  553.7 3.9 fusion.144
  563.5 3.0 fusion.143
  568.3 4.2 fusion.144
  582.4 29.2 %while.54 = (s32[]{:T(128)}, f32[1024,3,64]{0,2,1:T(8,128)}, f32[1024,3,64]{0,2,1:T(8,128)}, bf16[2,512,3,64]{1,3,2,0:T(8,128)(2,1)}, bf16[2,512,3,64]{1,3,2,0:T...) while((s32[]{:T(128)}, f32[1024,3,64]{0,2,1:T(8,128)}, ...), condition=%wide.region_25.25_spmd.clone, body=%wide.region_23.24_spmd.clone.sunk | while | flops 1031928320 | bytes 118710280 | solution.py:131
  592.8 3.9 fusion.144
  602.6 3.0 fusion.143
  607.4 4.2 fusion.144
  621.5 29.2 %while.54 = (s32[]{:T(128)}, f32[1024,3,64]{0,2,1:T(8,128)}, f32[1024,3,64]{0,2,1:T(8,128)}, bf16[2,512,3,64]{1,3,2,0:T(8,128)(2,1)}, bf16[2,512,3,64]{1,3,2,0:T...) while((s32[]{:T(128)}, f32[1024,3,64]{0,2,1:T(8,128)}, ...), condition=%wide.region_25.25_spmd.clone, body=%wide.region_23.24_spmd.clone.sunk | while | flops 1031928320 | bytes 118710280 | solution.py:131
  631.8 3.9 fusion.144
  641.6 3.0 fusion.143
  646.4 4.2 fusion.144
  655.1 14.2 %copy.203 = bf16[4,1024,3,3,64]{4,0,3,2,1:T(4,128)(2,1)} copy(bf16[4,1024,3,3,64]{1,4,3,2,0:T(8,128)(2,1)} %get-tuple-element.184) | data formatting | bytes 9437184 | tf_op jit(solution)/shard_map/while | solution.py:280
  669.3 10.3 reshape.385
  679.7 59.1 %all_to_all.66 = bf16[4,2,294912]{2,1,0:T(2,128)(2,1)} all-to-all(bf16[4,2,294912]{2,1,0:T(2,128)(2,1)} %reshape.385), channel_id=1, replica_groups=mesh['seq'=4,'shard'=8] {'seq'}, dimensions={0} | all-to-all | bytes 9437184 | tf_op jit(solution)/shard_map/all_to_all | solution.py:281
  738.8 10.2 reshape.386
  749.0 15.1 %copy.204 = bf16[4,4,256,3,3,64]{2,0,5,4,1,3:T(4,128)(2,1)} copy(bf16[4,4,256,3,3,64]{5,0,4,3,2,1:T(4,128)(2,1)} %bitcast.251) | data formatting | bytes 9437184 | tf_op jit(solution)/shard_map/all_to_all | solution.py:281
  764.1 4.0 copy.214
  768.1 6.2 convolution_bitcast_fusion
  775.1 8.3 concatenate.16
  783.4 7.3 pad.9
  792.6 9.2 fusion.69
  801.9 110.1 %reduce-scatter.3.cloned.1.call-done = f32[24,2560]{1,0:T(8,128)} async-done(((f32[768,2560]{1,0:T(8,128)}), f32[24,2560]{1,0:T(8,128)}) %reduce-scatter.3.cloned.1.call-update) | async-done | bytes 245776 | tf_op jit(solution)/shard_map/reduce_scatter | solution.py:293
  913.6 228.3 %reduce-scatter.5.cloned.1.call-done = f32[24,7168]{1,0:T(8,128)} async-done(((f32[768,7168]{1,0:T(8,128)}), f32[24,7168]{1,0:T(8,128)}) %reduce-scatter.5.cloned.1.call-update) | async-done | bytes 688144 | tf_op jit(solution)/shard_map/reduce_scatter | solution.py:274
  (579 shorter events, 227.8 us)
Async XLA Ops:
  7.2 123.3 %copy-start.38 = (bf16[4,256,768]{2,1,0:T(8,128)(2,1)S(1)}, bf16[4,256,768]{2,1,0:T(8,128)(2,1)}, u32[]{:S(2)}) copy-start(bf16[4,256,768]{2,1,0:T(8,128)(2,1)} %param.26) | copy-start | bytes 4718596
  7.2 119.7 %all-gather.2.cloned.1.call-start = ((), (), s32[]{:S(2)}) async-start(), calls=%async_computation.6 | async-start | bytes 14800896 | tf_op jit(solution)/shard_map/all_gather | solution.py:200
  155.0 5.3 copy-start.37
  155.0 58.9 %all-to-all-start = ((bf16[4,256,3,12,64]{1,0,4,2,3:T(4,128)(2,1)}), bf16[4,256,3,12,64]{1,0,4,2,3:T(4,128)(2,1)}, u32[]{:S(2)}, u32[]{:S(2)}) async-start(bf16[4,256,3,12,64]{1,0,4,2,3:T(4,128)(2,1)} %copy.188), calls=%async_computation | async-start | bytes 9437184 | tf_op jit(solution)/shard_map/all_to_all | solution.py:220
  309.3 23.5 %all-to-all-start.1 = ((bf16[4,2,98304]{2,1,0:T(2,128)(2,1)}), bf16[4,2,98304]{2,1,0:T(2,128)(2,1)}, u32[]{:S(2)}, u32[]{:S(2)}) async-start(bf16[4,2,98304]{2,1,0:T(2,128)(2,1)} %reshape.383), calls=%async_computation.1 | async-start | bytes 3145728 | tf_op jit(solution)/shard_map/all_to_all | solution.py:225
  320.3 8.6 copy-start.10
  320.3 8.6 copy-start.27
  336.6 5.8 copy-start.36
  345.9 12.0 %slice-start = ((s8[4718592]{0:T(1024)(128)(4,1)}), s8[4194304]{0:T(1024)(128)(4,1)S(1)}, s32[]{:S(2)}) async-start(s8[4718592]{0:T(1024)(128)(4,1)} %bitcast.263), calls=%async_computation.9 | async-start | bytes 8388608
  346.6 11.3 slice-start.1
  346.6 11.3 copy-start.35
  390.4 14.8 %copy-start.29 = (f32[768]{0:T(1024)S(1)}, f32[768]{0:T(1024)}, u32[]{:S(2)}) copy-start(f32[768]{0:T(1024)} %get-tuple-element.320) | copy-start | bytes 9220
  405.3 8.5 copy-start.18
  424.5 4.6 copy-start.31
  424.5 5.5 copy-start.33
  454.1 15.7 %copy-start.21 = (bf16[1024,768]{1,0:T(8,128)(2,1)S(1)}, bf16[1024,768]{1,0:T(8,128)(2,1)}, u32[]{:S(2)}) copy-start(bf16[1024,768]{1,0:T(8,128)(2,1)} %copy-done.20) | copy-start | bytes 4718596
  475.7 22.3 %all-to-all-start.2 = ((bf16[4,256,12,64]{1,0,3,2:T(4,128)(2,1)}), bf16[4,256,12,64]{1,0,3,2:T(4,128)(2,1)S(1)}, u32[]{:S(2)}, u32[]{:S(2)}) async-start(bf16[4,256,12,64]{1,0,3,2:T(4,128)(2,1)} %reshape.342), calls=%async_computation.2 | async-start | bytes 3145728 | tf_op jit(solution)/shard_map/all_to_all | solution.py:277
  479.2 432.7 %reduce-scatter.3.cloned.1.call-start = ((), (), s32[]{:S(2)}) async-start(), calls=%async_computation.7 | async-start | bytes 8110080 | tf_op jit(solution)/shard_map/reduce_scatter | solution.py:293
  498.9 4.3 copy-start.13
  510.2 4.5 copy-start.1
  514.6 3.9 copy-start.5
  514.6 3.9 copy-start.7
  514.7 3.9 copy-start.9
  524.5 4.8 copy-start.1
  529.2 4.2 copy-start.5
  529.2 4.2 copy-start.7
  529.2 4.2 copy-start.9
  529.3 4.2 copy-start.16
  533.5 4.5 copy-start.14
  537.9 4.3 copy-start.13
  549.2 4.5 copy-start.1
  553.7 3.9 copy-start.5
  553.7 3.9 copy-start.7
  553.7 3.9 copy-start.9
  563.5 4.8 copy-start.1
  568.3 4.2 copy-start.5
  568.3 4.2 copy-start.7
  568.3 4.2 copy-start.9
  568.3 4.2 copy-start.16
  572.5 4.5 copy-start.14
  577.0 4.3 copy-start.13
  588.3 4.5 copy-start.1
  592.7 3.9 copy-start.5
  592.7 3.9 copy-start.7
  592.8 3.9 copy-start.9
  602.6 4.8 copy-start.1
  607.3 4.2 copy-start.5
  607.3 4.2 copy-start.7
  607.3 4.2 copy-start.9
  607.3 4.2 copy-start.16
  611.6 4.5 copy-start.14
  616.0 4.3 copy-start.13
  627.3 4.5 copy-start.1
  631.8 3.9 copy-start.5
  631.8 3.9 copy-start.7
  641.6 4.8 copy-start.1
  646.4 4.2 copy-start.5
  646.4 4.2 copy-start.7
  646.4 4.2 copy-start.9
  646.4 4.2 copy-start.16
  650.6 4.4 copy-start.14
  764.1 4.0 copy-start.40
  768.0 6.2 copy-start.12
  790.8 351.2 %reduce-scatter.5.cloned.1.call-start = ((), (), s32[]{:S(2)}) async-start(), calls=%async_computation.8 | async-start | bytes 22708224 | tf_op jit(solution)/shard_map/reduce_scatter | solution.py:274
  (75 other events, 145.1 us)
Sparse Core Ops, SparseCore 0:
  20.8 105.9 all-gather.1
  790.9 121.0 reduce-scatter.2
  918.4 223.5 reduce-scatter.4

commit v2 on v1

--- a/solution.py
+++ b/solution.py
@@ -144,9 +144,12 @@
     return jnp.sum(jnp.where(lanes == index, block, 0.0), axis=1)
 
 
-def pad_lanes(block):
-    extra = -block.shape[1] % 256
-    block = jnp.pad(block, ((0, 0), (0, extra))) if extra else block
+def pack_lanes(pieces):
+    pieces = [p.astype(jnp.bfloat16) for p in pieces]
+    extra = -sum(p.shape[1] for p in pieces) % 256
+    if extra:
+        pieces.append(jnp.zeros((pieces[0].shape[0], extra), jnp.bfloat16))
+    block = jnp.concatenate(pieces, axis=1)
     return with_layout_constraint(block, Layout(major_to_minor=(0, 1)))
 
 
@@ -177,14 +180,11 @@
     def column(vector):
         return vector.reshape(rows, -1)
 
-    packed = jnp.concatenate(
+    first = jnp.concatenate(
         [
             query_weight,
             key_weight,
             value_weight,
-            out_weight,
-            up_weight,
-            down_weight.reshape(rows, -1),
             column(query_bias),
             column(value_bias),
             column(out_bias),
@@ -197,17 +197,21 @@
         ],
         axis=1,
     ).astype(jnp.bfloat16)
-    full = lax.all_gather(packed, axes, axis=0, tiled=True)
-    model = full.shape[0]
-    full_qkv = full[:, : 3 * width]
-    full_out = full[:, 3 * width : 4 * width]
-    full_up = full[:, 4 * width : 4 * width + ff]
-    full_down = full[:, 4 * width + ff : 4 * width + 2 * ff].reshape(ff, width)
-    base = 4 * width + 2 * ff
+    second = jnp.concatenate(
+        [out_weight, up_weight, down_weight.reshape(rows, -1)], axis=1
+    ).astype(jnp.bfloat16)
+    full_first = lax.all_gather(first, axes, axis=0, tiled=True)
+    full_second = lax.all_gather(second, axes, axis=0, tiled=True)
+    model = full_first.shape[0]
+    full_qkv = full_first[:, : 3 * width]
+    full_out = full_second[:, :width]
+    full_up = full_second[:, width : width + ff]
+    full_down = full_second[:, width + ff : width + 2 * ff].reshape(ff, width)
+    base = 3 * width
     bias_query, bias_value, bias_out, bias_down, gain_mixer, shift_mixer, gain_final, shift_final = (
-        full[:, base + i].astype(jnp.float32) for i in range(8)
-    )
-    bias_up = full[:, base + 8 :].reshape(ff).astype(jnp.float32)
+        full_first[:, base + i].astype(jnp.float32) for i in range(8)
+    )
+    bias_up = full_first[:, base + 8 :].reshape(ff).astype(jnp.float32)
 
     streams, part_len, _ = layer_in.shape
     row_count = streams * part_len
@@ -254,7 +258,7 @@
     grad_out_weight = contract_rows(context_rows, back_attn)
     grad_out_bias = jnp.sum(back_attn.astype(jnp.float32), axis=0)
 
-    early = jnp.concatenate(
+    early = pack_lanes(
         [
             grad_out_weight,
             grad_up_weight,
@@ -266,12 +270,10 @@
             grad_final_gain[:, None],
             grad_final_shift[:, None],
             grad_up_bias.reshape(model, -1),
-        ],
-        axis=1,
-    )
-    early = pad_lanes(early)
+        ]
+    )
     early, back_attn = lax.optimization_barrier((early, back_attn))
-    early_sum = lax.psum_scatter(early, axes, scatter_dimension=0, tiled=True)
+    early_sum = lax.psum_scatter(early, axes, scatter_dimension=0, tiled=True).astype(jnp.float32)
 
     back_context = times_transpose(back_attn, full_out).astype(jnp.bfloat16)
     head_back = lax.all_to_all(
@@ -287,10 +289,8 @@
     input_grad = (back_first + times_transpose(rows_back, full_qkv)).reshape(
         streams, part_len, width
     )
-    late = pad_lanes(
-        jnp.concatenate([grad_qkv_weight, grad_query_bias[:, None], grad_value_bias[:, None]], axis=1)
-    )
-    late_sum = lax.psum_scatter(late, axes, scatter_dimension=0, tiled=True)
+    late = pack_lanes([grad_qkv_weight, grad_query_bias[:, None], grad_value_bias[:, None]])
+    late_sum = lax.psum_scatter(late, axes, scatter_dimension=0, tiled=True).astype(jnp.float32)
 
     base = width + 2 * ff
     late_tail = late_sum[:, 3 * width :]

time: 1170 us -> 1010 us (0.86)
  waiting for transfers between devices: 520 us -> 399 us
  local copies, waits for them, and re-layouts: 259 us -> 229 us
    reduce_scatter x2, waiting for transfers between devices: 338 us -> 237 us  [the longest x1 146 us: per_device(): lax.psum_scatter(early, axes, scatter_dimension=0, tiled=True)]
    all_gather x1 -> x2, waiting for transfers between devices: 106 us -> 63.6 us  [the longest x1 63.6 us: per_device(): full_first = lax.all_gather(first, axes, axis=0, tiled=True)]
    pad x2 -> x0, local copies, waits for them, and re-layouts: 23 us -> none  [pad_lanes(): block = jnp.pad(block, ((0, 0), (0, extra))) if extra else block]
    convert_element_type x1 -> x11, local copies, waits for them, and re-layouts: 0.82 us -> 16 us  [the longest x10 15.8 us: pack_lanes(): pieces = [p.astype(jnp.bfloat16) for p in pieces]]
    reshape x3 -> x1, local copies, waits for them, and re-layouts: 21.9 us -> 8.48 us  [per_device(): full_down = full_second[:, width + ff:width + 2 * ff].reshape(ff, width)]
    all_to_all x1, waiting for transfers between devices: 2.35 us -> 15.3 us  [per_device(): lax.all_to_all(context, 'seq', split_axis=1, concat_axis=2, tiled=True)]
    unnamed x66 -> x62, local copies, waits for them, and re-layouts: 39.2 us -> 39.3 us
  transfers between devices with their start and end apart: 6 -> 7, of which waited for: 6 -> 6; matrix products, arithmetic and copies ran while one was open for 2% -> 11% of each run, Pallas kernels for 0% -> 0%
where the time goes in v2:
time: 1010 us; the launch traced here: 1000 us
  waiting for transfers between devices  399 us (40%)
  local copies, waits for them, and re-layouts  229 us (23%)
  matrix products  210 us (21%)
  other arithmetic  72.6 us (7%)
  blocking collectives  59.2 us (6%)
  between operations  14.5 us (1%)
  starting transfers between devices  12.9 us (1%)
    reduce_scatter x1, waiting for transfers between devices, per_device(): lax.psum_scatter(early, axes, scatter_dimension=0, tiled=True)  146 us
    reduce_scatter x1, waiting for transfers between devices, per_device(): lax.psum_scatter(late, axes, scatter_dimension=0, tiled=True)  90.5 us
    all_to_all x1, waiting for transfers between devices, per_device(): lax.all_to_all(qkv.reshape(streams, part_len, 3, heads, DH), 'seq', split...  64.1 us
    all_gather x1, waiting for transfers between devices, per_device(): full_first = lax.all_gather(first, axes, axis=0, tiled=True)  63.6 us
    all_to_all x1, blocking collectives, per_device(): lax.all_to_all(qkv_back, 'seq', split_axis=1, concat_axis=3, tiled=True)  59.2 us
    unnamed x62, local copies, waits for them, and re-layouts  39.3 us
    dot_general x4, matrix products, times_transpose(): lax.dot_general(left, right, (((1,), (1,)), ((), ())), preferred_element_...  32.9 us
    dot_general x8, matrix products, one(): jnp.einsum('hqk,qhd->khd', weights.astype(jnp.bfloat16), block_up, prefer...  32.1 us
  transfers between devices with their start and end apart: 7, of which 6 were waited for; matrix products, arithmetic and copies ran while one was open for 11% of the time, Pallas kernels for 0%

profile of v2, /device:TPU:0, one launch (start us, length us, event | category | flops | bytes accessed | tf_op | source)
XLA Modules:
  0.0 1000.6 jit_solution(7303467579804249140)
XLA Ops:
  17.5 63.6 %all-gather.3.cloned.1.call-done = bf16[768,2316]{1,0:T(8,128)(2,1)} async-done(((bf16[24,2316]{1,0:T(8,128)(2,1)}), bf16[768,2316]{1,0:T(8,128)(2,1)}) %all-gather.3.cloned.1.call-update) | async-done | bytes 3557392 | tf_op jit(solution)/shard_map/all_gather | solution.py:203
  81.1 3.6 convert_reduce_fusion.1
  84.8 9.1 fusion.50
  93.9 8.9 reshape.405
  102.7 7.5 copy.188
  110.2 5.1 all-to-all-start
  116.8 64.1 %all-to-all-done = bf16[4,256,3,12,64]{1,0,4,2,3:T(4,128)(2,1)} async-done(((bf16[4,256,3,12,64]{1,0,4,2,3:T(4,128)(2,1)}), bf16[4,256,3,12,64]{1,0,4,2,3:T(4,128)(2,1)}, u32[]{:S(2)}, u32[]{:S(2)}) %all-to-all-start) | async-done | bytes 4718624 | tf_op jit(solution)/shard_map/all_to_all | solution.py:224
  180.8 8.7 copy.189
  189.6 8.8 all_to_all.51
  198.4 67.0 %while.50 = (s32[]{:T(128)}, bf16[4,1024,3,64]{3,2,1,0:T(4,128)(2,1)}, f32[4,2,3,512]{3,2,1,0:T(4,128)S(1)}, bf16[4,1024,3,3,64]{1,4,3,2,0:T(8,128)(2,1)}, s32[4...) while((s32[]{:T(128)}, bf16[4,1024,3,64]{3,2,1,0:T(4,128)(2,1)}, f32[4,2,3,512]{3,2,1,0:T(4,128)S(1)}, ...), condition=%wide.region_6.7_spmd, body=%wide.region_1.6_spmd.sunk | while | flops 422148608 | bytes 30794536 | solution.py:228
  201.5 11.6 %while.53 = (s32[]{:T(128)}, bf16[2,512,3,64]{1,3,2,0:T(8,128)(2,1)S(1)}, f32[2,3,512]{2,1,0:T(4,128)S(1)}, s32[2,512]{1,0:T(2,128)S(1)}, s32[1024]{0:T(1024)S(1...) while((s32[]{:T(128)}, ...), condition=%wide.region_5.5_spmd, body=%wide.region_2.4_spmd.sunk | while | flops 422148608 | bytes 22220908 | solution.py:86
  218.2 11.6 %while.53 = (s32[]{:T(128)}, bf16[2,512,3,64]{1,3,2,0:T(8,128)(2,1)S(1)}, f32[2,3,512]{2,1,0:T(4,128)S(1)}, s32[2,512]{1,0:T(2,128)S(1)}, s32[1024]{0:T(1024)S(1...) while((s32[]{:T(128)}, ...), condition=%wide.region_5.5_spmd, body=%wide.region_2.4_spmd.sunk | while | flops 422148608 | bytes 22220908 | solution.py:86
  234.9 11.6 %while.53 = (s32[]{:T(128)}, bf16[2,512,3,64]{1,3,2,0:T(8,128)(2,1)S(1)}, f32[2,3,512]{2,1,0:T(4,128)S(1)}, s32[2,512]{1,0:T(2,128)S(1)}, s32[1024]{0:T(1024)S(1...) while((s32[]{:T(128)}, ...), condition=%wide.region_5.5_spmd, body=%wide.region_2.4_spmd.sunk | while | flops 422148608 | bytes 22220908 | solution.py:86
  251.7 11.6 %while.53 = (s32[]{:T(128)}, bf16[2,512,3,64]{1,3,2,0:T(8,128)(2,1)S(1)}, f32[2,3,512]{2,1,0:T(4,128)S(1)}, s32[2,512]{1,0:T(2,128)S(1)}, s32[1024]{0:T(1024)S(1...) while((s32[]{:T(128)}, ...), condition=%wide.region_5.5_spmd, body=%wide.region_2.4_spmd.sunk | while | flops 422148608 | bytes 22220908 | solution.py:86
  265.4 7.9 copy.216
  273.3 5.1 reshape.451
  278.5 3.9 all-to-all-start.1
  285.2 15.3 %all-to-all-done.1 = bf16[4,2,98304]{2,1,0:T(2,128)(2,1)S(1)} async-done(((bf16[4,2,98304]{2,1,0:T(2,128)(2,1)}), bf16[4,2,98304]{2,1,0:T(2,128)(2,1)S(1)}, u32[]{:S(2)}, u32[]{:S(2)}) %all-to-all-start.1) | async-done | bytes 1572896 | tf_op jit(solution)/shard_map/all_to_all | solution.py:229
  300.5 3.3 reshape.452
  303.8 4.8 copy.192
  310.0 3.9 fusion.85
  316.2 4.9 slice.125
  321.0 8.5 reshape.408
  329.5 12.7 %multiply_convert_fusion.1 = (bf16[1024,3072]{1,0:T(8,128)(2,1)S(1)}, f32[1024,3072]{1,0:T(8,128)}) fusion(f32[3072]{0:T(1024)S(1)} %reshape.420, bf16[768,6912]{1,0:T(8,128)(2,1)} %all-gather.5.cloned.1.call-done, f32[1024,768]{1,0:T(8,128)} %copy-done.12, f32[768]{0:T(1024)S(1)} %copy-done.36, f32[768]{0:T(1024)S(1)} %copy-done.31, ...), kind=kOutput, calls=%fused_computation.75 | convolution fusion | flops 4854644736 | bytes 26765312 | tf_op jit(solution)/shard_map/dot_general | solution.py:237
  342.3 5.5 fusion.86
  348.4 3.3 fusion.62
  355.1 7.0 convolution_convert_fusion
  362.2 8.6 convert_element_type.323
  370.8 12.8 %fusion.87 = (bf16[3072]{0:T(1024)(128)(2,1)}, bf16[1024,3072]{1,0:T(8,128)(2,1)S(1)}) fusion(f32[1024,3072]{1,0:T(8,128)} %get-tuple-element.438, f32[3072]{0:T(1024)S(1)} %reshape.420, bf16[3072,768]{1,0:T(8,128)(2,1)} %reshape.408, f32[1024,768]{1,0:T(8,128)S(1)} %copy-done.22), kind=kOutput, calls=%fused_computation.183 | convolution fusion | flops 4870370304 | bytes 26757120 | tf_op jit(solution)/shard_map/dot_general | solution.py:25
  383.6 7.9 convolution_convert_fusion.1
  391.4 8.3 multiply_reduce_fusion.1
  408.3 17.8 %concatenate.20 = bf16[768,7168]{1,0:T(8,128)(2,1)} concatenate(bf16[768,768]{1,0:T(8,128)(2,1)S(1)} %convolution_convert_fusion.4, bf16[768,3072]{1,0:T(8,128)(2,1)} %convolution_convert_fusion.1, bf16[768,3072]{1,0:T(8,128)(2,1)} %convert_element_type.323, bf16[768,1]{1,0:T(8,128)(2,1)S(1)} %convert_element_type.355, bf16[768,1]{1,0:T(8,128)(2,1)} %convert_element_type.356, ...), dimensions={1} | concatenate | bytes 22020096 | tf_op jit(solution)/shard_map/concatenate | solution.py:152
  426.1 2.7 convolution_convert_fusion.3
  432.0 3.6 all-to-all-start.2
  435.6 18.7 %all-to-all-done.2 = bf16[4,256,12,64]{1,0,3,2:T(4,128)(2,1)S(1)} async-done(((bf16[4,256,12,64]{1,0,3,2:T(4,128)(2,1)}), bf16[4,256,12,64]{1,0,3,2:T(4,128)(2,1)S(1)}, u32[]{:S(2)}, u32[]{:S(2)}) %all-to-all-start.2) | async-done | bytes 1572896 | tf_op jit(solution)/shard_map/all_to_all | solution.py:279
  454.8 156.3 %while.52 = (s32[]{:T(128)}, bf16[4,1024,3,3,64]{1,4,3,2,0:T(8,128)(2,1)}, bf16[4,1024,3,3,64]{1,4,3,2,0:T(8,128)(2,1)}, s32[4,1024]{1,0:T(4,128)}, f32[4,2,3,51...) while((s32[]{:T(128)}, ...), condition=%wide.region_26.27_spmd, body=%wide.region_22.26_spmd.sunk | while | flops 1035860480 | bytes 146281280 | solution.py:282
  460.6 29.1 %while.54 = (s32[]{:T(128)}, f32[1024,3,64]{0,2,1:T(8,128)}, f32[1024,3,64]{0,2,1:T(8,128)}, bf16[2,512,3,64]{1,3,2,0:T(8,128)(2,1)}, bf16[2,512,3,64]{1,3,2,0:T...) while((s32[]{:T(128)}, f32[1024,3,64]{0,2,1:T(8,128)}, ...), condition=%wide.region_25.25_spmd.clone, body=%wide.region_23.24_spmd.clone.sunk | while | flops 1031928320 | bytes 118710280 | solution.py:131
  471.0 3.9 fusion.144
  480.8 3.0 fusion.143
  485.5 4.2 fusion.144
  499.6 29.1 %while.54 = (s32[]{:T(128)}, f32[1024,3,64]{0,2,1:T(8,128)}, f32[1024,3,64]{0,2,1:T(8,128)}, bf16[2,512,3,64]{1,3,2,0:T(8,128)(2,1)}, bf16[2,512,3,64]{1,3,2,0:T...) while((s32[]{:T(128)}, f32[1024,3,64]{0,2,1:T(8,128)}, ...), condition=%wide.region_25.25_spmd.clone, body=%wide.region_23.24_spmd.clone.sunk | while | flops 1031928320 | bytes 118710280 | solution.py:131
  505.5 2.7 fusion.143
  509.9 3.9 fusion.144
  519.7 3.0 fusion.143
  524.5 4.2 fusion.144
  538.6 29.1 %while.54 = (s32[]{:T(128)}, f32[1024,3,64]{0,2,1:T(8,128)}, f32[1024,3,64]{0,2,1:T(8,128)}, bf16[2,512,3,64]{1,3,2,0:T(8,128)(2,1)}, bf16[2,512,3,64]{1,3,2,0:T...) while((s32[]{:T(128)}, f32[1024,3,64]{0,2,1:T(8,128)}, ...), condition=%wide.region_25.25_spmd.clone, body=%wide.region_23.24_spmd.clone.sunk | while | flops 1031928320 | bytes 118710280 | solution.py:131
  548.9 3.9 fusion.144
  558.7 3.0 fusion.143
  563.5 4.2 fusion.144
  577.5 29.1 %while.54 = (s32[]{:T(128)}, f32[1024,3,64]{0,2,1:T(8,128)}, f32[1024,3,64]{0,2,1:T(8,128)}, bf16[2,512,3,64]{1,3,2,0:T(8,128)(2,1)}, bf16[2,512,3,64]{1,3,2,0:T...) while((s32[]{:T(128)}, f32[1024,3,64]{0,2,1:T(8,128)}, ...), condition=%wide.region_25.25_spmd.clone, body=%wide.region_23.24_spmd.clone.sunk | while | flops 1031928320 | bytes 118710280 | solution.py:131
  587.9 3.9 fusion.144
  597.7 3.0 fusion.143
  602.5 4.2 fusion.144
  611.1 14.3 %copy.203 = bf16[4,1024,3,3,64]{4,0,3,2,1:T(4,128)(2,1)} copy(bf16[4,1024,3,3,64]{1,4,3,2,0:T(8,128)(2,1)} %get-tuple-element.184) | data formatting | bytes 9437184 | tf_op jit(solution)/shard_map/while | solution.py:282
  625.4 10.4 %reshape.453 = bf16[4,2,294912]{2,1,0:T(2,128)(2,1)} reshape(bf16[1024,3,3,4,64]{4,3,2,1,0:T(4,128)(2,1)} %bitcast.250) | data formatting | bytes 9437184
  635.7 59.2 %all_to_all.66 = bf16[4,2,294912]{2,1,0:T(2,128)(2,1)} all-to-all(bf16[4,2,294912]{2,1,0:T(2,128)(2,1)} %reshape.453), channel_id=1, replica_groups=mesh['seq'=4,'shard'=8] {'seq'}, dimensions={0} | all-to-all | bytes 9437184 | tf_op jit(solution)/shard_map/all_to_all | solution.py:283
  694.9 10.1 %reshape.454 = bf16[1024,3,3,4,64]{4,3,2,1,0:T(4,128)(2,1)} reshape(bf16[4,2,294912]{2,1,0:T(2,128)(2,1)} %all_to_all.66) | data formatting | bytes 9437184
  705.0 15.1 %copy.204 = bf16[4,4,256,3,3,64]{2,0,5,4,1,3:T(4,128)(2,1)} copy(bf16[4,4,256,3,3,64]{5,0,4,3,2,1:T(4,128)(2,1)} %bitcast.251) | data formatting | bytes 9437184 | tf_op jit(solution)/shard_map/all_to_all | solution.py:283
  720.1 4.0 copy.214
  724.1 4.2 fusion.51
  731.3 5.7 concatenate.21
  738.9 9.2 fusion.70
  748.1 90.5 %reduce-scatter.3.cloned.1.call-done = bf16[24,2560]{1,0:T(8,128)(2,1)} async-done(((bf16[768,2560]{1,0:T(8,128)(2,1)}), bf16[24,2560]{1,0:T(8,128)(2,1)}) %reduce-scatter.3.cloned.1.call-update) | async-done | bytes 122896 | tf_op jit(solution)/shard_map/reduce_scatter | solution.py:293
  841.0 146.3 %reduce-scatter.5.cloned.1.call-done = bf16[24,7168]{1,0:T(8,128)(2,1)} async-done(((bf16[768,7168]{1,0:T(8,128)(2,1)}), bf16[24,7168]{1,0:T(8,128)(2,1)}) %reduce-scatter.5.cloned.1.call-update) | async-done | bytes 344080 | tf_op jit(solution)/shard_map/reduce_scatter | solution.py:276
  (581 shorter events, 222.0 us)
Async XLA Ops:
  7.2 73.9 %all-gather.3.cloned.1.call-start = ((), (), s32[]{:S(2)}) async-start(), calls=%async_computation.6 | async-start | bytes 3852288 | tf_op jit(solution)/shard_map/all_gather | solution.py:203
  110.2 5.3 copy-start.25
  110.2 5.5 copy-start.26
  110.2 5.5 copy-start.29
  110.2 6.3 copy-start.39
  110.2 70.6 %all-to-all-start = ((bf16[4,256,3,12,64]{1,0,4,2,3:T(4,128)(2,1)}), bf16[4,256,3,12,64]{1,0,4,2,3:T(4,128)(2,1)}, u32[]{:S(2)}, u32[]{:S(2)}) async-start(bf16[4,256,3,12,64]{1,0,4,2,3:T(4,128)(2,1)} %copy.188), calls=%async_computation | async-start | bytes 9437184 | tf_op jit(solution)/shard_map/all_to_all | solution.py:224
  115.3 194.7 %all-gather.5.cloned.1.call-start = ((), (), s32[]{:S(2)}) async-start(), calls=%async_computation.7 | async-start | bytes 10948608 | tf_op jit(solution)/shard_map/all_gather | solution.py:204
  265.4 7.9 copy-start.27
  265.4 7.9 copy-start.28
  273.3 9.1 copy-start.10
  278.5 6.3 copy-start.30
  278.5 22.0 %all-to-all-start.1 = ((bf16[4,2,98304]{2,1,0:T(2,128)(2,1)}), bf16[4,2,98304]{2,1,0:T(2,128)(2,1)S(1)}, u32[]{:S(2)}, u32[]{:S(2)}) async-start(bf16[4,2,98304]{2,1,0:T(2,128)(2,1)} %reshape.451), calls=%async_computation.1 | async-start | bytes 3145728 | tf_op jit(solution)/shard_map/all_to_all | solution.py:229
  303.8 6.3 copy-start.38
  321.0 8.5 copy-start.31
  321.0 8.5 copy-start.36
  329.5 12.7 %copy-start.13 = (f32[1024,768]{1,0:T(8,128)S(1)}, f32[1024,768]{1,0:T(8,128)}, u32[]{:S(2)}) copy-start(f32[1024,768]{1,0:T(8,128)} %copy-done.12) | copy-start | bytes 9437188
  329.5 12.7 %copy-start.19 = (bf16[3072,768]{1,0:T(8,128)(2,1)S(1)}, bf16[3072,768]{1,0:T(8,128)(2,1)}, u32[]{:S(2)}) copy-start(bf16[3072,768]{1,0:T(8,128)(2,1)} %reshape.408) | copy-start | bytes 14155780
  329.5 12.7 %copy-start.37 = (f32[768]{0:T(1024)S(1)}, f32[768]{0:T(1024)}, u32[]{:S(2)}) copy-start(f32[768]{0:T(1024)} %get-tuple-element.325) | copy-start | bytes 9220
  362.2 8.6 copy-start.22
  370.8 12.8 %copy-start.14 = (f32[1024,768]{1,0:T(8,128)S(1)}, f32[1024,768]{1,0:T(8,128)}, u32[]{:S(2)}) copy-start(f32[1024,768]{1,0:T(8,128)} %copy-done.12) | copy-start | bytes 9437188
  402.1 4.4 copy-start.34
  402.1 5.3 copy-start.33
  402.1 6.1 copy-start.24
  432.0 22.3 %all-to-all-start.2 = ((bf16[4,256,12,64]{1,0,3,2:T(4,128)(2,1)}), bf16[4,256,12,64]{1,0,3,2:T(4,128)(2,1)S(1)}, u32[]{:S(2)}, u32[]{:S(2)}) async-start(bf16[4,256,12,64]{1,0,3,2:T(4,128)(2,1)} %reshape.410), calls=%async_computation.2 | async-start | bytes 3145728 | tf_op jit(solution)/shard_map/all_to_all | solution.py:279
  435.5 403.1 %reduce-scatter.3.cloned.1.call-start = ((), (), s32[]{:S(2)}) async-start(), calls=%async_computation.8 | async-start | bytes 4055040 | tf_op jit(solution)/shard_map/reduce_scatter | solution.py:293
  455.2 4.3 copy-start.15
  466.5 4.4 copy-start.1
  470.9 3.9 copy-start.5
  470.9 3.9 copy-start.7
  480.8 4.7 copy-start.1
  485.5 4.2 copy-start.5
  485.5 4.2 copy-start.7
  485.5 4.2 copy-start.9
  485.5 4.2 copy-start.18
  489.7 4.4 copy-start.16
  494.2 4.3 copy-start.15
  505.4 4.4 copy-start.1
  509.9 3.9 copy-start.7
  519.7 4.7 copy-start.1
  524.4 4.2 copy-start.5
  524.4 4.2 copy-start.7
  524.5 4.2 copy-start.9
  524.5 4.2 copy-start.18
  528.7 4.5 copy-start.16
  533.2 4.3 copy-start.15
  544.5 4.4 copy-start.1
  558.7 4.7 copy-start.1
  563.5 4.2 copy-start.5
  563.5 4.2 copy-start.7
  563.5 4.2 copy-start.9
  563.5 4.2 copy-start.18
  567.7 4.5 copy-start.16
  572.1 4.3 copy-start.15
  583.4 4.4 copy-start.1
  587.9 3.9 copy-start.7
  597.7 4.7 copy-start.1
  602.4 4.2 copy-start.5
  602.4 4.2 copy-start.7
  602.4 4.2 copy-start.9
  602.4 4.2 copy-start.18
  606.6 4.5 copy-start.16
  720.1 4.0 copy-start.40
  724.1 4.2 copy-start.11
  737.0 250.3 %reduce-scatter.5.cloned.1.call-start = ((), (), s32[]{:S(2)}) async-start(), calls=%async_computation.9 | async-start | bytes 11354112 | tf_op jit(solution)/shard_map/reduce_scatter | solution.py:276
  (74 other events, 161.0 us)
Sparse Core Ops, SparseCore 0:
  17.6 63.4 all-gather.2
  119.1 108.7 all-gather.4
  737.1 101.4 reduce-scatter.2
  844.4 142.8 reduce-scatter.4

commit v3 on v2

--- a/solution.py
+++ b/solution.py
@@ -151,6 +151,14 @@
         pieces.append(jnp.zeros((pieces[0].shape[0], extra), jnp.bfloat16))
     block = jnp.concatenate(pieces, axis=1)
     return with_layout_constraint(block, Layout(major_to_minor=(0, 1)))
+
+
+def scatter_two_stage(block):
+    outer = lax.axis_size("seq")
+    part = lax.psum_scatter(
+        block.reshape(outer, block.shape[0] // outer, -1), "shard", scatter_dimension=1, tiled=True
+    )
+    return lax.psum_scatter(part.reshape(-1, block.shape[1]), "seq", scatter_dimension=0, tiled=True)
 
 
 def per_device(
@@ -218,17 +226,23 @@
     heads = width // DH
     flat = layer_in.reshape(row_count, width)
     qkv_bias = jnp.concatenate([bias_query, jnp.zeros_like(bias_query), bias_value])
-    qkv = (jnp.dot(flat, full_qkv, preferred_element_type=jnp.float32) + qkv_bias).astype(
-        jnp.bfloat16
-    )
-    head_qkv = lax.all_to_all(
-        qkv.reshape(streams, part_len, 3, heads, DH), "seq", split_axis=3, concat_axis=1, tiled=True
-    )
     segment = segment_ids(doc_starts, LEN)
-    context, logsum = lax.map(attend_forward, (head_qkv, segment))
-    context_rows = lax.all_to_all(context, "seq", split_axis=1, concat_axis=2, tiled=True).reshape(
-        row_count, width
-    )
+    head_qkv, context_parts, logsum = [], [], []
+    for s in range(streams):
+        qkv = (
+            jnp.dot(flat[s * part_len : (s + 1) * part_len], full_qkv, preferred_element_type=jnp.float32)
+            + qkv_bias
+        ).astype(jnp.bfloat16)
+        one_qkv = lax.all_to_all(
+            qkv.reshape(part_len, 3, heads, DH), "seq", split_axis=2, concat_axis=0, tiled=True
+        )
+        context, one_sum = attend_forward((one_qkv, segment[s]))
+        context_parts.append(
+            lax.all_to_all(context, "seq", split_axis=0, concat_axis=1, tiled=True)
+        )
+        head_qkv.append(one_qkv)
+        logsum.append(one_sum)
+    context_rows = jnp.stack(context_parts).reshape(row_count, width)
     attn = jnp.dot(context_rows, full_out, preferred_element_type=jnp.float32) + bias_out
     mixed, normed_mixer, inverse_mixer = norm_forward(
         flat.astype(jnp.float32) + attn, gain_mixer, shift_mixer
@@ -276,13 +290,18 @@
     early_sum = lax.psum_scatter(early, axes, scatter_dimension=0, tiled=True).astype(jnp.float32)
 
     back_context = times_transpose(back_attn, full_out).astype(jnp.bfloat16)
-    head_back = lax.all_to_all(
-        back_context.reshape(streams, part_len, heads, DH), "seq", split_axis=2, concat_axis=1, tiled=True
-    )
-    qkv_back = lax.map(attend_backward, (head_qkv, segment, logsum, head_back))
-    rows_back = lax.all_to_all(qkv_back, "seq", split_axis=1, concat_axis=3, tiled=True).reshape(
-        row_count, 3 * width
-    )
+    back_parts = []
+    for s in range(streams):
+        one_back = lax.all_to_all(
+            back_context[s * part_len : (s + 1) * part_len].reshape(part_len, heads, DH),
+            "seq",
+            split_axis=1,
+            concat_axis=0,
+            tiled=True,
+        )
+        one_grads = attend_backward((head_qkv[s], segment[s], logsum[s], one_back))
+        back_parts.append(lax.all_to_all(one_grads, "seq", split_axis=0, concat_axis=2, tiled=True))
+    rows_back = jnp.stack(back_parts).reshape(row_count, 3 * width)
     grad_qkv_weight = contract_rows(flat, rows_back)
     grad_query_bias = jnp.sum(rows_back[:, :width].astype(jnp.float32), axis=0)
     grad_value_bias = jnp.sum(rows_back[:, 2 * width :].astype(jnp.float32), axis=0)
@@ -290,7 +309,7 @@
         streams, part_len, width
     )
     late = pack_lanes([grad_qkv_weight, grad_query_bias[:, None], grad_value_bias[:, None]])
-    late_sum = lax.psum_scatter(late, axes, scatter_dimension=0, tiled=True).astype(jnp.float32)
+    late_sum = scatter_two_stage(late).astype(jnp.float32)
 
     base = width + 2 * ff
     late_tail = late_sum[:, 3 * width :]

time: 1010 us -> 946 us (0.937)
  waiting for transfers between devices: 399 us -> 300 us
  blocking collectives: 59.2 us -> 10.4 us
  starting transfers between devices: 12.9 us -> 61.5 us
  matrix products: 210 us -> 225 us
    reduce_scatter x1 -> x0, waiting for transfers between devices: 90.5 us -> none  [per_device(): lax.psum_scatter(late, axes, scatter_dimension=0, tiled=True)]
    all_to_all x3 -> x15, waiting for transfers between devices: 98 us -> 29.9 us  [the longest x4 24.8 us: per_device(): lax.all_to_all(qkv.reshape(part_len, 3, heads, DH), 'seq', split_axis=2,...]
    unnamed x4 -> x7, waiting for transfers between devices: 0.57 us -> 59.4 us
    all_to_all x3 -> x15, starting transfers between devices: 12.5 us -> 61.3 us  [the longest x4 17.9 us: per_device(): lax.all_to_all(one_grads, 'seq', split_axis=0, concat_axis=2, tiled=True)]
    all_to_all x1, blocking collectives: 59.2 us -> 10.4 us  [per_device(): lax.all_to_all(back_context[s * part_len:(s + 1) * part_len].reshape(part...]
    another operation x0 -> x30, local copies, waits for them, and re-layouts: none -> 37.6 us  [the longest x8 19.4 us: attend_backward(): jnp.stack([query_grad.reshape(length, heads, depth), key_grad.astype(jnp....]
    unnamed x62 -> x164, local copies, waits for them, and re-layouts: 39.3 us -> 62.3 us
    squeeze x24 -> x0, local copies, waits for them, and re-layouts: 18.8 us -> none  [the longest x8 13.3 us: per_device(): context, logsum = lax.map(attend_forward, (head_qkv, segment))]
  transfers between devices with their start and end apart: 7 -> 20, of which waited for: 6 -> 8; matrix products, arithmetic and copies ran while one was open for 11% -> 37% of each run, Pallas kernels for 0% -> 0%
where the time goes in v3:
time: 946 us; the launch traced here: 933 us
  waiting for transfers between devices  300 us (32%)
  local copies, waits for them, and re-layouts  237 us (25%)
  matrix products  225 us (24%)
  other arithmetic  81.5 us (9%)
  starting transfers between devices  61.5 us (7%)
  between operations  15.7 us (2%)
  blocking collectives  10.4 us (1%)
    reduce_scatter x1, waiting for transfers between devices, per_device(): lax.psum_scatter(early, axes, scatter_dimension=0, tiled=True)  147 us
    all_gather x1, waiting for transfers between devices, per_device(): full_first = lax.all_gather(first, axes, axis=0, tiled=True)  63.6 us
    unnamed x164, local copies, waits for them, and re-layouts  62.3 us
    unnamed x7, waiting for transfers between devices  59.4 us
    dot_general x4, matrix products, times_transpose(): lax.dot_general(left, right, (((1,), (1,)), ((), ())), preferred_element_...  32.5 us
    dot_general x8, matrix products, one(): jnp.einsum('hqk,qhd->khd', weights.astype(jnp.bfloat16), block_up, prefer...  32.1 us
    dot_general x16, matrix products, masked_scores(): jnp.einsum('qhd,khd->hqk', queries, keys, preferred_element_type=jnp.floa...  27.8 us
    all_to_all x4, waiting for transfers between devices, per_device(): lax.all_to_all(qkv.reshape(part_len, 3, heads, DH), 'seq', split_axis=2,...  24.8 us
  transfers between devices with their start and end apart: 20, of which 8 were waited for; matrix products, arithmetic and copies ran while one was open for 37% of the time, Pallas kernels for 0%

profile of v3, /device:TPU:0, one launch (start us, length us, event | category | flops | bytes accessed | tf_op | source)
XLA Modules:
  0.0 933.2 jit_solution(9251341695008688326)
XLA Ops:
  17.5 63.6 %all-gather.3.cloned.1.call-done = bf16[768,2316]{1,0:T(8,128)(2,1)} async-done(((bf16[24,2316]{1,0:T(8,128)(2,1)}), bf16[768,2316]{1,0:T(8,128)(2,1)}) %all-gather.3.cloned.1.call-update) | async-done | bytes 3557392 | tf_op jit(solution)/shard_map/all_gather | solution.py:211
  97.4 11.0 %all-to-all-done = bf16[256,3,12,64]{0,3,1,2:T(8,128)(2,1)S(1)} async-done(((bf16[256,3,12,64]{0,3,1,2:T(8,128)(2,1)}), bf16[256,3,12,64]{0,3,1,2:T(8,128)(2,1)S(1)}, u32[]{:S(2)}, u32[]{:S(2)}) %all-to-all-start) | async-done | bytes 1179680 | tf_op jit(solution)/shard_map/all_to_all | solution.py:236
  121.5 6.3 all-to-all-done.2
  140.9 7.5 all-to-all-done.4
  148.4 3.7 all-to-all-start.6
  153.6 14.0 %while.108 = (s32[]{:T(128)}, bf16[2,512,3,64]{1,3,2,0:T(8,128)(2,1)}, f32[2,3,512]{2,1,0:T(4,128)}, s32[2,512]{1,0:T(2,128)S(1)}, s32[1,1024]{1,0:T(1,128)S(1)}...) while((s32[]{:T(128)}, ...), condition=%wide.region_4.5_spmd, body=%wide.region_1.4_spmd.sunk | while | flops 422148608 | bytes 22213732 | solution.py:86
  184.4 4.2 all-to-all-start.1
  190.0 14.0 %while.109 = (s32[]{:T(128)}, bf16[2,512,3,64]{1,3,2,0:T(8,128)(2,1)}, f32[2,3,512]{2,1,0:T(4,128)}, s32[2,512]{1,0:T(2,128)S(1)}, s32[1,1024]{1,0:T(1,128)S(1)}...) while((s32[]{:T(128)}, ...), condition=%wide.region_8.9_spmd, body=%wide.region_5.8_spmd.sunk | while | flops 422148608 | bytes 22213732 | solution.py:86
  215.8 4.6 all-to-all-start.3
  220.4 11.6 %while.110 = (s32[]{:T(128)}, bf16[2,512,3,64]{1,3,2,0:T(8,128)(2,1)S(1)}, f32[2,3,512]{2,1,0:T(4,128)S(1)}, s32[2,512]{1,0:T(2,128)S(1)}, s32[1,1024]{1,0:T(1,1...) while((s32[]{:T(128)}, ...), condition=%wide.region_12.13_spmd, body=%wide.region_9.12_spmd.sunk | while | flops 422148608 | bytes 22220908 | solution.py:86
  239.7 4.2 all-to-all-start.5
  245.3 16.0 %while.111 = (s32[]{:T(128)}, bf16[2,512,3,64]{1,3,2,0:T(8,128)(2,1)}, f32[2,3,512]{2,1,0:T(4,128)}, s32[2,512]{1,0:T(2,128)S(1)}, s32[1,1024]{1,0:T(1,128)S(1)}...) while((s32[]{:T(128)}, ...), condition=%wide.region_16.17_spmd, body=%wide.region_13.16_spmd.sunk | while | flops 422148608 | bytes 22213732 | solution.py:86
  249.5 3.8 fusion.361
  257.5 3.8 fusion.361
  264.6 4.4 all-to-all-start.7
  284.5 3.9 fusion.226
  290.6 4.9 slice.245
  295.5 8.5 reshape.726
  304.0 12.4 %multiply_convert_fusion.4 = (bf16[1024,3072]{1,0:T(8,128)(2,1)S(1)}, f32[1024,3072]{1,0:T(8,128)}) fusion(f32[3072]{0:T(1024)S(1)} %reshape.747, bf16[768,6912]{1,0:T(8,128)(2,1)} %all-gather.5.cloned.1.call-done, f32[1024,768]{1,0:T(8,128)} %copy-done.41, f32[768]{0:T(1024)S(1)} %copy-done.98, f32[768]{0:T(1024)S(1)} %copy-done.94, ...), kind=kOutput, calls=%fused_computation.215 | convolution fusion | flops 4854644736 | bytes 26765312 | tf_op jit(solution)/shard_map/dot_general | solution.py:251
  316.5 5.4 fusion.227
  328.1 7.1 convolution_convert_fusion
  335.2 8.6 convert_element_type.428
  343.9 12.4 %fusion.228 = (bf16[3072]{0:T(1024)(128)(2,1)S(1)}, bf16[1024,3072]{1,0:T(8,128)(2,1)S(1)}) fusion(f32[1024,3072]{1,0:T(8,128)} %get-tuple-element.1210, f32[3072]{0:T(1024)S(1)} %reshape.747, bf16[3072,768]{1,0:T(8,128)(2,1)} %reshape.726, f32[1024,768]{1,0:T(8,128)S(1)} %copy-done.58), kind=kOutput, calls=%fused_computation.365 | convolution fusion | flops 4870370304 | bytes 26757120 | tf_op jit(solution)/shard_map/dot_general | solution.py:25
  356.3 8.0 convolution_convert_fusion.1
  364.3 8.3 multiply_reduce_fusion.4
  381.3 17.8 %concatenate.20 = bf16[768,7168]{1,0:T(8,128)(2,1)} concatenate(bf16[768,768]{1,0:T(8,128)(2,1)S(1)} %convolution_convert_fusion.4, bf16[768,3072]{1,0:T(8,128)(2,1)} %convolution_convert_fusion.1, bf16[768,3072]{1,0:T(8,128)(2,1)} %convert_element_type.428, bf16[768,1]{1,0:T(8,128)(2,1)S(1)} %convert_element_type.480, bf16[768,1]{1,0:T(8,128)(2,1)} %convert_element_type.481, ...), dimensions={1} | concatenate | bytes 22020096 | tf_op jit(solution)/shard_map/concatenate | solution.py:152
  402.9 10.4 %all_to_all.252 = bf16[256,12,64]{0,2,1:T(8,128)(2,1)S(1)} all-to-all(bf16[256,12,64]{0,2,1:T(8,128)(2,1)S(1)} %bitcast.665), channel_id=1, replica_groups=mesh['seq'=4,'shard'=8] {'seq'}, dimensions={1} | all-to-all | bytes 786432 | tf_op jit(solution)/shard_map/all_to_all | solution.py:295
  417.5 5.1 all-to-all-done.10
  422.6 4.1 all-to-all-start.12
  427.6 32.6 %while.112 = (s32[]{:T(128)}, f32[1024,3,64]{0,2,1:T(8,128)}, f32[1024,3,64]{0,2,1:T(8,128)}, bf16[2,512,3,64]{1,3,2,0:T(8,128)(2,1)}, bf16[2,512,3,64]{1,3,2,0:...) while((s32[]{:T(128)}, f32[1024,3,64]{0,2,1:T(8,128)}, ...), condition=%wide.region_34.35_spmd.clone, body=%wide.region_32.34_spmd.clone.sunk | while | flops 1031928320 | bytes 117039024 | solution.py:131
  439.7 3.8 fusion.373
  456.0 4.1 fusion.373
  463.2 4.2 all-to-all-start.14
  468.5 4.6 copy.353
  477.9 4.5 all-to-all-start.9
  483.2 32.7 %while.113 = (s32[]{:T(128)}, f32[1024,3,64]{0,2,1:T(8,128)}, f32[1024,3,64]{0,2,1:T(8,128)}, bf16[2,512,3,64]{1,3,2,0:T(8,128)(2,1)}, bf16[2,512,3,64]{1,3,2,0:...) while((s32[]{:T(128)}, f32[1024,3,64]{0,2,1:T(8,128)}, ...), condition=%wide.region_37.38_spmd.clone, body=%wide.region_35.37_spmd.clone.sunk | while | flops 1031928320 | bytes 117039024 | solution.py:131
  495.4 3.9 fusion.386
  511.7 4.2 fusion.386
  521.1 4.6 copy.360
  530.5 4.7 all-to-all-start.11
  536.0 32.6 %while.114 = (s32[]{:T(128)}, f32[1024,3,64]{0,2,1:T(8,128)}, f32[1024,3,64]{0,2,1:T(8,128)}, bf16[2,512,3,64]{1,3,2,0:T(8,128)(2,1)}, bf16[2,512,3,64]{1,3,2,0:...) while((s32[]{:T(128)}, f32[1024,3,64]{0,2,1:T(8,128)}, ...), condition=%wide.region_40.41_spmd.clone, body=%wide.region_38.40_spmd.clone.sunk | while | flops 1031928320 | bytes 117039024 | solution.py:131
  548.1 3.8 fusion.399
  564.4 4.1 fusion.399
  573.7 4.6 copy.367
  582.1 4.5 all-to-all-start.13
  587.4 35.1 %while.115 = (s32[]{:T(128)}, f32[1024,3,64]{0,2,1:T(8,128)}, f32[1024,3,64]{0,2,1:T(8,128)}, bf16[2,512,3,64]{1,3,2,0:T(8,128)(2,1)}, bf16[2,512,3,64]{1,3,2,0:...) while((s32[]{:T(128)}, f32[1024,3,64]{0,2,1:T(8,128)}, ...), condition=%wide.region_43.44_spmd.clone, body=%wide.region_41.43_spmd.clone.sunk | while | flops 1031928320 | bytes 115466120 | solution.py:131
  590.6 3.8 multiply_reduce_fusion.16
  600.8 3.8 fusion.412
  607.9 3.8 multiply_reduce_fusion.16
  618.4 4.1 fusion.412
  627.7 4.6 copy.374
  635.3 4.3 all-to-all-start.15
  639.7 3.7 reshape.800
  650.4 3.5 copy.362
  657.4 3.6 copy.369
  664.4 3.5 copy.376
  670.6 4.5 copy.377
  676.7 4.4 fusion.178
  684.1 5.8 concatenate.21
  689.8 5.1 copy.404
  697.8 46.2 %reduce-scatter.10.cloned.1.call-done = bf16[24,10240]{1,0:T(8,128)(2,1)} async-done(((bf16[192,10240]{1,0:T(8,128)(2,1)}), bf16[24,10240]{1,0:T(8,128)(2,1)}) %reduce-scatter.10.cloned.1.call-update) | async-done | bytes 491536
  748.2 9.0 fusion.204
  757.2 12.7 %reduce-scatter.12.cloned.1.call-done = bf16[24,2560]{1,0:T(8,128)(2,1)} async-done(((bf16[96,2560]{1,0:T(8,128)(2,1)}), bf16[24,2560]{1,0:T(8,128)(2,1)}) %reduce-scatter.12.cloned.1.call-update) | async-done | bytes 122896
  772.3 147.4 %reduce-scatter.8.cloned.1.call-done = bf16[24,7168]{1,0:T(8,128)(2,1)} async-done(((bf16[768,7168]{1,0:T(8,128)(2,1)}), bf16[24,7168]{1,0:T(8,128)(2,1)}) %reduce-scatter.8.cloned.1.call-update) | async-done | bytes 344080 | tf_op jit(solution)/shard_map/reduce_scatter | solution.py:290
  (606 shorter events, 352.8 us)
Async XLA Ops:
  7.2 73.9 %all-gather.3.cloned.1.call-start = ((), (), s32[]{:S(2)}) async-start(), calls=%async_computation.19 | async-start | bytes 3852288 | tf_op jit(solution)/shard_map/all_gather | solution.py:211
  84.7 32.4 %copy-start.96 = (f32[2304]{0:T(1024)}, f32[2304]{0:T(1024)S(1)}, u32[]{:S(2)}) copy-start(f32[2304]{0:T(1024)S(1)} %pad_maximum_fusion.7) | copy-start | bytes 27652
  89.2 19.2 %all-to-all-start = ((bf16[256,3,12,64]{0,3,1,2:T(8,128)(2,1)}), bf16[256,3,12,64]{0,3,1,2:T(8,128)(2,1)S(1)}, u32[]{:S(2)}, u32[]{:S(2)}) async-start(bf16[256,3,12,64]{0,3,1,2:T(8,128)(2,1)} %copy.313), calls=%async_computation | async-start | bytes 2359296 | tf_op jit(solution)/shard_map/all_to_all | solution.py:236
  96.3 17.5 %copy-start.101 = (s32[4,17]{1,0:T(4,128)S(1)}, s32[4,17]{1,0:T(4,128)}, u32[]{:S(2)}) copy-start(s32[4,17]{1,0:T(4,128)} %param.36) | copy-start | bytes 820
  96.3 19.6 %copy-start.29 = (bf16[4,256,768]{2,1,0:T(8,128)(2,1)S(1)}, bf16[4,256,768]{2,1,0:T(8,128)(2,1)}, u32[]{:S(2)}) copy-start(bf16[4,256,768]{2,1,0:T(8,128)(2,1)} %param.35) | copy-start | bytes 4718596
  109.4 18.4 %all-to-all-start.2 = ((bf16[256,3,12,64]{0,3,1,2:T(8,128)(2,1)}), bf16[256,3,12,64]{0,3,1,2:T(8,128)(2,1)S(1)}, u32[]{:S(2)}, u32[]{:S(2)}) async-start(bf16[256,3,12,64]{0,3,1,2:T(8,128)(2,1)} %copy.320), calls=%async_computation.2 | async-start | bytes 2359296 | tf_op jit(solution)/shard_map/all_to_all | solution.py:236
  113.0 171.5 %all-gather.5.cloned.1.call-start = ((), (), s32[]{:S(2)}) async-start(), calls=%async_computation.20 | async-start | bytes 10948608 | tf_op jit(solution)/shard_map/all_gather | solution.py:212
  120.4 12.0 %copy-start.97 = (f32[2304]{0:T(1024)S(1)}, f32[2304]{0:T(1024)}, u32[]{:S(2)}) copy-start(f32[2304]{0:T(1024)} %copy-done.96) | copy-start | bytes 27652
  128.9 19.5 %all-to-all-start.4 = ((bf16[256,3,12,64]{0,3,1,2:T(8,128)(2,1)}), bf16[256,3,12,64]{0,3,1,2:T(8,128)(2,1)S(1)}, u32[]{:S(2)}, u32[]{:S(2)}) async-start(bf16[256,3,12,64]{0,3,1,2:T(8,128)(2,1)} %copy.327), calls=%async_computation.4 | async-start | bytes 2359296 | tf_op jit(solution)/shard_map/all_to_all | solution.py:236
  148.4 36.0 %all-to-all-start.6 = ((bf16[256,3,12,64]{0,3,1,2:T(8,128)(2,1)}), bf16[256,3,12,64]{0,3,1,2:T(8,128)(2,1)S(1)}, u32[]{:S(2)}, u32[]{:S(2)}) async-start(bf16[256,3,12,64]{0,3,1,2:T(8,128)(2,1)} %copy.334), calls=%async_computation.6 | async-start | bytes 2359296 | tf_op jit(solution)/shard_map/all_to_all | solution.py:236
  167.6 8.2 copy-start.22
  167.6 8.2 copy-start.37
  167.6 11.6 %copy-start.28 = (bf16[2,512,3,64]{1,3,2,0:T(8,128)(2,1)}, bf16[2,512,3,64]{1,3,2,0:T(8,128)(2,1)S(1)}, u32[]{:S(2)}) copy-start(bf16[2,512,3,64]{1,3,2,0:T(8,128)(2,1)S(1)} %get-tuple-element.2002) | copy-start | bytes 1179652
  167.6 11.6 %copy-start.79 = (s32[1,1024]{1,0:T(1,128)}, s32[1,1024]{1,0:T(1,128)S(1)}, u32[]{:S(2)}) copy-start(s32[1,1024]{1,0:T(1,128)S(1)} %get-tuple-element.2087) | copy-start | bytes 12292
  167.6 11.6 %copy-start.90 = (s32[2,512]{1,0:T(2,128)}, s32[2,512]{1,0:T(2,128)S(1)}, u32[]{:S(2)}) copy-start(s32[2,512]{1,0:T(2,128)S(1)} %get-tuple-element.2094) | copy-start | bytes 12292
  184.4 31.4 %all-to-all-start.1 = ((bf16[4,2,24576]{2,1,0:T(2,128)(2,1)}), bf16[4,2,24576]{2,1,0:T(2,128)(2,1)}, u32[]{:S(2)}, u32[]{:S(2)}) async-start(bf16[4,2,24576]{2,1,0:T(2,128)(2,1)} %reshape.791), calls=%async_computation.1 | async-start | bytes 786432 | tf_op jit(solution)/shard_map/all_to_all | solution.py:241
  204.0 7.0 copy-start.20
  204.0 7.0 copy-start.34
  204.0 9.6 %copy-start.27 = (bf16[2,512,3,64]{1,3,2,0:T(8,128)(2,1)}, bf16[2,512,3,64]{1,3,2,0:T(8,128)(2,1)S(1)}, u32[]{:S(2)}) copy-start(bf16[2,512,3,64]{1,3,2,0:T(8,128)(2,1)S(1)} %get-tuple-element.2001) | copy-start | bytes 1179652
  204.0 9.6 %copy-start.88 = (s32[2,512]{1,0:T(2,128)}, s32[2,512]{1,0:T(2,128)S(1)}, u32[]{:S(2)}) copy-start(s32[2,512]{1,0:T(2,128)S(1)} %get-tuple-element.2093) | copy-start | bytes 12292
  210.9 9.5 %copy-start.75 = (s32[1,1024]{1,0:T(1,128)S(1)}, s32[1,1024]{1,0:T(1,128)}, u32[]{:S(2)}) copy-start(s32[1,1024]{1,0:T(1,128)} %get-tuple-element.1877) | copy-start | bytes 12292
  210.9 9.5 %copy-start.86 = (s32[2,512]{1,0:T(2,128)S(1)}, s32[2,512]{1,0:T(2,128)}, u32[]{:S(2)}) copy-start(s32[2,512]{1,0:T(2,128)} %reshape_squeeze.36) | copy-start | bytes 12292
  215.8 23.9 %all-to-all-start.3 = ((bf16[4,2,24576]{2,1,0:T(2,128)(2,1)}), bf16[4,2,24576]{2,1,0:T(2,128)(2,1)}, u32[]{:S(2)}, u32[]{:S(2)}) async-start(bf16[4,2,24576]{2,1,0:T(2,128)(2,1)} %reshape.789), calls=%async_computation.3 | async-start | bytes 786432 | tf_op jit(solution)/shard_map/all_to_all | solution.py:241
  237.6 7.7 copy-start.73
  237.6 7.7 copy-start.84
  239.7 24.9 %all-to-all-start.5 = ((bf16[4,2,24576]{2,1,0:T(2,128)(2,1)}), bf16[4,2,24576]{2,1,0:T(2,128)(2,1)}, u32[]{:S(2)}, u32[]{:S(2)}) async-start(bf16[4,2,24576]{2,1,0:T(2,128)(2,1)} %reshape.787), calls=%async_computation.5 | async-start | bytes 786432 | tf_op jit(solution)/shard_map/all_to_all | solution.py:241
  261.3 11.0 %copy-start.16 = (bf16[1024,3,64]{0,2,1:T(8,128)(2,1)}, bf16[1024,3,64]{0,2,1:T(8,128)(2,1)S(1)}, u32[]{:S(2)}) copy-start(bf16[1024,3,64]{0,2,1:T(8,128)(2,1)S(1)} %get-tuple-element.1993) | copy-start | bytes 1179652
  261.3 11.0 %copy-start.25 = (bf16[2,512,3,64]{1,3,2,0:T(8,128)(2,1)}, bf16[2,512,3,64]{1,3,2,0:T(8,128)(2,1)S(1)}, u32[]{:S(2)}) copy-start(bf16[2,512,3,64]{1,3,2,0:T(8,128)(2,1)S(1)} %get-tuple-element.1999) | copy-start | bytes 1179652
  261.3 7.7 copy-start.30
  261.3 7.7 copy-start.93
  264.6 13.1 %all-to-all-start.7 = ((bf16[4,2,24576]{2,1,0:T(2,128)(2,1)}), bf16[4,2,24576]{2,1,0:T(2,128)(2,1)}, u32[]{:S(2)}, u32[]{:S(2)}) async-start(bf16[4,2,24576]{2,1,0:T(2,128)(2,1)} %reshape.785), calls=%async_computation.7 | async-start | bytes 786432 | tf_op jit(solution)/shard_map/all_to_all | solution.py:241
  295.5 8.5 copy-start.94
  295.5 8.5 copy-start.98
  304.0 12.5 %copy-start.42 = (f32[1024,768]{1,0:T(8,128)S(1)}, f32[1024,768]{1,0:T(8,128)}, u32[]{:S(2)}) copy-start(f32[1024,768]{1,0:T(8,128)} %copy-done.41) | copy-start | bytes 9437188
  304.0 12.5 %copy-start.52 = (bf16[3072,768]{1,0:T(8,128)(2,1)S(1)}, bf16[3072,768]{1,0:T(8,128)(2,1)}, u32[]{:S(2)}) copy-start(bf16[3072,768]{1,0:T(8,128)(2,1)} %reshape.726) | copy-start | bytes 14155780
  304.0 12.5 %copy-start.99 = (f32[768]{0:T(1024)S(1)}, f32[768]{0:T(1024)}, u32[]{:S(2)}) copy-start(f32[768]{0:T(1024)} %get-tuple-element.981) | copy-start | bytes 9220
  316.5 6.0 copy-start.95
  335.2 8.6 copy-start.58
  343.9 12.4 %copy-start.43 = (f32[1024,768]{1,0:T(8,128)S(1)}, f32[1024,768]{1,0:T(8,128)}, u32[]{:S(2)}) copy-start(f32[1024,768]{1,0:T(8,128)} %copy-done.41) | copy-start | bytes 9437188
  375.1 6.1 copy-start.72
  401.7 25.8 %copy-start.23 = (bf16[1024,3,64]{0,2,1:T(8,128)(2,1)S(1)}, bf16[1024,3,64]{0,2,1:T(8,128)(2,1)}, u32[]{:S(2)}) copy-start(bf16[1024,3,64]{0,2,1:T(8,128)(2,1)} %copy-done.22) | copy-start | bytes 1179652
  401.8 25.8 %copy-start.38 = (bf16[1024,3,64]{0,2,1:T(8,128)(2,1)S(1)}, bf16[1024,3,64]{0,2,1:T(8,128)(2,1)}, u32[]{:S(2)}) copy-start(bf16[1024,3,64]{0,2,1:T(8,128)(2,1)} %copy-done.37) | copy-start | bytes 1179652
  401.8 25.8 %copy-start.80 = (s32[1,1024]{1,0:T(1,128)S(1)}, s32[1,1024]{1,0:T(1,128)}, u32[]{:S(2)}) copy-start(s32[1,1024]{1,0:T(1,128)} %copy-done.79) | copy-start | bytes 12292
  401.8 25.8 %copy-start.91 = (s32[2,512]{1,0:T(2,128)S(1)}, s32[2,512]{1,0:T(2,128)}, u32[]{:S(2)}) copy-start(s32[2,512]{1,0:T(2,128)} %copy-done.90) | copy-start | bytes 12292
  413.3 9.3 all-to-all-start.10
  422.6 40.5 %all-to-all-start.12 = ((bf16[256,12,64]{0,2,1:T(8,128)(2,1)}), bf16[256,12,64]{0,2,1:T(8,128)(2,1)}, u32[]{:S(2)}, u32[]{:S(2)}) async-start(bf16[256,12,64]{0,2,1:T(8,128)(2,1)} %bitcast.101), calls=%async_computation.12 | async-start | bytes 786432 | tf_op jit(solution)/shard_map/all_to_all | solution.py:295
  460.2 7.1 copy-start.24
  463.2 14.7 %all-to-all-start.14 = ((bf16[256,12,64]{0,2,1:T(8,128)(2,1)}), bf16[256,12,64]{0,2,1:T(8,128)(2,1)S(1)}, u32[]{:S(2)}, u32[]{:S(2)}) async-start(bf16[256,12,64]{0,2,1:T(8,128)(2,1)} %bitcast.659), calls=%async_computation.14 | async-start | bytes 786432 | tf_op jit(solution)/shard_map/all_to_all | solution.py:295
  476.2 7.0 copy-start.21
  476.2 7.0 copy-start.35
  476.2 7.0 copy-start.78
  476.2 7.0 copy-start.89
  477.9 52.5 %all-to-all-start.9 = ((bf16[4,2,73728]{2,1,0:T(2,128)(2,1)}), bf16[4,2,73728]{2,1,0:T(2,128)(2,1)}, u32[]{:S(2)}, u32[]{:S(2)}) async-start(bf16[4,2,73728]{2,1,0:T(2,128)(2,1)} %reshape.799), calls=%async_computation.9 | async-start | bytes 2359296 | tf_op jit(solution)/shard_map/all_to_all | solution.py:303
  528.8 7.2 copy-start.19
  528.8 7.2 copy-start.32
  528.8 7.2 copy-start.76
  528.8 7.2 copy-start.87
  530.5 51.6 %all-to-all-start.11 = ((bf16[4,2,73728]{2,1,0:T(2,128)(2,1)}), bf16[4,2,73728]{2,1,0:T(2,128)(2,1)}, u32[]{:S(2)}, u32[]{:S(2)}) async-start(bf16[4,2,73728]{2,1,0:T(2,128)(2,1)} %reshape.797), calls=%async_computation.11 | async-start | bytes 2359296 | tf_op jit(solution)/shard_map/all_to_all | solution.py:303
  573.7 7.7 copy-start.61
  582.1 53.2 %all-to-all-start.13 = ((bf16[4,2,73728]{2,1,0:T(2,128)(2,1)}), bf16[4,2,73728]{2,1,0:T(2,128)(2,1)}, u32[]{:S(2)}, u32[]{:S(2)}) async-start(bf16[4,2,73728]{2,1,0:T(2,128)(2,1)} %reshape.795), calls=%async_computation.13 | async-start | bytes 2359296 | tf_op jit(solution)/shard_map/all_to_all | solution.py:303
  635.3 25.6 %all-to-all-start.15 = ((bf16[4,2,73728]{2,1,0:T(2,128)(2,1)}), bf16[4,2,73728]{2,1,0:T(2,128)(2,1)}, u32[]{:S(2)}, u32[]{:S(2)}) async-start(bf16[4,2,73728]{2,1,0:T(2,128)(2,1)} %reshape.793), calls=%async_computation.15 | async-start | bytes 2359296 | tf_op jit(solution)/shard_map/all_to_all | solution.py:303
  639.6 104.4 %reduce-scatter.10.cloned.1.call-start = ((), (), s32[]{:S(2)}) async-start(), calls=%async_computation.22 | async-start | bytes 4423680
  697.8 72.1 %reduce-scatter.12.cloned.1.call-start = ((), (), s32[]{:S(2)}) async-start(), calls=%async_computation.23 | async-start | bytes 614400
  746.3 173.4 %reduce-scatter.8.cloned.1.call-start = ((), (), s32[]{:S(2)}) async-start(), calls=%async_computation.21 | async-start | bytes 11354112 | tf_op jit(solution)/shard_map/reduce_scatter | solution.py:290
  (94 other events, 330.5 us)
Sparse Core Ops, SparseCore 0:
  17.6 63.4 all-gather.2
  116.8 94.3 all-gather.4
  697.9 46.0 reduce-scatter.9
  746.7 23.1 reduce-scatter.11
  775.7 143.9 reduce-scatter.7

commit v4 on v3

--- a/solution.py
+++ b/solution.py
@@ -1,6 +1,8 @@
 import jax
 import jax.numpy as jnp
 from jax import lax
+from jax.experimental import pallas as pl
+from jax.experimental.pallas import tpu as pltpu
 from jax.experimental.layout import Layout, with_layout_constraint
 from jax.sharding import PartitionSpec as P
 
@@ -59,86 +61,6 @@
     )
 
 
-def masked_scores(queries, keys, seg_rows, seg_all, scale):
-    scores = jnp.einsum("qhd,khd->hqk", queries, keys, preferred_element_type=jnp.float32) * scale
-    allowed = seg_rows[:, None] == seg_all[None, :]
-    return jnp.where(allowed[None], scores, NEG)
-
-
-def attend_forward(item):
-    qkv, segment = item
-    queries, keys, values = qkv[:, 0], qkv[:, 1], qkv[:, 2]
-    length, heads, depth = queries.shape
-    rows = min(512, length)
-    blocks = length // rows
-    scale = depth ** (-0.5)
-
-    def one(piece):
-        block_q, block_seg = piece
-        scores = masked_scores(block_q, keys, block_seg, segment, scale)
-        highest = jnp.max(scores, axis=-1, keepdims=True)
-        raised = jnp.exp(scores - highest)
-        total = jnp.sum(raised, axis=-1, keepdims=True)
-        weights = (raised / total).astype(jnp.bfloat16)
-        context = jnp.einsum("hqk,khd->qhd", weights, values, preferred_element_type=jnp.float32)
-        return (context.astype(jnp.bfloat16), (highest + jnp.log(total))[..., 0])
-
-    context, logsum = lax.map(
-        one, (queries.reshape(blocks, rows, heads, depth), segment.reshape(blocks, rows))
-    )
-    return (context.reshape(length, heads, depth), logsum)
-
-
-def attend_backward(item):
-    qkv, segment, logsum, upstream = item
-    queries, keys, values = qkv[:, 0], qkv[:, 1], qkv[:, 2]
-    length, heads, depth = queries.shape
-    rows = min(512, length)
-    blocks = length // rows
-    scale = depth ** (-0.5)
-
-    def one(carry, piece):
-        key_acc, value_acc = carry
-        block_q, block_seg, block_sum, block_up = piece
-        scores = masked_scores(block_q, keys, block_seg, segment, scale)
-        weights = jnp.exp(scores - block_sum[..., None])
-        value_acc = value_acc + jnp.einsum(
-            "hqk,qhd->khd",
-            weights.astype(jnp.bfloat16),
-            block_up,
-            preferred_element_type=jnp.float32,
-        )
-        slope = jnp.einsum("qhd,khd->hqk", block_up, values, preferred_element_type=jnp.float32)
-        inner = jnp.sum(weights * slope, axis=-1, keepdims=True)
-        score_grad = (weights * (slope - inner)).astype(jnp.bfloat16)
-        query_grad = (
-            jnp.einsum("hqk,khd->qhd", score_grad, keys, preferred_element_type=jnp.float32) * scale
-        )
-        key_acc = (
-            key_acc
-            + jnp.einsum("hqk,qhd->khd", score_grad, block_q, preferred_element_type=jnp.float32)
-            * scale
-        )
-        return ((key_acc, value_acc), query_grad.astype(jnp.bfloat16))
-
-    empty = jnp.zeros((length, heads, depth), jnp.float32)
-    pieces = (
-        queries.reshape(blocks, rows, heads, depth),
-        segment.reshape(blocks, rows),
-        logsum,
-        upstream.reshape(blocks, rows, heads, depth),
-    )
-    (key_grad, value_grad), query_grad = lax.scan(one, (empty, empty), pieces)
-    return jnp.stack(
-        [
-            query_grad.reshape(length, heads, depth),
-            key_grad.astype(jnp.bfloat16),
-            value_grad.astype(jnp.bfloat16),
-        ],
-        axis=1,
-    )
-
-
 def lane_pick(block, index):
     lanes = lax.broadcasted_iota(jnp.int32, block.shape, 1)
     return jnp.sum(jnp.where(lanes == index, block, 0.0), axis=1)
@@ -151,6 +73,92 @@
         pieces.append(jnp.zeros((pieces[0].shape[0], extra), jnp.bfloat16))
     block = jnp.concatenate(pieces, axis=1)
     return with_layout_constraint(block, Layout(major_to_minor=(0, 1)))
+
+
+ROWS_PER_STEP = 256
+
+
+def attention_forward_kernel(qkv_ref, seg_col_ref, seg_row_ref, ctx_ref, lse_ref):
+    length = qkv_ref.shape[0]
+    heads = ctx_ref.shape[1] // DH
+    scale = DH ** (-0.5)
+    seg_row = seg_row_ref[...]
+    for h in range(heads):
+        keys = qkv_ref[:, pl.ds((heads + h) * DH, DH)]
+        values = qkv_ref[:, pl.ds((2 * heads + h) * DH, DH)]
+        for c in range(length // ROWS_PER_STEP):
+            rows = pl.ds(c * ROWS_PER_STEP, ROWS_PER_STEP)
+            queries = qkv_ref[rows, pl.ds(h * DH, DH)]
+            scores = times_transpose(queries, keys) * scale
+            scores = jnp.where(seg_col_ref[rows, :] == seg_row, scores, NEG)
+            highest = jnp.max(scores, axis=-1, keepdims=True)
+            raised = jnp.exp(scores - highest)
+            total = jnp.sum(raised, axis=-1, keepdims=True)
+            weights = (raised / total).astype(jnp.bfloat16)
+            context = jnp.dot(weights, values, preferred_element_type=jnp.float32)
+            ctx_ref[rows, pl.ds(h * DH, DH)] = context.astype(ctx_ref.dtype)
+            lse_ref[rows, pl.ds(h, 1)] = highest + jnp.log(total)
+
+
+def attention_backward_kernel(qkv_ref, seg_col_ref, seg_row_ref, lse_ref, up_ref, grad_ref):
+    length = qkv_ref.shape[0]
+    heads = up_ref.shape[1] // DH
+    scale = DH ** (-0.5)
+    seg_row = seg_row_ref[...]
+    for h in range(heads):
+        keys = qkv_ref[:, pl.ds((heads + h) * DH, DH)]
+        values = qkv_ref[:, pl.ds((2 * heads + h) * DH, DH)]
+        key_acc = jnp.zeros((length, DH), jnp.float32)
+        value_acc = jnp.zeros((length, DH), jnp.float32)
+        for c in range(length // ROWS_PER_STEP):
+            rows = pl.ds(c * ROWS_PER_STEP, ROWS_PER_STEP)
+            queries = qkv_ref[rows, pl.ds(h * DH, DH)]
+            upstream = up_ref[rows, pl.ds(h * DH, DH)]
+            scores = times_transpose(queries, keys) * scale
+            scores = jnp.where(seg_col_ref[rows, :] == seg_row, scores, NEG)
+            weights = jnp.exp(scores - lse_ref[rows, pl.ds(h, 1)])
+            value_acc = value_acc + contract_rows(weights.astype(jnp.bfloat16), upstream)
+            slope = times_transpose(upstream, values)
+            inner = jnp.sum(weights * slope, axis=-1, keepdims=True)
+            score_grad = (weights * (slope - inner)).astype(jnp.bfloat16)
+            query_grad = jnp.dot(score_grad, keys, preferred_element_type=jnp.float32) * scale
+            grad_ref[rows, pl.ds(h * DH, DH)] = query_grad.astype(grad_ref.dtype)
+            key_acc = key_acc + contract_rows(score_grad, queries) * scale
+        grad_ref[:, pl.ds((heads + h) * DH, DH)] = key_acc.astype(grad_ref.dtype)
+        grad_ref[:, pl.ds((2 * heads + h) * DH, DH)] = value_acc.astype(grad_ref.dtype)
+
+
+def attention_forward(qkv, segment):
+    length, width = qkv.shape
+    heads = width // (3 * DH)
+    flops = 4 * heads * length * length * DH
+    return pl.pallas_call(
+        attention_forward_kernel,
+        out_shape=(
+            jax.ShapeDtypeStruct((length, heads * DH), jnp.bfloat16),
+            jax.ShapeDtypeStruct((length, heads), jnp.float32),
+        ),
+        in_specs=[pl.BlockSpec(memory_space=pltpu.VMEM)] * 3,
+        out_specs=(pl.BlockSpec(memory_space=pltpu.VMEM),) * 2,
+        cost_estimate=pl.CostEstimate(
+            flops=flops, transcendentals=heads * length * length, bytes_accessed=3 * length * width
+        ),
+    )(qkv, segment.reshape(length, 1), segment.reshape(1, length))
+
+
+def attention_backward(qkv, segment, logsum, upstream):
+    length, width = qkv.shape
+    heads = width // (3 * DH)
+    flops = 10 * heads * length * length * DH
+    return pl.pallas_call(
+        attention_backward_kernel,
+        out_shape=jax.ShapeDtypeStruct((length, width), jnp.bfloat16),
+        in_specs=[pl.BlockSpec(memory_space=pltpu.VMEM)] * 5,
+        out_specs=pl.BlockSpec(memory_space=pltpu.VMEM),
+        cost_estimate=pl.CostEstimate(
+            flops=flops, transcendentals=heads * length * length, bytes_accessed=5 * length * width
+        ),
+    )(qkv, segment.reshape(length, 1), segment.reshape(1, length), logsum, upstream)
 
 
 def scatter_two_stage(block):
@@ -236,9 +244,12 @@
         one_qkv = lax.all_to_all(
             qkv.reshape(part_len, 3, heads, DH), "seq", split_axis=2, concat_axis=0, tiled=True
         )
-        context, one_sum = attend_forward((one_qkv, segment[s]))
+        local_heads = one_qkv.shape[2]
+        context, one_sum = attention_forward(one_qkv.reshape(LEN, -1), segment[s])
         context_parts.append(
-            lax.all_to_all(context, "seq", split_axis=0, concat_axis=1, tiled=True)
+            lax.all_to_all(
+                context.reshape(LEN, local_heads, DH), "seq", split_axis=0, concat_axis=1, tiled=True
+            )
         )
         head_qkv.append(one_qkv)
         logsum.append(one_sum)
@@ -299,8 +310,15 @@
             concat_axis=0,
             tiled=True,
         )
-        one_grads = attend_backward((head_qkv[s], segment[s], logsum[s], one_back))
-        back_parts.append(lax.all_to_all(one_grads, "seq", split_axis=0, concat_axis=2, tiled=True))
+        local_heads = one_back.shape[1]
+        one_grads = attention_backward(
+            head_qkv[s].reshape(LEN, -1), segment[s], logsum[s], one_back.reshape(LEN, -1)
+        )
+        back_parts.append(
+            lax.all_to_all(
+                one_grads.reshape(LEN, 3, local_heads, DH), "seq", split_axis=0, concat_axis=2, tiled=True
+            )
+        )
     rows_back = jnp.stack(back_parts).reshape(row_count, 3 * width)
     grad_qkv_weight = contract_rows(flat, rows_back)
     grad_query_bias = jnp.sum(rows_back[:, :width].astype(jnp.float32), axis=0)

time: 946 us -> 870 us (0.920)
  matrix products: 225 us -> 88.3 us
  Pallas kernels: 0 us -> 101 us
  other arithmetic: 81.5 us -> 33.3 us
  blocking collectives: 10.4 us -> 32.2 us
  local copies, waits for them, and re-layouts: 237 us -> 218 us
  waiting for transfers between devices: 300 us -> 318 us
    dot_general x56 -> x0, matrix products: 137 us -> none  [the longest x8 32.1 us: one(): jnp.einsum('hqk,qhd->khd', weights.astype(jnp.bfloat16), block_up, prefer...]
    pallas_call x0 -> x8, Pallas kernels: none -> 101 us  [the longest x4 59.8 us: attention_backward(): pl.pallas_call(attention_backward_kernel, out_shape=jax.ShapeDtypeStruct(...]
    another operation x28 -> x4, local copies, waits for them, and re-layouts: 31.9 us -> 4.77 us  [attention_forward(): segment.reshape(length, 1)]
    reshape x8 -> x16, local copies, waits for them, and re-layouts: 9.75 us -> 34.9 us  [the longest x4 18.3 us: per_device(): one_grads.reshape(LEN, 3, local_heads, DH)]
    all_to_all x4, waiting for transfers between devices: 24.8 us -> 49.3 us  [per_device(): lax.all_to_all(qkv.reshape(part_len, 3, heads, DH), 'seq', split_axis=2,...]
    all_to_all x1 -> x3, blocking collectives: 10.4 us -> 32.2 us  [per_device(): lax.all_to_all(back_context[s * part_len:(s + 1) * part_len].reshape(part...]
    pallas_call x0 -> x8, local copies, waits for them, and re-layouts: none -> 14.8 us  [the longest x4 9.62 us: attention_backward(): pl.pallas_call(attention_backward_kernel, out_shape=jax.ShapeDtypeStruct(...]
    convert_element_type x8 -> x0, other arithmetic: 14.5 us -> none  [one(): score_grad = (weights * (slope - inner)).astype(jnp.bfloat16)]
  transfers between devices with their start and end apart: 20 -> 18, of which waited for: 8 -> 7; matrix products, arithmetic and copies ran while one was open for 37% -> 19% of each run, Pallas kernels for 0% -> 12%
where the time goes in v4:
time: 870 us; the launch traced here: 859 us
  waiting for transfers between devices  318 us (37%)
  local copies, waits for them, and re-layouts  218 us (25%)
  Pallas kernels  101 us (12%)
  matrix products  88.3 us (10%)
  starting transfers between devices  53.2 us (6%)
  other arithmetic  33.3 us (4%)
  blocking collectives  32.2 us (4%)
  between operations  14.8 us (2%)
    reduce_scatter x1, waiting for transfers between devices, per_device(): lax.psum_scatter(early, axes, scatter_dimension=0, tiled=True)  147 us
    unnamed x86, local copies, waits for them, and re-layouts  62.6 us
    unnamed x7, waiting for transfers between devices  62 us
    pallas_call x4, Pallas kernels, attention_backward(): pl.pallas_call(attention_backward_kernel, out_shape=jax.ShapeDtypeStruct(...  59.8 us
    all_gather x1, waiting for transfers between devices, per_device(): full_first = lax.all_gather(first, axes, axis=0, tiled=True)  59.8 us
    all_to_all x4, waiting for transfers between devices, per_device(): lax.all_to_all(qkv.reshape(part_len, 3, heads, DH), 'seq', split_axis=2,...  49.3 us
    pallas_call x4, Pallas kernels, attention_forward(): pl.pallas_call(attention_forward_kernel, out_shape=(jax.ShapeDtypeStruct(...  41.4 us
    all_to_all x3, blocking collectives, per_device(): lax.all_to_all(back_context[s * part_len:(s + 1) * part_len].reshape(part...  32.2 us
  transfers between devices with their start and end apart: 18, of which 7 were waited for; matrix products, arithmetic and copies ran while one was open for 19% of the time, Pallas kernels for 12%

profile of v4, /device:TPU:0, one launch (start us, length us, event | category | flops | bytes accessed | tf_op | source)
XLA Modules:
  0.0 859.4 jit_solution(7521995323499063572)
XLA Ops:
  21.5 59.8 %all-gather.3.cloned.1.call-done = bf16[768,2316]{1,0:T(8,128)(2,1)} async-done(((bf16[24,2316]{1,0:T(8,128)(2,1)}), bf16[768,2316]{1,0:T(8,128)(2,1)}) %all-gather.3.cloned.1.call-update) | async-done | bytes 3557392 | tf_op jit(solution)/shard_map/all_gather | solution.py:219
  81.3 3.4 convert_reduce_fusion.1
  84.7 3.3 fusion.11
  89.1 3.5 all-to-all-start
  92.7 3.3 fusion.12
  97.1 12.2 %all-to-all-done = bf16[256,3,12,64]{0,3,1,2:T(8,128)(2,1)S(1)} async-done(((bf16[256,3,12,64]{0,3,1,2:T(8,128)(2,1)}), bf16[256,3,12,64]{0,3,1,2:T(8,128)(2,1)S(1)}, u32[]{:S(2)}, u32[]{:S(2)}) %all-to-all-start) | async-done | bytes 1179680 | tf_op jit(solution)/shard_map/all_to_all | solution.py:244
  110.3 3.5 all-to-all-start.2
  118.2 20.5 %all-to-all-done.2 = bf16[256,3,12,64]{0,3,1,2:T(8,128)(2,1)S(1)} async-done(((bf16[256,3,12,64]{0,3,1,2:T(8,128)(2,1)}), bf16[256,3,12,64]{0,3,1,2:T(8,128)(2,1)S(1)}, u32[]{:S(2)}, u32[]{:S(2)}) %all-to-all-start.2) | async-done | bytes 1179680 | tf_op jit(solution)/shard_map/all_to_all | solution.py:244
  139.8 3.5 all-to-all-start.4
  143.3 3.3 fusion.14
  147.8 16.6 %all-to-all-done.4 = bf16[256,3,12,64]{0,3,1,2:T(8,128)(2,1)S(1)} async-done(((bf16[256,3,12,64]{0,3,1,2:T(8,128)(2,1)}), bf16[256,3,12,64]{0,3,1,2:T(8,128)(2,1)S(1)}, u32[]{:S(2)}, u32[]{:S(2)}) %all-to-all-start.4) | async-done | bytes 1179680 | tf_op jit(solution)/shard_map/all_to_all | solution.py:244
  164.3 3.7 all-to-all-start.6
  175.9 10.4 %shard_map.305 = (bf16[1024,192]{1,0:T(8,128)(2,1)}, f32[1024,3]{1,0:T(8,128)}) custom-call(bf16[1024,576]{1,0:T(8,128)(2,1)} %copy.285.qkv_ref, s32[1024,1]{1,0:T(8,128)} %copy.286.seg_col_ref, s32[1,1024]{1,0:T(1,128)} %get-tuple-element.83.seg_row_ref), custom_call_target="tpu_custom_call" | custom-call | flops 805306368 | bytes 1769472 | tf_op jit(solution)/shard_map/pallas_call | solution.py:135
  191.4 4.4 all-to-all-start.1
  199.5 10.3 %shard_map.306 = (bf16[1024,192]{1,0:T(8,128)(2,1)}, f32[1024,3]{1,0:T(8,128)}) custom-call(bf16[1024,576]{1,0:T(8,128)(2,1)} %copy.294.qkv_ref, s32[1024,1]{1,0:T(8,128)} %copy.295.seg_col_ref, s32[1,1024]{1,0:T(1,128)} %get-tuple-element.90.seg_row_ref), custom_call_target="tpu_custom_call" | custom-call | flops 805306368 | bytes 1769472 | tf_op jit(solution)/shard_map/pallas_call | solution.py:135
  215.0 4.6 all-to-all-start.3
  229.4 10.3 %shard_map.307 = (bf16[1024,192]{1,0:T(8,128)(2,1)}, f32[1024,3]{1,0:T(8,128)}) custom-call(bf16[1024,576]{1,0:T(8,128)(2,1)} %copy.303.qkv_ref, s32[1024,1]{1,0:T(8,128)} %copy.304.seg_col_ref, s32[1,1024]{1,0:T(1,128)} %get-tuple-element.89.seg_row_ref), custom_call_target="tpu_custom_call" | custom-call | flops 805306368 | bytes 1769472 | tf_op jit(solution)/shard_map/pallas_call | solution.py:135
  244.8 4.4 all-to-all-start.5
  252.9 10.3 %shard_map.308 = (bf16[1024,192]{1,0:T(8,128)(2,1)}, f32[1024,3]{1,0:T(8,128)}) custom-call(bf16[1024,576]{1,0:T(8,128)(2,1)} %copy.312.qkv_ref, s32[1024,1]{1,0:T(8,128)} %copy.313.seg_col_ref, s32[1,1024]{1,0:T(1,128)} %get-tuple-element.88.seg_row_ref), custom_call_target="tpu_custom_call" | custom-call | flops 805306368 | bytes 1769472 | tf_op jit(solution)/shard_map/pallas_call | solution.py:135
  266.6 4.4 all-to-all-start.7
  284.0 4.0 fusion.55
  290.2 4.9 slice.173
  295.1 8.5 reshape.410
  303.6 12.7 %multiply_convert_fusion = (bf16[1024,3072]{1,0:T(8,128)(2,1)S(1)}, f32[1024,3072]{1,0:T(8,128)}) fusion(f32[3072]{0:T(1024)S(1)} %copy-done.18, bf16[768,6912]{1,0:T(8,128)(2,1)} %all-gather.5.cloned.1.call-done, f32[1024,768]{1,0:T(8,128)} %copy-done.2, f32[768]{0:T(1024)S(1)} %copy-done.21, f32[768]{0:T(1024)S(1)} %get-tuple-element.47, ...), kind=kOutput, calls=%fused_computation.7 | convolution fusion | flops 4854644736 | bytes 26765312 | tf_op jit(solution)/shard_map/dot_general | solution.py:262
  316.4 5.4 fusion.56
  322.4 3.3 fusion.21
  329.1 7.0 convolution_convert_fusion
  336.2 8.6 %convert_element_type.320 = bf16[768,3072]{1,0:T(8,128)(2,1)} reshape(bf16[3072,768]{1,0:T(8,128)(2,1)} %convolution_convert_fusion) | data formatting | bytes 9437184 | tf_op jit(solution)/shard_map/convert_element_type | solution.py:70
  344.8 12.2 %fusion.57 = (bf16[3072]{0:T(1024)(128)(2,1)S(1)}, bf16[1024,3072]{1,0:T(8,128)(2,1)S(1)}) fusion(f32[1024,3072]{1,0:T(8,128)} %get-tuple-element.94, f32[3072]{0:T(1024)S(1)} %copy-done.18, bf16[3072,768]{1,0:T(8,128)(2,1)} %reshape.410, f32[1024,768]{1,0:T(8,128)S(1)} %copy-done.12), kind=kOutput, calls=%fused_computation.138 | convolution fusion | flops 4870370304 | bytes 26757120 | tf_op jit(solution)/shard_map/dot_general | solution.py:27
  357.0 8.0 convolution_convert_fusion.1
  365.0 8.3 multiply_reduce_fusion
  381.8 17.8 %concatenate.20 = bf16[768,7168]{1,0:T(8,128)(2,1)} concatenate(bf16[768,768]{1,0:T(8,128)(2,1)S(1)} %convolution_convert_fusion.4, bf16[768,3072]{1,0:T(8,128)(2,1)} %convolution_convert_fusion.1, bf16[768,3072]{1,0:T(8,128)(2,1)} %convert_element_type.320, bf16[768,1]{1,0:T(8,128)(2,1)S(1)} %convert_element_type.348, bf16[768,1]{1,0:T(8,128)(2,1)} %convert_element_type.349, ...), dimensions={1} | concatenate | bytes 22020096 | tf_op jit(solution)/shard_map/concatenate | solution.py:74
  403.2 10.7 %all_to_all.240 = bf16[256,12,64]{0,2,1:T(8,128)(2,1)S(1)} all-to-all(bf16[256,12,64]{0,2,1:T(8,128)(2,1)S(1)} %bitcast.271), channel_id=1, replica_groups=mesh['seq'=4,'shard'=8] {'seq'}, dimensions={1} | all-to-all | bytes 786432 | tf_op jit(solution)/shard_map/all_to_all | solution.py:306
  413.9 10.6 %all_to_all.241 = bf16[256,12,64]{0,2,1:T(8,128)(2,1)} all-to-all(bf16[256,12,64]{0,2,1:T(8,128)(2,1)S(1)} %bitcast.270), channel_id=1, replica_groups=mesh['seq'=4,'shard'=8] {'seq'}, dimensions={1} | all-to-all | bytes 786432 | tf_op jit(solution)/shard_map/all_to_all | solution.py:306
  424.5 10.9 %all_to_all.242 = bf16[256,12,64]{0,2,1:T(8,128)(2,1)} all-to-all(bf16[256,12,64]{0,2,1:T(8,128)(2,1)S(1)} %bitcast.269), channel_id=1, replica_groups=mesh['seq'=4,'shard'=8] {'seq'}, dimensions={1} | all-to-all | bytes 786432 | tf_op jit(solution)/shard_map/all_to_all | solution.py:306
  435.4 3.9 all-to-all-start.14
  440.7 14.8 %shard_map.309 = bf16[1024,576]{1,0:T(8,128)(2,1)} custom-call(bf16[1024,576]{1,0:T(8,128)(2,1)} %copy.285.qkv_ref, s32[1024,1]{1,0:T(8,128)} %copy.286.seg_col_ref, s32[1,1024]{1,0:T(1,128)} %get-tuple-element.83.seg_row_ref, f32[1024,3]{1,0:T(8,128)} %get-tuple-element.31.lse_ref, bf16[1024,192]{1,0:T(8,128)(2,1)} %copy.329.up_ref), custom_call_target="tpu_custom_call" | custom-call | flops 2013265920 | bytes 2949120 | tf_op jit(solution)/shard_map/pallas_call | solution.py:153
  457.9 4.6 copy.331
  465.6 4.3 all-to-all-start.9
  472.2 15.1 %shard_map.310 = bf16[1024,576]{1,0:T(8,128)(2,1)} custom-call(bf16[1024,576]{1,0:T(8,128)(2,1)} %copy.294.qkv_ref, s32[1024,1]{1,0:T(8,128)} %copy.295.seg_col_ref, s32[1,1024]{1,0:T(1,128)} %get-tuple-element.90.seg_row_ref, f32[1024,3]{1,0:T(8,128)} %get-tuple-element.33.lse_ref, bf16[1024,192]{1,0:T(8,128)(2,1)} %copy.337.up_ref), custom_call_target="tpu_custom_call" | custom-call | flops 2013265920 | bytes 2949120 | tf_op jit(solution)/shard_map/pallas_call | solution.py:153
  489.7 4.6 copy.339
  497.4 4.3 all-to-all-start.11
  504.0 14.8 %shard_map.311 = bf16[1024,576]{1,0:T(8,128)(2,1)} custom-call(bf16[1024,576]{1,0:T(8,128)(2,1)} %copy.303.qkv_ref, s32[1024,1]{1,0:T(8,128)} %copy.304.seg_col_ref, s32[1,1024]{1,0:T(1,128)} %get-tuple-element.89.seg_row_ref, f32[1024,3]{1,0:T(8,128)} %get-tuple-element.34.lse_ref, bf16[1024,192]{1,0:T(8,128)(2,1)} %copy.345.up_ref), custom_call_target="tpu_custom_call" | custom-call | flops 2013265920 | bytes 2949120 | tf_op jit(solution)/shard_map/pallas_call | solution.py:153
  521.3 4.6 copy.347
  529.0 4.3 all-to-all-start.13
  534.6 15.1 %shard_map.312 = bf16[1024,576]{1,0:T(8,128)(2,1)} custom-call(bf16[1024,576]{1,0:T(8,128)(2,1)} %copy.312.qkv_ref, s32[1024,1]{1,0:T(8,128)} %copy.313.seg_col_ref, s32[1,1024]{1,0:T(1,128)} %get-tuple-element.88.seg_row_ref, f32[1024,3]{1,0:T(8,128)} %get-tuple-element.35.lse_ref, bf16[1024,192]{1,0:T(8,128)(2,1)} %copy.353.up_ref), custom_call_target="tpu_custom_call" | custom-call | flops 2013265920 | bytes 2949120 | tf_op jit(solution)/shard_map/pallas_call | solution.py:153
  552.1 4.6 copy.355
  559.8 4.3 all-to-all-start.15
  564.1 3.5 reshape.466
  567.6 3.5 copy.333
  571.1 3.5 reshape.464
  574.6 3.5 copy.341
  578.1 3.5 reshape.462
  581.5 3.5 copy.349
  585.1 3.5 reshape.460
  588.5 3.5 copy.357
  594.7 4.5 copy.358
  600.8 4.3 fusion.6
  608.1 5.7 concatenate.21
  613.8 5.1 copy.385
  621.8 48.7 %reduce-scatter.10.cloned.1.call-done = bf16[24,10240]{1,0:T(8,128)(2,1)} async-done(((bf16[192,10240]{1,0:T(8,128)(2,1)}), bf16[24,10240]{1,0:T(8,128)(2,1)}) %reduce-scatter.10.cloned.1.call-update) | async-done | bytes 491536
  674.7 9.0 %fusion.32 = f32[1024,768]{1,0:T(8,128)} fusion(f32[1024,768]{1,0:T(8,128)S(1)} %copy-done.10, bf16[1024,2304]{0,1:T(8,128)(2,1)} %bitcast.228, bf16[768,2316]{1,0:T(8,128)(2,1)} %all-gather.3.cloned.1.call-done), kind=kOutput, calls=%fused_computation.56 | convolution fusion | flops 3624665088 | bytes 14548992 | tf_op jit(solution)/shard_map/dot_general | solution.py:27
  683.8 12.6 %reduce-scatter.12.cloned.1.call-done = bf16[24,2560]{1,0:T(8,128)(2,1)} async-done(((bf16[96,2560]{1,0:T(8,128)(2,1)}), bf16[24,2560]{1,0:T(8,128)(2,1)}) %reduce-scatter.12.cloned.1.call-update) | async-done | bytes 122896
  698.8 147.4 %reduce-scatter.8.cloned.1.call-done = bf16[24,7168]{1,0:T(8,128)(2,1)} async-done(((bf16[768,7168]{1,0:T(8,128)(2,1)}), bf16[24,7168]{1,0:T(8,128)(2,1)}) %reduce-scatter.8.cloned.1.call-update) | async-done | bytes 344080 | tf_op jit(solution)/shard_map/reduce_scatter | solution.py:301
  (222 shorter events, 151.2 us)
Async XLA Ops:
  7.2 77.5 %copy-start.25 = (bf16[4,256,768]{2,1,0:T(8,128)(2,1)S(1)}, bf16[4,256,768]{2,1,0:T(8,128)(2,1)}, u32[]{:S(2)}) copy-start(bf16[4,256,768]{2,1,0:T(8,128)(2,1)} %param.18) | copy-start | bytes 4718596
  7.2 74.1 %all-gather.3.cloned.1.call-start = ((), (), s32[]{:S(2)}) async-start(), calls=%async_computation.19 | async-start | bytes 3852288 | tf_op jit(solution)/shard_map/all_gather | solution.py:219
  17.6 266.4 %all-gather.5.cloned.1.call-start = ((), (), s32[]{:S(2)}) async-start(), calls=%async_computation.20 | async-start | bytes 10948608 | tf_op jit(solution)/shard_map/all_gather | solution.py:220
  89.1 20.2 %all-to-all-start = ((bf16[256,3,12,64]{0,3,1,2:T(8,128)(2,1)}), bf16[256,3,12,64]{0,3,1,2:T(8,128)(2,1)S(1)}, u32[]{:S(2)}, u32[]{:S(2)}) async-start(bf16[256,3,12,64]{0,3,1,2:T(8,128)(2,1)} %copy.281), calls=%async_computation | async-start | bytes 2359296 | tf_op jit(solution)/shard_map/all_to_all | solution.py:244
  109.3 1.0 copy-start.9
  110.3 28.4 %all-to-all-start.2 = ((bf16[256,3,12,64]{0,3,1,2:T(8,128)(2,1)}), bf16[256,3,12,64]{0,3,1,2:T(8,128)(2,1)S(1)}, u32[]{:S(2)}, u32[]{:S(2)}) async-start(bf16[256,3,12,64]{0,3,1,2:T(8,128)(2,1)} %copy.291), calls=%async_computation.2 | async-start | bytes 2359296 | tf_op jit(solution)/shard_map/all_to_all | solution.py:244
  138.7 1.1 copy-start.7
  139.8 24.6 %all-to-all-start.4 = ((bf16[256,3,12,64]{0,3,1,2:T(8,128)(2,1)}), bf16[256,3,12,64]{0,3,1,2:T(8,128)(2,1)S(1)}, u32[]{:S(2)}, u32[]{:S(2)}) async-start(bf16[256,3,12,64]{0,3,1,2:T(8,128)(2,1)} %copy.300), calls=%async_computation.4 | async-start | bytes 2359296 | tf_op jit(solution)/shard_map/all_to_all | solution.py:244
  146.7 21.4 %copy-start.24 = (s32[4,17]{1,0:T(4,128)S(1)}, s32[4,17]{1,0:T(4,128)}, u32[]{:S(2)}) copy-start(s32[4,17]{1,0:T(4,128)} %param.20) | copy-start | bytes 820
  164.3 9.1 %copy-start.6 = (bf16[256,3,12,64]{0,3,1,2:T(8,128)(2,1)}, bf16[256,3,12,64]{0,3,1,2:T(8,128)(2,1)S(1)}, u32[]{:S(2)}) copy-start(bf16[256,3,12,64]{0,3,1,2:T(8,128)(2,1)S(1)} %all-to-all-done.4) | copy-start | bytes 3538948
  164.3 27.1 %all-to-all-start.6 = ((bf16[256,3,12,64]{0,3,1,2:T(8,128)(2,1)}), bf16[256,3,12,64]{0,3,1,2:T(8,128)(2,1)S(1)}, u32[]{:S(2)}, u32[]{:S(2)}) async-start(bf16[256,3,12,64]{0,3,1,2:T(8,128)(2,1)} %copy.309), calls=%async_computation.6 | async-start | bytes 2359296 | tf_op jit(solution)/shard_map/all_to_all | solution.py:244
  186.2 10.6 %copy-start.8 = (bf16[256,3,12,64]{0,3,1,2:T(8,128)(2,1)S(1)}, bf16[256,3,12,64]{0,3,1,2:T(8,128)(2,1)}, u32[]{:S(2)}) copy-start(bf16[256,3,12,64]{0,3,1,2:T(8,128)(2,1)} %copy-done.7) | copy-start | bytes 3538948
  191.4 23.6 %all-to-all-start.1 = ((bf16[4,2,24576]{2,1,0:T(2,128)(2,1)}), bf16[4,2,24576]{2,1,0:T(2,128)(2,1)S(1)}, u32[]{:S(2)}, u32[]{:S(2)}) async-start(bf16[4,2,24576]{2,1,0:T(2,128)(2,1)} %reshape.457), calls=%async_computation.1 | async-start | bytes 786432 | tf_op jit(solution)/shard_map/all_to_all | solution.py:250
  209.8 12.6 %copy-start = (bf16[4,256,768]{2,1,0:T(8,128)(2,1)S(1)}, bf16[4,256,768]{2,1,0:T(8,128)(2,1)}, u32[]{:S(2)}) copy-start(bf16[4,256,768]{2,1,0:T(8,128)(2,1)} %param.19) | copy-start | bytes 4718596
  215.0 12.0 %copy-start.15 = (bf16[4,2,24576]{2,1,0:T(2,128)(2,1)}, bf16[4,2,24576]{2,1,0:T(2,128)(2,1)S(1)}, u32[]{:S(2)}) copy-start(bf16[4,2,24576]{2,1,0:T(2,128)(2,1)S(1)} %all-to-all-done.1) | copy-start | bytes 1179652
  215.0 29.8 %all-to-all-start.3 = ((bf16[4,2,24576]{2,1,0:T(2,128)(2,1)}), bf16[4,2,24576]{2,1,0:T(2,128)(2,1)}, u32[]{:S(2)}, u32[]{:S(2)}) async-start(bf16[4,2,24576]{2,1,0:T(2,128)(2,1)} %reshape.455), calls=%async_computation.3 | async-start | bytes 786432 | tf_op jit(solution)/shard_map/all_to_all | solution.py:250
  244.8 21.8 %all-to-all-start.5 = ((bf16[4,2,24576]{2,1,0:T(2,128)(2,1)}), bf16[4,2,24576]{2,1,0:T(2,128)(2,1)}, u32[]{:S(2)}, u32[]{:S(2)}) async-start(bf16[4,2,24576]{2,1,0:T(2,128)(2,1)} %reshape.453), calls=%async_computation.5 | async-start | bytes 786432 | tf_op jit(solution)/shard_map/all_to_all | solution.py:250
  265.2 7.1 copy-start.16
  266.6 11.7 %all-to-all-start.7 = ((bf16[4,2,24576]{2,1,0:T(2,128)(2,1)}), bf16[4,2,24576]{2,1,0:T(2,128)(2,1)}, u32[]{:S(2)}, u32[]{:S(2)}) async-start(bf16[4,2,24576]{2,1,0:T(2,128)(2,1)} %reshape.451), calls=%async_computation.7 | async-start | bytes 786432 | tf_op jit(solution)/shard_map/all_to_all | solution.py:250
  282.4 1.6 copy-start.23
  284.0 4.0 copy-start.13
  288.0 1.7 copy-start.2
  295.1 8.5 copy-start.18
  295.1 8.5 copy-start.21
  303.6 12.7 %copy-start.3 = (f32[1024,768]{1,0:T(8,128)S(1)}, f32[1024,768]{1,0:T(8,128)}, u32[]{:S(2)}) copy-start(f32[1024,768]{1,0:T(8,128)} %copy-done.2) | copy-start | bytes 9437188
  303.6 12.7 %copy-start.5 = (bf16[3072,768]{1,0:T(8,128)(2,1)S(1)}, bf16[3072,768]{1,0:T(8,128)(2,1)}, u32[]{:S(2)}) copy-start(bf16[3072,768]{1,0:T(8,128)(2,1)} %reshape.410) | copy-start | bytes 14155780
  303.6 12.7 %copy-start.22 = (f32[768]{0:T(1024)S(1)}, f32[768]{0:T(1024)}, u32[]{:S(2)}) copy-start(f32[768]{0:T(1024)} %get-tuple-element.45) | copy-start | bytes 9220
  327.4 1.7 copy-start.11
  336.2 8.6 %copy-start.12 = (f32[1024,768]{1,0:T(8,128)S(1)}, f32[1024,768]{1,0:T(8,128)}, u32[]{:S(2)}) copy-start(f32[1024,768]{1,0:T(8,128)} %copy-done.11) | copy-start | bytes 9437188
  344.8 12.2 %copy-start.4 = (f32[1024,768]{1,0:T(8,128)S(1)}, f32[1024,768]{1,0:T(8,128)}, u32[]{:S(2)}) copy-start(f32[1024,768]{1,0:T(8,128)} %copy-done.2) | copy-start | bytes 9437188
  373.3 2.3 copy-start.14
  375.6 4.4 copy-start.20
  375.6 5.3 copy-start.19
  375.6 6.1 copy-start.17
  435.4 30.2 %all-to-all-start.14 = ((bf16[256,12,64]{0,2,1:T(8,128)(2,1)}), bf16[256,12,64]{0,2,1:T(8,128)(2,1)S(1)}, u32[]{:S(2)}, u32[]{:S(2)}) async-start(bf16[256,12,64]{0,2,1:T(8,128)(2,1)} %bitcast.83), calls=%async_computation.14 | async-start | bytes 786432 | tf_op jit(solution)/shard_map/all_to_all | solution.py:306
  465.6 31.8 %all-to-all-start.9 = ((bf16[4,2,73728]{2,1,0:T(2,128)(2,1)}), bf16[4,2,73728]{2,1,0:T(2,128)(2,1)}, u32[]{:S(2)}, u32[]{:S(2)}) async-start(bf16[4,2,73728]{2,1,0:T(2,128)(2,1)} %reshape.465), calls=%async_computation.9 | async-start | bytes 2359296 | tf_op jit(solution)/shard_map/all_to_all | solution.py:318
  497.4 31.6 %all-to-all-start.11 = ((bf16[4,2,73728]{2,1,0:T(2,128)(2,1)}), bf16[4,2,73728]{2,1,0:T(2,128)(2,1)}, u32[]{:S(2)}, u32[]{:S(2)}) async-start(bf16[4,2,73728]{2,1,0:T(2,128)(2,1)} %reshape.463), calls=%async_computation.11 | async-start | bytes 2359296 | tf_op jit(solution)/shard_map/all_to_all | solution.py:318
  529.0 30.8 %all-to-all-start.13 = ((bf16[4,2,73728]{2,1,0:T(2,128)(2,1)}), bf16[4,2,73728]{2,1,0:T(2,128)(2,1)}, u32[]{:S(2)}, u32[]{:S(2)}) async-start(bf16[4,2,73728]{2,1,0:T(2,128)(2,1)} %reshape.461), calls=%async_computation.13 | async-start | bytes 2359296 | tf_op jit(solution)/shard_map/all_to_all | solution.py:318
  559.8 25.3 %all-to-all-start.15 = ((bf16[4,2,73728]{2,1,0:T(2,128)(2,1)}), bf16[4,2,73728]{2,1,0:T(2,128)(2,1)}, u32[]{:S(2)}, u32[]{:S(2)}) async-start(bf16[4,2,73728]{2,1,0:T(2,128)(2,1)} %reshape.459), calls=%async_computation.15 | async-start | bytes 2359296 | tf_op jit(solution)/shard_map/all_to_all | solution.py:318
  564.0 106.5 %reduce-scatter.10.cloned.1.call-start = ((), (), s32[]{:S(2)}) async-start(), calls=%async_computation.22 | async-start | bytes 4423680
  599.2 1.5 copy-start.26
  600.8 4.4 copy-start.1
  621.8 74.6 %reduce-scatter.12.cloned.1.call-start = ((), (), s32[]{:S(2)}) async-start(), calls=%async_computation.23 | async-start | bytes 614400
  672.8 1.9 copy-start.10
  672.9 173.4 %reduce-scatter.8.cloned.1.call-start = ((), (), s32[]{:S(2)}) async-start(), calls=%async_computation.21 | async-start | bytes 11354112 | tf_op jit(solution)/shard_map/reduce_scatter | solution.py:301
Sparse Core Ops, SparseCore 0:
  17.8 63.4 all-gather.2
  84.3 119.2 all-gather.4
  621.9 48.6 reduce-scatter.9
  673.2 23.1 reduce-scatter.11
  702.2 143.9 reduce-scatter.7

commit v5 on v4

--- a/solution.py
+++ b/solution.py
@@ -234,21 +234,35 @@
     heads = width // DH
     flat = layer_in.reshape(row_count, width)
     qkv_bias = jnp.concatenate([bias_query, jnp.zeros_like(bias_query), bias_value])
+    ways = lax.axis_size("seq")
+    local_heads = heads // ways
+
+    def by_owner(columns):
+        lead = columns.shape[:-1]
+        split = columns.reshape(*lead, 3, ways, local_heads * DH)
+        return jnp.swapaxes(split, -3, -2).reshape(*lead, 3 * width)
+
+    def by_kind(columns):
+        lead = columns.shape[:-1]
+        split = columns.reshape(*lead, ways, 3, local_heads * DH)
+        return jnp.swapaxes(split, -3, -2).reshape(*lead, 3 * width)
+
+    owner_qkv = by_owner(full_qkv)
+    owner_bias = by_owner(qkv_bias)
     segment = segment_ids(doc_starts, LEN)
     head_qkv, context_parts, logsum = [], [], []
     for s in range(streams):
         qkv = (
-            jnp.dot(flat[s * part_len : (s + 1) * part_len], full_qkv, preferred_element_type=jnp.float32)
-            + qkv_bias
+            jnp.dot(flat[s * part_len : (s + 1) * part_len], owner_qkv, preferred_element_type=jnp.float32)
+            + owner_bias
         ).astype(jnp.bfloat16)
         one_qkv = lax.all_to_all(
-            qkv.reshape(part_len, 3, heads, DH), "seq", split_axis=2, concat_axis=0, tiled=True
-        )
-        local_heads = one_qkv.shape[2]
-        context, one_sum = attention_forward(one_qkv.reshape(LEN, -1), segment[s])
+            qkv.reshape(part_len, ways, -1), "seq", split_axis=1, concat_axis=0, tiled=True
+        ).reshape(LEN, -1)
+        context, one_sum = attention_forward(one_qkv, segment[s])
         context_parts.append(
             lax.all_to_all(
-                context.reshape(LEN, local_heads, DH), "seq", split_axis=0, concat_axis=1, tiled=True
+                context.reshape(LEN, 1, -1), "seq", split_axis=0, concat_axis=1, tiled=True
             )
         )
         head_qkv.append(one_qkv)
@@ -304,26 +318,24 @@
     back_parts = []
     for s in range(streams):
         one_back = lax.all_to_all(
-            back_context[s * part_len : (s + 1) * part_len].reshape(part_len, heads, DH),
+            back_context[s * part_len : (s + 1) * part_len].reshape(part_len, ways, -1),
             "seq",
             split_axis=1,
             concat_axis=0,
             tiled=True,
-        )
-        local_heads = one_back.shape[1]
-        one_grads = attention_backward(
-            head_qkv[s].reshape(LEN, -1), segment[s], logsum[s], one_back.reshape(LEN, -1)
-        )
+        ).reshape(LEN, -1)
+        one_grads = attention_backward(head_qkv[s], segment[s], logsum[s], one_back)
         back_parts.append(
             lax.all_to_all(
-                one_grads.reshape(LEN, 3, local_heads, DH), "seq", split_axis=0, concat_axis=2, tiled=True
+                one_grads.reshape(LEN, 1, -1), "seq", split_axis=0, concat_axis=1, tiled=True
             )
         )
     rows_back = jnp.stack(back_parts).reshape(row_count, 3 * width)
-    grad_qkv_weight = contract_rows(flat, rows_back)
-    grad_query_bias = jnp.sum(rows_back[:, :width].astype(jnp.float32), axis=0)
-    grad_value_bias = jnp.sum(rows_back[:, 2 * width :].astype(jnp.float32), axis=0)
-    input_grad = (back_first + times_transpose(rows_back, full_qkv)).reshape(
+    grad_qkv_weight = by_kind(contract_rows(flat, rows_back))
+    grad_qkv_bias = by_kind(jnp.sum(rows_back.astype(jnp.float32), axis=0))
+    grad_query_bias = grad_qkv_bias[:width]
+    grad_value_bias = grad_qkv_bias[2 * width :]
+    input_grad = (back_first + times_transpose(rows_back, owner_qkv)).reshape(
         streams, part_len, width
     )
     late = pack_lanes([grad_qkv_weight, grad_query_bias[:, None], grad_value_bias[:, None]])

time: 870 us -> 875 us (level)
  other arithmetic: 33.3 us -> 61.7 us
  local copies, waits for them, and re-layouts: 218 us -> 196 us
    reshape x20 -> x1, local copies, waits for them, and re-layouts: 39.3 us -> 0.51 us  [per_device(): context.reshape(LEN, 1, -1)]
    reshape x0 -> x8, other arithmetic: none -> 21.1 us  [the longest x4 13.1 us: per_device(): one_grads.reshape(LEN, 1, -1)]
    pallas_call x8 -> x0, local copies, waits for them, and re-layouts: 14.8 us -> none  [the longest x4 9.62 us: attention_backward(): pl.pallas_call(attention_backward_kernel, out_shape=jax.ShapeDtypeStruct(...]
    all_to_all x12 -> x20, local copies, waits for them, and re-layouts: 23.6 us -> 34.4 us  [the longest x8 13.6 us: per_device(): lax.all_to_all(context.reshape(LEN, 1, -1), 'seq', split_axis=0, concat_a...]
    unnamed x86 -> x83, local copies, waits for them, and re-layouts: 62.6 us -> 70.5 us
    convert_element_type x10 -> x12, local copies, waits for them, and re-layouts: 15.8 us -> 20.4 us  [pack_lanes(): pieces = [p.astype(jnp.bfloat16) for p in pieces]]
  transfers between devices with their start and end apart: 18 -> 18, of which waited for: 7 -> 7; matrix products, arithmetic and copies ran while one was open for 19% -> 17% of each run, Pallas kernels for 12% -> 12%
where the time goes in v5:
time: 875 us; the launch traced here: 864 us
  waiting for transfers between devices  321 us (37%)
  local copies, waits for them, and re-layouts  196 us (22%)
  Pallas kernels  100 us (11%)
  matrix products  86.8 us (10%)
  other arithmetic  61.7 us (7%)
  starting transfers between devices  55.9 us (6%)
  blocking collectives  28.7 us (3%)
  between operations  14.8 us (2%)
    reduce_scatter x1, waiting for transfers between devices, per_device(): lax.psum_scatter(early, axes, scatter_dimension=0, tiled=True)  147 us
    unnamed x83, local copies, waits for them, and re-layouts  70.5 us
    unnamed x7, waiting for transfers between devices  60.9 us
    all_gather x1, waiting for transfers between devices, per_device(): full_first = lax.all_gather(first, axes, axis=0, tiled=True)  59.7 us
    pallas_call x4, Pallas kernels, attention_backward(): pl.pallas_call(attention_backward_kernel, out_shape=jax.ShapeDtypeStruct(...  58.6 us
    all_to_all x4, waiting for transfers between devices, per_device(): lax.all_to_all(qkv.reshape(part_len, ways, -1), 'seq', split_axis=1, conc...  52.9 us
    pallas_call x4, Pallas kernels, attention_forward(): pl.pallas_call(attention_forward_kernel, out_shape=(jax.ShapeDtypeStruct(...  41.4 us
    dot_general x4, matrix products, times_transpose(): lax.dot_general(left, right, (((1,), (1,)), ((), ())), preferred_element_...  31.6 us
  transfers between devices with their start and end apart: 18, of which 7 were waited for; matrix products, arithmetic and copies ran while one was open for 17% of the time, Pallas kernels for 12%

profile of v5, /device:TPU:0, one launch (start us, length us, event | category | flops | bytes accessed | tf_op | source)
XLA Modules:
  0.0 864.4 jit_solution(10960988777387565825)
XLA Ops:
  21.4 59.7 %all-gather.3.cloned.1.call-done = bf16[768,2316]{1,0:T(8,128)(2,1)} async-done(((bf16[24,2316]{1,0:T(8,128)(2,1)}), bf16[768,2316]{1,0:T(8,128)(2,1)}) %all-gather.3.cloned.1.call-update) | async-done | bytes 3557392 | tf_op jit(solution)/shard_map/all_gather | solution.py:219
  81.1 3.7 convert_reduce_fusion.1
  87.8 3.6 copy.401
  93.7 3.4 fusion.10
  97.2 4.3 all-to-all-start
  101.5 3.1 fusion.11
  104.6 18.4 %all-to-all-done = bf16[256,4,576]{0,2,1:T(8,128)(2,1)} async-done(((bf16[256,4,576]{0,2,1:T(8,128)(2,1)}), bf16[256,4,576]{0,2,1:T(8,128)(2,1)}, u32[]{:S(2)}, u32[]{:S(2)}) %all-to-all-start) | async-done | bytes 1179680 | tf_op jit(solution)/shard_map/all_to_all | solution.py:259
  123.0 4.3 all-to-all-start.2
  127.3 3.2 fusion.12
  130.5 11.3 %all-to-all-done.2 = bf16[256,4,576]{0,2,1:T(8,128)(2,1)} async-done(((bf16[256,4,576]{0,2,1:T(8,128)(2,1)}), bf16[256,4,576]{0,2,1:T(8,128)(2,1)}, u32[]{:S(2)}, u32[]{:S(2)}) %all-to-all-start.2) | async-done | bytes 1179680 | tf_op jit(solution)/shard_map/all_to_all | solution.py:259
  141.7 4.3 all-to-all-start.4
  146.0 3.2 fusion.13
  149.2 23.2 %all-to-all-done.4 = bf16[256,4,576]{0,2,1:T(8,128)(2,1)} async-done(((bf16[256,4,576]{0,2,1:T(8,128)(2,1)}), bf16[256,4,576]{0,2,1:T(8,128)(2,1)}, u32[]{:S(2)}, u32[]{:S(2)}) %all-to-all-start.4) | async-done | bytes 1179680 | tf_op jit(solution)/shard_map/all_to_all | solution.py:259
  172.4 3.8 all-to-all-start.6
  180.6 10.4 %shard_map.305 = (bf16[1024,192]{1,0:T(8,128)(2,1)}, f32[1024,3]{1,0:T(8,128)}) custom-call(bf16[1024,576]{1,0:T(8,128)(2,1)} %bitcast.257, s32[1024,1]{1,0:T(8,128)} %copy.335.seg_col_ref, s32[1,1024]{1,0:T(1,128)} %get-tuple-element.83.seg_row_ref), custom_call_target="tpu_custom_call" | custom-call | flops 805306368 | bytes 1769472 | tf_op jit(solution)/shard_map/pallas_call | solution.py:135
  194.8 4.9 all-to-all-start.1
  203.1 10.3 %shard_map.306 = (bf16[1024,192]{1,0:T(8,128)(2,1)}, f32[1024,3]{1,0:T(8,128)}) custom-call(bf16[1024,576]{1,0:T(8,128)(2,1)} %bitcast.259, s32[1024,1]{1,0:T(8,128)} %copy.340.seg_col_ref, s32[1,1024]{1,0:T(1,128)} %get-tuple-element.90.seg_row_ref), custom_call_target="tpu_custom_call" | custom-call | flops 805306368 | bytes 1769472 | tf_op jit(solution)/shard_map/pallas_call | solution.py:135
  217.0 4.4 all-to-all-start.3
  227.0 10.3 %shard_map.307 = (bf16[1024,192]{1,0:T(8,128)(2,1)}, f32[1024,3]{1,0:T(8,128)}) custom-call(bf16[1024,576]{1,0:T(8,128)(2,1)} %bitcast.263, s32[1024,1]{1,0:T(8,128)} %copy.345.seg_col_ref, s32[1,1024]{1,0:T(1,128)} %get-tuple-element.89.seg_row_ref), custom_call_target="tpu_custom_call" | custom-call | flops 805306368 | bytes 1769472 | tf_op jit(solution)/shard_map/pallas_call | solution.py:135
  240.6 4.4 all-to-all-start.5
  247.5 10.3 %shard_map.308 = (bf16[1024,192]{1,0:T(8,128)(2,1)}, f32[1024,3]{1,0:T(8,128)}) custom-call(bf16[1024,576]{1,0:T(8,128)(2,1)} %bitcast.261, s32[1024,1]{1,0:T(8,128)} %copy.350.seg_col_ref, s32[1,1024]{1,0:T(1,128)} %get-tuple-element.88.seg_row_ref), custom_call_target="tpu_custom_call" | custom-call | flops 805306368 | bytes 1769472 | tf_op jit(solution)/shard_map/pallas_call | solution.py:135
  261.2 4.6 all-to-all-start.7
  291.6 4.0 fusion.45
  297.8 4.9 slice.177
  302.7 8.5 reshape.460
  311.2 12.4 %multiply_convert_fusion = (bf16[1024,3072]{1,0:T(8,128)(2,1)S(1)}, f32[1024,3072]{1,0:T(8,128)}) fusion(f32[3072]{0:T(1024)S(1)} %copy-done.18, bf16[768,6912]{1,0:T(8,128)(2,1)} %all-gather.5.cloned.1.call-done, f32[1024,768]{1,0:T(8,128)} %copy-done.4, f32[768]{0:T(1024)S(1)} %copy-done.22, f32[768]{0:T(1024)S(1)} %get-tuple-element.45, ...), kind=kOutput, calls=%fused_computation.7 | convolution fusion | flops 4854644736 | bytes 26765312 | tf_op jit(solution)/shard_map/dot_general | solution.py:276
  323.7 5.4 fusion.46
  329.7 3.3 fusion.20
  336.5 7.0 convolution_convert_fusion
  343.5 8.6 convert_element_type.345
  352.1 12.4 %fusion.47 = (bf16[3072]{0:T(1024)(128)(2,1)S(1)}, bf16[1024,3072]{1,0:T(8,128)(2,1)S(1)}) fusion(f32[1024,3072]{1,0:T(8,128)} %get-tuple-element.94, f32[3072]{0:T(1024)S(1)} %copy-done.18, bf16[3072,768]{1,0:T(8,128)(2,1)} %reshape.460, f32[1024,768]{1,0:T(8,128)S(1)} %copy-done.13), kind=kOutput, calls=%fused_computation.144 | convolution fusion | flops 4870370304 | bytes 26757120 | tf_op jit(solution)/shard_map/dot_general | solution.py:27
  364.6 8.0 convolution_convert_fusion.1
  372.5 8.3 multiply_reduce_fusion
  389.4 17.8 %concatenate.21 = bf16[768,7168]{1,0:T(8,128)(2,1)} concatenate(bf16[768,768]{1,0:T(8,128)(2,1)S(1)} %convolution_convert_fusion.4, bf16[768,3072]{1,0:T(8,128)(2,1)} %convolution_convert_fusion.1, bf16[768,3072]{1,0:T(8,128)(2,1)} %convert_element_type.345, bf16[768,1]{1,0:T(8,128)(2,1)S(1)} %convert_element_type.377, bf16[768,1]{1,0:T(8,128)(2,1)} %convert_element_type.378, ...), dimensions={1} | concatenate | bytes 22020096 | tf_op jit(solution)/shard_map/concatenate | solution.py:74
  410.8 10.4 %all_to_all.240 = bf16[256,4,192]{0,2,1:T(8,128)(2,1)S(1)} all-to-all(bf16[256,4,192]{0,2,1:T(8,128)(2,1)S(1)} %bitcast.251), channel_id=1, replica_groups=mesh['seq'=4,'shard'=8] {'seq'}, dimensions={1} | all-to-all | bytes 786432 | tf_op jit(solution)/shard_map/all_to_all | solution.py:320
  421.2 9.5 %all_to_all.241 = bf16[256,4,192]{0,2,1:T(8,128)(2,1)} all-to-all(bf16[256,4,192]{0,2,1:T(8,128)(2,1)S(1)} %bitcast.250), channel_id=1, replica_groups=mesh['seq'=4,'shard'=8] {'seq'}, dimensions={1} | all-to-all | bytes 786432 | tf_op jit(solution)/shard_map/all_to_all | solution.py:320
  430.7 8.8 %all_to_all.242 = bf16[256,4,192]{0,2,1:T(8,128)(2,1)S(1)} all-to-all(bf16[256,4,192]{0,2,1:T(8,128)(2,1)S(1)} %bitcast.249), channel_id=1, replica_groups=mesh['seq'=4,'shard'=8] {'seq'}, dimensions={1} | all-to-all | bytes 786432 | tf_op jit(solution)/shard_map/all_to_all | solution.py:320
  439.5 3.6 all-to-all-start.14
  444.1 14.6 %shard_map.309 = bf16[1024,576]{1,0:T(8,128)(2,1)} custom-call(bf16[1024,576]{1,0:T(8,128)(2,1)} %bitcast.258, s32[1024,1]{1,0:T(8,128)} %copy.335.seg_col_ref, s32[1,1024]{1,0:T(1,128)} %get-tuple-element.83.seg_row_ref, f32[1024,3]{1,0:T(8,128)} %get-tuple-element.31.lse_ref, bf16[1024,192]{1,0:T(8,128)(2,1)} %bitcast.274), custom_call_target="tpu_custom_call" | custom-call | flops 2013265920 | bytes 2949120 | tf_op jit(solution)/shard_map/pallas_call | solution.py:153
  458.8 3.4 reduce.47
  464.8 4.1 all-to-all-start.9
  471.0 14.6 %shard_map.310 = bf16[1024,576]{1,0:T(8,128)(2,1)} custom-call(bf16[1024,576]{1,0:T(8,128)(2,1)} %bitcast.260, s32[1024,1]{1,0:T(8,128)} %copy.340.seg_col_ref, s32[1,1024]{1,0:T(1,128)} %get-tuple-element.90.seg_row_ref, f32[1024,3]{1,0:T(8,128)} %get-tuple-element.33.lse_ref, bf16[1024,192]{1,0:T(8,128)(2,1)} %bitcast.275), custom_call_target="tpu_custom_call" | custom-call | flops 2013265920 | bytes 2949120 | tf_op jit(solution)/shard_map/pallas_call | solution.py:153
  485.6 3.1 reduce.46
  491.4 4.3 all-to-all-start.11
  496.7 14.6 %shard_map.311 = bf16[1024,576]{1,0:T(8,128)(2,1)} custom-call(bf16[1024,576]{1,0:T(8,128)(2,1)} %bitcast.264, s32[1024,1]{1,0:T(8,128)} %copy.345.seg_col_ref, s32[1,1024]{1,0:T(1,128)} %get-tuple-element.89.seg_row_ref, f32[1024,3]{1,0:T(8,128)} %get-tuple-element.34.lse_ref, bf16[1024,192]{1,0:T(8,128)(2,1)} %bitcast.276), custom_call_target="tpu_custom_call" | custom-call | flops 2013265920 | bytes 2949120 | tf_op jit(solution)/shard_map/pallas_call | solution.py:153
  511.3 3.2 reduce.45
  517.1 4.2 all-to-all-start.13
  522.3 14.6 %shard_map.312 = bf16[1024,576]{1,0:T(8,128)(2,1)} custom-call(bf16[1024,576]{1,0:T(8,128)(2,1)} %bitcast.262, s32[1024,1]{1,0:T(8,128)} %copy.350.seg_col_ref, s32[1,1024]{1,0:T(1,128)} %get-tuple-element.88.seg_row_ref, f32[1024,3]{1,0:T(8,128)} %get-tuple-element.35.lse_ref, bf16[1024,192]{1,0:T(8,128)(2,1)} %bitcast.277), custom_call_target="tpu_custom_call" | custom-call | flops 2013265920 | bytes 2949120 | tf_op jit(solution)/shard_map/pallas_call | solution.py:153
  537.0 3.4 reduce.44
  543.0 4.3 all-to-all-start.15
  547.3 3.5 reshape.525
  554.9 4.8 reshape.523
  565.4 3.4 reshape.521
  578.8 4.7 reshape.519
  586.5 3.4 copy.393
  599.0 3.6 copy.382
  604.2 4.0 convolution_convert_fusion.2
  608.6 4.0 copy.385
  612.5 6.8 concatenate.22
  619.3 5.1 copy.395
  627.5 47.1 %reduce-scatter.10.cloned.1.call-done = bf16[24,10240]{1,0:T(8,128)(2,1)} async-done(((bf16[192,10240]{1,0:T(8,128)(2,1)}), bf16[24,10240]{1,0:T(8,128)(2,1)}) %reduce-scatter.10.cloned.1.call-update) | async-done | bytes 491536
  679.2 8.1 convolution_add_fusion.4
  687.3 13.2 %reduce-scatter.12.cloned.1.call-done = bf16[24,2560]{1,0:T(8,128)(2,1)} async-done(((bf16[96,2560]{1,0:T(8,128)(2,1)}), bf16[24,2560]{1,0:T(8,128)(2,1)}) %reduce-scatter.12.cloned.1.call-update) | async-done | bytes 122896
  702.9 147.4 %reduce-scatter.8.cloned.1.call-done = bf16[24,7168]{1,0:T(8,128)(2,1)} async-done(((bf16[768,7168]{1,0:T(8,128)(2,1)}), bf16[24,7168]{1,0:T(8,128)(2,1)}) %reduce-scatter.8.cloned.1.call-update) | async-done | bytes 344080 | tf_op jit(solution)/shard_map/reduce_scatter | solution.py:315
  (226 shorter events, 159.6 us)
Async XLA Ops:
  7.2 73.9 %all-gather.3.cloned.1.call-start = ((), (), s32[]{:S(2)}) async-start(), calls=%async_computation.19 | async-start | bytes 3852288 | tf_op jit(solution)/shard_map/all_gather | solution.py:219
  17.5 274.0 %all-gather.5.cloned.1.call-start = ((), (), s32[]{:S(2)}) async-start(), calls=%async_computation.20 | async-start | bytes 10948608 | tf_op jit(solution)/shard_map/all_gather | solution.py:220
  85.8 2.0 slice-start
  91.4 2.4 copy-start.19
  93.7 52.3 %copy-start.2 = (bf16[768,4,3,192]{0,3,2,1:T(8,128)(2,1)}, bf16[768,4,3,192]{0,3,2,1:T(8,128)(2,1)S(1)}, u32[]{:S(2)}) copy-start(bf16[768,4,3,192]{0,3,2,1:T(8,128)(2,1)S(1)} %copy.331) | copy-start | bytes 10616836
  97.2 25.8 %all-to-all-start = ((bf16[256,4,576]{0,2,1:T(8,128)(2,1)}), bf16[256,4,576]{0,2,1:T(8,128)(2,1)}, u32[]{:S(2)}, u32[]{:S(2)}) async-start(bf16[256,4,576]{0,2,1:T(8,128)(2,1)} %bitcast.272), calls=%async_computation | async-start | bytes 2359296 | tf_op jit(solution)/shard_map/all_to_all | solution.py:259
  123.0 18.7 %all-to-all-start.2 = ((bf16[256,4,576]{0,2,1:T(8,128)(2,1)}), bf16[256,4,576]{0,2,1:T(8,128)(2,1)}, u32[]{:S(2)}, u32[]{:S(2)}) async-start(bf16[256,4,576]{0,2,1:T(8,128)(2,1)} %bitcast.271), calls=%async_computation.2 | async-start | bytes 2359296 | tf_op jit(solution)/shard_map/all_to_all | solution.py:259
  141.7 30.7 %all-to-all-start.4 = ((bf16[256,4,576]{0,2,1:T(8,128)(2,1)}), bf16[256,4,576]{0,2,1:T(8,128)(2,1)}, u32[]{:S(2)}, u32[]{:S(2)}) async-start(bf16[256,4,576]{0,2,1:T(8,128)(2,1)} %bitcast.270), calls=%async_computation.4 | async-start | bytes 2359296 | tf_op jit(solution)/shard_map/all_to_all | solution.py:259
  146.0 30.2 %copy-start.25 = (s32[4,17]{1,0:T(4,128)S(1)}, s32[4,17]{1,0:T(4,128)}, u32[]{:S(2)}) copy-start(s32[4,17]{1,0:T(4,128)} %param.20) | copy-start | bytes 820
  172.4 22.4 %all-to-all-start.6 = ((bf16[256,4,576]{0,2,1:T(8,128)(2,1)}), bf16[256,4,576]{0,2,1:T(8,128)(2,1)S(1)}, u32[]{:S(2)}, u32[]{:S(2)}) async-start(bf16[256,4,576]{0,2,1:T(8,128)(2,1)} %bitcast.269), calls=%async_computation.6 | async-start | bytes 2359296 | tf_op jit(solution)/shard_map/all_to_all | solution.py:259
  194.8 22.2 %all-to-all-start.1 = ((bf16[4,2,24576]{2,1,0:T(2,128)(2,1)}), bf16[4,2,24576]{2,1,0:T(2,128)(2,1)}, u32[]{:S(2)}, u32[]{:S(2)}) async-start(bf16[4,2,24576]{2,1,0:T(2,128)(2,1)} %reshape.516), calls=%async_computation.1 | async-start | bytes 786432 | tf_op jit(solution)/shard_map/all_to_all | solution.py:264
  213.5 9.9 %copy-start = (bf16[4,256,768]{2,1,0:T(8,128)(2,1)S(1)}, bf16[4,256,768]{2,1,0:T(8,128)(2,1)}, u32[]{:S(2)}) copy-start(bf16[4,256,768]{2,1,0:T(8,128)(2,1)} %param.19) | copy-start | bytes 4718596
  217.0 23.7 %all-to-all-start.3 = ((bf16[4,2,24576]{2,1,0:T(2,128)(2,1)}), bf16[4,2,24576]{2,1,0:T(2,128)(2,1)}, u32[]{:S(2)}, u32[]{:S(2)}) async-start(bf16[4,2,24576]{2,1,0:T(2,128)(2,1)} %reshape.514), calls=%async_computation.3 | async-start | bytes 786432 | tf_op jit(solution)/shard_map/all_to_all | solution.py:264
  240.6 20.6 %all-to-all-start.5 = ((bf16[4,2,24576]{2,1,0:T(2,128)(2,1)}), bf16[4,2,24576]{2,1,0:T(2,128)(2,1)S(1)}, u32[]{:S(2)}, u32[]{:S(2)}) async-start(bf16[4,2,24576]{2,1,0:T(2,128)(2,1)} %reshape.512), calls=%async_computation.5 | async-start | bytes 786432 | tf_op jit(solution)/shard_map/all_to_all | solution.py:264
  261.2 21.9 %all-to-all-start.7 = ((bf16[4,2,24576]{2,1,0:T(2,128)(2,1)}), bf16[4,2,24576]{2,1,0:T(2,128)(2,1)}, u32[]{:S(2)}, u32[]{:S(2)}) async-start(bf16[4,2,24576]{2,1,0:T(2,128)(2,1)} %reshape.510), calls=%async_computation.7 | async-start | bytes 786432 | tf_op jit(solution)/shard_map/all_to_all | solution.py:264
  279.3 9.2 %copy-start.16 = (bf16[4,256,1,192]{1,0,3,2:T(4,128)(2,1)S(1)}, bf16[4,256,1,192]{1,0,3,2:T(4,128)(2,1)}, u32[]{:S(2)}) copy-start(bf16[4,256,1,192]{1,0,3,2:T(4,128)(2,1)} %all_to_all.186) | copy-start | bytes 1179652
  289.9 1.6 copy-start.24
  291.5 4.0 copy-start.14
  295.6 1.7 copy-start.4
  302.7 8.5 copy-start.18
  302.7 8.5 copy-start.22
  311.2 12.5 %copy-start.5 = (f32[1024,768]{1,0:T(8,128)S(1)}, f32[1024,768]{1,0:T(8,128)}, u32[]{:S(2)}) copy-start(f32[1024,768]{1,0:T(8,128)} %copy-done.4) | copy-start | bytes 9437188
  311.2 12.5 %copy-start.8 = (bf16[3072,768]{1,0:T(8,128)(2,1)S(1)}, bf16[3072,768]{1,0:T(8,128)(2,1)}, u32[]{:S(2)}) copy-start(bf16[3072,768]{1,0:T(8,128)(2,1)} %reshape.460) | copy-start | bytes 14155780
  311.2 12.5 %copy-start.23 = (f32[768]{0:T(1024)S(1)}, f32[768]{0:T(1024)}, u32[]{:S(2)}) copy-start(f32[768]{0:T(1024)} %get-tuple-element.43) | copy-start | bytes 9220
  334.8 1.7 copy-start.12
  343.5 8.6 copy-start.13
  352.1 12.4 %copy-start.6 = (f32[1024,768]{1,0:T(8,128)S(1)}, f32[1024,768]{1,0:T(8,128)}, u32[]{:S(2)}) copy-start(f32[1024,768]{1,0:T(8,128)} %copy-done.4) | copy-start | bytes 9437188
  380.9 2.3 copy-start.15
  383.2 4.4 copy-start.21
  383.2 5.3 copy-start.20
  383.2 6.1 copy-start.17
  439.5 25.3 %all-to-all-start.14 = ((bf16[256,4,192]{0,2,1:T(8,128)(2,1)}), bf16[256,4,192]{0,2,1:T(8,128)(2,1)S(1)}, u32[]{:S(2)}, u32[]{:S(2)}) async-start(bf16[256,4,192]{0,2,1:T(8,128)(2,1)} %bitcast.76), calls=%async_computation.14 | async-start | bytes 786432 | tf_op jit(solution)/shard_map/all_to_all | solution.py:320
  464.8 26.6 %all-to-all-start.9 = ((bf16[4,2,73728]{2,1,0:T(2,128)(2,1)}), bf16[4,2,73728]{2,1,0:T(2,128)(2,1)S(1)}, u32[]{:S(2)}, u32[]{:S(2)}) async-start(bf16[4,2,73728]{2,1,0:T(2,128)(2,1)} %reshape.524), calls=%async_computation.9 | async-start | bytes 2359296 | tf_op jit(solution)/shard_map/all_to_all | solution.py:329
  491.4 19.9 %copy-start.9 = (bf16[4,2,73728]{2,1,0:T(2,128)(2,1)}, bf16[4,2,73728]{2,1,0:T(2,128)(2,1)S(1)}, u32[]{:S(2)}) copy-start(bf16[4,2,73728]{2,1,0:T(2,128)(2,1)S(1)} %all-to-all-done.9) | copy-start | bytes 3538948
  491.4 25.8 %all-to-all-start.11 = ((bf16[4,2,73728]{2,1,0:T(2,128)(2,1)}), bf16[4,2,73728]{2,1,0:T(2,128)(2,1)}, u32[]{:S(2)}, u32[]{:S(2)}) async-start(bf16[4,2,73728]{2,1,0:T(2,128)(2,1)} %reshape.522), calls=%async_computation.11 | async-start | bytes 2359296 | tf_op jit(solution)/shard_map/all_to_all | solution.py:329
  517.1 25.8 %all-to-all-start.13 = ((bf16[4,2,73728]{2,1,0:T(2,128)(2,1)}), bf16[4,2,73728]{2,1,0:T(2,128)(2,1)S(1)}, u32[]{:S(2)}, u32[]{:S(2)}) async-start(bf16[4,2,73728]{2,1,0:T(2,128)(2,1)} %reshape.520), calls=%async_computation.13 | async-start | bytes 2359296 | tf_op jit(solution)/shard_map/all_to_all | solution.py:329
  543.0 4.3 copy-start.10
  543.0 35.8 %all-to-all-start.15 = ((bf16[4,2,73728]{2,1,0:T(2,128)(2,1)}), bf16[4,2,73728]{2,1,0:T(2,128)(2,1)}, u32[]{:S(2)}, u32[]{:S(2)}) async-start(bf16[4,2,73728]{2,1,0:T(2,128)(2,1)} %reshape.518), calls=%async_computation.15 | async-start | bytes 2359296 | tf_op jit(solution)/shard_map/all_to_all | solution.py:329
  547.3 127.3 %reduce-scatter.10.cloned.1.call-start = ((), (), s32[]{:S(2)}) async-start(), calls=%async_computation.22 | async-start | bytes 4423680
  559.6 5.8 copy-start.11
  596.8 1.3 copy-start.7
  602.7 1.6 copy-start.26
  604.2 4.1 copy-start.1
  627.2 73.3 %reduce-scatter.12.cloned.1.call-start = ((), (), s32[]{:S(2)}) async-start(), calls=%async_computation.23 | async-start | bytes 614400
  676.9 2.3 copy-start.3
  676.9 173.4 %reduce-scatter.8.cloned.1.call-start = ((), (), s32[]{:S(2)}) async-start(), calls=%async_computation.21 | async-start | bytes 11354112 | tf_op jit(solution)/shard_map/reduce_scatter | solution.py:315
Sparse Core Ops, SparseCore 0:
  17.6 63.4 all-gather.2
  84.2 102.3 all-gather.4
  627.4 47.2 reduce-scatter.9
  677.3 23.1 reduce-scatter.11
  706.3 143.9 reduce-scatter.7

commit v6 on v5

--- a/solution.py
+++ b/solution.py
@@ -325,31 +325,32 @@
             tiled=True,
         ).reshape(LEN, -1)
         one_grads = attention_backward(head_qkv[s], segment[s], logsum[s], one_back)
-        back_parts.append(
-            lax.all_to_all(
-                one_grads.reshape(LEN, 1, -1), "seq", split_axis=0, concat_axis=1, tiled=True
-            )
-        )
-    rows_back = jnp.stack(back_parts).reshape(row_count, 3 * width)
-    grad_qkv_weight = by_kind(contract_rows(flat, rows_back))
-    grad_qkv_bias = by_kind(jnp.sum(rows_back.astype(jnp.float32), axis=0))
-    grad_query_bias = grad_qkv_bias[:width]
-    grad_value_bias = grad_qkv_bias[2 * width :]
-    input_grad = (back_first + times_transpose(rows_back, owner_qkv)).reshape(
-        streams, part_len, width
-    )
-    late = pack_lanes([grad_qkv_weight, grad_query_bias[:, None], grad_value_bias[:, None]])
+        rows = lax.all_to_all(
+            one_grads.reshape(LEN, 1, -1), "seq", split_axis=0, concat_axis=1, tiled=True
+        ).reshape(part_len, 3 * width)
+        block = slice(s * part_len, (s + 1) * part_len)
+        weight_part = contract_rows(flat[block], rows)
+        bias_part = jnp.sum(rows.astype(jnp.float32), axis=0)
+        grad_qkv_weight = weight_part if s == 0 else grad_qkv_weight + weight_part
+        grad_qkv_bias = bias_part if s == 0 else grad_qkv_bias + bias_part
+        back_parts.append(back_first[block] + times_transpose(rows, owner_qkv))
+    input_grad = jnp.stack(back_parts).reshape(streams, part_len, width)
+    grad_qkv_bias = by_kind(grad_qkv_bias)
+    late = pack_lanes(
+        [grad_qkv_weight, grad_qkv_bias[:width, None], grad_qkv_bias[2 * width :, None]]
+    )
     late_sum = scatter_two_stage(late).astype(jnp.float32)
 
     base = width + 2 * ff
     late_tail = late_sum[:, 3 * width :]
+    late_weight = by_kind(late_sum[:, : 3 * width])
     early_tail = early_sum[:, base:]
     return (
         layer_out,
         input_grad,
-        late_sum[:, :width],
-        late_sum[:, width : 2 * width],
-        late_sum[:, 2 * width : 3 * width],
+        late_weight[:, :width],
+        late_weight[:, width : 2 * width],
+        late_weight[:, 2 * width : 3 * width],
         early_sum[:, :width],
         early_sum[:, width : width + ff],
         early_sum[:, width + ff : width + 2 * ff].reshape(-1, width),

time: 875 us -> 879 us (level)
  matrix products: 86.8 us -> 98.2 us
    dot_general x4 -> x7, matrix products: 20.4 us -> 29.4 us  [contract_rows(): lax.dot_general(left, right, (((0,), (0,)), ((), ())), preferred_element_...]
    convert_element_type x12 -> x10, local copies, waits for them, and re-layouts: 20.4 us -> 16.2 us  [pack_lanes(): pieces = [p.astype(jnp.bfloat16) for p in pieces]]
    unnamed x83 -> x108, local copies, waits for them, and re-layouts: 70.5 us -> 73.8 us
    dot_general x4 -> x7, matrix products: 31.6 us -> 31.6 us  [times_transpose(): lax.dot_general(left, right, (((1,), (1,)), ((), ())), preferred_element_...]
  transfers between devices with their start and end apart: 18 -> 18, of which waited for: 7 -> 7; matrix products, arithmetic and copies ran while one was open for 17% -> 18% of each run, Pallas kernels for 12% -> 12%
where the time goes in v6:
time: 879 us; the launch traced here: 868 us
  waiting for transfers between devices  316 us (36%)
  local copies, waits for them, and re-layouts  197 us (22%)
  Pallas kernels  100 us (11%)
  matrix products  98.2 us (11%)
  other arithmetic  59.8 us (7%)
  starting transfers between devices  53.4 us (6%)
  blocking collectives  28.7 us (3%)
  between operations  14.9 us (2%)
    reduce_scatter x1, waiting for transfers between devices, per_device(): lax.psum_scatter(early, axes, scatter_dimension=0, tiled=True)  147 us
    unnamed x108, local copies, waits for them, and re-layouts  73.8 us
    unnamed x7, waiting for transfers between devices  59.7 us
    all_gather x1, waiting for transfers between devices, per_device(): full_first = lax.all_gather(first, axes, axis=0, tiled=True)  59.7 us
    pallas_call x4, Pallas kernels, attention_backward(): pl.pallas_call(attention_backward_kernel, out_shape=jax.ShapeDtypeStruct(...  58.6 us
    all_to_all x4, waiting for transfers between devices, per_device(): lax.all_to_all(qkv.reshape(part_len, ways, -1), 'seq', split_axis=1, conc...  50.2 us
    pallas_call x4, Pallas kernels, attention_forward(): pl.pallas_call(attention_forward_kernel, out_shape=(jax.ShapeDtypeStruct(...  41.4 us
    dot_general x7, matrix products, times_transpose(): lax.dot_general(left, right, (((1,), (1,)), ((), ())), preferred_element_...  31.6 us
  transfers between devices with their start and end apart: 18, of which 7 were waited for; matrix products, arithmetic and copies ran while one was open for 18% of the time, Pallas kernels for 12%

profile of v6, /device:TPU:0, one launch (start us, length us, event | category | flops | bytes accessed | tf_op | source)
XLA Modules:
  0.0 868.1 jit_solution(10175622750716039141)
XLA Ops:
  21.4 59.7 %all-gather.3.cloned.1.call-done = bf16[768,2316]{1,0:T(8,128)(2,1)} async-done(((bf16[24,2316]{1,0:T(8,128)(2,1)}), bf16[768,2316]{1,0:T(8,128)(2,1)}) %all-gather.3.cloned.1.call-update) | async-done | bytes 3557392 | tf_op jit(solution)/shard_map/all_gather | solution.py:219
  81.1 3.7 convert_reduce_fusion.5
  85.8 4.0 slice.188
  89.8 4.6 copy.492
  95.1 3.6 fusion.11
  98.6 3.5 all-to-all-start
  102.2 4.1 fusion.12
  106.3 18.0 %all-to-all-done = bf16[256,4,576]{0,2,1:T(8,128)(2,1)S(1)} async-done(((bf16[256,4,576]{0,2,1:T(8,128)(2,1)}), bf16[256,4,576]{0,2,1:T(8,128)(2,1)S(1)}, u32[]{:S(2)}, u32[]{:S(2)}) %all-to-all-start) | async-done | bytes 1179680 | tf_op jit(solution)/shard_map/all_to_all | solution.py:259
  125.3 3.5 all-to-all-start.2
  128.9 4.1 fusion.13
  133.0 12.3 %all-to-all-done.2 = bf16[256,4,576]{0,2,1:T(8,128)(2,1)S(1)} async-done(((bf16[256,4,576]{0,2,1:T(8,128)(2,1)}), bf16[256,4,576]{0,2,1:T(8,128)(2,1)S(1)}, u32[]{:S(2)}, u32[]{:S(2)}) %all-to-all-start.2) | async-done | bytes 1179680 | tf_op jit(solution)/shard_map/all_to_all | solution.py:259
  146.3 3.5 all-to-all-start.4
  149.9 4.1 fusion.14
  154.0 19.9 %all-to-all-done.4 = bf16[256,4,576]{0,2,1:T(8,128)(2,1)S(1)} async-done(((bf16[256,4,576]{0,2,1:T(8,128)(2,1)}), bf16[256,4,576]{0,2,1:T(8,128)(2,1)S(1)}, u32[]{:S(2)}, u32[]{:S(2)}) %all-to-all-start.4) | async-done | bytes 1179680 | tf_op jit(solution)/shard_map/all_to_all | solution.py:259
  174.0 3.8 all-to-all-start.6
  182.1 10.4 %shard_map.305 = (bf16[1024,192]{1,0:T(8,128)(2,1)}, f32[1024,3]{1,0:T(8,128)}) custom-call(bf16[1024,576]{1,0:T(8,128)(2,1)} %bitcast.270, s32[1024,1]{1,0:T(8,128)} %copy.418.seg_col_ref, s32[1,1024]{1,0:T(1,128)} %get-tuple-element.83.seg_row_ref), custom_call_target="tpu_custom_call" | custom-call | flops 805306368 | bytes 1769472 | tf_op jit(solution)/shard_map/pallas_call | solution.py:135
  196.4 4.7 all-to-all-start.1
  204.5 10.3 %shard_map.306 = (bf16[1024,192]{1,0:T(8,128)(2,1)}, f32[1024,3]{1,0:T(8,128)}) custom-call(bf16[1024,576]{1,0:T(8,128)(2,1)} %bitcast.272, s32[1024,1]{1,0:T(8,128)} %copy.423.seg_col_ref, s32[1,1024]{1,0:T(1,128)} %get-tuple-element.90.seg_row_ref), custom_call_target="tpu_custom_call" | custom-call | flops 805306368 | bytes 1769472 | tf_op jit(solution)/shard_map/pallas_call | solution.py:135
  218.3 4.4 all-to-all-start.3
  228.3 10.3 %shard_map.307 = (bf16[1024,192]{1,0:T(8,128)(2,1)}, f32[1024,3]{1,0:T(8,128)}) custom-call(bf16[1024,576]{1,0:T(8,128)(2,1)} %bitcast.276, s32[1024,1]{1,0:T(8,128)} %copy.428.seg_col_ref, s32[1,1024]{1,0:T(1,128)} %get-tuple-element.89.seg_row_ref), custom_call_target="tpu_custom_call" | custom-call | flops 805306368 | bytes 1769472 | tf_op jit(solution)/shard_map/pallas_call | solution.py:135
  242.0 4.4 all-to-all-start.5
  248.9 10.3 %shard_map.308 = (bf16[1024,192]{1,0:T(8,128)(2,1)}, f32[1024,3]{1,0:T(8,128)}) custom-call(bf16[1024,576]{1,0:T(8,128)(2,1)} %bitcast.274, s32[1024,1]{1,0:T(8,128)} %copy.433.seg_col_ref, s32[1,1024]{1,0:T(1,128)} %get-tuple-element.88.seg_row_ref), custom_call_target="tpu_custom_call" | custom-call | flops 805306368 | bytes 1769472 | tf_op jit(solution)/shard_map/pallas_call | solution.py:135
  262.6 4.6 all-to-all-start.7
  294.0 3.4 fusion.61
  299.7 4.9 slice.201
  304.6 8.5 reshape.486
  313.1 12.4 %multiply_convert_fusion = (bf16[1024,3072]{1,0:T(8,128)(2,1)S(1)}, f32[1024,3072]{1,0:T(8,128)}) fusion(f32[3072]{0:T(1024)S(1)} %copy-done.31, bf16[768,6912]{1,0:T(8,128)(2,1)} %all-gather.5.cloned.1.call-done, f32[1024,768]{1,0:T(8,128)} %copy-done.1, f32[768]{0:T(1024)S(1)} %copy-done.36, f32[768]{0:T(1024)S(1)} %get-tuple-element.45, ...), kind=kOutput, calls=%fused_computation.7 | convolution fusion | flops 4854644736 | bytes 26765312 | tf_op jit(solution)/shard_map/dot_general | solution.py:276
  325.6 5.4 fusion.62
  331.6 3.3 fusion.21
  338.3 7.0 convolution_convert_fusion
  345.4 8.6 convert_element_type.352
  354.0 12.4 %fusion.63 = (bf16[3072]{0:T(1024)(128)(2,1)S(1)}, bf16[1024,3072]{1,0:T(8,128)(2,1)S(1)}) fusion(f32[1024,3072]{1,0:T(8,128)} %get-tuple-element.94, f32[3072]{0:T(1024)S(1)} %copy-done.31, bf16[3072,768]{1,0:T(8,128)(2,1)} %reshape.486, f32[1024,768]{1,0:T(8,128)S(1)} %copy-done.24), kind=kOutput, calls=%fused_computation.159 | convolution fusion | flops 4870370304 | bytes 26757120 | tf_op jit(solution)/shard_map/dot_general | solution.py:27
  366.5 8.0 convolution_convert_fusion.1
  374.4 8.3 multiply_reduce_fusion
  391.3 17.8 %concatenate.21 = bf16[768,7168]{1,0:T(8,128)(2,1)} concatenate(bf16[768,768]{1,0:T(8,128)(2,1)S(1)} %convolution_convert_fusion.3, bf16[768,3072]{1,0:T(8,128)(2,1)} %convolution_convert_fusion.1, bf16[768,3072]{1,0:T(8,128)(2,1)} %convert_element_type.352, bf16[768,1]{1,0:T(8,128)(2,1)S(1)} %convert_element_type.385, bf16[768,1]{1,0:T(8,128)(2,1)} %convert_element_type.386, ...), dimensions={1} | concatenate | bytes 22020096 | tf_op jit(solution)/shard_map/concatenate | solution.py:74
  412.7 10.4 %all_to_all.240 = bf16[256,4,192]{0,2,1:T(8,128)(2,1)S(1)} all-to-all(bf16[256,4,192]{0,2,1:T(8,128)(2,1)S(1)} %bitcast.263), channel_id=1, replica_groups=mesh['seq'=4,'shard'=8] {'seq'}, dimensions={1} | all-to-all | bytes 786432 | tf_op jit(solution)/shard_map/all_to_all | solution.py:320
  423.1 9.5 %all_to_all.241 = bf16[256,4,192]{0,2,1:T(8,128)(2,1)} all-to-all(bf16[256,4,192]{0,2,1:T(8,128)(2,1)S(1)} %bitcast.262), channel_id=1, replica_groups=mesh['seq'=4,'shard'=8] {'seq'}, dimensions={1} | all-to-all | bytes 786432 | tf_op jit(solution)/shard_map/all_to_all | solution.py:320
  432.6 8.8 %all_to_all.242 = bf16[256,4,192]{0,2,1:T(8,128)(2,1)S(1)} all-to-all(bf16[256,4,192]{0,2,1:T(8,128)(2,1)S(1)} %bitcast.261), channel_id=1, replica_groups=mesh['seq'=4,'shard'=8] {'seq'}, dimensions={1} | all-to-all | bytes 786432 | tf_op jit(solution)/shard_map/all_to_all | solution.py:320
  441.4 3.6 all-to-all-start.14
  446.0 14.6 %shard_map.309 = bf16[1024,576]{1,0:T(8,128)(2,1)} custom-call(bf16[1024,576]{1,0:T(8,128)(2,1)} %bitcast.271, s32[1024,1]{1,0:T(8,128)} %copy.418.seg_col_ref, s32[1,1024]{1,0:T(1,128)} %get-tuple-element.83.seg_row_ref, f32[1024,3]{1,0:T(8,128)} %get-tuple-element.31.lse_ref, bf16[1024,192]{1,0:T(8,128)(2,1)} %bitcast.286), custom_call_target="tpu_custom_call" | custom-call | flops 2013265920 | bytes 2949120 | tf_op jit(solution)/shard_map/pallas_call | solution.py:153
  460.7 3.4 reduce.41
  466.7 4.1 all-to-all-start.9
  472.9 14.6 %shard_map.310 = bf16[1024,576]{1,0:T(8,128)(2,1)} custom-call(bf16[1024,576]{1,0:T(8,128)(2,1)} %bitcast.273, s32[1024,1]{1,0:T(8,128)} %copy.423.seg_col_ref, s32[1,1024]{1,0:T(1,128)} %get-tuple-element.90.seg_row_ref, f32[1024,3]{1,0:T(8,128)} %get-tuple-element.33.lse_ref, bf16[1024,192]{1,0:T(8,128)(2,1)} %bitcast.287), custom_call_target="tpu_custom_call" | custom-call | flops 2013265920 | bytes 2949120 | tf_op jit(solution)/shard_map/pallas_call | solution.py:153
  487.5 3.1 reduce.40
  493.3 4.3 all-to-all-start.11
  498.6 14.6 %shard_map.311 = bf16[1024,576]{1,0:T(8,128)(2,1)} custom-call(bf16[1024,576]{1,0:T(8,128)(2,1)} %bitcast.277, s32[1024,1]{1,0:T(8,128)} %copy.428.seg_col_ref, s32[1,1024]{1,0:T(1,128)} %get-tuple-element.89.seg_row_ref, f32[1024,3]{1,0:T(8,128)} %get-tuple-element.34.lse_ref, bf16[1024,192]{1,0:T(8,128)(2,1)} %bitcast.288), custom_call_target="tpu_custom_call" | custom-call | flops 2013265920 | bytes 2949120 | tf_op jit(solution)/shard_map/pallas_call | solution.py:153
  513.2 3.2 reduce.39
  519.0 4.2 all-to-all-start.13
  524.2 14.6 %shard_map.312 = bf16[1024,576]{1,0:T(8,128)(2,1)} custom-call(bf16[1024,576]{1,0:T(8,128)(2,1)} %bitcast.275, s32[1024,1]{1,0:T(8,128)} %copy.433.seg_col_ref, s32[1,1024]{1,0:T(1,128)} %get-tuple-element.88.seg_row_ref, f32[1024,3]{1,0:T(8,128)} %get-tuple-element.35.lse_ref, bf16[1024,192]{1,0:T(8,128)(2,1)} %bitcast.289), custom_call_target="tpu_custom_call" | custom-call | flops 2013265920 | bytes 2949120 | tf_op jit(solution)/shard_map/pallas_call | solution.py:153
  538.9 3.4 reduce.38
  544.9 4.3 all-to-all-start.15
  549.2 3.5 reshape.555
  557.6 4.8 reshape.553
  571.2 3.3 reshape.551
  583.4 4.7 reshape.549
  591.1 3.5 copy.485
  607.5 4.0 fusion.34
  611.7 5.3 fusion.6
  617.8 5.8 concatenate.22
  623.5 5.1 copy.486
  631.6 47.5 %reduce-scatter.10.cloned.1.call-done = bf16[24,10240]{1,0:T(8,128)(2,1)} async-done(((bf16[192,10240]{1,0:T(8,128)(2,1)}), bf16[24,10240]{1,0:T(8,128)(2,1)}) %reduce-scatter.10.cloned.1.call-update) | async-done | bytes 491536
  682.7 3.5 fusion.29
  693.2 11.8 %reduce-scatter.12.cloned.1.call-done = bf16[24,2560]{1,0:T(8,128)(2,1)} async-done(((bf16[96,2560]{1,0:T(8,128)(2,1)}), bf16[24,2560]{1,0:T(8,128)(2,1)}) %reduce-scatter.12.cloned.1.call-update) | async-done | bytes 122896
  708.1 146.8 %reduce-scatter.8.cloned.1.call-done = bf16[24,7168]{1,0:T(8,128)(2,1)} async-done(((bf16[768,7168]{1,0:T(8,128)(2,1)}), bf16[24,7168]{1,0:T(8,128)(2,1)}) %reduce-scatter.8.cloned.1.call-update) | async-done | bytes 344080 | tf_op jit(solution)/shard_map/reduce_scatter | solution.py:315
  (261 shorter events, 170.3 us)
Async XLA Ops:
  7.2 73.9 %all-gather.3.cloned.1.call-start = ((), (), s32[]{:S(2)}) async-start(), calls=%async_computation.19 | async-start | bytes 3852288 | tf_op jit(solution)/shard_map/all_gather | solution.py:219
  17.5 276.5 %all-gather.5.cloned.1.call-start = ((), (), s32[]{:S(2)}) async-start(), calls=%async_computation.20 | async-start | bytes 10948608 | tf_op jit(solution)/shard_map/all_gather | solution.py:220
  94.4 0.7 copy-start.32
  94.6 4.0 copy-start.20
  95.1 7.1 copy-start.25
  95.1 7.1 copy-start.33
  98.6 25.7 %all-to-all-start = ((bf16[256,4,576]{0,2,1:T(8,128)(2,1)}), bf16[256,4,576]{0,2,1:T(8,128)(2,1)S(1)}, u32[]{:S(2)}, u32[]{:S(2)}) async-start(bf16[256,4,576]{0,2,1:T(8,128)(2,1)} %bitcast.285), calls=%async_computation | async-start | bytes 2359296 | tf_op jit(solution)/shard_map/all_to_all | solution.py:259
  124.3 1.0 copy-start.16
  125.3 20.0 %all-to-all-start.2 = ((bf16[256,4,576]{0,2,1:T(8,128)(2,1)}), bf16[256,4,576]{0,2,1:T(8,128)(2,1)S(1)}, u32[]{:S(2)}, u32[]{:S(2)}) async-start(bf16[256,4,576]{0,2,1:T(8,128)(2,1)} %bitcast.284), calls=%async_computation.2 | async-start | bytes 2359296 | tf_op jit(solution)/shard_map/all_to_all | solution.py:259
  145.3 1.0 copy-start.15
  146.3 27.6 %all-to-all-start.4 = ((bf16[256,4,576]{0,2,1:T(8,128)(2,1)}), bf16[256,4,576]{0,2,1:T(8,128)(2,1)S(1)}, u32[]{:S(2)}, u32[]{:S(2)}) async-start(bf16[256,4,576]{0,2,1:T(8,128)(2,1)} %bitcast.283), calls=%async_computation.4 | async-start | bytes 2359296 | tf_op jit(solution)/shard_map/all_to_all | solution.py:259
  149.9 27.9 %copy-start.39 = (s32[4,17]{1,0:T(4,128)S(1)}, s32[4,17]{1,0:T(4,128)}, u32[]{:S(2)}) copy-start(s32[4,17]{1,0:T(4,128)} %param.20) | copy-start | bytes 820
  174.0 18.5 %copy-start.14 = (bf16[256,4,576]{0,2,1:T(8,128)(2,1)}, bf16[256,4,576]{0,2,1:T(8,128)(2,1)S(1)}, u32[]{:S(2)}) copy-start(bf16[256,4,576]{0,2,1:T(8,128)(2,1)S(1)} %all-to-all-done.4) | copy-start | bytes 3538948
  174.0 22.4 %all-to-all-start.6 = ((bf16[256,4,576]{0,2,1:T(8,128)(2,1)}), bf16[256,4,576]{0,2,1:T(8,128)(2,1)S(1)}, u32[]{:S(2)}, u32[]{:S(2)}) async-start(bf16[256,4,576]{0,2,1:T(8,128)(2,1)} %bitcast.282), calls=%async_computation.6 | async-start | bytes 2359296 | tf_op jit(solution)/shard_map/all_to_all | solution.py:259
  196.4 21.9 %all-to-all-start.1 = ((bf16[4,2,24576]{2,1,0:T(2,128)(2,1)}), bf16[4,2,24576]{2,1,0:T(2,128)(2,1)}, u32[]{:S(2)}, u32[]{:S(2)}) async-start(bf16[4,2,24576]{2,1,0:T(2,128)(2,1)} %reshape.546), calls=%async_computation.1 | async-start | bytes 786432 | tf_op jit(solution)/shard_map/all_to_all | solution.py:264
  214.8 9.9 %copy-start = (bf16[4,256,768]{2,1,0:T(8,128)(2,1)S(1)}, bf16[4,256,768]{2,1,0:T(8,128)(2,1)}, u32[]{:S(2)}) copy-start(bf16[4,256,768]{2,1,0:T(8,128)(2,1)} %param.19) | copy-start | bytes 4718596
  218.3 23.7 %all-to-all-start.3 = ((bf16[4,2,24576]{2,1,0:T(2,128)(2,1)}), bf16[4,2,24576]{2,1,0:T(2,128)(2,1)}, u32[]{:S(2)}, u32[]{:S(2)}) async-start(bf16[4,2,24576]{2,1,0:T(2,128)(2,1)} %reshape.544), calls=%async_computation.3 | async-start | bytes 786432 | tf_op jit(solution)/shard_map/all_to_all | solution.py:264
  242.0 20.6 %all-to-all-start.5 = ((bf16[4,2,24576]{2,1,0:T(2,128)(2,1)}), bf16[4,2,24576]{2,1,0:T(2,128)(2,1)S(1)}, u32[]{:S(2)}, u32[]{:S(2)}) async-start(bf16[4,2,24576]{2,1,0:T(2,128)(2,1)} %reshape.542), calls=%async_computation.5 | async-start | bytes 786432 | tf_op jit(solution)/shard_map/all_to_all | solution.py:264
  262.6 21.9 %all-to-all-start.7 = ((bf16[4,2,24576]{2,1,0:T(2,128)(2,1)}), bf16[4,2,24576]{2,1,0:T(2,128)(2,1)}, u32[]{:S(2)}, u32[]{:S(2)}) async-start(bf16[4,2,24576]{2,1,0:T(2,128)(2,1)} %reshape.540), calls=%async_computation.7 | async-start | bytes 786432 | tf_op jit(solution)/shard_map/all_to_all | solution.py:264
  280.7 9.2 %copy-start.29 = (bf16[4,256,1,192]{1,0,3,2:T(4,128)(2,1)S(1)}, bf16[4,256,1,192]{1,0,3,2:T(4,128)(2,1)}, u32[]{:S(2)}) copy-start(bf16[4,256,1,192]{1,0,3,2:T(4,128)(2,1)} %all_to_all.186) | copy-start | bytes 1179652
  291.3 2.7 copy-start.26
  291.3 2.7 copy-start.38
  297.5 1.7 copy-start.1
  304.6 8.5 copy-start.31
  304.6 8.5 copy-start.36
  313.1 12.5 %copy-start.2 = (f32[1024,768]{1,0:T(8,128)S(1)}, f32[1024,768]{1,0:T(8,128)}, u32[]{:S(2)}) copy-start(f32[1024,768]{1,0:T(8,128)} %copy-done.1) | copy-start | bytes 9437188
  313.1 12.5 %copy-start.13 = (bf16[3072,768]{1,0:T(8,128)(2,1)S(1)}, bf16[3072,768]{1,0:T(8,128)(2,1)}, u32[]{:S(2)}) copy-start(bf16[3072,768]{1,0:T(8,128)(2,1)} %reshape.486) | copy-start | bytes 14155780
  313.1 12.5 %copy-start.37 = (f32[768]{0:T(1024)S(1)}, f32[768]{0:T(1024)}, u32[]{:S(2)}) copy-start(f32[768]{0:T(1024)} %get-tuple-element.43) | copy-start | bytes 9220
  336.7 1.7 copy-start.23
  345.4 8.6 copy-start.24
  354.0 12.5 %copy-start.3 = (f32[1024,768]{1,0:T(8,128)S(1)}, f32[1024,768]{1,0:T(8,128)}, u32[]{:S(2)}) copy-start(f32[1024,768]{1,0:T(8,128)} %copy-done.1) | copy-start | bytes 9437188
  382.8 2.3 copy-start.28
  385.1 4.4 copy-start.35
  385.1 5.3 copy-start.34
  385.1 6.1 copy-start.30
  441.4 25.3 %all-to-all-start.14 = ((bf16[256,4,192]{0,2,1:T(8,128)(2,1)}), bf16[256,4,192]{0,2,1:T(8,128)(2,1)S(1)}, u32[]{:S(2)}, u32[]{:S(2)}) async-start(bf16[256,4,192]{0,2,1:T(8,128)(2,1)} %bitcast.79), calls=%async_computation.14 | async-start | bytes 786432 | tf_op jit(solution)/shard_map/all_to_all | solution.py:320
  466.7 26.6 %all-to-all-start.9 = ((bf16[4,2,73728]{2,1,0:T(2,128)(2,1)}), bf16[4,2,73728]{2,1,0:T(2,128)(2,1)S(1)}, u32[]{:S(2)}, u32[]{:S(2)}) async-start(bf16[4,2,73728]{2,1,0:T(2,128)(2,1)} %reshape.554), calls=%async_computation.9 | async-start | bytes 2359296 | tf_op jit(solution)/shard_map/all_to_all | solution.py:328
  493.3 19.9 %copy-start.17 = (bf16[4,2,73728]{2,1,0:T(2,128)(2,1)}, bf16[4,2,73728]{2,1,0:T(2,128)(2,1)S(1)}, u32[]{:S(2)}) copy-start(bf16[4,2,73728]{2,1,0:T(2,128)(2,1)S(1)} %all-to-all-done.9) | copy-start | bytes 3538948
  493.3 25.8 %all-to-all-start.11 = ((bf16[4,2,73728]{2,1,0:T(2,128)(2,1)}), bf16[4,2,73728]{2,1,0:T(2,128)(2,1)}, u32[]{:S(2)}, u32[]{:S(2)}) async-start(bf16[4,2,73728]{2,1,0:T(2,128)(2,1)} %reshape.552), calls=%async_computation.11 | async-start | bytes 2359296 | tf_op jit(solution)/shard_map/all_to_all | solution.py:328
  519.0 25.8 %all-to-all-start.13 = ((bf16[4,2,73728]{2,1,0:T(2,128)(2,1)}), bf16[4,2,73728]{2,1,0:T(2,128)(2,1)S(1)}, u32[]{:S(2)}, u32[]{:S(2)}) async-start(bf16[4,2,73728]{2,1,0:T(2,128)(2,1)} %reshape.550), calls=%async_computation.13 | async-start | bytes 2359296 | tf_op jit(solution)/shard_map/all_to_all | solution.py:328
  544.9 4.3 copy-start.18
  544.9 38.5 %all-to-all-start.15 = ((bf16[4,2,73728]{2,1,0:T(2,128)(2,1)}), bf16[4,2,73728]{2,1,0:T(2,128)(2,1)}, u32[]{:S(2)}, u32[]{:S(2)}) async-start(bf16[4,2,73728]{2,1,0:T(2,128)(2,1)} %reshape.548), calls=%async_computation.15 | async-start | bytes 2359296 | tf_op jit(solution)/shard_map/all_to_all | solution.py:328
  549.2 129.9 %reduce-scatter.10.cloned.1.call-start = ((), (), s32[]{:S(2)}) async-start(), calls=%async_computation.22 | async-start | bytes 4423680
  562.3 8.9 %copy-start.19 = (bf16[4,2,73728]{2,1,0:T(2,128)(2,1)S(1)}, bf16[4,2,73728]{2,1,0:T(2,128)(2,1)}, u32[]{:S(2)}) copy-start(bf16[4,2,73728]{2,1,0:T(2,128)(2,1)} %copy-done.18) | copy-start | bytes 3538948
  603.4 2.6 copy-start.5
  603.4 2.7 copy-start.27
  606.1 1.2 copy-start.7
  607.5 4.1 copy-start.9
  607.5 4.0 copy-start.4
  611.7 5.3 copy-start.11
  631.5 73.4 %reduce-scatter.12.cloned.1.call-start = ((), (), s32[]{:S(2)}) async-start(), calls=%async_computation.23 | async-start | bytes 614400
  681.4 1.3 copy-start.6
  681.4 173.4 %reduce-scatter.8.cloned.1.call-start = ((), (), s32[]{:S(2)}) async-start(), calls=%async_computation.21 | async-start | bytes 11354112 | tf_op jit(solution)/shard_map/reduce_scatter | solution.py:315
  682.7 3.5 copy-start.8
  682.7 3.7 copy-start.21
  686.4 2.4 copy-start.10
  686.4 2.5 copy-start.22
  688.8 1.3 copy-start.12
Sparse Core Ops, SparseCore 0:
  17.6 63.4 all-gather.2
  84.2 102.9 all-gather.4
  631.7 47.3 reduce-scatter.9
  681.8 23.1 reduce-scatter.11
  710.8 143.9 reduce-scatter.7

commit v7 on v4

--- a/solution.py
+++ b/solution.py
@@ -86,8 +86,10 @@
     for h in range(heads):
         keys = qkv_ref[:, pl.ds((heads + h) * DH, DH)]
         values = qkv_ref[:, pl.ds((2 * heads + h) * DH, DH)]
-        for c in range(length // ROWS_PER_STEP):
-            rows = pl.ds(c * ROWS_PER_STEP, ROWS_PER_STEP)
+
+        @pl.loop(0, length // ROWS_PER_STEP)
+        def _(c):
+            rows = pl.ds(pl.multiple_of(c * ROWS_PER_STEP, ROWS_PER_STEP), ROWS_PER_STEP)
             queries = qkv_ref[rows, pl.ds(h * DH, DH)]
             scores = times_transpose(queries, keys) * scale
             scores = jnp.where(seg_col_ref[rows, :] == seg_row, scores, NEG)
@@ -100,7 +102,9 @@
             lse_ref[rows, pl.ds(h, 1)] = highest + jnp.log(total)
 
 
-def attention_backward_kernel(qkv_ref, seg_col_ref, seg_row_ref, lse_ref, up_ref, grad_ref):
+def attention_backward_kernel(
+    qkv_ref, seg_col_ref, seg_row_ref, lse_ref, up_ref, grad_ref, key_acc_ref, value_acc_ref
+):
     length = qkv_ref.shape[0]
     heads = up_ref.shape[1] // DH
     scale = DH ** (-0.5)
@@ -108,24 +112,27 @@
     for h in range(heads):
         keys = qkv_ref[:, pl.ds((heads + h) * DH, DH)]
         values = qkv_ref[:, pl.ds((2 * heads + h) * DH, DH)]
-        key_acc = jnp.zeros((length, DH), jnp.float32)
-        value_acc = jnp.zeros((length, DH), jnp.float32)
-        for c in range(length // ROWS_PER_STEP):
-            rows = pl.ds(c * ROWS_PER_STEP, ROWS_PER_STEP)
+        key_acc_ref[...] = jnp.zeros_like(key_acc_ref)
+        value_acc_ref[...] = jnp.zeros_like(value_acc_ref)
+
+        @pl.loop(0, length // ROWS_PER_STEP)
+        def _(c):
+            rows = pl.ds(pl.multiple_of(c * ROWS_PER_STEP, ROWS_PER_STEP), ROWS_PER_STEP)
             queries = qkv_ref[rows, pl.ds(h * DH, DH)]
             upstream = up_ref[rows, pl.ds(h * DH, DH)]
             scores = times_transpose(queries, keys) * scale
             scores = jnp.where(seg_col_ref[rows, :] == seg_row, scores, NEG)
             weights = jnp.exp(scores - lse_ref[rows, pl.ds(h, 1)])
-            value_acc = value_acc + contract_rows(weights.astype(jnp.bfloat16), upstream)
+            value_acc_ref[...] += contract_rows(weights.astype(jnp.bfloat16), upstream)
             slope = times_transpose(upstream, values)
             inner = jnp.sum(weights * slope, axis=-1, keepdims=True)
             score_grad = (weights * (slope - inner)).astype(jnp.bfloat16)
             query_grad = jnp.dot(score_grad, keys, preferred_element_type=jnp.float32) * scale
             grad_ref[rows, pl.ds(h * DH, DH)] = query_grad.astype(grad_ref.dtype)
-            key_acc = key_acc + contract_rows(score_grad, queries) * scale
-        grad_ref[:, pl.ds((heads + h) * DH, DH)] = key_acc.astype(grad_ref.dtype)
-        grad_ref[:, pl.ds((2 * heads + h) * DH, DH)] = value_acc.astype(grad_ref.dtype)
+            key_acc_ref[...] += contract_rows(score_grad, queries) * scale
+
+        grad_ref[:, pl.ds((heads + h) * DH, DH)] = key_acc_ref[...].astype(grad_ref.dtype)
+        grad_ref[:, pl.ds((2 * heads + h) * DH, DH)] = value_acc_ref[...].astype(grad_ref.dtype)
 
 
 def attention_forward(qkv, segment):
@@ -155,6 +162,7 @@
         out_shape=jax.ShapeDtypeStruct((length, width), jnp.bfloat16),
         in_specs=[pl.BlockSpec(memory_space=pltpu.VMEM)] * 5,
         out_specs=pl.BlockSpec(memory_space=pltpu.VMEM),
+        scratch_shapes=[pltpu.VMEM((length, DH), jnp.float32)] * 2,
         cost_estimate=pl.CostEstimate(
             flops=flops, transcendentals=heads * length * length, bytes_accessed=5 * length * width
         ),
@@ -300,11 +308,13 @@
     early, back_attn = lax.optimization_barrier((early, back_attn))
     early_sum = lax.psum_scatter(early, axes, scatter_dimension=0, tiled=True).astype(jnp.float32)
 
-    back_context = times_transpose(back_attn, full_out).astype(jnp.bfloat16)
     back_parts = []
     for s in range(streams):
+        back_context = times_transpose(
+            back_attn[s * part_len : (s + 1) * part_len], full_out
+        ).astype(jnp.bfloat16)
         one_back = lax.all_to_all(
-            back_context[s * part_len : (s + 1) * part_len].reshape(part_len, heads, DH),
+            back_context.reshape(part_len, heads, DH),
             "seq",
             split_axis=1,
             concat_axis=0,

time: 870 us -> 914 us (1.051)
  Pallas kernels: 101 us -> 144 us
  blocking collectives: 32.2 us -> 0 us
  waiting for transfers between devices: 318 us -> 332 us
  starting transfers between devices: 53.2 us -> 64.1 us
    all_to_all x3 -> x0, blocking collectives: 32.2 us -> none  [per_device(): lax.all_to_all(back_context[s * part_len:(s + 1) * part_len].reshape(part...]
    pallas_call x4, Pallas kernels: 59.8 us -> 90.8 us  [attention_backward(): pl.pallas_call(attention_backward_kernel, out_shape=jax.ShapeDtypeStruct(...]
    all_to_all x1 -> x4, waiting for transfers between devices: 0.01 us -> 13.2 us  [per_device(): lax.all_to_all(back_context.reshape(part_len, heads, DH), 'seq', split_ax...]
    pallas_call x4, Pallas kernels: 41.4 us -> 53.6 us  [attention_forward(): pl.pallas_call(attention_forward_kernel, out_shape=(jax.ShapeDtypeStruct(...]
    all_to_all x1 -> x4, starting transfers between devices: 3.86 us -> 14.6 us  [per_device(): lax.all_to_all(back_context.reshape(part_len, heads, DH), 'seq', split_ax...]
    dot_general x4 -> x7, matrix products: 32.2 us -> 36.6 us  [times_transpose(): lax.dot_general(left, right, (((1,), (1,)), ((), ())), preferred_element_...]
    unnamed x86 -> x90, local copies, waits for them, and re-layouts: 62.6 us -> 63.9 us
  transfers between devices with their start and end apart: 18 -> 21, of which waited for: 7 -> 10; matrix products, arithmetic and copies ran while one was open for 19% -> 19% of each run, Pallas kernels for 12% -> 16%
where the time goes in v7:
time: 914 us; the launch traced here: 904 us
  waiting for transfers between devices  332 us (36%)
  local copies, waits for them, and re-layouts  222 us (24%)
  Pallas kernels  144 us (16%)
  matrix products  92.5 us (10%)
  starting transfers between devices  64.1 us (7%)
  other arithmetic  33.7 us (4%)
  between operations  14.9 us (2%)
    reduce_scatter x1, waiting for transfers between devices, per_device(): lax.psum_scatter(early, axes, scatter_dimension=0, tiled=True)  147 us
    pallas_call x4, Pallas kernels, attention_backward(): pl.pallas_call(attention_backward_kernel, out_shape=jax.ShapeDtypeStruct(...  90.8 us
    unnamed x90, local copies, waits for them, and re-layouts  63.9 us
    unnamed x7, waiting for transfers between devices  62.3 us
    all_gather x1, waiting for transfers between devices, per_device(): full_first = lax.all_gather(first, axes, axis=0, tiled=True)  59.8 us
    pallas_call x4, Pallas kernels, attention_forward(): pl.pallas_call(attention_forward_kernel, out_shape=(jax.ShapeDtypeStruct(...  53.6 us
    all_to_all x4, waiting for transfers between devices, per_device(): lax.all_to_all(qkv.reshape(part_len, 3, heads, DH), 'seq', split_axis=2,...  49.3 us
    dot_general x7, matrix products, times_transpose(): lax.dot_general(left, right, (((1,), (1,)), ((), ())), preferred_element_...  36.6 us
  transfers between devices with their start and end apart: 21, of which 10 were waited for; matrix products, arithmetic and copies ran while one was open for 19% of the time, Pallas kernels for 16%

profile of v7, /device:TPU:0, one launch (start us, length us, event | category | flops | bytes accessed | tf_op | source)
XLA Modules:
  0.0 903.6 jit_solution(18378330273016384232)
XLA Ops:
  21.5 59.8 %all-gather.3.cloned.1.call-done = bf16[768,2316]{1,0:T(8,128)(2,1)} async-done(((bf16[24,2316]{1,0:T(8,128)(2,1)}), bf16[768,2316]{1,0:T(8,128)(2,1)}) %all-gather.3.cloned.1.call-update) | async-done | bytes 3557392 | tf_op jit(solution)/shard_map/all_gather | solution.py:227
  81.3 3.4 convert_reduce_fusion.1
  89.1 3.5 all-to-all-start
  97.1 12.2 %all-to-all-done = bf16[256,3,12,64]{0,3,1,2:T(8,128)(2,1)S(1)} async-done(((bf16[256,3,12,64]{0,3,1,2:T(8,128)(2,1)}), bf16[256,3,12,64]{0,3,1,2:T(8,128)(2,1)S(1)}, u32[]{:S(2)}, u32[]{:S(2)}) %all-to-all-start) | async-done | bytes 1179680 | tf_op jit(solution)/shard_map/all_to_all | solution.py:252
  110.3 3.5 all-to-all-start.2
  118.2 20.5 %all-to-all-done.2 = bf16[256,3,12,64]{0,3,1,2:T(8,128)(2,1)S(1)} async-done(((bf16[256,3,12,64]{0,3,1,2:T(8,128)(2,1)}), bf16[256,3,12,64]{0,3,1,2:T(8,128)(2,1)S(1)}, u32[]{:S(2)}, u32[]{:S(2)}) %all-to-all-start.2) | async-done | bytes 1179680 | tf_op jit(solution)/shard_map/all_to_all | solution.py:252
  139.8 3.5 all-to-all-start.4
  147.8 16.6 %all-to-all-done.4 = bf16[256,3,12,64]{0,3,1,2:T(8,128)(2,1)S(1)} async-done(((bf16[256,3,12,64]{0,3,1,2:T(8,128)(2,1)}), bf16[256,3,12,64]{0,3,1,2:T(8,128)(2,1)S(1)}, u32[]{:S(2)}, u32[]{:S(2)}) %all-to-all-start.4) | async-done | bytes 1179680 | tf_op jit(solution)/shard_map/all_to_all | solution.py:252
  164.3 3.7 all-to-all-start.6
  175.9 13.4 %shard_map.305 = (bf16[1024,192]{1,0:T(8,128)(2,1)}, f32[1024,3]{1,0:T(8,128)}) custom-call(bf16[1024,576]{1,0:T(8,128)(2,1)} %copy.297.qkv_ref, s32[1024,1]{1,0:T(8,128)} %copy.298.seg_col_ref, s32[1,1024]{1,0:T(1,128)} %get-tuple-element.79.seg_row_ref), custom_call_target="tpu_custom_call" | custom-call | flops 805306368 | bytes 1769472 | tf_op jit(solution)/shard_map/pallas_call | solution.py:142
  194.6 4.1 all-to-all-start.1
  202.3 13.4 %shard_map.306 = (bf16[1024,192]{1,0:T(8,128)(2,1)}, f32[1024,3]{1,0:T(8,128)}) custom-call(bf16[1024,576]{1,0:T(8,128)(2,1)} %copy.306.qkv_ref, s32[1024,1]{1,0:T(8,128)} %copy.307.seg_col_ref, s32[1,1024]{1,0:T(1,128)} %get-tuple-element.86.seg_row_ref), custom_call_target="tpu_custom_call" | custom-call | flops 805306368 | bytes 1769472 | tf_op jit(solution)/shard_map/pallas_call | solution.py:142
  220.9 4.4 all-to-all-start.3
  235.1 13.4 %shard_map.307 = (bf16[1024,192]{1,0:T(8,128)(2,1)}, f32[1024,3]{1,0:T(8,128)}) custom-call(bf16[1024,576]{1,0:T(8,128)(2,1)} %copy.315.qkv_ref, s32[1024,1]{1,0:T(8,128)} %copy.316.seg_col_ref, s32[1,1024]{1,0:T(1,128)} %get-tuple-element.85.seg_row_ref), custom_call_target="tpu_custom_call" | custom-call | flops 805306368 | bytes 1769472 | tf_op jit(solution)/shard_map/pallas_call | solution.py:142
  253.6 4.2 all-to-all-start.5
  261.4 13.4 %shard_map.308 = (bf16[1024,192]{1,0:T(8,128)(2,1)}, f32[1024,3]{1,0:T(8,128)}) custom-call(bf16[1024,576]{1,0:T(8,128)(2,1)} %copy.324.qkv_ref, s32[1024,1]{1,0:T(8,128)} %copy.325.seg_col_ref, s32[1,1024]{1,0:T(1,128)} %get-tuple-element.84.seg_row_ref), custom_call_target="tpu_custom_call" | custom-call | flops 805306368 | bytes 1769472 | tf_op jit(solution)/shard_map/pallas_call | solution.py:142
  278.2 4.6 all-to-all-start.7
  295.8 4.0 fusion.61
  302.0 4.9 slice.173
  306.9 8.5 reshape.410
  315.4 12.4 %multiply_convert_fusion = (bf16[1024,3072]{1,0:T(8,128)(2,1)S(1)}, f32[1024,3072]{1,0:T(8,128)}) fusion(f32[3072]{0:T(1024)S(1)} %copy-done.20, bf16[768,6912]{1,0:T(8,128)(2,1)} %all-gather.5.cloned.1.call-done, f32[1024,768]{1,0:T(8,128)} %copy-done.2, f32[768]{0:T(1024)S(1)} %copy-done.23, f32[768]{0:T(1024)S(1)} %get-tuple-element.47, ...), kind=kOutput, calls=%fused_computation.7 | convolution fusion | flops 4854644736 | bytes 26765312 | tf_op jit(solution)/shard_map/dot_general | solution.py:270
  327.9 5.4 fusion.62
  333.9 3.3 fusion.21
  340.7 7.0 convolution_convert_fusion
  347.7 8.6 convert_element_type.329
  356.4 12.2 %fusion.63 = (bf16[3072]{0:T(1024)(128)(2,1)S(1)}, bf16[1024,3072]{1,0:T(8,128)(2,1)S(1)}) fusion(f32[1024,3072]{1,0:T(8,128)} %get-tuple-element.90, f32[3072]{0:T(1024)S(1)} %copy-done.20, bf16[3072,768]{1,0:T(8,128)(2,1)} %reshape.410, f32[1024,768]{1,0:T(8,128)S(1)} %copy-done.12), kind=kOutput, calls=%fused_computation.147 | convolution fusion | flops 4870370304 | bytes 26757120 | tf_op jit(solution)/shard_map/dot_general | solution.py:27
  368.6 8.0 convolution_convert_fusion.1
  376.5 8.3 multiply_reduce_fusion
  393.8 17.8 %concatenate.20 = bf16[768,7168]{1,0:T(8,128)(2,1)} concatenate(bf16[768,768]{1,0:T(8,128)(2,1)S(1)} %convolution_convert_fusion.3, bf16[768,3072]{1,0:T(8,128)(2,1)} %convolution_convert_fusion.1, bf16[768,3072]{1,0:T(8,128)(2,1)} %convert_element_type.329, bf16[768,1]{1,0:T(8,128)(2,1)S(1)} %convert_element_type.360, bf16[768,1]{1,0:T(8,128)(2,1)} %convert_element_type.361, ...), dimensions={1} | concatenate | bytes 22020096 | tf_op jit(solution)/shard_map/concatenate | solution.py:74
  414.3 4.2 all-to-all-start.8
  421.2 4.6 all-to-all-done.8
  425.9 3.5 all-to-all-start.10
  432.0 5.0 all-to-all-done.10
  437.8 3.5 all-to-all-start.12
  443.9 3.6 all-to-all-done.12
  447.6 3.5 all-to-all-start.14
  452.4 22.7 %shard_map.309 = bf16[1024,576]{1,0:T(8,128)(2,1)} custom-call(bf16[1024,576]{1,0:T(8,128)(2,1)} %copy.297.qkv_ref, s32[1024,1]{1,0:T(8,128)} %copy.298.seg_col_ref, s32[1,1024]{1,0:T(1,128)} %get-tuple-element.79.seg_row_ref, f32[1024,3]{1,0:T(8,128)} %get-tuple-element.31.lse_ref, bf16[1024,192]{1,0:T(8,128)(2,1)} %copy.342.up_ref), custom_call_target="tpu_custom_call" | custom-call | flops 2013265920 | bytes 2949120 | tf_op jit(solution)/shard_map/pallas_call | solution.py:160
  477.6 4.6 copy.344
  485.2 4.4 all-to-all-start.9
  492.0 22.7 %shard_map.310 = bf16[1024,576]{1,0:T(8,128)(2,1)} custom-call(bf16[1024,576]{1,0:T(8,128)(2,1)} %copy.306.qkv_ref, s32[1024,1]{1,0:T(8,128)} %copy.307.seg_col_ref, s32[1,1024]{1,0:T(1,128)} %get-tuple-element.86.seg_row_ref, f32[1024,3]{1,0:T(8,128)} %get-tuple-element.33.lse_ref, bf16[1024,192]{1,0:T(8,128)(2,1)} %copy.351.up_ref), custom_call_target="tpu_custom_call" | custom-call | flops 2013265920 | bytes 2949120 | tf_op jit(solution)/shard_map/pallas_call | solution.py:160
  517.1 4.6 copy.353
  524.8 4.5 all-to-all-start.11
  531.7 22.7 %shard_map.311 = bf16[1024,576]{1,0:T(8,128)(2,1)} custom-call(bf16[1024,576]{1,0:T(8,128)(2,1)} %copy.315.qkv_ref, s32[1024,1]{1,0:T(8,128)} %copy.316.seg_col_ref, s32[1,1024]{1,0:T(1,128)} %get-tuple-element.85.seg_row_ref, f32[1024,3]{1,0:T(8,128)} %get-tuple-element.34.lse_ref, bf16[1024,192]{1,0:T(8,128)(2,1)} %copy.360.up_ref), custom_call_target="tpu_custom_call" | custom-call | flops 2013265920 | bytes 2949120 | tf_op jit(solution)/shard_map/pallas_call | solution.py:160
  556.8 4.6 copy.362
  564.5 4.5 all-to-all-start.13
  570.4 22.7 %shard_map.312 = bf16[1024,576]{1,0:T(8,128)(2,1)} custom-call(bf16[1024,576]{1,0:T(8,128)(2,1)} %copy.324.qkv_ref, s32[1024,1]{1,0:T(8,128)} %copy.325.seg_col_ref, s32[1,1024]{1,0:T(1,128)} %get-tuple-element.84.seg_row_ref, f32[1024,3]{1,0:T(8,128)} %get-tuple-element.35.lse_ref, bf16[1024,192]{1,0:T(8,128)(2,1)} %copy.369.up_ref), custom_call_target="tpu_custom_call" | custom-call | flops 2013265920 | bytes 2949120 | tf_op jit(solution)/shard_map/pallas_call | solution.py:160
  595.5 4.6 copy.371
  603.2 4.3 all-to-all-start.15
  607.5 3.9 reshape.466
  611.4 3.5 copy.346
  614.9 3.5 reshape.464
  618.4 3.5 copy.355
  621.9 3.5 reshape.462
  625.4 3.5 copy.364
  628.9 3.5 reshape.460
  632.4 3.5 copy.373
  638.6 4.5 copy.374
  644.6 4.3 fusion.6
  652.0 5.7 concatenate.21
  657.7 5.1 copy.401
  665.7 49.0 %reduce-scatter.10.cloned.1.call-done = bf16[24,10240]{1,0:T(8,128)(2,1)} async-done(((bf16[192,10240]{1,0:T(8,128)(2,1)}), bf16[24,10240]{1,0:T(8,128)(2,1)}) %reduce-scatter.10.cloned.1.call-update) | async-done | bytes 491536
  718.9 9.0 fusion.32
  727.9 12.7 %reduce-scatter.12.cloned.1.call-done = bf16[24,2560]{1,0:T(8,128)(2,1)} async-done(((bf16[96,2560]{1,0:T(8,128)(2,1)}), bf16[24,2560]{1,0:T(8,128)(2,1)}) %reduce-scatter.12.cloned.1.call-update) | async-done | bytes 122896
  743.0 147.4 %reduce-scatter.8.cloned.1.call-done = bf16[24,7168]{1,0:T(8,128)(2,1)} async-done(((bf16[768,7168]{1,0:T(8,128)(2,1)}), bf16[24,7168]{1,0:T(8,128)(2,1)}) %reduce-scatter.8.cloned.1.call-update) | async-done | bytes 344080 | tf_op jit(solution)/shard_map/reduce_scatter | solution.py:309
  (235 shorter events, 169.6 us)
Async XLA Ops:
  7.2 77.5 %copy-start.27 = (bf16[4,256,768]{2,1,0:T(8,128)(2,1)S(1)}, bf16[4,256,768]{2,1,0:T(8,128)(2,1)}, u32[]{:S(2)}) copy-start(bf16[4,256,768]{2,1,0:T(8,128)(2,1)} %param.18) | copy-start | bytes 4718596
  7.2 74.1 %all-gather.3.cloned.1.call-start = ((), (), s32[]{:S(2)}) async-start(), calls=%async_computation.19 | async-start | bytes 3852288 | tf_op jit(solution)/shard_map/all_gather | solution.py:227
  17.6 278.2 %all-gather.5.cloned.1.call-start = ((), (), s32[]{:S(2)}) async-start(), calls=%async_computation.20 | async-start | bytes 10948608 | tf_op jit(solution)/shard_map/all_gather | solution.py:228
  89.1 20.2 %all-to-all-start = ((bf16[256,3,12,64]{0,3,1,2:T(8,128)(2,1)}), bf16[256,3,12,64]{0,3,1,2:T(8,128)(2,1)S(1)}, u32[]{:S(2)}, u32[]{:S(2)}) async-start(bf16[256,3,12,64]{0,3,1,2:T(8,128)(2,1)} %copy.293), calls=%async_computation | async-start | bytes 2359296 | tf_op jit(solution)/shard_map/all_to_all | solution.py:252
  109.3 1.0 copy-start.9
  110.3 28.4 %all-to-all-start.2 = ((bf16[256,3,12,64]{0,3,1,2:T(8,128)(2,1)}), bf16[256,3,12,64]{0,3,1,2:T(8,128)(2,1)S(1)}, u32[]{:S(2)}, u32[]{:S(2)}) async-start(bf16[256,3,12,64]{0,3,1,2:T(8,128)(2,1)} %copy.303), calls=%async_computation.2 | async-start | bytes 2359296 | tf_op jit(solution)/shard_map/all_to_all | solution.py:252
  138.7 1.1 copy-start.7
  139.8 24.6 %all-to-all-start.4 = ((bf16[256,3,12,64]{0,3,1,2:T(8,128)(2,1)}), bf16[256,3,12,64]{0,3,1,2:T(8,128)(2,1)S(1)}, u32[]{:S(2)}, u32[]{:S(2)}) async-start(bf16[256,3,12,64]{0,3,1,2:T(8,128)(2,1)} %copy.312), calls=%async_computation.4 | async-start | bytes 2359296 | tf_op jit(solution)/shard_map/all_to_all | solution.py:252
  146.7 21.4 %copy-start.26 = (s32[4,17]{1,0:T(4,128)S(1)}, s32[4,17]{1,0:T(4,128)}, u32[]{:S(2)}) copy-start(s32[4,17]{1,0:T(4,128)} %param.20) | copy-start | bytes 820
  164.3 9.1 %copy-start.6 = (bf16[256,3,12,64]{0,3,1,2:T(8,128)(2,1)}, bf16[256,3,12,64]{0,3,1,2:T(8,128)(2,1)S(1)}, u32[]{:S(2)}) copy-start(bf16[256,3,12,64]{0,3,1,2:T(8,128)(2,1)S(1)} %all-to-all-done.4) | copy-start | bytes 3538948
  164.3 30.2 %all-to-all-start.6 = ((bf16[256,3,12,64]{0,3,1,2:T(8,128)(2,1)}), bf16[256,3,12,64]{0,3,1,2:T(8,128)(2,1)S(1)}, u32[]{:S(2)}, u32[]{:S(2)}) async-start(bf16[256,3,12,64]{0,3,1,2:T(8,128)(2,1)} %copy.321), calls=%async_computation.6 | async-start | bytes 2359296 | tf_op jit(solution)/shard_map/all_to_all | solution.py:252
  189.3 10.4 %copy-start.8 = (bf16[256,3,12,64]{0,3,1,2:T(8,128)(2,1)S(1)}, bf16[256,3,12,64]{0,3,1,2:T(8,128)(2,1)}, u32[]{:S(2)}) copy-start(bf16[256,3,12,64]{0,3,1,2:T(8,128)(2,1)} %copy-done.7) | copy-start | bytes 3538948
  194.6 26.3 %all-to-all-start.1 = ((bf16[4,2,24576]{2,1,0:T(2,128)(2,1)}), bf16[4,2,24576]{2,1,0:T(2,128)(2,1)S(1)}, u32[]{:S(2)}, u32[]{:S(2)}) async-start(bf16[4,2,24576]{2,1,0:T(2,128)(2,1)} %reshape.457), calls=%async_computation.1 | async-start | bytes 786432 | tf_op jit(solution)/shard_map/all_to_all | solution.py:258
  215.7 12.4 %copy-start = (bf16[4,256,768]{2,1,0:T(8,128)(2,1)S(1)}, bf16[4,256,768]{2,1,0:T(8,128)(2,1)}, u32[]{:S(2)}) copy-start(bf16[4,256,768]{2,1,0:T(8,128)(2,1)} %param.19) | copy-start | bytes 4718596
  220.9 11.8 %copy-start.17 = (bf16[4,2,24576]{2,1,0:T(2,128)(2,1)}, bf16[4,2,24576]{2,1,0:T(2,128)(2,1)S(1)}, u32[]{:S(2)}) copy-start(bf16[4,2,24576]{2,1,0:T(2,128)(2,1)S(1)} %all-to-all-done.1) | copy-start | bytes 1179652
  220.9 32.7 %all-to-all-start.3 = ((bf16[4,2,24576]{2,1,0:T(2,128)(2,1)}), bf16[4,2,24576]{2,1,0:T(2,128)(2,1)}, u32[]{:S(2)}, u32[]{:S(2)}) async-start(bf16[4,2,24576]{2,1,0:T(2,128)(2,1)} %reshape.455), calls=%async_computation.3 | async-start | bytes 786432 | tf_op jit(solution)/shard_map/all_to_all | solution.py:258
  253.6 24.6 %all-to-all-start.5 = ((bf16[4,2,24576]{2,1,0:T(2,128)(2,1)}), bf16[4,2,24576]{2,1,0:T(2,128)(2,1)}, u32[]{:S(2)}, u32[]{:S(2)}) async-start(bf16[4,2,24576]{2,1,0:T(2,128)(2,1)} %reshape.453), calls=%async_computation.5 | async-start | bytes 786432 | tf_op jit(solution)/shard_map/all_to_all | solution.py:258
  276.8 7.3 copy-start.18
  278.2 11.9 %all-to-all-start.7 = ((bf16[4,2,24576]{2,1,0:T(2,128)(2,1)}), bf16[4,2,24576]{2,1,0:T(2,128)(2,1)}, u32[]{:S(2)}, u32[]{:S(2)}) async-start(bf16[4,2,24576]{2,1,0:T(2,128)(2,1)} %reshape.451), calls=%async_computation.7 | async-start | bytes 786432 | tf_op jit(solution)/shard_map/all_to_all | solution.py:258
  294.2 1.6 copy-start.25
  295.8 4.0 copy-start.13
  299.8 1.7 copy-start.2
  306.9 8.5 copy-start.20
  306.9 8.5 copy-start.23
  315.4 12.5 %copy-start.3 = (f32[1024,768]{1,0:T(8,128)S(1)}, f32[1024,768]{1,0:T(8,128)}, u32[]{:S(2)}) copy-start(f32[1024,768]{1,0:T(8,128)} %copy-done.2) | copy-start | bytes 9437188
  315.4 12.5 %copy-start.5 = (bf16[3072,768]{1,0:T(8,128)(2,1)S(1)}, bf16[3072,768]{1,0:T(8,128)(2,1)}, u32[]{:S(2)}) copy-start(bf16[3072,768]{1,0:T(8,128)(2,1)} %reshape.410) | copy-start | bytes 14155780
  315.4 12.5 %copy-start.24 = (f32[768]{0:T(1024)S(1)}, f32[768]{0:T(1024)}, u32[]{:S(2)}) copy-start(f32[768]{0:T(1024)} %get-tuple-element.45) | copy-start | bytes 9220
  339.0 1.7 copy-start.11
  347.7 8.6 copy-start.12
  356.4 12.2 %copy-start.4 = (f32[1024,768]{1,0:T(8,128)S(1)}, f32[1024,768]{1,0:T(8,128)}, u32[]{:S(2)}) copy-start(f32[1024,768]{1,0:T(8,128)} %copy-done.2) | copy-start | bytes 9437188
  384.9 2.7 copy-start.14
  387.6 4.4 copy-start.22
  387.6 5.3 copy-start.21
  387.6 6.1 copy-start.19
  414.3 11.5 %all-to-all-start.8 = ((bf16[256,12,64]{0,2,1:T(8,128)(2,1)}), bf16[256,12,64]{0,2,1:T(8,128)(2,1)S(1)}, u32[]{:S(2)}, u32[]{:S(2)}) async-start(bf16[256,12,64]{0,2,1:T(8,128)(2,1)} %bitcast.59), calls=%async_computation.8 | async-start | bytes 786432 | tf_op jit(solution)/shard_map/all_to_all | solution.py:316
  425.9 11.1 %all-to-all-start.10 = ((bf16[256,12,64]{0,2,1:T(8,128)(2,1)}), bf16[256,12,64]{0,2,1:T(8,128)(2,1)S(1)}, u32[]{:S(2)}, u32[]{:S(2)}) async-start(bf16[256,12,64]{0,2,1:T(8,128)(2,1)} %bitcast.67), calls=%async_computation.10 | async-start | bytes 786432 | tf_op jit(solution)/shard_map/all_to_all | solution.py:316
  437.0 0.8 copy-start.16
  437.8 9.8 %all-to-all-start.12 = ((bf16[256,12,64]{0,2,1:T(8,128)(2,1)}), bf16[256,12,64]{0,2,1:T(8,128)(2,1)S(1)}, u32[]{:S(2)}, u32[]{:S(2)}) async-start(bf16[256,12,64]{0,2,1:T(8,128)(2,1)} %bitcast.75), calls=%async_computation.12 | async-start | bytes 786432 | tf_op jit(solution)/shard_map/all_to_all | solution.py:316
  447.6 27.5 %copy-start.15 = (bf16[256,12,64]{0,2,1:T(8,128)(2,1)}, bf16[256,12,64]{0,2,1:T(8,128)(2,1)S(1)}, u32[]{:S(2)}) copy-start(bf16[256,12,64]{0,2,1:T(8,128)(2,1)S(1)} %all-to-all-done.12) | copy-start | bytes 1179652
  447.6 37.6 %all-to-all-start.14 = ((bf16[256,12,64]{0,2,1:T(8,128)(2,1)}), bf16[256,12,64]{0,2,1:T(8,128)(2,1)S(1)}, u32[]{:S(2)}, u32[]{:S(2)}) async-start(bf16[256,12,64]{0,2,1:T(8,128)(2,1)} %bitcast.83), calls=%async_computation.14 | async-start | bytes 786432 | tf_op jit(solution)/shard_map/all_to_all | solution.py:316
  485.2 39.6 %all-to-all-start.9 = ((bf16[4,2,73728]{2,1,0:T(2,128)(2,1)}), bf16[4,2,73728]{2,1,0:T(2,128)(2,1)}, u32[]{:S(2)}, u32[]{:S(2)}) async-start(bf16[4,2,73728]{2,1,0:T(2,128)(2,1)} %reshape.465), calls=%async_computation.9 | async-start | bytes 2359296 | tf_op jit(solution)/shard_map/all_to_all | solution.py:328
  524.8 39.7 %all-to-all-start.11 = ((bf16[4,2,73728]{2,1,0:T(2,128)(2,1)}), bf16[4,2,73728]{2,1,0:T(2,128)(2,1)}, u32[]{:S(2)}, u32[]{:S(2)}) async-start(bf16[4,2,73728]{2,1,0:T(2,128)(2,1)} %reshape.463), calls=%async_computation.11 | async-start | bytes 2359296 | tf_op jit(solution)/shard_map/all_to_all | solution.py:328
  564.5 38.7 %all-to-all-start.13 = ((bf16[4,2,73728]{2,1,0:T(2,128)(2,1)}), bf16[4,2,73728]{2,1,0:T(2,128)(2,1)}, u32[]{:S(2)}, u32[]{:S(2)}) async-start(bf16[4,2,73728]{2,1,0:T(2,128)(2,1)} %reshape.461), calls=%async_computation.13 | async-start | bytes 2359296 | tf_op jit(solution)/shard_map/all_to_all | solution.py:328
  603.2 25.8 %all-to-all-start.15 = ((bf16[4,2,73728]{2,1,0:T(2,128)(2,1)}), bf16[4,2,73728]{2,1,0:T(2,128)(2,1)}, u32[]{:S(2)}, u32[]{:S(2)}) async-start(bf16[4,2,73728]{2,1,0:T(2,128)(2,1)} %reshape.459), calls=%async_computation.15 | async-start | bytes 2359296 | tf_op jit(solution)/shard_map/all_to_all | solution.py:328
  607.4 107.3 %reduce-scatter.10.cloned.1.call-start = ((), (), s32[]{:S(2)}) async-start(), calls=%async_computation.22 | async-start | bytes 4423680
  643.1 1.5 copy-start.28
  644.6 4.4 copy-start.1
  665.6 74.9 %reduce-scatter.12.cloned.1.call-start = ((), (), s32[]{:S(2)}) async-start(), calls=%async_computation.23 | async-start | bytes 614400
  717.0 1.9 copy-start.10
  717.0 173.4 %reduce-scatter.8.cloned.1.call-start = ((), (), s32[]{:S(2)}) async-start(), calls=%async_computation.21 | async-start | bytes 11354112 | tf_op jit(solution)/shard_map/reduce_scatter | solution.py:309
Sparse Core Ops, SparseCore 0:
  17.8 63.4 all-gather.2
  84.3 119.2 all-gather.4
  665.7 48.8 reduce-scatter.9
  717.4 23.1 reduce-scatter.11
  746.4 143.9 reduce-scatter.7

commit v8 on v4

--- a/solution.py
+++ b/solution.py
@@ -300,11 +300,13 @@
     early, back_attn = lax.optimization_barrier((early, back_attn))
     early_sum = lax.psum_scatter(early, axes, scatter_dimension=0, tiled=True).astype(jnp.float32)
 
-    back_context = times_transpose(back_attn, full_out).astype(jnp.bfloat16)
     back_parts = []
     for s in range(streams):
+        back_context = times_transpose(
+            back_attn[s * part_len : (s + 1) * part_len], full_out
+        ).astype(jnp.bfloat16)
         one_back = lax.all_to_all(
-            back_context[s * part_len : (s + 1) * part_len].reshape(part_len, heads, DH),
+            back_context.reshape(part_len, heads, DH),
             "seq",
             split_axis=1,
             concat_axis=0,

time: 870 us -> 870 us (level)
  blocking collectives: 32.2 us -> 0 us
  waiting for transfers between devices: 318 us -> 331 us
  starting transfers between devices: 53.2 us -> 64.3 us
    all_to_all x3 -> x0, blocking collectives: 32.2 us -> none  [per_device(): lax.all_to_all(back_context[s * part_len:(s + 1) * part_len].reshape(part...]
    all_to_all x1 -> x4, waiting for transfers between devices: 0.01 us -> 12.6 us  [per_device(): lax.all_to_all(back_context.reshape(part_len, heads, DH), 'seq', split_ax...]
    all_to_all x1 -> x4, starting transfers between devices: 3.86 us -> 15 us  [per_device(): lax.all_to_all(back_context.reshape(part_len, heads, DH), 'seq', split_ax...]
    dot_general x4 -> x7, matrix products: 32.2 us -> 36.6 us  [times_transpose(): lax.dot_general(left, right, (((1,), (1,)), ((), ())), preferred_element_...]
    unnamed x86 -> x90, local copies, waits for them, and re-layouts: 62.6 us -> 63.4 us
  transfers between devices with their start and end apart: 18 -> 21, of which waited for: 7 -> 10; matrix products, arithmetic and copies ran while one was open for 19% -> 20% of each run, Pallas kernels for 12% -> 12%
where the time goes in v8:
time: 870 us; the launch traced here: 859 us
  waiting for transfers between devices  331 us (38%)
  local copies, waits for them, and re-layouts  221 us (25%)
  Pallas kernels  101 us (12%)
  matrix products  92.7 us (11%)
  starting transfers between devices  64.3 us (7%)
  other arithmetic  33.3 us (4%)
  between operations  14.8 us (2%)
    reduce_scatter x1, waiting for transfers between devices, per_device(): lax.psum_scatter(early, axes, scatter_dimension=0, tiled=True)  147 us
    unnamed x90, local copies, waits for them, and re-layouts  63.4 us
    unnamed x7, waiting for transfers between devices  62 us
    pallas_call x4, Pallas kernels, attention_backward(): pl.pallas_call(attention_backward_kernel, out_shape=jax.ShapeDtypeStruct(...  59.8 us
    all_gather x1, waiting for transfers between devices, per_device(): full_first = lax.all_gather(first, axes, axis=0, tiled=True)  59.8 us
    all_to_all x4, waiting for transfers between devices, per_device(): lax.all_to_all(qkv.reshape(part_len, 3, heads, DH), 'seq', split_axis=2,...  49.3 us
    pallas_call x4, Pallas kernels, attention_forward(): pl.pallas_call(attention_forward_kernel, out_shape=(jax.ShapeDtypeStruct(...  41.4 us
    dot_general x7, matrix products, times_transpose(): lax.dot_general(left, right, (((1,), (1,)), ((), ())), preferred_element_...  36.6 us
  transfers between devices with their start and end apart: 21, of which 10 were waited for; matrix products, arithmetic and copies ran while one was open for 20% of the time, Pallas kernels for 12%

profile of v8, /device:TPU:0, one launch (start us, length us, event | category | flops | bytes accessed | tf_op | source)
XLA Modules:
  0.0 859.0 jit_solution(9187852077014229743)
XLA Ops:
  21.5 59.8 %all-gather.3.cloned.1.call-done = bf16[768,2316]{1,0:T(8,128)(2,1)} async-done(((bf16[24,2316]{1,0:T(8,128)(2,1)}), bf16[768,2316]{1,0:T(8,128)(2,1)}) %all-gather.3.cloned.1.call-update) | async-done | bytes 3557392 | tf_op jit(solution)/shard_map/all_gather | solution.py:219
  81.3 3.4 convert_reduce_fusion.1
  89.1 3.5 all-to-all-start
  97.1 12.2 %all-to-all-done = bf16[256,3,12,64]{0,3,1,2:T(8,128)(2,1)S(1)} async-done(((bf16[256,3,12,64]{0,3,1,2:T(8,128)(2,1)}), bf16[256,3,12,64]{0,3,1,2:T(8,128)(2,1)S(1)}, u32[]{:S(2)}, u32[]{:S(2)}) %all-to-all-start) | async-done | bytes 1179680 | tf_op jit(solution)/shard_map/all_to_all | solution.py:244
  110.3 3.5 all-to-all-start.2
  118.2 20.5 %all-to-all-done.2 = bf16[256,3,12,64]{0,3,1,2:T(8,128)(2,1)S(1)} async-done(((bf16[256,3,12,64]{0,3,1,2:T(8,128)(2,1)}), bf16[256,3,12,64]{0,3,1,2:T(8,128)(2,1)S(1)}, u32[]{:S(2)}, u32[]{:S(2)}) %all-to-all-start.2) | async-done | bytes 1179680 | tf_op jit(solution)/shard_map/all_to_all | solution.py:244
  139.8 3.5 all-to-all-start.4
  147.8 16.6 %all-to-all-done.4 = bf16[256,3,12,64]{0,3,1,2:T(8,128)(2,1)S(1)} async-done(((bf16[256,3,12,64]{0,3,1,2:T(8,128)(2,1)}), bf16[256,3,12,64]{0,3,1,2:T(8,128)(2,1)S(1)}, u32[]{:S(2)}, u32[]{:S(2)}) %all-to-all-start.4) | async-done | bytes 1179680 | tf_op jit(solution)/shard_map/all_to_all | solution.py:244
  164.3 3.7 all-to-all-start.6
  175.9 10.4 %shard_map.305 = (bf16[1024,192]{1,0:T(8,128)(2,1)}, f32[1024,3]{1,0:T(8,128)}) custom-call(bf16[1024,576]{1,0:T(8,128)(2,1)} %copy.297.qkv_ref, s32[1024,1]{1,0:T(8,128)} %copy.298.seg_col_ref, s32[1,1024]{1,0:T(1,128)} %get-tuple-element.79.seg_row_ref), custom_call_target="tpu_custom_call" | custom-call | flops 805306368 | bytes 1769472 | tf_op jit(solution)/shard_map/pallas_call | solution.py:135
  191.4 4.4 all-to-all-start.1
  199.5 10.3 %shard_map.306 = (bf16[1024,192]{1,0:T(8,128)(2,1)}, f32[1024,3]{1,0:T(8,128)}) custom-call(bf16[1024,576]{1,0:T(8,128)(2,1)} %copy.306.qkv_ref, s32[1024,1]{1,0:T(8,128)} %copy.307.seg_col_ref, s32[1,1024]{1,0:T(1,128)} %get-tuple-element.86.seg_row_ref), custom_call_target="tpu_custom_call" | custom-call | flops 805306368 | bytes 1769472 | tf_op jit(solution)/shard_map/pallas_call | solution.py:135
  215.0 4.6 all-to-all-start.3
  229.4 10.3 %shard_map.307 = (bf16[1024,192]{1,0:T(8,128)(2,1)}, f32[1024,3]{1,0:T(8,128)}) custom-call(bf16[1024,576]{1,0:T(8,128)(2,1)} %copy.315.qkv_ref, s32[1024,1]{1,0:T(8,128)} %copy.316.seg_col_ref, s32[1,1024]{1,0:T(1,128)} %get-tuple-element.85.seg_row_ref), custom_call_target="tpu_custom_call" | custom-call | flops 805306368 | bytes 1769472 | tf_op jit(solution)/shard_map/pallas_call | solution.py:135
  244.8 4.4 all-to-all-start.5
  252.9 10.3 %shard_map.308 = (bf16[1024,192]{1,0:T(8,128)(2,1)}, f32[1024,3]{1,0:T(8,128)}) custom-call(bf16[1024,576]{1,0:T(8,128)(2,1)} %copy.324.qkv_ref, s32[1024,1]{1,0:T(8,128)} %copy.325.seg_col_ref, s32[1,1024]{1,0:T(1,128)} %get-tuple-element.84.seg_row_ref), custom_call_target="tpu_custom_call" | custom-call | flops 805306368 | bytes 1769472 | tf_op jit(solution)/shard_map/pallas_call | solution.py:135
  266.6 4.4 all-to-all-start.7
  284.0 4.0 fusion.61
  290.2 4.9 slice.173
  295.1 8.5 reshape.410
  303.6 12.7 %multiply_convert_fusion = (bf16[1024,3072]{1,0:T(8,128)(2,1)S(1)}, f32[1024,3072]{1,0:T(8,128)}) fusion(f32[3072]{0:T(1024)S(1)} %copy-done.20, bf16[768,6912]{1,0:T(8,128)(2,1)} %all-gather.5.cloned.1.call-done, f32[1024,768]{1,0:T(8,128)} %copy-done.2, f32[768]{0:T(1024)S(1)} %copy-done.23, f32[768]{0:T(1024)S(1)} %get-tuple-element.47, ...), kind=kOutput, calls=%fused_computation.7 | convolution fusion | flops 4854644736 | bytes 26765312 | tf_op jit(solution)/shard_map/dot_general | solution.py:262
  316.4 5.4 fusion.62
  322.4 3.3 fusion.21
  329.1 7.0 convolution_convert_fusion
  336.2 8.6 %convert_element_type.329 = bf16[768,3072]{1,0:T(8,128)(2,1)} reshape(bf16[3072,768]{1,0:T(8,128)(2,1)} %convolution_convert_fusion) | data formatting | bytes 9437184 | tf_op jit(solution)/shard_map/convert_element_type | solution.py:70
  344.8 12.2 %fusion.63 = (bf16[3072]{0:T(1024)(128)(2,1)S(1)}, bf16[1024,3072]{1,0:T(8,128)(2,1)S(1)}) fusion(f32[1024,3072]{1,0:T(8,128)} %get-tuple-element.90, f32[3072]{0:T(1024)S(1)} %copy-done.20, bf16[3072,768]{1,0:T(8,128)(2,1)} %reshape.410, f32[1024,768]{1,0:T(8,128)S(1)} %copy-done.12), kind=kOutput, calls=%fused_computation.147 | convolution fusion | flops 4870370304 | bytes 26757120 | tf_op jit(solution)/shard_map/dot_general | solution.py:27
  357.0 8.0 convolution_convert_fusion.1
  365.0 8.3 multiply_reduce_fusion
  381.8 17.8 %concatenate.20 = bf16[768,7168]{1,0:T(8,128)(2,1)} concatenate(bf16[768,768]{1,0:T(8,128)(2,1)S(1)} %convolution_convert_fusion.3, bf16[768,3072]{1,0:T(8,128)(2,1)} %convolution_convert_fusion.1, bf16[768,3072]{1,0:T(8,128)(2,1)} %convert_element_type.329, bf16[768,1]{1,0:T(8,128)(2,1)S(1)} %convert_element_type.360, bf16[768,1]{1,0:T(8,128)(2,1)} %convert_element_type.361, ...), dimensions={1} | concatenate | bytes 22020096 | tf_op jit(solution)/shard_map/concatenate | solution.py:74
  402.3 4.2 all-to-all-start.8
  409.2 3.9 all-to-all-done.8
  413.1 3.5 all-to-all-start.10
  419.3 4.3 all-to-all-done.10
  424.4 3.5 all-to-all-start.12
  430.6 4.3 all-to-all-done.12
  434.9 3.9 all-to-all-start.14
  440.1 14.8 %shard_map.309 = bf16[1024,576]{1,0:T(8,128)(2,1)} custom-call(bf16[1024,576]{1,0:T(8,128)(2,1)} %copy.297.qkv_ref, s32[1024,1]{1,0:T(8,128)} %copy.298.seg_col_ref, s32[1,1024]{1,0:T(1,128)} %get-tuple-element.79.seg_row_ref, f32[1024,3]{1,0:T(8,128)} %get-tuple-element.31.lse_ref, bf16[1024,192]{1,0:T(8,128)(2,1)} %copy.342.up_ref), custom_call_target="tpu_custom_call" | custom-call | flops 2013265920 | bytes 2949120 | tf_op jit(solution)/shard_map/pallas_call | solution.py:153
  457.4 4.6 copy.344
  465.1 4.3 all-to-all-start.9
  471.7 15.1 %shard_map.310 = bf16[1024,576]{1,0:T(8,128)(2,1)} custom-call(bf16[1024,576]{1,0:T(8,128)(2,1)} %copy.306.qkv_ref, s32[1024,1]{1,0:T(8,128)} %copy.307.seg_col_ref, s32[1,1024]{1,0:T(1,128)} %get-tuple-element.86.seg_row_ref, f32[1024,3]{1,0:T(8,128)} %get-tuple-element.33.lse_ref, bf16[1024,192]{1,0:T(8,128)(2,1)} %copy.351.up_ref), custom_call_target="tpu_custom_call" | custom-call | flops 2013265920 | bytes 2949120 | tf_op jit(solution)/shard_map/pallas_call | solution.py:153
  489.2 4.6 copy.353
  496.9 4.3 all-to-all-start.11
  503.5 14.8 %shard_map.311 = bf16[1024,576]{1,0:T(8,128)(2,1)} custom-call(bf16[1024,576]{1,0:T(8,128)(2,1)} %copy.315.qkv_ref, s32[1024,1]{1,0:T(8,128)} %copy.316.seg_col_ref, s32[1,1024]{1,0:T(1,128)} %get-tuple-element.85.seg_row_ref, f32[1024,3]{1,0:T(8,128)} %get-tuple-element.34.lse_ref, bf16[1024,192]{1,0:T(8,128)(2,1)} %copy.360.up_ref), custom_call_target="tpu_custom_call" | custom-call | flops 2013265920 | bytes 2949120 | tf_op jit(solution)/shard_map/pallas_call | solution.py:153
  520.8 4.6 copy.362
  528.5 4.3 all-to-all-start.13
  534.1 15.1 %shard_map.312 = bf16[1024,576]{1,0:T(8,128)(2,1)} custom-call(bf16[1024,576]{1,0:T(8,128)(2,1)} %copy.324.qkv_ref, s32[1024,1]{1,0:T(8,128)} %copy.325.seg_col_ref, s32[1,1024]{1,0:T(1,128)} %get-tuple-element.84.seg_row_ref, f32[1024,3]{1,0:T(8,128)} %get-tuple-element.35.lse_ref, bf16[1024,192]{1,0:T(8,128)(2,1)} %copy.369.up_ref), custom_call_target="tpu_custom_call" | custom-call | flops 2013265920 | bytes 2949120 | tf_op jit(solution)/shard_map/pallas_call | solution.py:153
  551.6 4.6 copy.371
  559.3 4.3 all-to-all-start.15
  563.6 3.5 reshape.466
  567.0 3.5 copy.346
  570.6 3.5 reshape.464
  574.0 3.5 copy.355
  577.6 3.5 reshape.462
  581.0 3.5 copy.364
  584.5 3.5 reshape.460
  588.0 3.5 copy.373
  594.2 4.5 copy.374
  600.3 4.3 fusion.6
  607.6 5.7 concatenate.21
  613.3 5.1 copy.401
  621.3 48.8 %reduce-scatter.10.cloned.1.call-done = bf16[24,10240]{1,0:T(8,128)(2,1)} async-done(((bf16[192,10240]{1,0:T(8,128)(2,1)}), bf16[24,10240]{1,0:T(8,128)(2,1)}) %reduce-scatter.10.cloned.1.call-update) | async-done | bytes 491536
  674.3 9.0 %fusion.32 = f32[1024,768]{1,0:T(8,128)} fusion(f32[1024,768]{1,0:T(8,128)S(1)} %copy-done.10, bf16[1024,2304]{0,1:T(8,128)(2,1)} %bitcast.227, bf16[768,2316]{1,0:T(8,128)(2,1)} %all-gather.3.cloned.1.call-done), kind=kOutput, calls=%fused_computation.56 | convolution fusion | flops 3624665088 | bytes 14548992 | tf_op jit(solution)/shard_map/dot_general | solution.py:27
  683.3 12.7 %reduce-scatter.12.cloned.1.call-done = bf16[24,2560]{1,0:T(8,128)(2,1)} async-done(((bf16[96,2560]{1,0:T(8,128)(2,1)}), bf16[24,2560]{1,0:T(8,128)(2,1)}) %reduce-scatter.12.cloned.1.call-update) | async-done | bytes 122896
  698.4 147.4 %reduce-scatter.8.cloned.1.call-done = bf16[24,7168]{1,0:T(8,128)(2,1)} async-done(((bf16[768,7168]{1,0:T(8,128)(2,1)}), bf16[24,7168]{1,0:T(8,128)(2,1)}) %reduce-scatter.8.cloned.1.call-update) | async-done | bytes 344080 | tf_op jit(solution)/shard_map/reduce_scatter | solution.py:301
  (235 shorter events, 169.1 us)
Async XLA Ops:
  7.2 77.5 %copy-start.27 = (bf16[4,256,768]{2,1,0:T(8,128)(2,1)S(1)}, bf16[4,256,768]{2,1,0:T(8,128)(2,1)}, u32[]{:S(2)}) copy-start(bf16[4,256,768]{2,1,0:T(8,128)(2,1)} %param.18) | copy-start | bytes 4718596
  7.2 74.1 %all-gather.3.cloned.1.call-start = ((), (), s32[]{:S(2)}) async-start(), calls=%async_computation.19 | async-start | bytes 3852288 | tf_op jit(solution)/shard_map/all_gather | solution.py:219
  17.6 266.4 %all-gather.5.cloned.1.call-start = ((), (), s32[]{:S(2)}) async-start(), calls=%async_computation.20 | async-start | bytes 10948608 | tf_op jit(solution)/shard_map/all_gather | solution.py:220
  89.1 20.2 %all-to-all-start = ((bf16[256,3,12,64]{0,3,1,2:T(8,128)(2,1)}), bf16[256,3,12,64]{0,3,1,2:T(8,128)(2,1)S(1)}, u32[]{:S(2)}, u32[]{:S(2)}) async-start(bf16[256,3,12,64]{0,3,1,2:T(8,128)(2,1)} %copy.293), calls=%async_computation | async-start | bytes 2359296 | tf_op jit(solution)/shard_map/all_to_all | solution.py:244
  109.3 1.0 copy-start.9
  110.3 28.4 %all-to-all-start.2 = ((bf16[256,3,12,64]{0,3,1,2:T(8,128)(2,1)}), bf16[256,3,12,64]{0,3,1,2:T(8,128)(2,1)S(1)}, u32[]{:S(2)}, u32[]{:S(2)}) async-start(bf16[256,3,12,64]{0,3,1,2:T(8,128)(2,1)} %copy.303), calls=%async_computation.2 | async-start | bytes 2359296 | tf_op jit(solution)/shard_map/all_to_all | solution.py:244
  138.7 1.1 copy-start.7
  139.8 24.6 %all-to-all-start.4 = ((bf16[256,3,12,64]{0,3,1,2:T(8,128)(2,1)}), bf16[256,3,12,64]{0,3,1,2:T(8,128)(2,1)S(1)}, u32[]{:S(2)}, u32[]{:S(2)}) async-start(bf16[256,3,12,64]{0,3,1,2:T(8,128)(2,1)} %copy.312), calls=%async_computation.4 | async-start | bytes 2359296 | tf_op jit(solution)/shard_map/all_to_all | solution.py:244
  146.7 21.4 %copy-start.26 = (s32[4,17]{1,0:T(4,128)S(1)}, s32[4,17]{1,0:T(4,128)}, u32[]{:S(2)}) copy-start(s32[4,17]{1,0:T(4,128)} %param.20) | copy-start | bytes 820
  164.3 9.1 %copy-start.6 = (bf16[256,3,12,64]{0,3,1,2:T(8,128)(2,1)}, bf16[256,3,12,64]{0,3,1,2:T(8,128)(2,1)S(1)}, u32[]{:S(2)}) copy-start(bf16[256,3,12,64]{0,3,1,2:T(8,128)(2,1)S(1)} %all-to-all-done.4) | copy-start | bytes 3538948
  164.3 27.1 %all-to-all-start.6 = ((bf16[256,3,12,64]{0,3,1,2:T(8,128)(2,1)}), bf16[256,3,12,64]{0,3,1,2:T(8,128)(2,1)S(1)}, u32[]{:S(2)}, u32[]{:S(2)}) async-start(bf16[256,3,12,64]{0,3,1,2:T(8,128)(2,1)} %copy.321), calls=%async_computation.6 | async-start | bytes 2359296 | tf_op jit(solution)/shard_map/all_to_all | solution.py:244
  186.2 10.6 %copy-start.8 = (bf16[256,3,12,64]{0,3,1,2:T(8,128)(2,1)S(1)}, bf16[256,3,12,64]{0,3,1,2:T(8,128)(2,1)}, u32[]{:S(2)}) copy-start(bf16[256,3,12,64]{0,3,1,2:T(8,128)(2,1)} %copy-done.7) | copy-start | bytes 3538948
  191.4 23.6 %all-to-all-start.1 = ((bf16[4,2,24576]{2,1,0:T(2,128)(2,1)}), bf16[4,2,24576]{2,1,0:T(2,128)(2,1)S(1)}, u32[]{:S(2)}, u32[]{:S(2)}) async-start(bf16[4,2,24576]{2,1,0:T(2,128)(2,1)} %reshape.457), calls=%async_computation.1 | async-start | bytes 786432 | tf_op jit(solution)/shard_map/all_to_all | solution.py:250
  209.8 12.6 %copy-start = (bf16[4,256,768]{2,1,0:T(8,128)(2,1)S(1)}, bf16[4,256,768]{2,1,0:T(8,128)(2,1)}, u32[]{:S(2)}) copy-start(bf16[4,256,768]{2,1,0:T(8,128)(2,1)} %param.19) | copy-start | bytes 4718596
  215.0 12.0 %copy-start.17 = (bf16[4,2,24576]{2,1,0:T(2,128)(2,1)}, bf16[4,2,24576]{2,1,0:T(2,128)(2,1)S(1)}, u32[]{:S(2)}) copy-start(bf16[4,2,24576]{2,1,0:T(2,128)(2,1)S(1)} %all-to-all-done.1) | copy-start | bytes 1179652
  215.0 29.8 %all-to-all-start.3 = ((bf16[4,2,24576]{2,1,0:T(2,128)(2,1)}), bf16[4,2,24576]{2,1,0:T(2,128)(2,1)}, u32[]{:S(2)}, u32[]{:S(2)}) async-start(bf16[4,2,24576]{2,1,0:T(2,128)(2,1)} %reshape.455), calls=%async_computation.3 | async-start | bytes 786432 | tf_op jit(solution)/shard_map/all_to_all | solution.py:250
  244.8 21.8 %all-to-all-start.5 = ((bf16[4,2,24576]{2,1,0:T(2,128)(2,1)}), bf16[4,2,24576]{2,1,0:T(2,128)(2,1)}, u32[]{:S(2)}, u32[]{:S(2)}) async-start(bf16[4,2,24576]{2,1,0:T(2,128)(2,1)} %reshape.453), calls=%async_computation.5 | async-start | bytes 786432 | tf_op jit(solution)/shard_map/all_to_all | solution.py:250
  265.2 7.1 copy-start.18
  266.6 11.7 %all-to-all-start.7 = ((bf16[4,2,24576]{2,1,0:T(2,128)(2,1)}), bf16[4,2,24576]{2,1,0:T(2,128)(2,1)}, u32[]{:S(2)}, u32[]{:S(2)}) async-start(bf16[4,2,24576]{2,1,0:T(2,128)(2,1)} %reshape.451), calls=%async_computation.7 | async-start | bytes 786432 | tf_op jit(solution)/shard_map/all_to_all | solution.py:250
  282.4 1.6 copy-start.25
  284.0 4.0 copy-start.13
  288.0 1.7 copy-start.2
  295.1 8.5 copy-start.20
  295.1 8.5 copy-start.23
  303.6 12.7 %copy-start.3 = (f32[1024,768]{1,0:T(8,128)S(1)}, f32[1024,768]{1,0:T(8,128)}, u32[]{:S(2)}) copy-start(f32[1024,768]{1,0:T(8,128)} %copy-done.2) | copy-start | bytes 9437188
  303.6 12.7 %copy-start.5 = (bf16[3072,768]{1,0:T(8,128)(2,1)S(1)}, bf16[3072,768]{1,0:T(8,128)(2,1)}, u32[]{:S(2)}) copy-start(bf16[3072,768]{1,0:T(8,128)(2,1)} %reshape.410) | copy-start | bytes 14155780
  303.6 12.7 %copy-start.24 = (f32[768]{0:T(1024)S(1)}, f32[768]{0:T(1024)}, u32[]{:S(2)}) copy-start(f32[768]{0:T(1024)} %get-tuple-element.45) | copy-start | bytes 9220
  327.4 1.7 copy-start.11
  336.2 8.6 %copy-start.12 = (f32[1024,768]{1,0:T(8,128)S(1)}, f32[1024,768]{1,0:T(8,128)}, u32[]{:S(2)}) copy-start(f32[1024,768]{1,0:T(8,128)} %copy-done.11) | copy-start | bytes 9437188
  344.8 12.2 %copy-start.4 = (f32[1024,768]{1,0:T(8,128)S(1)}, f32[1024,768]{1,0:T(8,128)}, u32[]{:S(2)}) copy-start(f32[1024,768]{1,0:T(8,128)} %copy-done.2) | copy-start | bytes 9437188
  373.3 2.3 copy-start.14
  375.6 4.4 copy-start.22
  375.6 5.3 copy-start.21
  375.6 6.1 copy-start.19
  402.3 10.8 %all-to-all-start.8 = ((bf16[256,12,64]{0,2,1:T(8,128)(2,1)}), bf16[256,12,64]{0,2,1:T(8,128)(2,1)S(1)}, u32[]{:S(2)}, u32[]{:S(2)}) async-start(bf16[256,12,64]{0,2,1:T(8,128)(2,1)} %bitcast.59), calls=%async_computation.8 | async-start | bytes 786432 | tf_op jit(solution)/shard_map/all_to_all | solution.py:308
  413.1 10.5 %all-to-all-start.10 = ((bf16[256,12,64]{0,2,1:T(8,128)(2,1)}), bf16[256,12,64]{0,2,1:T(8,128)(2,1)S(1)}, u32[]{:S(2)}, u32[]{:S(2)}) async-start(bf16[256,12,64]{0,2,1:T(8,128)(2,1)} %bitcast.67), calls=%async_computation.10 | async-start | bytes 786432 | tf_op jit(solution)/shard_map/all_to_all | solution.py:308
  423.6 0.8 copy-start.16
  424.4 10.5 %all-to-all-start.12 = ((bf16[256,12,64]{0,2,1:T(8,128)(2,1)}), bf16[256,12,64]{0,2,1:T(8,128)(2,1)S(1)}, u32[]{:S(2)}, u32[]{:S(2)}) async-start(bf16[256,12,64]{0,2,1:T(8,128)(2,1)} %bitcast.75), calls=%async_computation.12 | async-start | bytes 786432 | tf_op jit(solution)/shard_map/all_to_all | solution.py:308
  434.9 20.1 %copy-start.15 = (bf16[256,12,64]{0,2,1:T(8,128)(2,1)}, bf16[256,12,64]{0,2,1:T(8,128)(2,1)S(1)}, u32[]{:S(2)}) copy-start(bf16[256,12,64]{0,2,1:T(8,128)(2,1)S(1)} %all-to-all-done.12) | copy-start | bytes 1179652
  434.9 30.2 %all-to-all-start.14 = ((bf16[256,12,64]{0,2,1:T(8,128)(2,1)}), bf16[256,12,64]{0,2,1:T(8,128)(2,1)S(1)}, u32[]{:S(2)}, u32[]{:S(2)}) async-start(bf16[256,12,64]{0,2,1:T(8,128)(2,1)} %bitcast.83), calls=%async_computation.14 | async-start | bytes 786432 | tf_op jit(solution)/shard_map/all_to_all | solution.py:308
  465.1 31.8 %all-to-all-start.9 = ((bf16[4,2,73728]{2,1,0:T(2,128)(2,1)}), bf16[4,2,73728]{2,1,0:T(2,128)(2,1)}, u32[]{:S(2)}, u32[]{:S(2)}) async-start(bf16[4,2,73728]{2,1,0:T(2,128)(2,1)} %reshape.465), calls=%async_computation.9 | async-start | bytes 2359296 | tf_op jit(solution)/shard_map/all_to_all | solution.py:320
  496.9 31.6 %all-to-all-start.11 = ((bf16[4,2,73728]{2,1,0:T(2,128)(2,1)}), bf16[4,2,73728]{2,1,0:T(2,128)(2,1)}, u32[]{:S(2)}, u32[]{:S(2)}) async-start(bf16[4,2,73728]{2,1,0:T(2,128)(2,1)} %reshape.463), calls=%async_computation.11 | async-start | bytes 2359296 | tf_op jit(solution)/shard_map/all_to_all | solution.py:320
  528.5 30.8 %all-to-all-start.13 = ((bf16[4,2,73728]{2,1,0:T(2,128)(2,1)}), bf16[4,2,73728]{2,1,0:T(2,128)(2,1)}, u32[]{:S(2)}, u32[]{:S(2)}) async-start(bf16[4,2,73728]{2,1,0:T(2,128)(2,1)} %reshape.461), calls=%async_computation.13 | async-start | bytes 2359296 | tf_op jit(solution)/shard_map/all_to_all | solution.py:320
  559.3 25.3 %all-to-all-start.15 = ((bf16[4,2,73728]{2,1,0:T(2,128)(2,1)}), bf16[4,2,73728]{2,1,0:T(2,128)(2,1)}, u32[]{:S(2)}, u32[]{:S(2)}) async-start(bf16[4,2,73728]{2,1,0:T(2,128)(2,1)} %reshape.459), calls=%async_computation.15 | async-start | bytes 2359296 | tf_op jit(solution)/shard_map/all_to_all | solution.py:320
  563.5 106.6 %reduce-scatter.10.cloned.1.call-start = ((), (), s32[]{:S(2)}) async-start(), calls=%async_computation.22 | async-start | bytes 4423680
  598.7 1.5 copy-start.28
  600.3 4.4 copy-start.1
  621.3 74.7 %reduce-scatter.12.cloned.1.call-start = ((), (), s32[]{:S(2)}) async-start(), calls=%async_computation.23 | async-start | bytes 614400
  672.4 1.9 copy-start.10
  672.4 173.4 %reduce-scatter.8.cloned.1.call-start = ((), (), s32[]{:S(2)}) async-start(), calls=%async_computation.21 | async-start | bytes 11354112 | tf_op jit(solution)/shard_map/reduce_scatter | solution.py:301
Sparse Core Ops, SparseCore 0:
  17.8 63.4 all-gather.2
  84.3 119.2 all-gather.4
  621.4 48.6 reduce-scatter.9
  672.8 23.1 reduce-scatter.11
  701.8 143.9 reduce-scatter.7

commit v9 on v8

--- a/solution.py
+++ b/solution.py
@@ -300,11 +300,11 @@
     early, back_attn = lax.optimization_barrier((early, back_attn))
     early_sum = lax.psum_scatter(early, axes, scatter_dimension=0, tiled=True).astype(jnp.float32)
 
-    back_parts = []
+    input_parts = [None] * streams
+    weight_acc, bias_acc = [None, None], [None, None]
     for s in range(streams):
-        back_context = times_transpose(
-            back_attn[s * part_len : (s + 1) * part_len], full_out
-        ).astype(jnp.bfloat16)
+        block = slice(s * part_len, (s + 1) * part_len)
+        back_context = times_transpose(back_attn[block], full_out).astype(jnp.bfloat16)
         one_back = lax.all_to_all(
             back_context.reshape(part_len, heads, DH),
             "seq",
@@ -312,22 +312,32 @@
             concat_axis=0,
             tiled=True,
         )
+        if s >= 2:
+            one_back, input_parts[s - 2], weight_acc[s % 2], bias_acc[s % 2] = (
+                lax.optimization_barrier(
+                    (one_back, input_parts[s - 2], weight_acc[s % 2], bias_acc[s % 2])
+                )
+            )
         local_heads = one_back.shape[1]
         one_grads = attention_backward(
             head_qkv[s].reshape(LEN, -1), segment[s], logsum[s], one_back.reshape(LEN, -1)
         )
-        back_parts.append(
-            lax.all_to_all(
-                one_grads.reshape(LEN, 3, local_heads, DH), "seq", split_axis=0, concat_axis=2, tiled=True
-            )
-        )
-    rows_back = jnp.stack(back_parts).reshape(row_count, 3 * width)
-    grad_qkv_weight = contract_rows(flat, rows_back)
-    grad_query_bias = jnp.sum(rows_back[:, :width].astype(jnp.float32), axis=0)
-    grad_value_bias = jnp.sum(rows_back[:, 2 * width :].astype(jnp.float32), axis=0)
-    input_grad = (back_first + times_transpose(rows_back, full_qkv)).reshape(
-        streams, part_len, width
-    )
+        rows = lax.all_to_all(
+            one_grads.reshape(LEN, 3, local_heads, DH), "seq", split_axis=0, concat_axis=2, tiled=True
+        ).reshape(part_len, 3 * width)
+        weight_part = contract_rows(flat[block], rows)
+        bias_part = jnp.sum(rows.astype(jnp.float32), axis=0)
+        if s < 2:
+            weight_acc[s], bias_acc[s] = weight_part, bias_part
+        else:
+            weight_acc[s % 2] = weight_acc[s % 2] + weight_part
+            bias_acc[s % 2] = bias_acc[s % 2] + bias_part
+        input_parts[s] = back_first[block] + times_transpose(rows, full_qkv)
+    grad_qkv_weight = weight_acc[0] + weight_acc[1] if streams > 1 else weight_acc[0]
+    grad_qkv_bias = bias_acc[0] + bias_acc[1] if streams > 1 else bias_acc[0]
+    grad_query_bias = grad_qkv_bias[:width]
+    grad_value_bias = grad_qkv_bias[2 * width :]
+    input_grad = jnp.stack(input_parts).reshape(streams, part_len, width)
     late = pack_lanes([grad_qkv_weight, grad_query_bias[:, None], grad_value_bias[:, None]])
     late_sum = scatter_two_stage(late).astype(jnp.float32)
 

time: 870 us -> 918 us (1.055)
  matrix products: 92.7 us -> 116 us
  local copies, waits for them, and re-layouts: 221 us -> 235 us
    dot_general x4 -> x7, matrix products: 20.7 us -> 41.7 us  [contract_rows(): lax.dot_general(left, right, (((0,), (0,)), ((), ())), preferred_element_...]
    all_to_all x4 -> x8, local copies, waits for them, and re-layouts: 14.1 us -> 31.2 us  [per_device(): lax.all_to_all(one_grads.reshape(LEN, 3, local_heads, DH), 'seq', split_a...]
    dot_general x7 -> x10, matrix products: 36.6 us -> 39.9 us  [times_transpose(): lax.dot_general(left, right, (((1,), (1,)), ((), ())), preferred_element_...]
    unnamed x90 -> x105, local copies, waits for them, and re-layouts: 63.4 us -> 63.2 us
  transfers between devices with their start and end apart: 21 -> 21, of which waited for: 10 -> 11; matrix products, arithmetic and copies ran while one was open for 20% -> 22% of each run, Pallas kernels for 12% -> 11%
where the time goes in v9:
time: 918 us; the launch traced here: 907 us
  waiting for transfers between devices  334 us (36%)
  local copies, waits for them, and re-layouts  235 us (26%)
  matrix products  116 us (13%)
  Pallas kernels  101 us (11%)
  starting transfers between devices  65.4 us (7%)
  other arithmetic  40 us (4%)
  between operations  15.1 us (2%)
    reduce_scatter x1, waiting for transfers between devices, per_device(): lax.psum_scatter(early, axes, scatter_dimension=0, tiled=True)  147 us
    unnamed x105, local copies, waits for them, and re-layouts  63.2 us
    unnamed x7, waiting for transfers between devices  62.8 us
    all_gather x1, waiting for transfers between devices, per_device(): full_first = lax.all_gather(first, axes, axis=0, tiled=True)  59.8 us
    pallas_call x4, Pallas kernels, attention_backward(): pl.pallas_call(attention_backward_kernel, out_shape=jax.ShapeDtypeStruct(...  59.6 us
    all_to_all x4, waiting for transfers between devices, per_device(): lax.all_to_all(qkv.reshape(part_len, 3, heads, DH), 'seq', split_axis=2,...  49.2 us
    dot_general x7, matrix products, contract_rows(): lax.dot_general(left, right, (((0,), (0,)), ((), ())), preferred_element_...  41.7 us
    pallas_call x4, Pallas kernels, attention_forward(): pl.pallas_call(attention_forward_kernel, out_shape=(jax.ShapeDtypeStruct(...  41.4 us
  transfers between devices with their start and end apart: 21, of which 11 were waited for; matrix products, arithmetic and copies ran while one was open for 22% of the time, Pallas kernels for 11%

profile of v9, /device:TPU:0, one launch (start us, length us, event | category | flops | bytes accessed | tf_op | source)
XLA Modules:
  0.0 906.6 jit_solution(13788772246714515111)
XLA Ops:
  21.5 59.8 %all-gather.3.cloned.1.call-done = bf16[768,2316]{1,0:T(8,128)(2,1)} async-done(((bf16[24,2316]{1,0:T(8,128)(2,1)}), bf16[768,2316]{1,0:T(8,128)(2,1)}) %all-gather.3.cloned.1.call-update) | async-done | bytes 3557392 | tf_op jit(solution)/shard_map/all_gather | solution.py:219
  89.1 3.5 all-to-all-start
  97.1 12.2 %all-to-all-done = bf16[256,3,12,64]{0,3,1,2:T(8,128)(2,1)S(1)} async-done(((bf16[256,3,12,64]{0,3,1,2:T(8,128)(2,1)}), bf16[256,3,12,64]{0,3,1,2:T(8,128)(2,1)S(1)}, u32[]{:S(2)}, u32[]{:S(2)}) %all-to-all-start) | async-done | bytes 1179680 | tf_op jit(solution)/shard_map/all_to_all | solution.py:244
  110.3 3.5 all-to-all-start.2
  118.2 20.5 %all-to-all-done.2 = bf16[256,3,12,64]{0,3,1,2:T(8,128)(2,1)S(1)} async-done(((bf16[256,3,12,64]{0,3,1,2:T(8,128)(2,1)}), bf16[256,3,12,64]{0,3,1,2:T(8,128)(2,1)S(1)}, u32[]{:S(2)}, u32[]{:S(2)}) %all-to-all-start.2) | async-done | bytes 1179680 | tf_op jit(solution)/shard_map/all_to_all | solution.py:244
  139.8 3.5 all-to-all-start.4
  147.7 16.6 %all-to-all-done.4 = bf16[256,3,12,64]{0,3,1,2:T(8,128)(2,1)S(1)} async-done(((bf16[256,3,12,64]{0,3,1,2:T(8,128)(2,1)}), bf16[256,3,12,64]{0,3,1,2:T(8,128)(2,1)S(1)}, u32[]{:S(2)}, u32[]{:S(2)}) %all-to-all-start.4) | async-done | bytes 1179680 | tf_op jit(solution)/shard_map/all_to_all | solution.py:244
  164.3 3.7 all-to-all-start.6
  175.8 10.4 %shard_map.305 = (bf16[1024,192]{1,0:T(8,128)(2,1)}, f32[1024,3]{1,0:T(8,128)}) custom-call(bf16[1024,576]{1,0:T(8,128)(2,1)} %copy.476.qkv_ref, s32[1024,1]{1,0:T(8,128)} %copy.477.seg_col_ref, s32[1,1024]{1,0:T(1,128)} %get-tuple-element.93.seg_row_ref), custom_call_target="tpu_custom_call" | custom-call | flops 805306368 | bytes 1769472 | tf_op jit(solution)/shard_map/pallas_call | solution.py:135
  191.4 4.4 all-to-all-start.1
  199.4 10.3 %shard_map.306 = (bf16[1024,192]{1,0:T(8,128)(2,1)}, f32[1024,3]{1,0:T(8,128)}) custom-call(bf16[1024,576]{1,0:T(8,128)(2,1)} %copy.485.qkv_ref, s32[1024,1]{1,0:T(8,128)} %copy.486.seg_col_ref, s32[1,1024]{1,0:T(1,128)} %get-tuple-element.100.seg_row_ref), custom_call_target="tpu_custom_call" | custom-call | flops 805306368 | bytes 1769472 | tf_op jit(solution)/shard_map/pallas_call | solution.py:135
  215.0 4.6 all-to-all-start.3
  229.4 10.3 %shard_map.307 = (bf16[1024,192]{1,0:T(8,128)(2,1)}, f32[1024,3]{1,0:T(8,128)}) custom-call(bf16[1024,576]{1,0:T(8,128)(2,1)} %copy.494.qkv_ref, s32[1024,1]{1,0:T(8,128)} %copy.495.seg_col_ref, s32[1,1024]{1,0:T(1,128)} %get-tuple-element.99.seg_row_ref), custom_call_target="tpu_custom_call" | custom-call | flops 805306368 | bytes 1769472 | tf_op jit(solution)/shard_map/pallas_call | solution.py:135
  244.8 4.4 all-to-all-start.5
  252.9 10.3 %shard_map.308 = (bf16[1024,192]{1,0:T(8,128)(2,1)}, f32[1024,3]{1,0:T(8,128)}) custom-call(bf16[1024,576]{1,0:T(8,128)(2,1)} %copy.503.qkv_ref, s32[1024,1]{1,0:T(8,128)} %copy.504.seg_col_ref, s32[1,1024]{1,0:T(1,128)} %get-tuple-element.98.seg_row_ref), custom_call_target="tpu_custom_call" | custom-call | flops 805306368 | bytes 1769472 | tf_op jit(solution)/shard_map/pallas_call | solution.py:135
  266.6 4.4 all-to-all-start.7
  290.7 4.9 slice.195
  295.6 8.5 reshape.401
  304.1 12.7 %multiply_convert_fusion = (bf16[1024,3072]{1,0:T(8,128)(2,1)S(1)}, f32[1024,3072]{1,0:T(8,128)}) fusion(f32[3072]{0:T(1024)S(1)} %copy-done.31, bf16[768,6912]{1,0:T(8,128)(2,1)} %all-gather.5.cloned.1.call-done, f32[1024,768]{1,0:T(8,128)} %copy-done.2, f32[768]{0:T(1024)S(1)} %copy-done.34, f32[768]{0:T(1024)S(1)} %get-tuple-element.61, ...), kind=kOutput, calls=%fused_computation.7 | convolution fusion | flops 4854644736 | bytes 26765312 | tf_op jit(solution)/shard_map/dot_general | solution.py:262
  316.9 5.4 fusion.74
  329.6 7.0 convolution_convert_fusion
  336.7 8.6 convert_element_type.328
  345.3 12.2 %fusion.75 = (bf16[3072]{0:T(1024)(128)(2,1)S(1)}, bf16[1024,3072]{1,0:T(8,128)(2,1)S(1)}) fusion(f32[1024,3072]{1,0:T(8,128)} %get-tuple-element.106, f32[3072]{0:T(1024)S(1)} %copy-done.31, bf16[3072,768]{1,0:T(8,128)(2,1)} %reshape.401, f32[1024,768]{1,0:T(8,128)S(1)} %copy-done.15), kind=kOutput, calls=%fused_computation.171 | convolution fusion | flops 4870370304 | bytes 26757120 | tf_op jit(solution)/shard_map/dot_general | solution.py:27
  357.5 8.0 convolution_convert_fusion.1
  365.5 8.3 multiply_reduce_fusion
  382.3 17.8 %concatenate.20 = bf16[768,7168]{1,0:T(8,128)(2,1)} concatenate(bf16[768,768]{1,0:T(8,128)(2,1)S(1)} %convolution_convert_fusion.2, bf16[768,3072]{1,0:T(8,128)(2,1)} %convolution_convert_fusion.1, bf16[768,3072]{1,0:T(8,128)(2,1)} %convert_element_type.328, bf16[768,1]{1,0:T(8,128)(2,1)S(1)} %convert_element_type.363, bf16[768,1]{1,0:T(8,128)(2,1)} %convert_element_type.364, ...), dimensions={1} | concatenate | bytes 22020096 | tf_op jit(solution)/shard_map/concatenate | solution.py:74
  402.8 4.2 all-to-all-start.9
  409.7 3.9 all-to-all-done.9
  419.8 5.1 all-to-all-done.8
  431.1 5.1 all-to-all-done.12
  436.1 4.5 all-to-all-start.11
  442.0 14.8 %shard_map.309 = bf16[1024,576]{1,0:T(8,128)(2,1)} custom-call(bf16[1024,576]{1,0:T(8,128)(2,1)} %copy.476.qkv_ref, s32[1024,1]{1,0:T(8,128)} %copy.477.seg_col_ref, s32[1,1024]{1,0:T(1,128)} %get-tuple-element.93.seg_row_ref, f32[1024,3]{1,0:T(8,128)} %get-tuple-element.40.lse_ref, bf16[1024,192]{1,0:T(8,128)(2,1)} %copy.523.up_ref), custom_call_target="tpu_custom_call" | custom-call | flops 2013265920 | bytes 2949120 | tf_op jit(solution)/shard_map/pallas_call | solution.py:153
  459.3 4.6 copy.525
  467.0 4.4 all-to-all-start.10
  473.6 15.1 %shard_map.310 = bf16[1024,576]{1,0:T(8,128)(2,1)} custom-call(bf16[1024,576]{1,0:T(8,128)(2,1)} %copy.485.qkv_ref, s32[1024,1]{1,0:T(8,128)} %copy.486.seg_col_ref, s32[1,1024]{1,0:T(1,128)} %get-tuple-element.100.seg_row_ref, f32[1024,3]{1,0:T(8,128)} %get-tuple-element.42.lse_ref, bf16[1024,192]{1,0:T(8,128)(2,1)} %copy.536.up_ref), custom_call_target="tpu_custom_call" | custom-call | flops 2013265920 | bytes 2949120 | tf_op jit(solution)/shard_map/pallas_call | solution.py:153
  491.1 4.6 copy.538
  499.8 4.3 all-to-all-start.13
  507.6 3.5 copy.527
  511.1 3.8 copy.581
  517.2 5.5 convolution_bitcast_fusion.1
  526.9 14.8 %shard_map.311 = bf16[1024,576]{1,0:T(8,128)(2,1)} custom-call(bf16[1024,576]{1,0:T(8,128)(2,1)} %copy.494.qkv_ref, s32[1024,1]{1,0:T(8,128)} %copy.495.seg_col_ref, s32[1,1024]{1,0:T(1,128)} %get-tuple-element.99.seg_row_ref, f32[1024,3]{1,0:T(8,128)} %get-tuple-element.44.lse_ref, bf16[1024,192]{1,0:T(8,128)(2,1)} %copy.545.up_ref), custom_call_target="tpu_custom_call" | custom-call | flops 2013265920 | bytes 2949120 | tf_op jit(solution)/shard_map/pallas_call | solution.py:153
  544.2 4.6 copy.547
  551.9 4.3 all-to-all-start.14
  556.2 3.5 reshape.454
  559.6 3.5 copy.540
  563.1 3.9 copy.583
  569.8 5.5 convolution_bitcast_fusion
  579.5 14.9 %shard_map.312 = bf16[1024,576]{1,0:T(8,128)(2,1)} custom-call(bf16[1024,576]{1,0:T(8,128)(2,1)} %copy.503.qkv_ref, s32[1024,1]{1,0:T(8,128)} %copy.504.seg_col_ref, s32[1,1024]{1,0:T(1,128)} %get-tuple-element.98.seg_row_ref, f32[1024,3]{1,0:T(8,128)} %get-tuple-element.46.lse_ref, bf16[1024,192]{1,0:T(8,128)(2,1)} %copy.552.up_ref), custom_call_target="tpu_custom_call" | custom-call | flops 2013265920 | bytes 2949120 | tf_op jit(solution)/shard_map/pallas_call | solution.py:153
  596.8 4.6 copy.554
  604.5 4.3 all-to-all-start.15
  608.8 3.5 reshape.460
  612.3 3.9 copy.585
  619.0 4.7 reshape.456
  623.7 5.6 copy.587
  633.3 3.5 copy.549
  636.8 5.6 fusion.44
  642.3 3.5 copy.556
  645.8 8.8 fusion.7
  655.4 5.8 concatenate.21
  661.2 5.1 copy.589
  669.2 48.2 %reduce-scatter.10.cloned.1.call-done = bf16[24,10240]{1,0:T(8,128)(2,1)} async-done(((bf16[192,10240]{1,0:T(8,128)(2,1)}), bf16[24,10240]{1,0:T(8,128)(2,1)}) %reduce-scatter.10.cloned.1.call-update) | async-done | bytes 491536
  721.0 3.5 fusion.28
  729.1 14.3 %reduce-scatter.12.cloned.1.call-done = bf16[24,2560]{1,0:T(8,128)(2,1)} async-done(((bf16[96,2560]{1,0:T(8,128)(2,1)}), bf16[24,2560]{1,0:T(8,128)(2,1)}) %reduce-scatter.12.cloned.1.call-update) | async-done | bytes 122896
  745.7 147.4 %reduce-scatter.8.cloned.1.call-done = bf16[24,7168]{1,0:T(8,128)(2,1)} async-done(((bf16[768,7168]{1,0:T(8,128)(2,1)}), bf16[24,7168]{1,0:T(8,128)(2,1)}) %reduce-scatter.8.cloned.1.call-update) | async-done | bytes 344080 | tf_op jit(solution)/shard_map/reduce_scatter | solution.py:301
  (272 shorter events, 205.2 us)
Async XLA Ops:
  7.2 77.5 %copy-start.16 = (bf16[4,256,768]{2,1,0:T(8,128)(2,1)S(1)}, bf16[4,256,768]{2,1,0:T(8,128)(2,1)}, u32[]{:S(2)}) copy-start(bf16[4,256,768]{2,1,0:T(8,128)(2,1)} %param.18) | copy-start | bytes 4718596
  7.2 74.1 %all-gather.3.cloned.1.call-start = ((), (), s32[]{:S(2)}) async-start(), calls=%async_computation.19 | async-start | bytes 3852288 | tf_op jit(solution)/shard_map/all_gather | solution.py:219
  17.6 267.4 %all-gather.5.cloned.1.call-start = ((), (), s32[]{:S(2)}) async-start(), calls=%async_computation.20 | async-start | bytes 10948608 | tf_op jit(solution)/shard_map/all_gather | solution.py:220
  89.1 20.2 %all-to-all-start = ((bf16[256,3,12,64]{0,3,1,2:T(8,128)(2,1)}), bf16[256,3,12,64]{0,3,1,2:T(8,128)(2,1)S(1)}, u32[]{:S(2)}, u32[]{:S(2)}) async-start(bf16[256,3,12,64]{0,3,1,2:T(8,128)(2,1)} %copy.472), calls=%async_computation | async-start | bytes 2359296 | tf_op jit(solution)/shard_map/all_to_all | solution.py:244
  109.3 1.0 copy-start.13
  110.3 28.4 %all-to-all-start.2 = ((bf16[256,3,12,64]{0,3,1,2:T(8,128)(2,1)}), bf16[256,3,12,64]{0,3,1,2:T(8,128)(2,1)S(1)}, u32[]{:S(2)}, u32[]{:S(2)}) async-start(bf16[256,3,12,64]{0,3,1,2:T(8,128)(2,1)} %copy.482), calls=%async_computation.2 | async-start | bytes 2359296 | tf_op jit(solution)/shard_map/all_to_all | solution.py:244
  138.7 1.1 copy-start.11
  139.8 24.5 %all-to-all-start.4 = ((bf16[256,3,12,64]{0,3,1,2:T(8,128)(2,1)}), bf16[256,3,12,64]{0,3,1,2:T(8,128)(2,1)S(1)}, u32[]{:S(2)}, u32[]{:S(2)}) async-start(bf16[256,3,12,64]{0,3,1,2:T(8,128)(2,1)} %copy.491), calls=%async_computation.4 | async-start | bytes 2359296 | tf_op jit(solution)/shard_map/all_to_all | solution.py:244
  146.6 21.4 %copy-start.37 = (s32[4,17]{1,0:T(4,128)S(1)}, s32[4,17]{1,0:T(4,128)}, u32[]{:S(2)}) copy-start(s32[4,17]{1,0:T(4,128)} %param.20) | copy-start | bytes 820
  164.3 9.1 %copy-start.10 = (bf16[256,3,12,64]{0,3,1,2:T(8,128)(2,1)}, bf16[256,3,12,64]{0,3,1,2:T(8,128)(2,1)S(1)}, u32[]{:S(2)}) copy-start(bf16[256,3,12,64]{0,3,1,2:T(8,128)(2,1)S(1)} %all-to-all-done.4) | copy-start | bytes 3538948
  164.3 27.1 %all-to-all-start.6 = ((bf16[256,3,12,64]{0,3,1,2:T(8,128)(2,1)}), bf16[256,3,12,64]{0,3,1,2:T(8,128)(2,1)S(1)}, u32[]{:S(2)}, u32[]{:S(2)}) async-start(bf16[256,3,12,64]{0,3,1,2:T(8,128)(2,1)} %copy.500), calls=%async_computation.6 | async-start | bytes 2359296 | tf_op jit(solution)/shard_map/all_to_all | solution.py:244
  186.2 10.6 %copy-start.12 = (bf16[256,3,12,64]{0,3,1,2:T(8,128)(2,1)S(1)}, bf16[256,3,12,64]{0,3,1,2:T(8,128)(2,1)}, u32[]{:S(2)}) copy-start(bf16[256,3,12,64]{0,3,1,2:T(8,128)(2,1)} %copy-done.11) | copy-start | bytes 3538948
  191.4 23.5 %all-to-all-start.1 = ((bf16[4,2,24576]{2,1,0:T(2,128)(2,1)}), bf16[4,2,24576]{2,1,0:T(2,128)(2,1)S(1)}, u32[]{:S(2)}, u32[]{:S(2)}) async-start(bf16[4,2,24576]{2,1,0:T(2,128)(2,1)} %reshape.451), calls=%async_computation.1 | async-start | bytes 786432 | tf_op jit(solution)/shard_map/all_to_all | solution.py:250
  209.8 12.6 %copy-start.1 = (bf16[4,256,768]{2,1,0:T(8,128)(2,1)S(1)}, bf16[4,256,768]{2,1,0:T(8,128)(2,1)}, u32[]{:S(2)}) copy-start(bf16[4,256,768]{2,1,0:T(8,128)(2,1)} %param.19) | copy-start | bytes 4718596
  215.0 12.0 %copy-start.22 = (bf16[4,2,24576]{2,1,0:T(2,128)(2,1)}, bf16[4,2,24576]{2,1,0:T(2,128)(2,1)S(1)}, u32[]{:S(2)}) copy-start(bf16[4,2,24576]{2,1,0:T(2,128)(2,1)S(1)} %all-to-all-done.1) | copy-start | bytes 1179652
  215.0 29.8 %all-to-all-start.3 = ((bf16[4,2,24576]{2,1,0:T(2,128)(2,1)}), bf16[4,2,24576]{2,1,0:T(2,128)(2,1)}, u32[]{:S(2)}, u32[]{:S(2)}) async-start(bf16[4,2,24576]{2,1,0:T(2,128)(2,1)} %reshape.449), calls=%async_computation.3 | async-start | bytes 786432 | tf_op jit(solution)/shard_map/all_to_all | solution.py:250
  244.8 21.8 %all-to-all-start.5 = ((bf16[4,2,24576]{2,1,0:T(2,128)(2,1)}), bf16[4,2,24576]{2,1,0:T(2,128)(2,1)}, u32[]{:S(2)}, u32[]{:S(2)}) async-start(bf16[4,2,24576]{2,1,0:T(2,128)(2,1)} %reshape.447), calls=%async_computation.5 | async-start | bytes 786432 | tf_op jit(solution)/shard_map/all_to_all | solution.py:250
  265.2 7.1 copy-start.23
  266.6 11.7 %all-to-all-start.7 = ((bf16[4,2,24576]{2,1,0:T(2,128)(2,1)}), bf16[4,2,24576]{2,1,0:T(2,128)(2,1)}, u32[]{:S(2)}, u32[]{:S(2)}) async-start(bf16[4,2,24576]{2,1,0:T(2,128)(2,1)} %reshape.445), calls=%async_computation.7 | async-start | bytes 786432 | tf_op jit(solution)/shard_map/all_to_all | solution.py:250
  282.4 2.7 copy-start.17
  282.4 2.7 copy-start.36
  288.5 1.7 copy-start.2
  295.6 8.5 copy-start.31
  295.6 8.5 copy-start.34
  304.1 12.7 %copy-start.3 = (f32[1024,768]{1,0:T(8,128)S(1)}, f32[1024,768]{1,0:T(8,128)}, u32[]{:S(2)}) copy-start(f32[1024,768]{1,0:T(8,128)} %copy-done.2) | copy-start | bytes 9437188
  304.1 12.7 %copy-start.9 = (bf16[3072,768]{1,0:T(8,128)(2,1)S(1)}, bf16[3072,768]{1,0:T(8,128)(2,1)}, u32[]{:S(2)}) copy-start(bf16[3072,768]{1,0:T(8,128)(2,1)} %reshape.401) | copy-start | bytes 14155780
  304.1 12.7 %copy-start.35 = (f32[768]{0:T(1024)S(1)}, f32[768]{0:T(1024)}, u32[]{:S(2)}) copy-start(f32[768]{0:T(1024)} %get-tuple-element.59) | copy-start | bytes 9220
  327.9 1.7 copy-start.14
  336.7 8.6 copy-start.15
  345.3 12.2 %copy-start.4 = (f32[1024,768]{1,0:T(8,128)S(1)}, f32[1024,768]{1,0:T(8,128)}, u32[]{:S(2)}) copy-start(f32[1024,768]{1,0:T(8,128)} %copy-done.2) | copy-start | bytes 9437188
  373.8 2.3 copy-start.18
  376.1 4.4 copy-start.33
  376.1 5.3 copy-start.32
  376.1 6.1 copy-start.27
  402.8 10.8 %all-to-all-start.9 = ((bf16[256,12,64]{0,2,1:T(8,128)(2,1)}), bf16[256,12,64]{0,2,1:T(8,128)(2,1)S(1)}, u32[]{:S(2)}, u32[]{:S(2)}) async-start(bf16[256,12,64]{0,2,1:T(8,128)(2,1)} %bitcast.62), calls=%async_computation.9 | async-start | bytes 786432 | tf_op jit(solution)/shard_map/all_to_all | solution.py:308
  413.6 11.2 %all-to-all-start.8 = ((bf16[256,12,64]{0,2,1:T(8,128)(2,1)}), bf16[256,12,64]{0,2,1:T(8,128)(2,1)S(1)}, u32[]{:S(2)}, u32[]{:S(2)}) async-start(bf16[256,12,64]{0,2,1:T(8,128)(2,1)} %bitcast.59), calls=%async_computation.8 | async-start | bytes 786432 | tf_op jit(solution)/shard_map/all_to_all | solution.py:308
  424.9 11.2 %all-to-all-start.12 = ((bf16[256,12,64]{0,2,1:T(8,128)(2,1)}), bf16[256,12,64]{0,2,1:T(8,128)(2,1)S(1)}, u32[]{:S(2)}, u32[]{:S(2)}) async-start(bf16[256,12,64]{0,2,1:T(8,128)(2,1)} %bitcast.76), calls=%async_computation.12 | async-start | bytes 786432 | tf_op jit(solution)/shard_map/all_to_all | solution.py:308
  436.1 20.7 %copy-start.19 = (bf16[256,12,64]{0,2,1:T(8,128)(2,1)}, bf16[256,12,64]{0,2,1:T(8,128)(2,1)S(1)}, u32[]{:S(2)}) copy-start(bf16[256,12,64]{0,2,1:T(8,128)(2,1)S(1)} %all-to-all-done.12) | copy-start | bytes 1179652
  436.1 30.8 %all-to-all-start.11 = ((bf16[256,12,64]{0,2,1:T(8,128)(2,1)}), bf16[256,12,64]{0,2,1:T(8,128)(2,1)}, u32[]{:S(2)}, u32[]{:S(2)}) async-start(bf16[256,12,64]{0,2,1:T(8,128)(2,1)} %bitcast.73), calls=%async_computation.11 | async-start | bytes 786432 | tf_op jit(solution)/shard_map/all_to_all | solution.py:308
  467.0 5.3 copy-start.20
  467.0 32.9 %all-to-all-start.10 = ((bf16[4,2,73728]{2,1,0:T(2,128)(2,1)}), bf16[4,2,73728]{2,1,0:T(2,128)(2,1)}, u32[]{:S(2)}, u32[]{:S(2)}) async-start(bf16[4,2,73728]{2,1,0:T(2,128)(2,1)} %reshape.457), calls=%async_computation.10 | async-start | bytes 2359296 | tf_op jit(solution)/shard_map/all_to_all | solution.py:325
  499.8 52.0 %all-to-all-start.13 = ((bf16[4,2,73728]{2,1,0:T(2,128)(2,1)}), bf16[4,2,73728]{2,1,0:T(2,128)(2,1)}, u32[]{:S(2)}, u32[]{:S(2)}) async-start(bf16[4,2,73728]{2,1,0:T(2,128)(2,1)} %reshape.453), calls=%async_computation.13 | async-start | bytes 2359296 | tf_op jit(solution)/shard_map/all_to_all | solution.py:325
  517.1 5.5 copy-start.6
  517.1 5.5 copy-start.24
  522.7 3.2 copy-start.21
  551.9 52.6 %all-to-all-start.14 = ((bf16[4,2,73728]{2,1,0:T(2,128)(2,1)}), bf16[4,2,73728]{2,1,0:T(2,128)(2,1)}, u32[]{:S(2)}, u32[]{:S(2)}) async-start(bf16[4,2,73728]{2,1,0:T(2,128)(2,1)} %reshape.459), calls=%async_computation.14 | async-start | bytes 2359296 | tf_op jit(solution)/shard_map/all_to_all | solution.py:325
  569.8 5.5 copy-start.7
  569.8 5.5 copy-start.25
  604.5 14.5 %all-to-all-start.15 = ((bf16[4,2,73728]{2,1,0:T(2,128)(2,1)}), bf16[4,2,73728]{2,1,0:T(2,128)(2,1)}, u32[]{:S(2)}, u32[]{:S(2)}) async-start(bf16[4,2,73728]{2,1,0:T(2,128)(2,1)} %reshape.455), calls=%async_computation.15 | async-start | bytes 2359296 | tf_op jit(solution)/shard_map/all_to_all | solution.py:325
  608.8 108.7 %reduce-scatter.10.cloned.1.call-start = ((), (), s32[]{:S(2)}) async-start(), calls=%async_computation.22 | async-start | bytes 4423680
  623.7 7.9 copy-start.30
  636.8 5.6 copy-start
  669.2 74.1 %reduce-scatter.12.cloned.1.call-start = ((), (), s32[]{:S(2)}) async-start(), calls=%async_computation.23 | async-start | bytes 614400
  719.7 1.3 copy-start.5
  719.7 173.4 %reduce-scatter.8.cloned.1.call-start = ((), (), s32[]{:S(2)}) async-start(), calls=%async_computation.21 | async-start | bytes 11354112 | tf_op jit(solution)/shard_map/reduce_scatter | solution.py:301
  721.0 3.5 copy-start.8
  721.0 3.7 copy-start.26
  724.7 2.4 copy-start.28
  724.7 2.4 copy-start.29
Sparse Core Ops, SparseCore 0:
  17.8 63.4 all-gather.2
  84.3 119.2 all-gather.4
  669.3 48.0 reduce-scatter.9
  720.1 23.1 reduce-scatter.11
  749.1 143.9 reduce-scatter.7

commit v10 on v8

--- a/solution.py
+++ b/solution.py
@@ -234,27 +234,53 @@
     heads = width // DH
     flat = layer_in.reshape(row_count, width)
     qkv_bias = jnp.concatenate([bias_query, jnp.zeros_like(bias_query), bias_value])
+    ways = lax.axis_size("seq")
+    me = lax.axis_index("seq")
+    group = heads // ways * DH
+
+    def rolled(columns, axis):
+        shape = columns.shape
+        split = columns.reshape(*shape[:axis], ways, group, *shape[axis + 1 :])
+        return jnp.roll(split, -me, axis=axis).reshape(shape)
+
+    def unrolled(columns, axis):
+        shape = columns.shape
+        split = columns.reshape(*shape[:axis], ways, group, *shape[axis + 1 :])
+        return jnp.roll(split, me, axis=axis).reshape(shape)
+
+    def send(blocks, sign):
+        out = [blocks[0]]
+        for k in range(1, ways):
+            pairs = [(j, (j + sign * k) % ways) for j in range(ways)]
+            out.append(lax.ppermute(blocks[k], "seq", pairs))
+        return out
+
+    roll_qkv = rolled(full_qkv.reshape(model, 3, width), 2).reshape(model, 3 * width)
+    roll_bias = rolled(qkv_bias.reshape(3, width), 1).reshape(3 * width)
+    roll_out = rolled(full_out, 0)
     segment = segment_ids(doc_starts, LEN)
-    head_qkv, context_parts, logsum = [], [], []
+    sources = [(me - k) % ways for k in range(ways)]
+    head_qkv, context_parts, logsum, head_segment = [], [], [], []
     for s in range(streams):
         qkv = (
-            jnp.dot(flat[s * part_len : (s + 1) * part_len], full_qkv, preferred_element_type=jnp.float32)
-            + qkv_bias
-        ).astype(jnp.bfloat16)
-        one_qkv = lax.all_to_all(
-            qkv.reshape(part_len, 3, heads, DH), "seq", split_axis=2, concat_axis=0, tiled=True
+            jnp.dot(flat[s * part_len : (s + 1) * part_len], roll_qkv, preferred_element_type=jnp.float32)
+            + roll_bias
+        ).astype(jnp.bfloat16).reshape(part_len, 3, ways, group)
+        one_qkv = jnp.concatenate(send([qkv[:, :, k] for k in range(ways)], 1), axis=0).reshape(LEN, -1)
+        one_segment = jnp.concatenate(
+            [lax.dynamic_slice(segment[s], (src * part_len,), (part_len,)) for src in sources]
         )
-        local_heads = one_qkv.shape[2]
-        context, one_sum = attention_forward(one_qkv.reshape(LEN, -1), segment[s])
+        context, one_sum = attention_forward(one_qkv, one_segment)
         context_parts.append(
-            lax.all_to_all(
-                context.reshape(LEN, local_heads, DH), "seq", split_axis=0, concat_axis=1, tiled=True
+            jnp.concatenate(
+                send([context[k * part_len : (k + 1) * part_len] for k in range(ways)], -1), axis=1
             )
         )
         head_qkv.append(one_qkv)
         logsum.append(one_sum)
+        head_segment.append(one_segment)
     context_rows = jnp.stack(context_parts).reshape(row_count, width)
-    attn = jnp.dot(context_rows, full_out, preferred_element_type=jnp.float32) + bias_out
+    attn = jnp.dot(context_rows, roll_out, preferred_element_type=jnp.float32) + bias_out
     mixed, normed_mixer, inverse_mixer = norm_forward(
         flat.astype(jnp.float32) + attn, gain_mixer, shift_mixer
     )
@@ -280,7 +306,7 @@
     grad_mixer_shift = jnp.sum(back_mixed, axis=0)
     back_first = norm_backward(back_mixed, gain_mixer, normed_mixer, inverse_mixer)
     back_attn = back_first.astype(jnp.bfloat16)
-    grad_out_weight = contract_rows(context_rows, back_attn)
+    grad_out_weight = unrolled(contract_rows(context_rows, back_attn), 0)
     grad_out_bias = jnp.sum(back_attn.astype(jnp.float32), axis=0)
 
     early = pack_lanes(
@@ -303,29 +329,26 @@
     back_parts = []
     for s in range(streams):
         back_context = times_transpose(
-            back_attn[s * part_len : (s + 1) * part_len], full_out
+            back_attn[s * part_len : (s + 1) * part_len], roll_out
         ).astype(jnp.bfloat16)
-        one_back = lax.all_to_all(
-            back_context.reshape(part_len, heads, DH),
-            "seq",
-            split_axis=1,
-            concat_axis=0,
-            tiled=True,
+        one_back = jnp.concatenate(
+            send([back_context[:, k * group : (k + 1) * group] for k in range(ways)], 1), axis=0
         )
-        local_heads = one_back.shape[1]
-        one_grads = attention_backward(
-            head_qkv[s].reshape(LEN, -1), segment[s], logsum[s], one_back.reshape(LEN, -1)
-        )
+        one_grads = attention_backward(head_qkv[s], head_segment[s], logsum[s], one_back)
+        returned = send([one_grads[k * part_len : (k + 1) * part_len] for k in range(ways)], -1)
         back_parts.append(
-            lax.all_to_all(
-                one_grads.reshape(LEN, 3, local_heads, DH), "seq", split_axis=0, concat_axis=2, tiled=True
+            jnp.stack([r.reshape(part_len, 3, group) for r in returned], axis=2).reshape(
+                part_len, 3 * width
             )
         )
-    rows_back = jnp.stack(back_parts).reshape(row_count, 3 * width)
-    grad_qkv_weight = contract_rows(flat, rows_back)
-    grad_query_bias = jnp.sum(rows_back[:, :width].astype(jnp.float32), axis=0)
-    grad_value_bias = jnp.sum(rows_back[:, 2 * width :].astype(jnp.float32), axis=0)
-    input_grad = (back_first + times_transpose(rows_back, full_qkv)).reshape(
+    rows_back = jnp.concatenate(back_parts, axis=0)
+    grad_qkv_weight = unrolled(contract_rows(flat, rows_back).reshape(model, 3, width), 2).reshape(
+        model, 3 * width
+    )
+    grad_qkv_bias = unrolled(jnp.sum(rows_back.astype(jnp.float32), axis=0).reshape(3, width), 1)
+    grad_query_bias = grad_qkv_bias[0]
+    grad_value_bias = grad_qkv_bias[2]
+    input_grad = (back_first + times_transpose(rows_back, roll_qkv)).reshape(
         streams, part_len, width
     )
     late = pack_lanes([grad_qkv_weight, grad_query_bias[:, None], grad_value_bias[:, None]])

time: 870 us -> 764 us (0.88)
  local copies, waits for them, and re-layouts: 221 us -> 158 us
  waiting for transfers between devices: 331 us -> 282 us
  other arithmetic: 33.3 us -> 57.6 us
  matrix products: 92.7 us -> 81 us
    all_to_all x16 -> x0, starting transfers between devices: 64.1 us -> none  [the longest x4 17.8 us: per_device(): lax.all_to_all(context.reshape(LEN, local_heads, DH), 'seq', split_axis=0...]
    all_to_all x16 -> x0, waiting for transfers between devices: 61.9 us -> none  [the longest x4 49.3 us: per_device(): lax.all_to_all(qkv.reshape(part_len, 3, heads, DH), 'seq', split_axis=2,...]
    ppermute x0 -> x48, starting transfers between devices: none -> 58.5 us  [send(): out.append(lax.ppermute(blocks[k], 'seq', pairs))]
    unnamed x90 -> x93, local copies, waits for them, and re-layouts: 63.4 us -> 23.3 us
    reshape x20 -> x4, local copies, waits for them, and re-layouts: 39.3 us -> 4.14 us  [attention_forward(): segment.reshape(length, 1)]
    all_to_all x16 -> x0, local copies, waits for them, and re-layouts: 26.8 us -> none  [the longest x4 14.1 us: per_device(): lax.all_to_all(one_grads.reshape(LEN, 3, local_heads, DH), 'seq', split_a...]
    slice x1 -> x25, local copies, waits for them, and re-layouts: 0.62 us -> 23.8 us  [the longest x8 8.76 us: per_device(): one_grads[k * part_len:(k + 1) * part_len]]
    concatenate x0 -> x16, local copies, waits for them, and re-layouts: none -> 22.5 us  [per_device(): jnp.concatenate(send([qkv[:, :, k] for k in range(ways)], 1), axis=0)]
  transfers between devices with their start and end apart: 21 -> 53, of which waited for: 10 -> 15; matrix products, arithmetic and copies ran while one was open for 20% -> 16% of each run, Pallas kernels for 12% -> 13%
where the time goes in v10:
time: 764 us; the launch traced here: 753 us
  waiting for transfers between devices  282 us (37%)
  local copies, waits for them, and re-layouts  158 us (21%)
  Pallas kernels  101 us (13%)
  matrix products  81 us (11%)
  starting transfers between devices  58.9 us (8%)
  other arithmetic  57.6 us (8%)
  between operations  15.3 us (2%)
    reduce_scatter x1, waiting for transfers between devices, per_device(): lax.psum_scatter(early, axes, scatter_dimension=0, tiled=True)  147 us
    unnamed x7, waiting for transfers between devices  60.1 us
    pallas_call x4, Pallas kernels, attention_backward(): pl.pallas_call(attention_backward_kernel, out_shape=jax.ShapeDtypeStruct(...  58.5 us
    ppermute x48, starting transfers between devices, send(): out.append(lax.ppermute(blocks[k], 'seq', pairs))  58.5 us
    all_gather x1, waiting for transfers between devices, per_device(): full_first = lax.all_gather(first, axes, axis=0, tiled=True)  54 us
    pallas_call x4, Pallas kernels, attention_forward(): pl.pallas_call(attention_forward_kernel, out_shape=(jax.ShapeDtypeStruct(...  42.2 us
    dot_general x7, matrix products, times_transpose(): lax.dot_general(left, right, (((1,), (1,)), ((), ())), preferred_element_...  35.3 us
    concatenate x2, local copies, waits for them, and re-layouts, pack_lanes(): block = jnp.concatenate(pieces, axis=1)  24.4 us
  transfers between devices with their start and end apart: 53, of which 15 were waited for; matrix products, arithmetic and copies ran while one was open for 16% of the time, Pallas kernels for 13%

profile of v10, /device:TPU:0, one launch (start us, length us, event | category | flops | bytes accessed | tf_op | source)
XLA Modules:
  0.0 752.7 jit_solution(4099746560847948573)
XLA Ops:
  27.3 54.0 %all-gather.3.cloned.1.call-done = bf16[768,2316]{1,0:T(8,128)(2,1)} async-done(((bf16[24,2316]{1,0:T(8,128)(2,1)}), bf16[768,2316]{1,0:T(8,128)(2,1)}) %all-gather.3.cloned.1.call-update) | async-done | bytes 3557392 | tf_op jit(solution)/shard_map/all_gather | solution.py:219
  81.3 4.0 slice.428
  85.3 5.7 copy.302
  91.0 3.7 convert_reduce_fusion.2
  95.0 3.4 fusion.16
  102.4 2.4 collective-permute-start.2
  113.1 2.5 collective-permute-start.8
  115.6 6.8 collective-permute-done.1
  133.4 2.4 collective-permute-start.14
  137.0 1.9 copy.244
  140.3 1.9 copy.245
  142.1 3.9 collective-permute-done.12
  147.8 2.5 pad_maximum_fusion.2.qkv_ref
  150.3 10.3 %shard_map.305 = (bf16[1024,192]{1,0:T(8,128)(2,1)}, f32[1024,3]{1,0:T(8,128)}) custom-call(bf16[1024,576]{1,0:T(8,128)(2,1)} %pad_maximum_fusion.2.qkv_ref, s32[1024,1]{1,0:T(8,128)} %copy.237.seg_col_ref, s32[1,1024]{1,0:T(1,128)} %bitcast.306), custom_call_target="tpu_custom_call" | custom-call | flops 805306368 | bytes 1769472 | tf_op jit(solution)/shard_map/pallas_call | solution.py:135
  160.6 1.9 fusion.67
  162.5 2.7 collective-permute-start.3
  170.7 1.9 collective-permute-start.5
  172.6 1.9 copy.261
  174.5 2.3 pad_maximum_fusion.3.qkv_ref
  176.8 10.5 %shard_map.306 = (bf16[1024,192]{1,0:T(8,128)(2,1)}, f32[1024,3]{1,0:T(8,128)}) custom-call(bf16[1024,576]{1,0:T(8,128)(2,1)} %pad_maximum_fusion.3.qkv_ref, s32[1024,1]{1,0:T(8,128)} %copy.246.seg_col_ref, s32[1,1024]{1,0:T(1,128)} %bitcast.303), custom_call_target="tpu_custom_call" | custom-call | flops 805306368 | bytes 1769472 | tf_op jit(solution)/shard_map/pallas_call | solution.py:135
  190.0 1.9 copy.262
  193.4 1.9 copy.263
  196.5 10.6 %shard_map.307 = (bf16[1024,192]{1,0:T(8,128)(2,1)}, f32[1024,3]{1,0:T(8,128)}) custom-call(bf16[1024,576]{1,0:T(8,128)(2,1)} %pad_maximum_fusion.4.qkv_ref, s32[1024,1]{1,0:T(8,128)} %copy.255.seg_col_ref, s32[1,1024]{1,0:T(1,128)} %bitcast.300), custom_call_target="tpu_custom_call" | custom-call | flops 805306368 | bytes 1769472 | tf_op jit(solution)/shard_map/pallas_call | solution.py:135
  208.3 10.8 %shard_map.308 = (bf16[1024,192]{1,0:T(8,128)(2,1)}, f32[1024,3]{1,0:T(8,128)}) custom-call(bf16[1024,576]{1,0:T(8,128)(2,1)} %pad_maximum_fusion.5.qkv_ref, s32[1024,1]{1,0:T(8,128)} %copy.264.seg_col_ref, s32[1,1024]{1,0:T(1,128)} %bitcast.297), custom_call_target="tpu_custom_call" | custom-call | flops 805306368 | bytes 1769472 | tf_op jit(solution)/shard_map/pallas_call | solution.py:135
  221.8 1.9 collective-permute-start.15
  234.3 2.7 collective-permute-done.23
  245.9 2.9 slice.457
  248.8 8.5 %reshape.460 = bf16[3072,768]{1,0:T(8,128)(2,1)} reshape(bf16[768,3072]{1,0:T(8,128)(2,1)} %slice.457) | data formatting | bytes 9437184 | tf_op jit(solution)/shard_map/reshape | solution.py:225
  257.3 12.3 %multiply_convert_fusion = (bf16[1024,3072]{1,0:T(8,128)(2,1)S(1)}, f32[1024,3072]{1,0:T(8,128)}) fusion(f32[3072]{0:T(1024)S(1)} %copy-done.32, bf16[768,6912]{1,0:T(8,128)(2,1)} %all-gather.5.cloned.1.call-done, f32[1024,768]{1,0:T(8,128)} %copy-done.1, f32[768]{0:T(1024)S(1)} %copy-done.33, f32[768]{0:T(1024)S(1)} %get-tuple-element.46, ...), kind=kOutput, calls=%fused_computation.9 | convolution fusion | flops 4854644736 | bytes 26765312 | tf_op jit(solution)/shard_map/dot_general | solution.py:288
  269.6 5.5 fusion.80
  275.6 2.8 fusion.23
  281.4 7.1 convolution_convert_fusion
  288.5 8.5 %convert_element_type.348 = bf16[768,3072]{1,0:T(8,128)(2,1)} reshape(bf16[3072,768]{1,0:T(8,128)(2,1)} %convolution_convert_fusion) | data formatting | bytes 9437184 | tf_op jit(solution)/shard_map/convert_element_type | solution.py:70
  296.9 12.9 %fusion.81 = (bf16[3072]{0:T(1024)(128)(2,1)S(1)}, bf16[1024,3072]{1,0:T(8,128)(2,1)S(1)}) fusion(f32[1024,3072]{1,0:T(8,128)} %get-tuple-element.167, f32[3072]{0:T(1024)S(1)} %copy-done.32, bf16[3072,768]{1,0:T(8,128)(2,1)} %reshape.460, f32[1024,768]{1,0:T(8,128)} %copy-done.8), kind=kOutput, calls=%fused_computation.224 | convolution fusion | flops 4870370304 | bytes 26757120 | tf_op jit(solution)/shard_map/dot_general | solution.py:27
  309.9 8.1 %convolution_convert_fusion.1 = bf16[768,3072]{1,0:T(8,128)(2,1)} fusion(bf16[1024,3072]{1,0:T(8,128)(2,1)S(1)} %get-tuple-element.172, f32[1024,768]{1,0:T(8,128)S(1)} %copy-done.3, f32[768]{0:T(1024)S(1)} %copy-done.33, f32[768]{0:T(1024)S(1)} %get-tuple-element.46, f32[1024]{0:T(1024)S(1)} %add_rsqrt_fusion.1, f32[1024]{0:T(1024)S(1)} %broadcast_multiply_fusion.4), kind=kOutput, calls=%fused_computation.17 | convolution fusion | flops 4838129664 | bytes 14170112 | tf_op jit(solution)/shard_map/dot_general | solution.py:21
  318.1 8.4 %multiply_reduce_fusion = (bf16[768]{0:T(1024)(128)(2,1)S(1)}, f32[1024]{0:T(1024)S(1)}, f32[1024]{0:T(1024)S(1)}, bf16[768]{0:T(1024)(128)(2,1)S(1)}, f32[1024,768]{1,0:T(8,128)S(1)}) fusion(f32[1024,768]{1,0:T(8,128)S(1)} %copy-done.3, f32[1024]{0:T(1024)S(1)} %add_rsqrt_fusion.1, f32[1024]{0:T(1024)S(1)} %broadcast_multiply_fusion.4, ...), kind=kOutput, calls=%fused_computation.44 | convolution fusion | flops 4839698432 | bytes 20469760 | tf_op jit(solution)/shard_map/dot_general | solution.py:27
  326.5 2.3 fusion.58
  335.4 17.8 %concatenate.158 = bf16[768,7168]{1,0:T(8,128)(2,1)} concatenate(bf16[768,768]{1,0:T(8,128)(2,1)S(1)} %bitcast.239, bf16[768,3072]{1,0:T(8,128)(2,1)} %convolution_convert_fusion.1, bf16[768,3072]{1,0:T(8,128)(2,1)} %convert_element_type.348, bf16[768,1]{1,0:T(8,128)(2,1)S(1)} %convert_element_type.380, bf16[768,1]{1,0:T(8,128)(2,1)} %convert_element_type.381, ...), dimensions={1} | concatenate | bytes 22020096 | tf_op jit(solution)/shard_map/concatenate | solution.py:74
  353.2 1.9 convolution_convert_fusion.5
  358.5 2.8 collective-permute-start.26
  364.8 2.3 collective-permute-start.32
  368.3 2.5 collective-permute-start.37
  371.7 14.7 %shard_map.309 = bf16[1024,576]{1,0:T(8,128)(2,1)} custom-call(bf16[1024,576]{1,0:T(8,128)(2,1)} %pad_maximum_fusion.2.qkv_ref, s32[1024,1]{1,0:T(8,128)} %copy.237.seg_col_ref, s32[1,1024]{1,0:T(1,128)} %bitcast.307, f32[1024,3]{1,0:T(8,128)} %get-tuple-element.32.lse_ref, bf16[1024,192]{1,0:T(8,128)(2,1)} %pad_maximum_fusion.10.up_ref), custom_call_target="tpu_custom_call" | custom-call | flops 2013265920 | bytes 2949120 | tf_op jit(solution)/shard_map/pallas_call | solution.py:153
  387.8 2.2 collective-permute-start.42
  391.8 14.6 %shard_map.310 = bf16[1024,576]{1,0:T(8,128)(2,1)} custom-call(bf16[1024,576]{1,0:T(8,128)(2,1)} %pad_maximum_fusion.3.qkv_ref, s32[1024,1]{1,0:T(8,128)} %copy.246.seg_col_ref, s32[1,1024]{1,0:T(1,128)} %bitcast.304, f32[1024,3]{1,0:T(8,128)} %get-tuple-element.34.lse_ref, bf16[1024,192]{1,0:T(8,128)(2,1)} %pad_maximum_fusion.11.up_ref), custom_call_target="tpu_custom_call" | custom-call | flops 2013265920 | bytes 2949120 | tf_op jit(solution)/shard_map/pallas_call | solution.py:153
  406.4 2.2 fusion.60
  408.7 2.9 collective-permute-start.44
  413.4 1.9 pad_maximum_fusion.12.up_ref
  415.3 14.6 %shard_map.311 = bf16[1024,576]{1,0:T(8,128)(2,1)} custom-call(bf16[1024,576]{1,0:T(8,128)(2,1)} %pad_maximum_fusion.4.qkv_ref, s32[1024,1]{1,0:T(8,128)} %copy.255.seg_col_ref, s32[1,1024]{1,0:T(1,128)} %bitcast.301, f32[1024,3]{1,0:T(8,128)} %get-tuple-element.35.lse_ref, bf16[1024,192]{1,0:T(8,128)(2,1)} %pad_maximum_fusion.12.up_ref), custom_call_target="tpu_custom_call" | custom-call | flops 2013265920 | bytes 2949120 | tf_op jit(solution)/shard_map/pallas_call | solution.py:153
  429.9 2.2 fusion.61
  433.7 1.9 collective-permute-start.35
  436.6 1.9 pad_maximum_fusion.13.up_ref
  441.0 14.6 %shard_map.312 = bf16[1024,576]{1,0:T(8,128)(2,1)} custom-call(bf16[1024,576]{1,0:T(8,128)(2,1)} %pad_maximum_fusion.5.qkv_ref, s32[1024,1]{1,0:T(8,128)} %copy.264.seg_col_ref, s32[1,1024]{1,0:T(1,128)} %bitcast.298, f32[1024,3]{1,0:T(8,128)} %get-tuple-element.36.lse_ref, bf16[1024,192]{1,0:T(8,128)(2,1)} %pad_maximum_fusion.13.up_ref), custom_call_target="tpu_custom_call" | custom-call | flops 2013265920 | bytes 2949120 | tf_op jit(solution)/shard_map/pallas_call | solution.py:153
  457.5 2.2 fusion.62
  485.7 5.3 fusion.56
  491.8 5.1 fusion.7
  497.0 5.8 copy.296
  502.8 6.6 concatenate.165
  509.4 5.1 copy.300
  514.6 2.9 copy.320
  517.8 45.8 %reduce-scatter.10.cloned.1.call-done = bf16[24,10240]{1,0:T(8,128)(2,1)} async-done(((bf16[192,10240]{1,0:T(8,128)(2,1)}), bf16[24,10240]{1,0:T(8,128)(2,1)}) %reduce-scatter.10.cloned.1.call-update) | async-done | bytes 491536
  566.6 9.3 %convolution_add_fusion.4 = f32[1024,768]{1,0:T(8,128)} fusion(f32[1024,768]{1,0:T(8,128)} %get-tuple-element.68, bf16[768,2304]{0,1:T(8,128)(2,1)} %bitcast.259, bf16[256,2304]{0,1:T(8,128)(2,1)} %bitcast.251, bf16[256,2304]{0,1:T(8,128)(2,1)} %bitcast.246, bf16[256,2304]{0,1:T(8,128)(2,1)S(1)} %bitcast.245, bf16[256,2304]{0,1:T(8,128)(2,1)S(1)} %bitcast.242), kind=kOutput, calls=%fused_computation.62 | convolution fusion | flops 3643539456 | bytes 14548992 | tf_op jit(solution)/shard_map/dot_general | solution.py:27
  575.8 13.7 %reduce-scatter.12.cloned.1.call-done = bf16[24,2560]{1,0:T(8,128)(2,1)} async-done(((bf16[96,2560]{1,0:T(8,128)(2,1)}), bf16[24,2560]{1,0:T(8,128)(2,1)}) %reduce-scatter.12.cloned.1.call-update) | async-done | bytes 122896
  591.9 147.4 %reduce-scatter.8.cloned.1.call-done = bf16[24,7168]{1,0:T(8,128)(2,1)} async-done(((bf16[768,7168]{1,0:T(8,128)(2,1)}), bf16[24,7168]{1,0:T(8,128)(2,1)}) %reduce-scatter.8.cloned.1.call-update) | async-done | bytes 344080 | tf_op jit(solution)/shard_map/reduce_scatter | solution.py:327
  (342 shorter events, 151.9 us)
Async XLA Ops:
  7.2 14.4 %copy-start.36 = (s32[4,17]{1,0:T(4,128)S(1)}, s32[4,17]{1,0:T(4,128)}, u32[]{:S(2)}) copy-start(s32[4,17]{1,0:T(4,128)} %param.22) | copy-start | bytes 820
  7.2 18.9 %copy-start = (bf16[4,256,768]{2,1,0:T(8,128)(2,1)S(1)}, bf16[4,256,768]{2,1,0:T(8,128)(2,1)}, u32[]{:S(2)}) copy-start(bf16[4,256,768]{2,1,0:T(8,128)(2,1)} %param.21) | copy-start | bytes 4718596
  7.2 74.1 %all-gather.3.cloned.1.call-start = ((), (), s32[]{:S(2)}) async-start(), calls=%async_computation.3 | async-start | bytes 3852288 | tf_op jit(solution)/shard_map/all_gather | solution.py:219
  17.7 221.3 %all-gather.5.cloned.1.call-start = ((), (), s32[]{:S(2)}) async-start(), calls=%async_computation.4 | async-start | bytes 10948608 | tf_op jit(solution)/shard_map/all_gather | solution.py:220
  21.5 542.2 %reduce-scatter.10.cloned.1.call-start = ((), (), s32[]{:S(2)}) async-start(), calls=%async_computation.6 | async-start | bytes 4423680
  24.1 61.2 %copy-start.29 = (s32[1024]{0:T(1024)}, s32[1024]{0:T(1024)S(1)}, u32[]{:S(2)}) copy-start(s32[1024]{0:T(1024)S(1)} %pad_add_fusion.2) | copy-start | bytes 12292
  25.1 60.2 %copy-start.28 = (s32[1024]{0:T(1024)}, s32[1024]{0:T(1024)S(1)}, u32[]{:S(2)}) copy-start(s32[1024]{0:T(1024)S(1)} %pad_add_fusion.3) | copy-start | bytes 12292
  100.3 12.8 %collective-permute-start = (bf16[256,3,192]{0,2,1:T(8,128)(2,1)S(1)}, bf16[256,3,192]{0,2,1:T(8,128)(2,1)S(1)}, u32[]{:S(2)}, u32[]{:S(2)}) collective-permute-start(bf16[256,3,192]{0,2,1:T(8,128)(2,1)S(1)} %get-tuple-element.88), channel_id=1, source_target_pairs={{0,8},{8,16},{16,24},{24,0},{1,9},{9,17},{17,25},{25,1},{2,10},{10... | collective-permute-start | bytes 884744 | tf_op jit(solution)/shard_map/ppermute | solution.py:255
  101.7 20.7 %collective-permute-start.1 = (bf16[256,3,192]{0,2,1:T(8,128)(2,1)S(1)}, bf16[256,3,192]{0,2,1:T(8,128)(2,1)S(1)}, u32[]{:S(2)}, u32[]{:S(2)}) collective-permute-start(bf16[256,3,192]{0,2,1:T(8,128)(2,1)S(1)} %get-tuple-element.87), channel_id=1, source_target_pairs={{0,16},{8,24},{16,0},{24,8},{1,17},{9,25},{17,1},{25,9},{2,18},{10... | collective-permute-start | bytes 884744 | tf_op jit(solution)/shard_map/ppermute | solution.py:255
  102.4 27.5 %collective-permute-start.2 = (bf16[256,3,192]{0,2,1:T(8,128)(2,1)}, bf16[256,3,192]{0,2,1:T(8,128)(2,1)}, u32[]{:S(2)}, u32[]{:S(2)}) collective-permute-start(bf16[256,3,192]{0,2,1:T(8,128)(2,1)} %get-tuple-element.89), channel_id=1, source_target_pairs={{0,24},{8,0},{16,8},{24,16},{1,25},{9,1},{17,9},{25,17},{2,26},{10... | collective-permute-start | bytes 884744 | tf_op jit(solution)/shard_map/ppermute | solution.py:255
  106.9 26.5 %collective-permute-start.6 = (bf16[256,3,192]{0,2,1:T(8,128)(2,1)}, bf16[256,3,192]{0,2,1:T(8,128)(2,1)}, u32[]{:S(2)}, u32[]{:S(2)}) collective-permute-start(bf16[256,3,192]{0,2,1:T(8,128)(2,1)} %get-tuple-element.92), channel_id=1, source_target_pairs={{0,8},{8,16},{16,24},{24,0},{1,9},{9,17},{17,25},{25,1},{2,10},{10... | collective-permute-start | bytes 884744 | tf_op jit(solution)/shard_map/ppermute | solution.py:255
  106.9 30.0 %collective-permute-start.7 = (bf16[256,3,192]{0,2,1:T(8,128)(2,1)}, bf16[256,3,192]{0,2,1:T(8,128)(2,1)}, u32[]{:S(2)}, u32[]{:S(2)}) collective-permute-start(bf16[256,3,192]{0,2,1:T(8,128)(2,1)} %get-tuple-element.91), channel_id=1, source_target_pairs={{0,16},{8,24},{16,0},{24,8},{1,17},{9,25},{17,1},{25,9},{2,18},{10... | collective-permute-start | bytes 884744 | tf_op jit(solution)/shard_map/ppermute | solution.py:255
  113.1 26.6 %collective-permute-start.8 = (bf16[256,3,192]{0,2,1:T(8,128)(2,1)}, bf16[256,3,192]{0,2,1:T(8,128)(2,1)}, u32[]{:S(2)}, u32[]{:S(2)}) collective-permute-start(bf16[256,3,192]{0,2,1:T(8,128)(2,1)} %get-tuple-element.93), channel_id=1, source_target_pairs={{0,24},{8,0},{16,8},{24,16},{1,25},{9,1},{17,9},{25,17},{2,26},{10... | collective-permute-start | bytes 884744 | tf_op jit(solution)/shard_map/ppermute | solution.py:255
  123.2 22.9 %collective-permute-start.12 = (bf16[256,3,192]{0,2,1:T(8,128)(2,1)}, bf16[256,3,192]{0,2,1:T(8,128)(2,1)}, u32[]{:S(2)}, u32[]{:S(2)}) collective-permute-start(bf16[256,3,192]{0,2,1:T(8,128)(2,1)} %get-tuple-element.96), channel_id=1, source_target_pairs={{0,8},{8,16},{16,24},{24,0},{1,9},{9,17},{17,25},{25,1},{2,10},{10... | collective-permute-start | bytes 884744 | tf_op jit(solution)/shard_map/ppermute | solution.py:255
  129.8 32.7 %collective-permute-start.13 = (bf16[256,3,192]{0,2,1:T(8,128)(2,1)}, bf16[256,3,192]{0,2,1:T(8,128)(2,1)}, u32[]{:S(2)}, u32[]{:S(2)}) collective-permute-start(bf16[256,3,192]{0,2,1:T(8,128)(2,1)} %get-tuple-element.95), channel_id=1, source_target_pairs={{0,16},{8,24},{16,0},{24,8},{1,17},{9,25},{17,1},{25,9},{2,18},{10... | collective-permute-start | bytes 884744 | tf_op jit(solution)/shard_map/ppermute | solution.py:255
  133.4 33.6 %collective-permute-start.14 = (bf16[256,3,192]{0,2,1:T(8,128)(2,1)}, bf16[256,3,192]{0,2,1:T(8,128)(2,1)}, u32[]{:S(2)}, u32[]{:S(2)}) collective-permute-start(bf16[256,3,192]{0,2,1:T(8,128)(2,1)} %get-tuple-element.97), channel_id=1, source_target_pairs={{0,24},{8,0},{16,8},{24,16},{1,25},{9,1},{17,9},{25,17},{2,26},{10... | collective-permute-start | bytes 884744 | tf_op jit(solution)/shard_map/ppermute | solution.py:255
  136.9 33.8 %collective-permute-start.18 = (bf16[256,3,192]{0,2,1:T(8,128)(2,1)}, bf16[256,3,192]{0,2,1:T(8,128)(2,1)}, u32[]{:S(2)}, u32[]{:S(2)}) collective-permute-start(bf16[256,3,192]{0,2,1:T(8,128)(2,1)} %get-tuple-element.100), channel_id=1, source_target_pairs={{0,8},{8,16},{16,24},{24,0},{1,9},{9,17},{17,25},{25,1},{2,10},{10... | collective-permute-start | bytes 884744 | tf_op jit(solution)/shard_map/ppermute | solution.py:255
  139.7 49.4 %collective-permute-start.19 = (bf16[256,3,192]{0,2,1:T(8,128)(2,1)}, bf16[256,3,192]{0,2,1:T(8,128)(2,1)}, u32[]{:S(2)}, u32[]{:S(2)}) collective-permute-start(bf16[256,3,192]{0,2,1:T(8,128)(2,1)} %get-tuple-element.99), channel_id=1, source_target_pairs={{0,16},{8,24},{16,0},{24,8},{1,17},{9,25},{17,1},{25,9},{2,18},{10... | collective-permute-start | bytes 884744 | tf_op jit(solution)/shard_map/ppermute | solution.py:255
  146.1 45.8 %collective-permute-start.20 = (bf16[256,3,192]{0,2,1:T(8,128)(2,1)}, bf16[256,3,192]{0,2,1:T(8,128)(2,1)}, u32[]{:S(2)}, u32[]{:S(2)}) collective-permute-start(bf16[256,3,192]{0,2,1:T(8,128)(2,1)} %get-tuple-element.101), channel_id=1, source_target_pairs={{0,24},{8,0},{16,8},{24,16},{1,25},{9,1},{17,9},{25,17},{2,26},{10... | collective-permute-start | bytes 884744 | tf_op jit(solution)/shard_map/ppermute | solution.py:255
  162.5 57.8 %collective-permute-start.3 = (bf16[256,192]{1,0:T(8,128)(2,1)}, bf16[256,192]{1,0:T(8,128)(2,1)}, u32[]{:S(2)}, u32[]{:S(2)}) collective-permute-start(bf16[256,192]{1,0:T(8,128)(2,1)} %get-tuple-element.108), channel_id=1, source_target_pairs={{0,24},{8,0},{16,8},{24,16},{1,25},{9,1},{17,9},{25,17},{2,26},{10... | collective-permute-start | bytes 294920 | tf_op jit(solution)/shard_map/ppermute | solution.py:255
  167.0 54.8 %collective-permute-start.4 = (bf16[256,192]{1,0:T(8,128)(2,1)}, bf16[256,192]{1,0:T(8,128)(2,1)}, u32[]{:S(2)}, u32[]{:S(2)}) collective-permute-start(bf16[256,192]{1,0:T(8,128)(2,1)} %get-tuple-element.107), channel_id=1, source_target_pairs={{0,16},{8,24},{16,0},{24,8},{1,17},{9,25},{17,1},{25,9},{2,18},{10... | collective-permute-start | bytes 294920 | tf_op jit(solution)/shard_map/ppermute | solution.py:255
  170.7 53.0 %collective-permute-start.5 = (bf16[256,192]{1,0:T(8,128)(2,1)}, bf16[256,192]{1,0:T(8,128)(2,1)}, u32[]{:S(2)}, u32[]{:S(2)}) collective-permute-start(bf16[256,192]{1,0:T(8,128)(2,1)} %get-tuple-element.106), channel_id=1, source_target_pairs={{0,8},{8,16},{16,24},{24,0},{1,9},{9,17},{17,25},{25,1},{2,10},{10... | collective-permute-start | bytes 294920 | tf_op jit(solution)/shard_map/ppermute | solution.py:255
  176.8 18.5 %copy-start.11 = (bf16[256,576]{1,0:T(8,128)(2,1)S(1)}, bf16[256,576]{1,0:T(8,128)(2,1)}, u32[]{:S(2)}) copy-start(bf16[256,576]{1,0:T(8,128)(2,1)} %copy.253) | copy-start | bytes 884740
  176.8 18.5 %copy-start.12 = (bf16[256,576]{1,0:T(8,128)(2,1)S(1)}, bf16[256,576]{1,0:T(8,128)(2,1)}, u32[]{:S(2)}) copy-start(bf16[256,576]{1,0:T(8,128)(2,1)} %copy.254) | copy-start | bytes 884740
  189.1 36.0 %collective-permute-start.10 = (bf16[256,192]{1,0:T(8,128)(2,1)}, bf16[256,192]{1,0:T(8,128)(2,1)}, u32[]{:S(2)}, u32[]{:S(2)}) collective-permute-start(bf16[256,192]{1,0:T(8,128)(2,1)} %get-tuple-element.111), channel_id=1, source_target_pairs={{0,16},{8,24},{16,0},{24,8},{1,17},{9,25},{17,1},{25,9},{2,18},{10... | collective-permute-start | bytes 294920 | tf_op jit(solution)/shard_map/ppermute | solution.py:255
  191.9 34.4 %collective-permute-start.11 = (bf16[256,192]{1,0:T(8,128)(2,1)}, bf16[256,192]{1,0:T(8,128)(2,1)}, u32[]{:S(2)}, u32[]{:S(2)}) collective-permute-start(bf16[256,192]{1,0:T(8,128)(2,1)} %get-tuple-element.110), channel_id=1, source_target_pairs={{0,8},{8,16},{16,24},{24,0},{1,9},{9,17},{17,25},{25,1},{2,10},{10... | collective-permute-start | bytes 294920 | tf_op jit(solution)/shard_map/ppermute | solution.py:255
  220.3 7.7 %collective-permute-start.9 = (bf16[256,192]{1,0:T(8,128)(2,1)S(1)}, bf16[256,192]{1,0:T(8,128)(2,1)S(1)}, u32[]{:S(2)}, u32[]{:S(2)}) collective-permute-start(bf16[256,192]{1,0:T(8,128)(2,1)S(1)} %copy-done.25), channel_id=1, source_target_pairs={{0,24},{8,0},{16,8},{24,16},{1,25},{9,1},{17,9},{25,17},{2,26},{10... | collective-permute-start | bytes 294920 | tf_op jit(solution)/shard_map/ppermute | solution.py:255
  221.8 9.3 %collective-permute-start.15 = (bf16[256,192]{1,0:T(8,128)(2,1)S(1)}, bf16[256,192]{1,0:T(8,128)(2,1)S(1)}, u32[]{:S(2)}, u32[]{:S(2)}) collective-permute-start(bf16[256,192]{1,0:T(8,128)(2,1)S(1)} %get-tuple-element.116), channel_id=1, source_target_pairs={{0,24},{8,0},{16,8},{24,16},{1,25},{9,1},{17,9},{25,17},{2,26},{10... | collective-permute-start | bytes 294920 | tf_op jit(solution)/shard_map/ppermute | solution.py:255
  223.7 7.5 collective-permute-start.16
  225.1 7.9 %collective-permute-start.17 = (bf16[256,192]{1,0:T(8,128)(2,1)S(1)}, bf16[256,192]{1,0:T(8,128)(2,1)S(1)}, u32[]{:S(2)}, u32[]{:S(2)}) collective-permute-start(bf16[256,192]{1,0:T(8,128)(2,1)S(1)} %get-tuple-element.114), channel_id=1, source_target_pairs={{0,8},{8,16},{16,24},{24,0},{1,9},{9,17},{17,25},{25,1},{2,10},{10... | collective-permute-start | bytes 294920 | tf_op jit(solution)/shard_map/ppermute | solution.py:255
  226.3 7.5 collective-permute-start.21
  228.1 6.2 collective-permute-start.22
  231.1 5.9 collective-permute-start.23
  257.3 12.3 %copy-start.2 = (f32[1024,768]{1,0:T(8,128)S(1)}, f32[1024,768]{1,0:T(8,128)}, u32[]{:S(2)}) copy-start(f32[1024,768]{1,0:T(8,128)} %copy-done.1) | copy-start | bytes 9437188
  257.3 12.3 %copy-start.6 = (bf16[3072,768]{1,0:T(8,128)(2,1)S(1)}, bf16[3072,768]{1,0:T(8,128)(2,1)}, u32[]{:S(2)}) copy-start(bf16[3072,768]{1,0:T(8,128)(2,1)} %reshape.460) | copy-start | bytes 14155780
  296.9 13.0 %copy-start.3 = (f32[1024,768]{1,0:T(8,128)S(1)}, f32[1024,768]{1,0:T(8,128)}, u32[]{:S(2)}) copy-start(f32[1024,768]{1,0:T(8,128)} %copy-done.1) | copy-start | bytes 9437188
  358.0 6.8 collective-permute-start.24
  358.1 9.0 %collective-permute-start.25 = (bf16[256,192]{1,0:T(8,128)(2,1)S(1)}, bf16[256,192]{1,0:T(8,128)(2,1)S(1)}, u32[]{:S(2)}, u32[]{:S(2)}) collective-permute-start(bf16[256,192]{1,0:T(8,128)(2,1)S(1)} %get-tuple-element.123), channel_id=1, source_target_pairs={{0,16},{8,24},{16,0},{24,8},{1,17},{9,25},{17,1},{25,9},{2,18},{10... | collective-permute-start | bytes 294920 | tf_op jit(solution)/shard_map/ppermute | solution.py:255
  358.5 9.9 %collective-permute-start.26 = (bf16[256,192]{1,0:T(8,128)(2,1)S(1)}, bf16[256,192]{1,0:T(8,128)(2,1)S(1)}, u32[]{:S(2)}, u32[]{:S(2)}) collective-permute-start(bf16[256,192]{1,0:T(8,128)(2,1)S(1)} %get-tuple-element.122), channel_id=1, source_target_pairs={{0,24},{8,0},{16,8},{24,16},{1,25},{9,1},{17,9},{25,17},{2,26},{10... | collective-permute-start | bytes 294920 | tf_op jit(solution)/shard_map/ppermute | solution.py:255
  361.4 26.3 %collective-permute-start.30 = (bf16[256,192]{1,0:T(8,128)(2,1)S(1)}, bf16[256,192]{1,0:T(8,128)(2,1)S(1)}, u32[]{:S(2)}, u32[]{:S(2)}) collective-permute-start(bf16[256,192]{1,0:T(8,128)(2,1)S(1)} %get-tuple-element.128), channel_id=1, source_target_pairs={{0,8},{8,16},{16,24},{24,0},{1,9},{9,17},{17,25},{25,1},{2,10},{10... | collective-permute-start | bytes 294920 | tf_op jit(solution)/shard_map/ppermute | solution.py:255
  361.8 26.0 %collective-permute-start.31 = (bf16[256,192]{1,0:T(8,128)(2,1)S(1)}, bf16[256,192]{1,0:T(8,128)(2,1)S(1)}, u32[]{:S(2)}, u32[]{:S(2)}) collective-permute-start(bf16[256,192]{1,0:T(8,128)(2,1)S(1)} %get-tuple-element.127), channel_id=1, source_target_pairs={{0,16},{8,24},{16,0},{24,8},{1,17},{9,25},{17,1},{25,9},{2,18},{10... | collective-permute-start | bytes 294920 | tf_op jit(solution)/shard_map/ppermute | solution.py:255
  364.8 25.1 %collective-permute-start.32 = (bf16[256,192]{1,0:T(8,128)(2,1)S(1)}, bf16[256,192]{1,0:T(8,128)(2,1)}, u32[]{:S(2)}, u32[]{:S(2)}) collective-permute-start(bf16[256,192]{1,0:T(8,128)(2,1)S(1)} %get-tuple-element.126), channel_id=1, source_target_pairs={{0,24},{8,0},{16,8},{24,16},{1,25},{9,1},{17,9},{25,17},{2,26},{10... | collective-permute-start | bytes 294920 | tf_op jit(solution)/shard_map/ppermute | solution.py:255
  367.1 41.6 %collective-permute-start.36 = (bf16[256,192]{1,0:T(8,128)(2,1)S(1)}, bf16[256,192]{1,0:T(8,128)(2,1)S(1)}, u32[]{:S(2)}, u32[]{:S(2)}) collective-permute-start(bf16[256,192]{1,0:T(8,128)(2,1)S(1)} %get-tuple-element.132), channel_id=1, source_target_pairs={{0,8},{8,16},{16,24},{24,0},{1,9},{9,17},{17,25},{25,1},{2,10},{10... | collective-permute-start | bytes 294920 | tf_op jit(solution)/shard_map/ppermute | solution.py:255
  368.3 43.3 %collective-permute-start.37 = (bf16[256,192]{1,0:T(8,128)(2,1)S(1)}, bf16[256,192]{1,0:T(8,128)(2,1)S(1)}, u32[]{:S(2)}, u32[]{:S(2)}) collective-permute-start(bf16[256,192]{1,0:T(8,128)(2,1)S(1)} %get-tuple-element.131), channel_id=1, source_target_pairs={{0,16},{8,24},{16,0},{24,8},{1,17},{9,25},{17,1},{25,9},{2,18},{10... | collective-permute-start | bytes 294920 | tf_op jit(solution)/shard_map/ppermute | solution.py:255
  387.7 24.8 %collective-permute-start.38 = (bf16[256,192]{1,0:T(8,128)(2,1)S(1)}, bf16[256,192]{1,0:T(8,128)(2,1)S(1)}, u32[]{:S(2)}, u32[]{:S(2)}) collective-permute-start(bf16[256,192]{1,0:T(8,128)(2,1)S(1)} %get-tuple-element.130), channel_id=1, source_target_pairs={{0,24},{8,0},{16,8},{24,16},{1,25},{9,1},{17,9},{25,17},{2,26},{10... | collective-permute-start | bytes 294920 | tf_op jit(solution)/shard_map/ppermute | solution.py:255
  387.8 44.3 %collective-permute-start.42 = (bf16[256,192]{1,0:T(8,128)(2,1)S(1)}, bf16[256,192]{1,0:T(8,128)(2,1)}, u32[]{:S(2)}, u32[]{:S(2)}) collective-permute-start(bf16[256,192]{1,0:T(8,128)(2,1)S(1)} %get-tuple-element.136), channel_id=1, source_target_pairs={{0,8},{8,16},{16,24},{24,0},{1,9},{9,17},{17,25},{25,1},{2,10},{10... | collective-permute-start | bytes 294920 | tf_op jit(solution)/shard_map/ppermute | solution.py:255
  390.0 43.7 %collective-permute-start.43 = (bf16[256,192]{1,0:T(8,128)(2,1)S(1)}, bf16[256,192]{1,0:T(8,128)(2,1)}, u32[]{:S(2)}, u32[]{:S(2)}) collective-permute-start(bf16[256,192]{1,0:T(8,128)(2,1)S(1)} %get-tuple-element.135), channel_id=1, source_target_pairs={{0,16},{8,24},{16,0},{24,8},{1,17},{9,25},{17,1},{25,9},{2,18},{10... | collective-permute-start | bytes 294920 | tf_op jit(solution)/shard_map/ppermute | solution.py:255
  408.7 26.9 %collective-permute-start.44 = (bf16[256,192]{1,0:T(8,128)(2,1)}, bf16[256,192]{1,0:T(8,128)(2,1)}, u32[]{:S(2)}, u32[]{:S(2)}) collective-permute-start(bf16[256,192]{1,0:T(8,128)(2,1)} %get-tuple-element.134), channel_id=1, source_target_pairs={{0,24},{8,0},{16,8},{24,16},{1,25},{9,1},{17,9},{25,17},{2,26},{10... | collective-permute-start | bytes 294920 | tf_op jit(solution)/shard_map/ppermute | solution.py:255
  411.6 26.9 %collective-permute-start.27 = (bf16[256,576]{1,0:T(8,128)(2,1)S(1)}, bf16[256,576]{1,0:T(8,128)(2,1)S(1)}, u32[]{:S(2)}, u32[]{:S(2)}) collective-permute-start(bf16[256,576]{1,0:T(8,128)(2,1)S(1)} %get-tuple-element.73), channel_id=1, source_target_pairs={{0,24},{8,0},{16,8},{24,16},{1,25},{9,1},{17,9},{25,17},{2,26},{10... | collective-permute-start | bytes 884744 | tf_op jit(solution)/shard_map/ppermute | solution.py:255
  413.2 26.8 %collective-permute-start.28 = (bf16[256,576]{1,0:T(8,128)(2,1)S(1)}, bf16[256,576]{1,0:T(8,128)(2,1)S(1)}, u32[]{:S(2)}, u32[]{:S(2)}) collective-permute-start(bf16[256,576]{1,0:T(8,128)(2,1)S(1)} %get-tuple-element.72), channel_id=1, source_target_pairs={{0,16},{8,24},{16,0},{24,8},{1,17},{9,25},{17,1},{25,9},{2,18},{10... | collective-permute-start | bytes 884744 | tf_op jit(solution)/shard_map/ppermute | solution.py:255
  432.1 23.5 %collective-permute-start.29 = (bf16[256,576]{1,0:T(8,128)(2,1)S(1)}, bf16[256,576]{1,0:T(8,128)(2,1)}, u32[]{:S(2)}, u32[]{:S(2)}) collective-permute-start(bf16[256,576]{1,0:T(8,128)(2,1)S(1)} %get-tuple-element.71), channel_id=1, source_target_pairs={{0,8},{8,16},{16,24},{24,0},{1,9},{9,17},{17,25},{25,1},{2,10},{10... | collective-permute-start | bytes 884744 | tf_op jit(solution)/shard_map/ppermute | solution.py:255
  433.7 22.2 %collective-permute-start.35 = (bf16[256,576]{1,0:T(8,128)(2,1)S(1)}, bf16[256,576]{1,0:T(8,128)(2,1)S(1)}, u32[]{:S(2)}, u32[]{:S(2)}) collective-permute-start(bf16[256,576]{1,0:T(8,128)(2,1)S(1)} %get-tuple-element.75), channel_id=1, source_target_pairs={{0,8},{8,16},{16,24},{24,0},{1,9},{9,17},{17,25},{25,1},{2,10},{10... | collective-permute-start | bytes 884744 | tf_op jit(solution)/shard_map/ppermute | solution.py:255
  435.6 28.2 %collective-permute-start.33 = (bf16[256,576]{1,0:T(8,128)(2,1)}, bf16[256,576]{1,0:T(8,128)(2,1)}, u32[]{:S(2)}, u32[]{:S(2)}) collective-permute-start(bf16[256,576]{1,0:T(8,128)(2,1)} %get-tuple-element.77), channel_id=1, source_target_pairs={{0,24},{8,0},{16,8},{24,16},{1,25},{9,1},{17,9},{25,17},{2,26},{10... | collective-permute-start | bytes 884744 | tf_op jit(solution)/shard_map/ppermute | solution.py:255
  438.5 17.2 %copy-start.20 = (bf16[256,576]{1,0:T(8,128)(2,1)}, bf16[256,576]{1,0:T(8,128)(2,1)S(1)}, u32[]{:S(2)}) copy-start(bf16[256,576]{1,0:T(8,128)(2,1)S(1)} %collective-permute-done.27) | copy-start | bytes 884740
  438.5 26.9 %collective-permute-start.34 = (bf16[256,576]{1,0:T(8,128)(2,1)}, bf16[256,576]{1,0:T(8,128)(2,1)}, u32[]{:S(2)}, u32[]{:S(2)}) collective-permute-start(bf16[256,576]{1,0:T(8,128)(2,1)} %get-tuple-element.76), channel_id=1, source_target_pairs={{0,16},{8,24},{16,0},{24,8},{1,17},{9,25},{17,1},{25,9},{2,18},{10... | collective-permute-start | bytes 884744 | tf_op jit(solution)/shard_map/ppermute | solution.py:255
  440.0 15.6 %copy-start.22 = (bf16[256,576]{1,0:T(8,128)(2,1)}, bf16[256,576]{1,0:T(8,128)(2,1)S(1)}, u32[]{:S(2)}) copy-start(bf16[256,576]{1,0:T(8,128)(2,1)S(1)} %collective-permute-done.28) | copy-start | bytes 884740
  440.0 27.2 %collective-permute-start.39 = (bf16[256,576]{1,0:T(8,128)(2,1)}, bf16[256,576]{1,0:T(8,128)(2,1)}, u32[]{:S(2)}, u32[]{:S(2)}) collective-permute-start(bf16[256,576]{1,0:T(8,128)(2,1)} %get-tuple-element.81), channel_id=1, source_target_pairs={{0,24},{8,0},{16,8},{24,16},{1,25},{9,1},{17,9},{25,17},{2,26},{10... | collective-permute-start | bytes 884744 | tf_op jit(solution)/shard_map/ppermute | solution.py:255
  455.6 16.9 %collective-permute-start.40 = (bf16[256,576]{1,0:T(8,128)(2,1)}, bf16[256,576]{1,0:T(8,128)(2,1)}, u32[]{:S(2)}, u32[]{:S(2)}) collective-permute-start(bf16[256,576]{1,0:T(8,128)(2,1)} %get-tuple-element.80), channel_id=1, source_target_pairs={{0,16},{8,24},{16,0},{24,8},{1,17},{9,25},{17,1},{25,9},{2,18},{10... | collective-permute-start | bytes 884744 | tf_op jit(solution)/shard_map/ppermute | solution.py:255
  455.9 18.4 %collective-permute-start.41 = (bf16[256,576]{1,0:T(8,128)(2,1)}, bf16[256,576]{1,0:T(8,128)(2,1)}, u32[]{:S(2)}, u32[]{:S(2)}) collective-permute-start(bf16[256,576]{1,0:T(8,128)(2,1)} %get-tuple-element.79), channel_id=1, source_target_pairs={{0,8},{8,16},{16,24},{24,0},{1,9},{9,17},{17,25},{25,1},{2,10},{10... | collective-permute-start | bytes 884744 | tf_op jit(solution)/shard_map/ppermute | solution.py:255
  463.8 14.7 %collective-permute-start.45 = (bf16[256,576]{1,0:T(8,128)(2,1)}, bf16[256,576]{1,0:T(8,128)(2,1)}, u32[]{:S(2)}, u32[]{:S(2)}) collective-permute-start(bf16[256,576]{1,0:T(8,128)(2,1)} %get-tuple-element.85), channel_id=1, source_target_pairs={{0,24},{8,0},{16,8},{24,16},{1,25},{9,1},{17,9},{25,17},{2,26},{10... | collective-permute-start | bytes 884744 | tf_op jit(solution)/shard_map/ppermute | solution.py:255
  465.4 14.3 %collective-permute-start.46 = (bf16[256,576]{1,0:T(8,128)(2,1)}, bf16[256,576]{1,0:T(8,128)(2,1)}, u32[]{:S(2)}, u32[]{:S(2)}) collective-permute-start(bf16[256,576]{1,0:T(8,128)(2,1)} %get-tuple-element.84), channel_id=1, source_target_pairs={{0,16},{8,24},{16,0},{24,8},{1,17},{9,25},{17,1},{25,9},{2,18},{10... | collective-permute-start | bytes 884744 | tf_op jit(solution)/shard_map/ppermute | solution.py:255
  467.2 13.5 %collective-permute-start.47 = (bf16[256,576]{1,0:T(8,128)(2,1)}, bf16[256,576]{1,0:T(8,128)(2,1)}, u32[]{:S(2)}, u32[]{:S(2)}) collective-permute-start(bf16[256,576]{1,0:T(8,128)(2,1)} %get-tuple-element.83), channel_id=1, source_target_pairs={{0,8},{8,16},{16,24},{24,0},{1,9},{9,17},{17,25},{25,1},{2,10},{10... | collective-permute-start | bytes 884744 | tf_op jit(solution)/shard_map/ppermute | solution.py:255
  517.5 72.0 %reduce-scatter.12.cloned.1.call-start = ((), (), s32[]{:S(2)}) async-start(), calls=%async_computation.7 | async-start | bytes 614400
  565.9 173.4 %reduce-scatter.8.cloned.1.call-start = ((), (), s32[]{:S(2)}) async-start(), calls=%async_computation.5 | async-start | bytes 11354112 | tf_op jit(solution)/shard_map/reduce_scatter | solution.py:327
  (33 other events, 164.8 us)
Sparse Core Ops, SparseCore 0:
  17.8 63.4 all-gather.2
  84.3 114.2 all-gather.4
  517.6 45.9 reduce-scatter.9
  566.3 23.1 reduce-scatter.11
  595.3 143.9 reduce-scatter.7

commit v11 on v10

--- a/solution.py
+++ b/solution.py
@@ -336,19 +336,18 @@
         )
         one_grads = attention_backward(head_qkv[s], head_segment[s], logsum[s], one_back)
         returned = send([one_grads[k * part_len : (k + 1) * part_len] for k in range(ways)], -1)
-        back_parts.append(
-            jnp.stack([r.reshape(part_len, 3, group) for r in returned], axis=2).reshape(
-                part_len, 3 * width
+        placed = jnp.zeros((part_len, 3, ways, group), jnp.bfloat16)
+        for k in range(ways):
+            placed = lax.dynamic_update_slice(
+                placed, returned[k].reshape(part_len, 3, 1, group), (0, 0, (me + k) % ways, 0)
             )
-        )
+        back_parts.append(placed.reshape(part_len, 3 * width))
     rows_back = jnp.concatenate(back_parts, axis=0)
-    grad_qkv_weight = unrolled(contract_rows(flat, rows_back).reshape(model, 3, width), 2).reshape(
-        model, 3 * width
-    )
-    grad_qkv_bias = unrolled(jnp.sum(rows_back.astype(jnp.float32), axis=0).reshape(3, width), 1)
+    grad_qkv_weight = contract_rows(flat, rows_back)
+    grad_qkv_bias = jnp.sum(rows_back.astype(jnp.float32), axis=0).reshape(3, width)
     grad_query_bias = grad_qkv_bias[0]
     grad_value_bias = grad_qkv_bias[2]
-    input_grad = (back_first + times_transpose(rows_back, roll_qkv)).reshape(
+    input_grad = (back_first + times_transpose(rows_back, full_qkv)).reshape(
         streams, part_len, width
     )
     late = pack_lanes([grad_qkv_weight, grad_query_bias[:, None], grad_value_bias[:, None]])

time: 764 us -> 788 us (1.031)
  local copies, waits for them, and re-layouts: 158 us -> 179 us
    dynamic_update_slice x0 -> x16, local copies, waits for them, and re-layouts: none -> 15.9 us  [per_device(): lax.dynamic_update_slice(placed, returned[k].reshape(part_len, 3, 1, grou...]
    convert_element_type x11 -> x10, local copies, waits for them, and re-layouts: 20.5 us -> 16.2 us  [pack_lanes(): pieces = [p.astype(jnp.bfloat16) for p in pieces]]
    unnamed x93 -> x84, local copies, waits for them, and re-layouts: 23.3 us -> 27.3 us
  transfers between devices with their start and end apart: 53 -> 53, of which waited for: 15 -> 15; matrix products, arithmetic and copies ran while one was open for 16% -> 19% of each run, Pallas kernels for 13% -> 13%
where the time goes in v11:
time: 788 us; the launch traced here: 776 us
  waiting for transfers between devices  281 us (36%)
  local copies, waits for them, and re-layouts  179 us (23%)
  Pallas kernels  101 us (13%)
  matrix products  88 us (11%)
  starting transfers between devices  59.3 us (8%)
  other arithmetic  53.8 us (7%)
  between operations  15.3 us (2%)
    reduce_scatter x1, waiting for transfers between devices, per_device(): lax.psum_scatter(early, axes, scatter_dimension=0, tiled=True)  147 us
    ppermute x48, starting transfers between devices, send(): out.append(lax.ppermute(blocks[k], 'seq', pairs))  58.8 us
    pallas_call x4, Pallas kernels, attention_backward(): pl.pallas_call(attention_backward_kernel, out_shape=jax.ShapeDtypeStruct(...  58.6 us
    unnamed x7, waiting for transfers between devices  57.9 us
    all_gather x1, waiting for transfers between devices, per_device(): full_first = lax.all_gather(first, axes, axis=0, tiled=True)  53.9 us
    pallas_call x4, Pallas kernels, attention_forward(): pl.pallas_call(attention_forward_kernel, out_shape=(jax.ShapeDtypeStruct(...  42 us
    dot_general x7, matrix products, times_transpose(): lax.dot_general(left, right, (((1,), (1,)), ((), ())), preferred_element_...  38.2 us
    unnamed x84, local copies, waits for them, and re-layouts  27.3 us
  transfers between devices with their start and end apart: 53, of which 15 were waited for; matrix products, arithmetic and copies ran while one was open for 19% of the time, Pallas kernels for 13%

profile of v11, /device:TPU:0, one launch (start us, length us, event | category | flops | bytes accessed | tf_op | source)
XLA Modules:
  0.0 776.5 jit_solution(14516168301235335991)
XLA Ops:
  27.4 53.9 %all-gather.3.cloned.1.call-done = bf16[768,2316]{1,0:T(8,128)(2,1)} async-done(((bf16[24,2316]{1,0:T(8,128)(2,1)}), bf16[768,2316]{1,0:T(8,128)(2,1)}) %all-gather.3.cloned.1.call-update) | async-done | bytes 3557392 | tf_op jit(solution)/shard_map/all_gather | solution.py:219
  81.3 4.0 slice.430
  85.3 5.8 copy.338
  91.0 4.0 convert_reduce_fusion.1
  95.3 3.4 fusion.15
  102.7 2.4 collective-permute-start.2
  113.4 2.5 collective-permute-start.8
  115.9 6.9 collective-permute-done.1
  126.3 1.9 copy.256
  133.7 2.2 collective-permute-start.14
  142.4 4.0 collective-permute-done.12
  148.1 2.5 pad_maximum_fusion.2.qkv_ref
  150.6 10.3 %shard_map.305 = (bf16[1024,192]{1,0:T(8,128)(2,1)}, f32[1024,3]{1,0:T(8,128)}) custom-call(bf16[1024,576]{1,0:T(8,128)(2,1)} %pad_maximum_fusion.2.qkv_ref, s32[1024,1]{1,0:T(8,128)} %copy.260.seg_col_ref, s32[1,1024]{1,0:T(1,128)} %bitcast.328), custom_call_target="tpu_custom_call" | custom-call | flops 805306368 | bytes 1769472 | tf_op jit(solution)/shard_map/pallas_call | solution.py:135
  161.0 1.9 fusion.66
  162.8 3.0 collective-permute-start.3
  165.8 1.9 copy.276
  171.3 1.9 collective-permute-start.5
  175.1 2.2 pad_maximum_fusion.3.qkv_ref
  177.3 10.4 %shard_map.306 = (bf16[1024,192]{1,0:T(8,128)(2,1)}, f32[1024,3]{1,0:T(8,128)}) custom-call(bf16[1024,576]{1,0:T(8,128)(2,1)} %pad_maximum_fusion.3.qkv_ref, s32[1024,1]{1,0:T(8,128)} %copy.269.seg_col_ref, s32[1,1024]{1,0:T(1,128)} %bitcast.325), custom_call_target="tpu_custom_call" | custom-call | flops 805306368 | bytes 1769472 | tf_op jit(solution)/shard_map/pallas_call | solution.py:135
  197.1 10.4 %shard_map.307 = (bf16[1024,192]{1,0:T(8,128)(2,1)}, f32[1024,3]{1,0:T(8,128)}) custom-call(bf16[1024,576]{1,0:T(8,128)(2,1)} %pad_maximum_fusion.4.qkv_ref, s32[1024,1]{1,0:T(8,128)} %copy.278.seg_col_ref, s32[1,1024]{1,0:T(1,128)} %bitcast.322), custom_call_target="tpu_custom_call" | custom-call | flops 805306368 | bytes 1769472 | tf_op jit(solution)/shard_map/pallas_call | solution.py:135
  208.7 10.8 %shard_map.308 = (bf16[1024,192]{1,0:T(8,128)(2,1)}, f32[1024,3]{1,0:T(8,128)}) custom-call(bf16[1024,576]{1,0:T(8,128)(2,1)} %pad_maximum_fusion.5.qkv_ref, s32[1024,1]{1,0:T(8,128)} %copy.287.seg_col_ref, s32[1,1024]{1,0:T(1,128)} %bitcast.319), custom_call_target="tpu_custom_call" | custom-call | flops 805306368 | bytes 1769472 | tf_op jit(solution)/shard_map/pallas_call | solution.py:135
  222.3 1.9 collective-permute-start.15
  226.6 1.9 collective-permute-start.21
  228.5 2.0 collective-permute-start.22
  234.7 2.8 collective-permute-done.23
  246.5 2.9 slice.459
  249.4 8.5 %reshape.483 = bf16[3072,768]{1,0:T(8,128)(2,1)} reshape(bf16[768,3072]{1,0:T(8,128)(2,1)} %slice.459) | data formatting | bytes 9437184 | tf_op jit(solution)/shard_map/reshape | solution.py:225
  257.9 12.2 %multiply_convert_fusion = (bf16[1024,3072]{1,0:T(8,128)(2,1)S(1)}, f32[1024,3072]{1,0:T(8,128)}) fusion(f32[3072]{0:T(1024)S(1)} %copy-done.25, bf16[768,6912]{1,0:T(8,128)(2,1)} %all-gather.5.cloned.1.call-done, f32[1024,768]{1,0:T(8,128)} %copy-done.1, f32[768]{0:T(1024)S(1)} %copy-done.26, f32[768]{0:T(1024)S(1)} %get-tuple-element.45, ...), kind=kOutput, calls=%fused_computation.7 | convolution fusion | flops 4854644736 | bytes 26765312 | tf_op jit(solution)/shard_map/dot_general | solution.py:288
  270.2 5.5 fusion.79
  276.2 2.8 fusion.22
  281.9 7.1 convolution_convert_fusion
  289.0 8.6 %convert_element_type.332 = bf16[768,3072]{1,0:T(8,128)(2,1)} reshape(bf16[3072,768]{1,0:T(8,128)(2,1)} %convolution_convert_fusion) | data formatting | bytes 9437184 | tf_op jit(solution)/shard_map/convert_element_type | solution.py:70
  297.6 15.7 %fusion.80 = (bf16[3072]{0:T(1024)(128)(2,1)S(1)}, bf16[1024,3072]{1,0:T(8,128)(2,1)}) fusion(f32[1024,3072]{1,0:T(8,128)} %get-tuple-element.166, f32[3072]{0:T(1024)S(1)} %copy-done.25, bf16[3072,768]{1,0:T(8,128)(2,1)} %reshape.483, f32[1024,768]{1,0:T(8,128)} %copy-done.5), kind=kOutput, calls=%fused_computation.232 | convolution fusion | flops 4870370304 | bytes 26757120 | tf_op jit(solution)/shard_map/dot_general | solution.py:27
  313.3 10.1 %convolution_convert_fusion.1 = bf16[768,3072]{1,0:T(8,128)(2,1)} fusion(bf16[1024,3072]{1,0:T(8,128)(2,1)} %get-tuple-element.171, f32[1024,768]{1,0:T(8,128)S(1)} %copy-done.3, f32[768]{0:T(1024)S(1)} %copy-done.26, f32[768]{0:T(1024)S(1)} %get-tuple-element.45, f32[1024]{0:T(1024)S(1)} %add_rsqrt_fusion.1, f32[1024]{0:T(1024)S(1)} %broadcast_multiply_fusion.4), kind=kOutput, calls=%fused_computation.12 | convolution fusion | flops 4838129664 | bytes 14170112 | tf_op jit(solution)/shard_map/dot_general | solution.py:21
  323.4 8.1 %multiply_reduce_fusion = (bf16[768]{0:T(1024)(128)(2,1)S(1)}, f32[1024]{0:T(1024)S(1)}, f32[1024]{0:T(1024)S(1)}, bf16[768]{0:T(1024)(128)(2,1)S(1)}, f32[1024,768]{1,0:T(8,128)S(1)}) fusion(f32[1024,768]{1,0:T(8,128)S(1)} %copy-done.3, f32[1024]{0:T(1024)S(1)} %add_rsqrt_fusion.1, f32[1024]{0:T(1024)S(1)} %broadcast_multiply_fusion.4, ...), kind=kOutput, calls=%fused_computation.41 | convolution fusion | flops 4839698432 | bytes 20470784 | tf_op jit(solution)/shard_map/dot_general | solution.py:27
  331.6 2.3 fusion.57
  340.5 17.8 %concatenate.156 = bf16[768,7168]{1,0:T(8,128)(2,1)} concatenate(bf16[768,768]{1,0:T(8,128)(2,1)S(1)} %bitcast.267, bf16[768,3072]{1,0:T(8,128)(2,1)} %convolution_convert_fusion.1, bf16[768,3072]{1,0:T(8,128)(2,1)} %convert_element_type.332, bf16[768,1]{1,0:T(8,128)(2,1)S(1)} %convert_element_type.364, bf16[768,1]{1,0:T(8,128)(2,1)} %convert_element_type.365, ...), dimensions={1} | concatenate | bytes 22020096 | tf_op jit(solution)/shard_map/concatenate | solution.py:74
  358.3 1.9 convolution_convert_fusion.6
  363.5 2.6 collective-permute-start.26
  373.2 2.5 collective-permute-start.37
  376.5 14.7 %shard_map.309 = bf16[1024,576]{1,0:T(8,128)(2,1)} custom-call(bf16[1024,576]{1,0:T(8,128)(2,1)} %pad_maximum_fusion.2.qkv_ref, s32[1024,1]{1,0:T(8,128)} %copy.260.seg_col_ref, s32[1,1024]{1,0:T(1,128)} %bitcast.329, f32[1024,3]{1,0:T(8,128)} %get-tuple-element.31.lse_ref, bf16[1024,192]{1,0:T(8,128)(2,1)} %pad_maximum_fusion.8.up_ref), custom_call_target="tpu_custom_call" | custom-call | flops 2013265920 | bytes 2949120 | tf_op jit(solution)/shard_map/pallas_call | solution.py:153
  391.2 2.3 fusion.58
  393.5 2.4 collective-permute-start.38
  397.6 14.6 %shard_map.310 = bf16[1024,576]{1,0:T(8,128)(2,1)} custom-call(bf16[1024,576]{1,0:T(8,128)(2,1)} %pad_maximum_fusion.3.qkv_ref, s32[1024,1]{1,0:T(8,128)} %copy.269.seg_col_ref, s32[1,1024]{1,0:T(1,128)} %bitcast.326, f32[1024,3]{1,0:T(8,128)} %get-tuple-element.33.lse_ref, bf16[1024,192]{1,0:T(8,128)(2,1)} %pad_maximum_fusion.9.up_ref), custom_call_target="tpu_custom_call" | custom-call | flops 2013265920 | bytes 2949120 | tf_op jit(solution)/shard_map/pallas_call | solution.py:153
  412.2 2.3 fusion.59
  415.1 2.3 collective-permute-start.44
  420.5 14.6 %shard_map.311 = bf16[1024,576]{1,0:T(8,128)(2,1)} custom-call(bf16[1024,576]{1,0:T(8,128)(2,1)} %pad_maximum_fusion.4.qkv_ref, s32[1024,1]{1,0:T(8,128)} %copy.278.seg_col_ref, s32[1,1024]{1,0:T(1,128)} %bitcast.323, f32[1024,3]{1,0:T(8,128)} %get-tuple-element.34.lse_ref, bf16[1024,192]{1,0:T(8,128)(2,1)} %pad_maximum_fusion.10.up_ref), custom_call_target="tpu_custom_call" | custom-call | flops 2013265920 | bytes 2949120 | tf_op jit(solution)/shard_map/pallas_call | solution.py:153
  435.1 2.3 fusion.60
  438.4 2.0 collective-permute-start.29
  442.8 14.7 %shard_map.312 = bf16[1024,576]{1,0:T(8,128)(2,1)} custom-call(bf16[1024,576]{1,0:T(8,128)(2,1)} %pad_maximum_fusion.5.qkv_ref, s32[1024,1]{1,0:T(8,128)} %copy.287.seg_col_ref, s32[1,1024]{1,0:T(1,128)} %bitcast.320, f32[1024,3]{1,0:T(8,128)} %get-tuple-element.35.lse_ref, bf16[1024,192]{1,0:T(8,128)(2,1)} %pad_maximum_fusion.11.up_ref), custom_call_target="tpu_custom_call" | custom-call | flops 2013265920 | bytes 2949120 | tf_op jit(solution)/shard_map/pallas_call | solution.py:153
  457.5 2.3 fusion.61
  467.7 2.5 collective-permute-start.39
  479.4 2.8 collective-permute-start.45
  501.1 2.4 reduce.13
  515.8 7.4 fusion.6
  524.0 6.8 concatenate.162
  530.7 5.1 copy.336
  535.9 2.8 copy.356
  538.8 46.2 %reduce-scatter.10.cloned.1.call-done = bf16[24,10240]{1,0:T(8,128)(2,1)} async-done(((bf16[192,10240]{1,0:T(8,128)(2,1)}), bf16[24,10240]{1,0:T(8,128)(2,1)}) %reduce-scatter.10.cloned.1.call-update) | async-done | bytes 491536
  585.0 2.2 reshape.533
  587.2 1.9 copy.337
  591.3 9.8 %convolution_add_fusion.4 = f32[1024,768]{1,0:T(8,128)} fusion(f32[1024,768]{1,0:T(8,128)} %get-tuple-element.67, bf16[256,2304]{0,1:T(8,128)(2,1)S(1)} %bitcast.274, bf16[256,2304]{0,1:T(8,128)(2,1)} %bitcast.118, bf16[256,2304]{0,1:T(8,128)(2,1)S(1)} %bitcast.278, bf16[256,2304]{0,1:T(8,128)(2,1)S(1)} %bitcast.276, ...), kind=kOutput, calls=%fused_computation.59 | convolution fusion | flops 3643539456 | bytes 14548992 | tf_op jit(solution)/shard_map/dot_general | solution.py:27
  601.1 11.3 %reduce-scatter.12.cloned.1.call-done = bf16[24,2560]{1,0:T(8,128)(2,1)} async-done(((bf16[96,2560]{1,0:T(8,128)(2,1)}), bf16[24,2560]{1,0:T(8,128)(2,1)}) %reduce-scatter.12.cloned.1.call-update) | async-done | bytes 122896
  614.8 147.4 %reduce-scatter.8.cloned.1.call-done = bf16[24,7168]{1,0:T(8,128)(2,1)} async-done(((bf16[768,7168]{1,0:T(8,128)(2,1)}), bf16[24,7168]{1,0:T(8,128)(2,1)}) %reduce-scatter.8.cloned.1.call-update) | async-done | bytes 344080 | tf_op jit(solution)/shard_map/reduce_scatter | solution.py:327
  (345 shorter events, 174.8 us)
Async XLA Ops:
  7.2 14.4 %copy-start.29 = (s32[4,17]{1,0:T(4,128)S(1)}, s32[4,17]{1,0:T(4,128)}, u32[]{:S(2)}) copy-start(s32[4,17]{1,0:T(4,128)} %param.20) | copy-start | bytes 820
  7.2 19.0 %copy-start = (bf16[4,256,768]{2,1,0:T(8,128)(2,1)S(1)}, bf16[4,256,768]{2,1,0:T(8,128)(2,1)}, u32[]{:S(2)}) copy-start(bf16[4,256,768]{2,1,0:T(8,128)(2,1)} %param.19) | copy-start | bytes 4718596
  7.2 74.1 %all-gather.3.cloned.1.call-start = ((), (), s32[]{:S(2)}) async-start(), calls=%async_computation.3 | async-start | bytes 3852288 | tf_op jit(solution)/shard_map/all_gather | solution.py:219
  17.7 222.0 %all-gather.5.cloned.1.call-start = ((), (), s32[]{:S(2)}) async-start(), calls=%async_computation.4 | async-start | bytes 10948608 | tf_op jit(solution)/shard_map/all_gather | solution.py:220
  21.4 563.6 %reduce-scatter.10.cloned.1.call-start = ((), (), s32[]{:S(2)}) async-start(), calls=%async_computation.6 | async-start | bytes 4423680
  24.1 61.2 %copy-start.22 = (s32[1024]{0:T(1024)}, s32[1024]{0:T(1024)S(1)}, u32[]{:S(2)}) copy-start(s32[1024]{0:T(1024)S(1)} %pad_add_fusion.2) | copy-start | bytes 12292
  25.2 60.1 %copy-start.21 = (s32[1024]{0:T(1024)}, s32[1024]{0:T(1024)S(1)}, u32[]{:S(2)}) copy-start(s32[1024]{0:T(1024)S(1)} %pad_add_fusion.3) | copy-start | bytes 12292
  100.7 12.7 %collective-permute-start = (bf16[256,3,192]{0,2,1:T(8,128)(2,1)S(1)}, bf16[256,3,192]{0,2,1:T(8,128)(2,1)S(1)}, u32[]{:S(2)}, u32[]{:S(2)}) collective-permute-start(bf16[256,3,192]{0,2,1:T(8,128)(2,1)S(1)} %get-tuple-element.87), channel_id=1, source_target_pairs={{0,8},{8,16},{16,24},{24,0},{1,9},{9,17},{17,25},{25,1},{2,10},{10... | collective-permute-start | bytes 884744 | tf_op jit(solution)/shard_map/ppermute | solution.py:255
  102.0 20.7 %collective-permute-start.1 = (bf16[256,3,192]{0,2,1:T(8,128)(2,1)S(1)}, bf16[256,3,192]{0,2,1:T(8,128)(2,1)S(1)}, u32[]{:S(2)}, u32[]{:S(2)}) collective-permute-start(bf16[256,3,192]{0,2,1:T(8,128)(2,1)S(1)} %get-tuple-element.86), channel_id=1, source_target_pairs={{0,16},{8,24},{16,0},{24,8},{1,17},{9,25},{17,1},{25,9},{2,18},{10... | collective-permute-start | bytes 884744 | tf_op jit(solution)/shard_map/ppermute | solution.py:255
  102.7 27.4 %collective-permute-start.2 = (bf16[256,3,192]{0,2,1:T(8,128)(2,1)}, bf16[256,3,192]{0,2,1:T(8,128)(2,1)}, u32[]{:S(2)}, u32[]{:S(2)}) collective-permute-start(bf16[256,3,192]{0,2,1:T(8,128)(2,1)} %get-tuple-element.88), channel_id=1, source_target_pairs={{0,24},{8,0},{16,8},{24,16},{1,25},{9,1},{17,9},{25,17},{2,26},{10... | collective-permute-start | bytes 884744 | tf_op jit(solution)/shard_map/ppermute | solution.py:255
  107.2 26.5 %collective-permute-start.6 = (bf16[256,3,192]{0,2,1:T(8,128)(2,1)}, bf16[256,3,192]{0,2,1:T(8,128)(2,1)}, u32[]{:S(2)}, u32[]{:S(2)}) collective-permute-start(bf16[256,3,192]{0,2,1:T(8,128)(2,1)} %get-tuple-element.91), channel_id=1, source_target_pairs={{0,8},{8,16},{16,24},{24,0},{1,9},{9,17},{17,25},{25,1},{2,10},{10... | collective-permute-start | bytes 884744 | tf_op jit(solution)/shard_map/ppermute | solution.py:255
  107.2 30.0 %collective-permute-start.7 = (bf16[256,3,192]{0,2,1:T(8,128)(2,1)}, bf16[256,3,192]{0,2,1:T(8,128)(2,1)}, u32[]{:S(2)}, u32[]{:S(2)}) collective-permute-start(bf16[256,3,192]{0,2,1:T(8,128)(2,1)} %get-tuple-element.90), channel_id=1, source_target_pairs={{0,16},{8,24},{16,0},{24,8},{1,17},{9,25},{17,1},{25,9},{2,18},{10... | collective-permute-start | bytes 884744 | tf_op jit(solution)/shard_map/ppermute | solution.py:255
  113.4 26.7 %collective-permute-start.8 = (bf16[256,3,192]{0,2,1:T(8,128)(2,1)}, bf16[256,3,192]{0,2,1:T(8,128)(2,1)}, u32[]{:S(2)}, u32[]{:S(2)}) collective-permute-start(bf16[256,3,192]{0,2,1:T(8,128)(2,1)} %get-tuple-element.92), channel_id=1, source_target_pairs={{0,24},{8,0},{16,8},{24,16},{1,25},{9,1},{17,9},{25,17},{2,26},{10... | collective-permute-start | bytes 884744 | tf_op jit(solution)/shard_map/ppermute | solution.py:255
  123.4 23.0 %collective-permute-start.12 = (bf16[256,3,192]{0,2,1:T(8,128)(2,1)}, bf16[256,3,192]{0,2,1:T(8,128)(2,1)}, u32[]{:S(2)}, u32[]{:S(2)}) collective-permute-start(bf16[256,3,192]{0,2,1:T(8,128)(2,1)} %get-tuple-element.95), channel_id=1, source_target_pairs={{0,8},{8,16},{16,24},{24,0},{1,9},{9,17},{17,25},{25,1},{2,10},{10... | collective-permute-start | bytes 884744 | tf_op jit(solution)/shard_map/ppermute | solution.py:255
  130.1 32.7 %collective-permute-start.13 = (bf16[256,3,192]{0,2,1:T(8,128)(2,1)}, bf16[256,3,192]{0,2,1:T(8,128)(2,1)}, u32[]{:S(2)}, u32[]{:S(2)}) collective-permute-start(bf16[256,3,192]{0,2,1:T(8,128)(2,1)} %get-tuple-element.94), channel_id=1, source_target_pairs={{0,16},{8,24},{16,0},{24,8},{1,17},{9,25},{17,1},{25,9},{2,18},{10... | collective-permute-start | bytes 884744 | tf_op jit(solution)/shard_map/ppermute | solution.py:255
  133.7 34.0 %collective-permute-start.14 = (bf16[256,3,192]{0,2,1:T(8,128)(2,1)}, bf16[256,3,192]{0,2,1:T(8,128)(2,1)}, u32[]{:S(2)}, u32[]{:S(2)}) collective-permute-start(bf16[256,3,192]{0,2,1:T(8,128)(2,1)} %get-tuple-element.96), channel_id=1, source_target_pairs={{0,24},{8,0},{16,8},{24,16},{1,25},{9,1},{17,9},{25,17},{2,26},{10... | collective-permute-start | bytes 884744 | tf_op jit(solution)/shard_map/ppermute | solution.py:255
  137.1 34.2 %collective-permute-start.18 = (bf16[256,3,192]{0,2,1:T(8,128)(2,1)}, bf16[256,3,192]{0,2,1:T(8,128)(2,1)}, u32[]{:S(2)}, u32[]{:S(2)}) collective-permute-start(bf16[256,3,192]{0,2,1:T(8,128)(2,1)} %get-tuple-element.99), channel_id=1, source_target_pairs={{0,8},{8,16},{16,24},{24,0},{1,9},{9,17},{17,25},{25,1},{2,10},{10... | collective-permute-start | bytes 884744 | tf_op jit(solution)/shard_map/ppermute | solution.py:255
  140.1 49.5 %collective-permute-start.19 = (bf16[256,3,192]{0,2,1:T(8,128)(2,1)}, bf16[256,3,192]{0,2,1:T(8,128)(2,1)}, u32[]{:S(2)}, u32[]{:S(2)}) collective-permute-start(bf16[256,3,192]{0,2,1:T(8,128)(2,1)} %get-tuple-element.98), channel_id=1, source_target_pairs={{0,16},{8,24},{16,0},{24,8},{1,17},{9,25},{17,1},{25,9},{2,18},{10... | collective-permute-start | bytes 884744 | tf_op jit(solution)/shard_map/ppermute | solution.py:255
  146.4 46.0 %collective-permute-start.20 = (bf16[256,3,192]{0,2,1:T(8,128)(2,1)}, bf16[256,3,192]{0,2,1:T(8,128)(2,1)}, u32[]{:S(2)}, u32[]{:S(2)}) collective-permute-start(bf16[256,3,192]{0,2,1:T(8,128)(2,1)} %get-tuple-element.100), channel_id=1, source_target_pairs={{0,24},{8,0},{16,8},{24,16},{1,25},{9,1},{17,9},{25,17},{2,26},{10... | collective-permute-start | bytes 884744 | tf_op jit(solution)/shard_map/ppermute | solution.py:255
  162.8 57.9 %collective-permute-start.3 = (bf16[256,192]{1,0:T(8,128)(2,1)}, bf16[256,192]{1,0:T(8,128)(2,1)}, u32[]{:S(2)}, u32[]{:S(2)}) collective-permute-start(bf16[256,192]{1,0:T(8,128)(2,1)} %get-tuple-element.107), channel_id=1, source_target_pairs={{0,24},{8,0},{16,8},{24,16},{1,25},{9,1},{17,9},{25,17},{2,26},{10... | collective-permute-start | bytes 294920 | tf_op jit(solution)/shard_map/ppermute | solution.py:255
  167.7 54.7 %collective-permute-start.4 = (bf16[256,192]{1,0:T(8,128)(2,1)}, bf16[256,192]{1,0:T(8,128)(2,1)}, u32[]{:S(2)}, u32[]{:S(2)}) collective-permute-start(bf16[256,192]{1,0:T(8,128)(2,1)} %get-tuple-element.106), channel_id=1, source_target_pairs={{0,16},{8,24},{16,0},{24,8},{1,17},{9,25},{17,1},{25,9},{2,18},{10... | collective-permute-start | bytes 294920 | tf_op jit(solution)/shard_map/ppermute | solution.py:255
  171.3 52.9 %collective-permute-start.5 = (bf16[256,192]{1,0:T(8,128)(2,1)}, bf16[256,192]{1,0:T(8,128)(2,1)}, u32[]{:S(2)}, u32[]{:S(2)}) collective-permute-start(bf16[256,192]{1,0:T(8,128)(2,1)} %get-tuple-element.105), channel_id=1, source_target_pairs={{0,8},{8,16},{16,24},{24,0},{1,9},{9,17},{17,25},{25,1},{2,10},{10... | collective-permute-start | bytes 294920 | tf_op jit(solution)/shard_map/ppermute | solution.py:255
  177.3 18.6 %copy-start.8 = (bf16[256,576]{1,0:T(8,128)(2,1)S(1)}, bf16[256,576]{1,0:T(8,128)(2,1)}, u32[]{:S(2)}) copy-start(bf16[256,576]{1,0:T(8,128)(2,1)} %copy.276) | copy-start | bytes 884740
  177.3 18.6 %copy-start.9 = (bf16[256,576]{1,0:T(8,128)(2,1)S(1)}, bf16[256,576]{1,0:T(8,128)(2,1)}, u32[]{:S(2)}) copy-start(bf16[256,576]{1,0:T(8,128)(2,1)} %copy.277) | copy-start | bytes 884740
  189.6 35.9 %collective-permute-start.10 = (bf16[256,192]{1,0:T(8,128)(2,1)}, bf16[256,192]{1,0:T(8,128)(2,1)}, u32[]{:S(2)}, u32[]{:S(2)}) collective-permute-start(bf16[256,192]{1,0:T(8,128)(2,1)} %get-tuple-element.110), channel_id=1, source_target_pairs={{0,16},{8,24},{16,0},{24,8},{1,17},{9,25},{17,1},{25,9},{2,18},{10... | collective-permute-start | bytes 294920 | tf_op jit(solution)/shard_map/ppermute | solution.py:255
  192.4 34.2 %collective-permute-start.11 = (bf16[256,192]{1,0:T(8,128)(2,1)}, bf16[256,192]{1,0:T(8,128)(2,1)}, u32[]{:S(2)}, u32[]{:S(2)}) collective-permute-start(bf16[256,192]{1,0:T(8,128)(2,1)} %get-tuple-element.109), channel_id=1, source_target_pairs={{0,8},{8,16},{16,24},{24,0},{1,9},{9,17},{17,25},{25,1},{2,10},{10... | collective-permute-start | bytes 294920 | tf_op jit(solution)/shard_map/ppermute | solution.py:255
  220.7 7.7 collective-permute-start.9
  222.3 9.3 %collective-permute-start.15 = (bf16[256,192]{1,0:T(8,128)(2,1)S(1)}, bf16[256,192]{1,0:T(8,128)(2,1)S(1)}, u32[]{:S(2)}, u32[]{:S(2)}) collective-permute-start(bf16[256,192]{1,0:T(8,128)(2,1)S(1)} %get-tuple-element.115), channel_id=1, source_target_pairs={{0,24},{8,0},{16,8},{24,16},{1,25},{9,1},{17,9},{25,17},{2,26},{10... | collective-permute-start | bytes 294920 | tf_op jit(solution)/shard_map/ppermute | solution.py:255
  224.3 7.6 collective-permute-start.16
  225.5 7.9 %collective-permute-start.17 = (bf16[256,192]{1,0:T(8,128)(2,1)S(1)}, bf16[256,192]{1,0:T(8,128)(2,1)S(1)}, u32[]{:S(2)}, u32[]{:S(2)}) collective-permute-start(bf16[256,192]{1,0:T(8,128)(2,1)S(1)} %get-tuple-element.113), channel_id=1, source_target_pairs={{0,8},{8,16},{16,24},{24,0},{1,9},{9,17},{17,25},{25,1},{2,10},{10... | collective-permute-start | bytes 294920 | tf_op jit(solution)/shard_map/ppermute | solution.py:255
  226.6 7.6 collective-permute-start.21
  228.5 6.2 collective-permute-start.22
  231.7 5.9 collective-permute-start.23
  257.9 12.3 %copy-start.2 = (f32[1024,768]{1,0:T(8,128)S(1)}, f32[1024,768]{1,0:T(8,128)}, u32[]{:S(2)}) copy-start(f32[1024,768]{1,0:T(8,128)} %copy-done.1) | copy-start | bytes 9437188
  289.0 34.4 %slice-start.3 = ((s8[10616832]{0:T(1024)(128)(4,1)}), s8[2228224]{0:T(1024)(128)(4,1)S(1)}, s32[]{:S(2)}) async-start(s8[10616832]{0:T(1024)(128)(4,1)} %bitcast.270), calls=%async_computation.11 | async-start | bytes 4456448
  297.6 15.7 %copy-start.3 = (f32[1024,768]{1,0:T(8,128)S(1)}, f32[1024,768]{1,0:T(8,128)}, u32[]{:S(2)}) copy-start(f32[1024,768]{1,0:T(8,128)} %copy-done.1) | copy-start | bytes 9437188
  297.6 25.8 %slice-start.4 = ((s8[10616832]{0:T(1024)(128)(4,1)}), s8[4194304]{0:T(1024)(128)(4,1)S(1)}, s32[]{:S(2)}) async-start(s8[10616832]{0:T(1024)(128)(4,1)} %bitcast.270), calls=%async_computation.12 | async-start | bytes 8388608
  297.6 25.8 %slice-start.5 = ((s8[10616832]{0:T(1024)(128)(4,1)}), s8[4194304]{0:T(1024)(128)(4,1)S(1)}, s32[]{:S(2)}) async-start(s8[10616832]{0:T(1024)(128)(4,1)} %bitcast.270), calls=%async_computation.13 | async-start | bytes 8388608
  363.1 6.7 collective-permute-start.24
  363.2 8.8 %collective-permute-start.25 = (bf16[256,192]{1,0:T(8,128)(2,1)S(1)}, bf16[256,192]{1,0:T(8,128)(2,1)S(1)}, u32[]{:S(2)}, u32[]{:S(2)}) collective-permute-start(bf16[256,192]{1,0:T(8,128)(2,1)S(1)} %get-tuple-element.122), channel_id=1, source_target_pairs={{0,16},{8,24},{16,0},{24,8},{1,17},{9,25},{17,1},{25,9},{2,18},{10... | collective-permute-start | bytes 294920 | tf_op jit(solution)/shard_map/ppermute | solution.py:255
  363.5 9.7 %collective-permute-start.26 = (bf16[256,192]{1,0:T(8,128)(2,1)S(1)}, bf16[256,192]{1,0:T(8,128)(2,1)S(1)}, u32[]{:S(2)}, u32[]{:S(2)}) collective-permute-start(bf16[256,192]{1,0:T(8,128)(2,1)S(1)} %get-tuple-element.121), channel_id=1, source_target_pairs={{0,24},{8,0},{16,8},{24,16},{1,25},{9,1},{17,9},{25,17},{2,26},{10... | collective-permute-start | bytes 294920 | tf_op jit(solution)/shard_map/ppermute | solution.py:255
  366.2 27.3 %collective-permute-start.30 = (bf16[256,192]{1,0:T(8,128)(2,1)S(1)}, bf16[256,192]{1,0:T(8,128)(2,1)S(1)}, u32[]{:S(2)}, u32[]{:S(2)}) collective-permute-start(bf16[256,192]{1,0:T(8,128)(2,1)S(1)} %get-tuple-element.127), channel_id=1, source_target_pairs={{0,8},{8,16},{16,24},{24,0},{1,9},{9,17},{17,25},{25,1},{2,10},{10... | collective-permute-start | bytes 294920 | tf_op jit(solution)/shard_map/ppermute | solution.py:255
  366.8 29.1 %collective-permute-start.31 = (bf16[256,192]{1,0:T(8,128)(2,1)S(1)}, bf16[256,192]{1,0:T(8,128)(2,1)S(1)}, u32[]{:S(2)}, u32[]{:S(2)}) collective-permute-start(bf16[256,192]{1,0:T(8,128)(2,1)S(1)} %get-tuple-element.126), channel_id=1, source_target_pairs={{0,16},{8,24},{16,0},{24,8},{1,17},{9,25},{17,1},{25,9},{2,18},{10... | collective-permute-start | bytes 294920 | tf_op jit(solution)/shard_map/ppermute | solution.py:255
  369.8 26.3 %collective-permute-start.32 = (bf16[256,192]{1,0:T(8,128)(2,1)S(1)}, bf16[256,192]{1,0:T(8,128)(2,1)S(1)}, u32[]{:S(2)}, u32[]{:S(2)}) collective-permute-start(bf16[256,192]{1,0:T(8,128)(2,1)S(1)} %get-tuple-element.125), channel_id=1, source_target_pairs={{0,24},{8,0},{16,8},{24,16},{1,25},{9,1},{17,9},{25,17},{2,26},{10... | collective-permute-start | bytes 294920 | tf_op jit(solution)/shard_map/ppermute | solution.py:255
  371.9 43.2 %collective-permute-start.36 = (bf16[256,192]{1,0:T(8,128)(2,1)S(1)}, bf16[256,192]{1,0:T(8,128)(2,1)S(1)}, u32[]{:S(2)}, u32[]{:S(2)}) collective-permute-start(bf16[256,192]{1,0:T(8,128)(2,1)S(1)} %get-tuple-element.131), channel_id=1, source_target_pairs={{0,8},{8,16},{16,24},{24,0},{1,9},{9,17},{17,25},{25,1},{2,10},{10... | collective-permute-start | bytes 294920 | tf_op jit(solution)/shard_map/ppermute | solution.py:255
  373.2 44.3 %collective-permute-start.37 = (bf16[256,192]{1,0:T(8,128)(2,1)S(1)}, bf16[256,192]{1,0:T(8,128)(2,1)S(1)}, u32[]{:S(2)}, u32[]{:S(2)}) collective-permute-start(bf16[256,192]{1,0:T(8,128)(2,1)S(1)} %get-tuple-element.130), channel_id=1, source_target_pairs={{0,16},{8,24},{16,0},{24,8},{1,17},{9,25},{17,1},{25,9},{2,18},{10... | collective-permute-start | bytes 294920 | tf_op jit(solution)/shard_map/ppermute | solution.py:255
  393.5 24.6 %collective-permute-start.38 = (bf16[256,192]{1,0:T(8,128)(2,1)S(1)}, bf16[256,192]{1,0:T(8,128)(2,1)S(1)}, u32[]{:S(2)}, u32[]{:S(2)}) collective-permute-start(bf16[256,192]{1,0:T(8,128)(2,1)S(1)} %get-tuple-element.129), channel_id=1, source_target_pairs={{0,24},{8,0},{16,8},{24,16},{1,25},{9,1},{17,9},{25,17},{2,26},{10... | collective-permute-start | bytes 294920 | tf_op jit(solution)/shard_map/ppermute | solution.py:255
  395.9 42.4 %collective-permute-start.42 = (bf16[256,192]{1,0:T(8,128)(2,1)S(1)}, bf16[256,192]{1,0:T(8,128)(2,1)S(1)}, u32[]{:S(2)}, u32[]{:S(2)}) collective-permute-start(bf16[256,192]{1,0:T(8,128)(2,1)S(1)} %get-tuple-element.135), channel_id=1, source_target_pairs={{0,8},{8,16},{16,24},{24,0},{1,9},{9,17},{17,25},{25,1},{2,10},{10... | collective-permute-start | bytes 294920 | tf_op jit(solution)/shard_map/ppermute | solution.py:255
  396.1 44.2 %collective-permute-start.43 = (bf16[256,192]{1,0:T(8,128)(2,1)S(1)}, bf16[256,192]{1,0:T(8,128)(2,1)S(1)}, u32[]{:S(2)}, u32[]{:S(2)}) collective-permute-start(bf16[256,192]{1,0:T(8,128)(2,1)S(1)} %get-tuple-element.134), channel_id=1, source_target_pairs={{0,16},{8,24},{16,0},{24,8},{1,17},{9,25},{17,1},{25,9},{2,18},{10... | collective-permute-start | bytes 294920 | tf_op jit(solution)/shard_map/ppermute | solution.py:255
  415.1 26.2 %collective-permute-start.44 = (bf16[256,192]{1,0:T(8,128)(2,1)S(1)}, bf16[256,192]{1,0:T(8,128)(2,1)S(1)}, u32[]{:S(2)}, u32[]{:S(2)}) collective-permute-start(bf16[256,192]{1,0:T(8,128)(2,1)S(1)} %get-tuple-element.133), channel_id=1, source_target_pairs={{0,24},{8,0},{16,8},{24,16},{1,25},{9,1},{17,9},{25,17},{2,26},{10... | collective-permute-start | bytes 294920 | tf_op jit(solution)/shard_map/ppermute | solution.py:255
  417.4 46.9 %collective-permute-start.27 = (bf16[256,576]{1,0:T(8,128)(2,1)}, bf16[256,576]{1,0:T(8,128)(2,1)}, u32[]{:S(2)}, u32[]{:S(2)}) collective-permute-start(bf16[256,576]{1,0:T(8,128)(2,1)} %get-tuple-element.71), channel_id=1, source_target_pairs={{0,24},{8,0},{16,8},{24,16},{1,25},{9,1},{17,9},{25,17},{2,26},{10... | collective-permute-start | bytes 884744 | tf_op jit(solution)/shard_map/ppermute | solution.py:255
  418.1 49.6 %collective-permute-start.28 = (bf16[256,576]{1,0:T(8,128)(2,1)}, bf16[256,576]{1,0:T(8,128)(2,1)}, u32[]{:S(2)}, u32[]{:S(2)}) collective-permute-start(bf16[256,576]{1,0:T(8,128)(2,1)} %get-tuple-element.70), channel_id=1, source_target_pairs={{0,16},{8,24},{16,0},{24,8},{1,17},{9,25},{17,1},{25,9},{2,18},{10... | collective-permute-start | bytes 884744 | tf_op jit(solution)/shard_map/ppermute | solution.py:255
  438.4 39.0 %collective-permute-start.29 = (bf16[256,576]{1,0:T(8,128)(2,1)}, bf16[256,576]{1,0:T(8,128)(2,1)}, u32[]{:S(2)}, u32[]{:S(2)}) collective-permute-start(bf16[256,576]{1,0:T(8,128)(2,1)} %get-tuple-element.69), channel_id=1, source_target_pairs={{0,8},{8,16},{16,24},{24,0},{1,9},{9,17},{17,25},{25,1},{2,10},{10... | collective-permute-start | bytes 884744 | tf_op jit(solution)/shard_map/ppermute | solution.py:255
  440.3 31.7 %collective-permute-start.33 = (bf16[256,576]{1,0:T(8,128)(2,1)}, bf16[256,576]{1,0:T(8,128)(2,1)}, u32[]{:S(2)}, u32[]{:S(2)}) collective-permute-start(bf16[256,576]{1,0:T(8,128)(2,1)} %get-tuple-element.75), channel_id=1, source_target_pairs={{0,24},{8,0},{16,8},{24,16},{1,25},{9,1},{17,9},{25,17},{2,26},{10... | collective-permute-start | bytes 884744 | tf_op jit(solution)/shard_map/ppermute | solution.py:255
  441.3 38.1 %collective-permute-start.34 = (bf16[256,576]{1,0:T(8,128)(2,1)}, bf16[256,576]{1,0:T(8,128)(2,1)}, u32[]{:S(2)}, u32[]{:S(2)}) collective-permute-start(bf16[256,576]{1,0:T(8,128)(2,1)} %get-tuple-element.74), channel_id=1, source_target_pairs={{0,16},{8,24},{16,0},{24,8},{1,17},{9,25},{17,1},{25,9},{2,18},{10... | collective-permute-start | bytes 884744 | tf_op jit(solution)/shard_map/ppermute | solution.py:255
  464.3 21.6 %collective-permute-start.35 = (bf16[256,576]{1,0:T(8,128)(2,1)}, bf16[256,576]{1,0:T(8,128)(2,1)}, u32[]{:S(2)}, u32[]{:S(2)}) collective-permute-start(bf16[256,576]{1,0:T(8,128)(2,1)} %get-tuple-element.73), channel_id=1, source_target_pairs={{0,8},{8,16},{16,24},{24,0},{1,9},{9,17},{17,25},{25,1},{2,10},{10... | collective-permute-start | bytes 884744 | tf_op jit(solution)/shard_map/ppermute | solution.py:255
  467.7 20.7 %collective-permute-start.39 = (bf16[256,576]{1,0:T(8,128)(2,1)}, bf16[256,576]{1,0:T(8,128)(2,1)}, u32[]{:S(2)}, u32[]{:S(2)}) collective-permute-start(bf16[256,576]{1,0:T(8,128)(2,1)} %get-tuple-element.79), channel_id=1, source_target_pairs={{0,24},{8,0},{16,8},{24,16},{1,25},{9,1},{17,9},{25,17},{2,26},{10... | collective-permute-start | bytes 884744 | tf_op jit(solution)/shard_map/ppermute | solution.py:255
  472.1 21.0 %collective-permute-start.40 = (bf16[256,576]{1,0:T(8,128)(2,1)}, bf16[256,576]{1,0:T(8,128)(2,1)}, u32[]{:S(2)}, u32[]{:S(2)}) collective-permute-start(bf16[256,576]{1,0:T(8,128)(2,1)} %get-tuple-element.78), channel_id=1, source_target_pairs={{0,16},{8,24},{16,0},{24,8},{1,17},{9,25},{17,1},{25,9},{2,18},{10... | collective-permute-start | bytes 884744 | tf_op jit(solution)/shard_map/ppermute | solution.py:255
  477.4 17.5 %collective-permute-start.41 = (bf16[256,576]{1,0:T(8,128)(2,1)}, bf16[256,576]{1,0:T(8,128)(2,1)}, u32[]{:S(2)}, u32[]{:S(2)}) collective-permute-start(bf16[256,576]{1,0:T(8,128)(2,1)} %get-tuple-element.77), channel_id=1, source_target_pairs={{0,8},{8,16},{16,24},{24,0},{1,9},{9,17},{17,25},{25,1},{2,10},{10... | collective-permute-start | bytes 884744 | tf_op jit(solution)/shard_map/ppermute | solution.py:255
  479.4 24.0 %collective-permute-start.45 = (bf16[256,576]{1,0:T(8,128)(2,1)}, bf16[256,576]{1,0:T(8,128)(2,1)}, u32[]{:S(2)}, u32[]{:S(2)}) collective-permute-start(bf16[256,576]{1,0:T(8,128)(2,1)} %get-tuple-element.83), channel_id=1, source_target_pairs={{0,24},{8,0},{16,8},{24,16},{1,25},{9,1},{17,9},{25,17},{2,26},{10... | collective-permute-start | bytes 884744 | tf_op jit(solution)/shard_map/ppermute | solution.py:255
  486.0 19.3 %collective-permute-start.46 = (bf16[256,576]{1,0:T(8,128)(2,1)}, bf16[256,576]{1,0:T(8,128)(2,1)}, u32[]{:S(2)}, u32[]{:S(2)}) collective-permute-start(bf16[256,576]{1,0:T(8,128)(2,1)} %get-tuple-element.82), channel_id=1, source_target_pairs={{0,16},{8,24},{16,0},{24,8},{1,17},{9,25},{17,1},{25,9},{2,18},{10... | collective-permute-start | bytes 884744 | tf_op jit(solution)/shard_map/ppermute | solution.py:255
  488.5 20.6 %collective-permute-start.47 = (bf16[256,576]{1,0:T(8,128)(2,1)}, bf16[256,576]{1,0:T(8,128)(2,1)}, u32[]{:S(2)}, u32[]{:S(2)}) collective-permute-start(bf16[256,576]{1,0:T(8,128)(2,1)} %get-tuple-element.81), channel_id=1, source_target_pairs={{0,8},{8,16},{16,24},{24,0},{1,9},{9,17},{17,25},{25,1},{2,10},{10... | collective-permute-start | bytes 884744 | tf_op jit(solution)/shard_map/ppermute | solution.py:255
  538.8 73.7 %reduce-scatter.12.cloned.1.call-start = ((), (), s32[]{:S(2)}) async-start(), calls=%async_computation.7 | async-start | bytes 614400
  589.1 173.2 %reduce-scatter.8.cloned.1.call-start = ((), (), s32[]{:S(2)}) async-start(), calls=%async_computation.5 | async-start | bytes 11354112 | tf_op jit(solution)/shard_map/reduce_scatter | solution.py:327
  (28 other events, 159.5 us)
Sparse Core Ops, SparseCore 0:
  17.8 63.4 all-gather.2
  84.3 114.2 all-gather.4
  538.9 46.1 reduce-scatter.9
  589.2 23.1 reduce-scatter.11
  618.3 143.9 reduce-scatter.7

commit v12 on v10

--- a/solution.py
+++ b/solution.py
@@ -162,11 +162,8 @@
 
 
 def scatter_two_stage(block):
-    outer = lax.axis_size("seq")
-    part = lax.psum_scatter(
-        block.reshape(outer, block.shape[0] // outer, -1), "shard", scatter_dimension=1, tiled=True
-    )
-    return lax.psum_scatter(part.reshape(-1, block.shape[1]), "seq", scatter_dimension=0, tiled=True)
+    part = lax.psum_scatter(block, "seq", scatter_dimension=0, tiled=True)
+    return lax.psum_scatter(part, "shard", scatter_dimension=0, tiled=True)
 
 
 def per_device(

time: 764 us -> 766 us (level)
  waiting for transfers between devices: 282 us -> 295 us
  local copies, waits for them, and re-layouts: 158 us -> 147 us
    reduce_scatter x0 -> x2, waiting for transfers between devices: none -> 74.5 us  [the longest x1 49.8 us: scatter_two_stage(): part = lax.psum_scatter(block, 'seq', scatter_dimension=0, tiled=True)]
    unnamed x7 -> x5, waiting for transfers between devices: 60.1 us -> 0.43 us
    unnamed x93 -> x89, local copies, waits for them, and re-layouts: 23.3 us -> 13 us
where the time goes in v12:
time: 766 us; the launch traced here: 755 us
  waiting for transfers between devices  295 us (39%)
  local copies, waits for them, and re-layouts  147 us (19%)
  Pallas kernels  100 us (13%)
  matrix products  81 us (11%)
  starting transfers between devices  58.6 us (8%)
  other arithmetic  57.8 us (8%)
  between operations  15.1 us (2%)
    reduce_scatter x1, waiting for transfers between devices, per_device(): lax.psum_scatter(early, axes, scatter_dimension=0, tiled=True)  146 us
    pallas_call x4, Pallas kernels, attention_backward(): pl.pallas_call(attention_backward_kernel, out_shape=jax.ShapeDtypeStruct(...  58.5 us
    ppermute x48, starting transfers between devices, send(): out.append(lax.ppermute(blocks[k], 'seq', pairs))  58.3 us
    all_gather x1, waiting for transfers between devices, per_device(): full_first = lax.all_gather(first, axes, axis=0, tiled=True)  54 us
    reduce_scatter x1, waiting for transfers between devices, scatter_two_stage(): part = lax.psum_scatter(block, 'seq', scatter_dimension=0, tiled=True)  49.8 us
    pallas_call x4, Pallas kernels, attention_forward(): pl.pallas_call(attention_forward_kernel, out_shape=(jax.ShapeDtypeStruct(...  42 us
    dot_general x7, matrix products, times_transpose(): lax.dot_general(left, right, (((1,), (1,)), ((), ())), preferred_element_...  35.3 us
    reduce_scatter x1, waiting for transfers between devices, scatter_two_stage(): return lax.psum_scatter(part, 'shard', scatter_dimension=0, tiled=True)  24.6 us
  transfers between devices with their start and end apart: 53, of which 15 were waited for; matrix products, arithmetic and copies ran while one was open for 16% of the time, Pallas kernels for 13%

profile of v12, /device:TPU:0, one launch (start us, length us, event | category | flops | bytes accessed | tf_op | source)
XLA Modules:
  0.0 755.5 jit_solution(12969964062750514678)
XLA Ops:
  27.3 54.0 %all-gather.3.cloned.1.call-done = bf16[768,2316]{1,0:T(8,128)(2,1)} async-done(((bf16[24,2316]{1,0:T(8,128)(2,1)}), bf16[768,2316]{1,0:T(8,128)(2,1)}) %all-gather.3.cloned.1.call-update) | async-done | bytes 3557392 | tf_op jit(solution)/shard_map/all_gather | solution.py:216
  81.3 4.0 slice.428
  85.3 5.7 copy.300
  91.0 3.7 convert_reduce_fusion.2
  95.0 3.4 fusion.16
  102.4 2.4 collective-permute-start.2
  113.1 2.5 collective-permute-start.8
  115.6 6.8 collective-permute-done.1
  127.9 1.9 copy.234
  130.9 1.9 copy.235
  133.4 2.3 collective-permute-start.14
  136.9 1.9 copy.244
  140.3 1.9 copy.245
  142.2 3.9 collective-permute-done.12
  147.8 2.5 pad_maximum_fusion.2.qkv_ref
  150.3 10.3 %shard_map.305 = (bf16[1024,192]{1,0:T(8,128)(2,1)}, f32[1024,3]{1,0:T(8,128)}) custom-call(bf16[1024,576]{1,0:T(8,128)(2,1)} %pad_maximum_fusion.2.qkv_ref, s32[1024,1]{1,0:T(8,128)} %copy.237.seg_col_ref, s32[1,1024]{1,0:T(1,128)} %bitcast.294), custom_call_target="tpu_custom_call" | custom-call | flops 805306368 | bytes 1769472 | tf_op jit(solution)/shard_map/pallas_call | solution.py:135
  160.6 1.9 fusion.67
  162.5 2.7 collective-permute-start.3
  167.3 1.9 copy.254
  172.5 1.9 copy.261
  174.3 2.3 pad_maximum_fusion.3.qkv_ref
  176.6 10.5 %shard_map.306 = (bf16[1024,192]{1,0:T(8,128)(2,1)}, f32[1024,3]{1,0:T(8,128)}) custom-call(bf16[1024,576]{1,0:T(8,128)(2,1)} %pad_maximum_fusion.3.qkv_ref, s32[1024,1]{1,0:T(8,128)} %copy.246.seg_col_ref, s32[1,1024]{1,0:T(1,128)} %bitcast.291), custom_call_target="tpu_custom_call" | custom-call | flops 805306368 | bytes 1769472 | tf_op jit(solution)/shard_map/pallas_call | solution.py:135
  189.8 1.9 copy.262
  193.5 1.9 copy.263
  196.6 10.6 %shard_map.307 = (bf16[1024,192]{1,0:T(8,128)(2,1)}, f32[1024,3]{1,0:T(8,128)}) custom-call(bf16[1024,576]{1,0:T(8,128)(2,1)} %pad_maximum_fusion.4.qkv_ref, s32[1024,1]{1,0:T(8,128)} %copy.255.seg_col_ref, s32[1,1024]{1,0:T(1,128)} %bitcast.288), custom_call_target="tpu_custom_call" | custom-call | flops 805306368 | bytes 1769472 | tf_op jit(solution)/shard_map/pallas_call | solution.py:135
  208.4 10.6 %shard_map.308 = (bf16[1024,192]{1,0:T(8,128)(2,1)}, f32[1024,3]{1,0:T(8,128)}) custom-call(bf16[1024,576]{1,0:T(8,128)(2,1)} %pad_maximum_fusion.5.qkv_ref, s32[1024,1]{1,0:T(8,128)} %copy.264.seg_col_ref, s32[1,1024]{1,0:T(1,128)} %bitcast.285), custom_call_target="tpu_custom_call" | custom-call | flops 805306368 | bytes 1769472 | tf_op jit(solution)/shard_map/pallas_call | solution.py:135
  221.7 1.9 collective-permute-start.15
  227.9 1.9 collective-permute-start.22
  234.1 2.7 collective-permute-done.23
  245.7 2.9 slice.457
  248.6 8.5 %reshape.454 = bf16[3072,768]{1,0:T(8,128)(2,1)} reshape(bf16[768,3072]{1,0:T(8,128)(2,1)} %slice.457) | data formatting | bytes 9437184 | tf_op jit(solution)/shard_map/reshape | solution.py:222
  257.1 12.3 %multiply_convert_fusion = (bf16[1024,3072]{1,0:T(8,128)(2,1)S(1)}, f32[1024,3072]{1,0:T(8,128)}) fusion(f32[3072]{0:T(1024)S(1)} %copy-done.32, bf16[768,6912]{1,0:T(8,128)(2,1)} %all-gather.5.cloned.1.call-done, f32[1024,768]{1,0:T(8,128)} %copy-done.1, f32[768]{0:T(1024)S(1)} %copy-done.33, f32[768]{0:T(1024)S(1)} %get-tuple-element.46, ...), kind=kOutput, calls=%fused_computation.9 | convolution fusion | flops 4854644736 | bytes 26765312 | tf_op jit(solution)/shard_map/dot_general | solution.py:285
  269.4 5.5 fusion.80
  275.4 2.8 fusion.23
  281.5 7.1 convolution_convert_fusion
  288.6 8.5 %convert_element_type.348 = bf16[768,3072]{1,0:T(8,128)(2,1)} reshape(bf16[3072,768]{1,0:T(8,128)(2,1)} %convolution_convert_fusion) | data formatting | bytes 9437184 | tf_op jit(solution)/shard_map/convert_element_type | solution.py:70
  297.0 13.0 %fusion.81 = (bf16[3072]{0:T(1024)(128)(2,1)S(1)}, bf16[1024,3072]{1,0:T(8,128)(2,1)S(1)}) fusion(f32[1024,3072]{1,0:T(8,128)} %get-tuple-element.167, f32[3072]{0:T(1024)S(1)} %copy-done.32, bf16[3072,768]{1,0:T(8,128)(2,1)} %reshape.454, f32[1024,768]{1,0:T(8,128)} %copy-done.8), kind=kOutput, calls=%fused_computation.224 | convolution fusion | flops 4870370304 | bytes 26757120 | tf_op jit(solution)/shard_map/dot_general | solution.py:27
  310.0 8.1 %convolution_convert_fusion.1 = bf16[768,3072]{1,0:T(8,128)(2,1)} fusion(bf16[1024,3072]{1,0:T(8,128)(2,1)S(1)} %get-tuple-element.172, f32[1024,768]{1,0:T(8,128)S(1)} %copy-done.3, f32[768]{0:T(1024)S(1)} %copy-done.33, f32[768]{0:T(1024)S(1)} %get-tuple-element.46, f32[1024]{0:T(1024)S(1)} %add_rsqrt_fusion.1, f32[1024]{0:T(1024)S(1)} %broadcast_multiply_fusion.4), kind=kOutput, calls=%fused_computation.17 | convolution fusion | flops 4838129664 | bytes 14170112 | tf_op jit(solution)/shard_map/dot_general | solution.py:21
  318.1 8.4 %multiply_reduce_fusion = (bf16[768]{0:T(1024)(128)(2,1)S(1)}, f32[1024]{0:T(1024)S(1)}, f32[1024]{0:T(1024)S(1)}, bf16[768]{0:T(1024)(128)(2,1)S(1)}, f32[1024,768]{1,0:T(8,128)S(1)}) fusion(f32[1024,768]{1,0:T(8,128)S(1)} %copy-done.3, f32[1024]{0:T(1024)S(1)} %add_rsqrt_fusion.1, f32[1024]{0:T(1024)S(1)} %broadcast_multiply_fusion.4, ...), kind=kOutput, calls=%fused_computation.44 | convolution fusion | flops 4839698432 | bytes 20469760 | tf_op jit(solution)/shard_map/dot_general | solution.py:27
  326.6 2.3 fusion.58
  335.4 17.8 %concatenate.158 = bf16[768,7168]{1,0:T(8,128)(2,1)} concatenate(bf16[768,768]{1,0:T(8,128)(2,1)S(1)} %bitcast.229, bf16[768,3072]{1,0:T(8,128)(2,1)} %convolution_convert_fusion.1, bf16[768,3072]{1,0:T(8,128)(2,1)} %convert_element_type.348, bf16[768,1]{1,0:T(8,128)(2,1)S(1)} %convert_element_type.380, bf16[768,1]{1,0:T(8,128)(2,1)} %convert_element_type.381, ...), dimensions={1} | concatenate | bytes 22020096 | tf_op jit(solution)/shard_map/concatenate | solution.py:74
  353.2 1.9 convolution_convert_fusion.5
  358.6 2.7 collective-permute-start.26
  365.0 2.1 collective-permute-start.32
  368.2 2.5 collective-permute-start.37
  371.6 14.6 %shard_map.309 = bf16[1024,576]{1,0:T(8,128)(2,1)} custom-call(bf16[1024,576]{1,0:T(8,128)(2,1)} %pad_maximum_fusion.2.qkv_ref, s32[1024,1]{1,0:T(8,128)} %copy.237.seg_col_ref, s32[1,1024]{1,0:T(1,128)} %bitcast.295, f32[1024,3]{1,0:T(8,128)} %get-tuple-element.32.lse_ref, bf16[1024,192]{1,0:T(8,128)(2,1)} %pad_maximum_fusion.10.up_ref), custom_call_target="tpu_custom_call" | custom-call | flops 2013265920 | bytes 2949120 | tf_op jit(solution)/shard_map/pallas_call | solution.py:153
  388.0 2.1 collective-permute-start.42
  392.0 14.6 %shard_map.310 = bf16[1024,576]{1,0:T(8,128)(2,1)} custom-call(bf16[1024,576]{1,0:T(8,128)(2,1)} %pad_maximum_fusion.3.qkv_ref, s32[1024,1]{1,0:T(8,128)} %copy.246.seg_col_ref, s32[1,1024]{1,0:T(1,128)} %bitcast.292, f32[1024,3]{1,0:T(8,128)} %get-tuple-element.34.lse_ref, bf16[1024,192]{1,0:T(8,128)(2,1)} %pad_maximum_fusion.11.up_ref), custom_call_target="tpu_custom_call" | custom-call | flops 2013265920 | bytes 2949120 | tf_op jit(solution)/shard_map/pallas_call | solution.py:153
  406.6 2.2 fusion.60
  408.8 2.9 collective-permute-start.44
  413.6 1.9 pad_maximum_fusion.12.up_ref
  415.4 14.6 %shard_map.311 = bf16[1024,576]{1,0:T(8,128)(2,1)} custom-call(bf16[1024,576]{1,0:T(8,128)(2,1)} %pad_maximum_fusion.4.qkv_ref, s32[1024,1]{1,0:T(8,128)} %copy.255.seg_col_ref, s32[1,1024]{1,0:T(1,128)} %bitcast.289, f32[1024,3]{1,0:T(8,128)} %get-tuple-element.35.lse_ref, bf16[1024,192]{1,0:T(8,128)(2,1)} %pad_maximum_fusion.12.up_ref), custom_call_target="tpu_custom_call" | custom-call | flops 2013265920 | bytes 2949120 | tf_op jit(solution)/shard_map/pallas_call | solution.py:153
  430.1 2.2 fusion.61
  436.8 1.9 pad_maximum_fusion.13.up_ref
  440.9 14.7 %shard_map.312 = bf16[1024,576]{1,0:T(8,128)(2,1)} custom-call(bf16[1024,576]{1,0:T(8,128)(2,1)} %pad_maximum_fusion.5.qkv_ref, s32[1024,1]{1,0:T(8,128)} %copy.264.seg_col_ref, s32[1,1024]{1,0:T(1,128)} %bitcast.286, f32[1024,3]{1,0:T(8,128)} %get-tuple-element.36.lse_ref, bf16[1024,192]{1,0:T(8,128)(2,1)} %pad_maximum_fusion.13.up_ref), custom_call_target="tpu_custom_call" | custom-call | flops 2013265920 | bytes 2949120 | tf_op jit(solution)/shard_map/pallas_call | solution.py:153
  457.9 2.2 fusion.62
  486.0 5.3 fusion.56
  492.1 5.1 fusion.7
  497.2 5.8 copy.296
  503.1 6.6 concatenate.165
  509.8 49.8 %reduce-scatter.4.cloned.1.call-done = bf16[192,2560]{1,0:T(8,128)(2,1)} async-done(((bf16[768,2560]{1,0:T(8,128)(2,1)}), bf16[192,2560]{1,0:T(8,128)(2,1)}) %reduce-scatter.4.cloned.1.call-update) | async-done | bytes 983056 | tf_op jit(solution)/shard_map/reduce_scatter | solution.py:165
  560.3 9.3 %convolution_add_fusion.4 = f32[1024,768]{1,0:T(8,128)} fusion(f32[1024,768]{1,0:T(8,128)} %get-tuple-element.68, bf16[768,2304]{0,1:T(8,128)(2,1)} %bitcast.249, bf16[256,2304]{0,1:T(8,128)(2,1)} %bitcast.241, bf16[256,2304]{0,1:T(8,128)(2,1)} %bitcast.236, bf16[256,2304]{0,1:T(8,128)(2,1)S(1)} %bitcast.235, bf16[256,2304]{0,1:T(8,128)(2,1)S(1)} %bitcast.232), kind=kOutput, calls=%fused_computation.62 | convolution fusion | flops 3643539456 | bytes 14548992 | tf_op jit(solution)/shard_map/dot_general | solution.py:27
  569.5 24.6 %reduce-scatter.6.cloned.1.call-done = bf16[24,2560]{1,0:T(8,128)(2,1)} async-done(((bf16[192,2560]{1,0:T(8,128)(2,1)}), bf16[24,2560]{1,0:T(8,128)(2,1)}) %reduce-scatter.6.cloned.1.call-update) | async-done | bytes 122896 | tf_op jit(solution)/shard_map/reduce_scatter | solution.py:166
  596.6 145.7 %reduce-scatter.8.cloned.1.call-done = bf16[24,7168]{1,0:T(8,128)(2,1)} async-done(((bf16[768,7168]{1,0:T(8,128)(2,1)}), bf16[24,7168]{1,0:T(8,128)(2,1)}) %reduce-scatter.8.cloned.1.call-update) | async-done | bytes 344080 | tf_op jit(solution)/shard_map/reduce_scatter | solution.py:324
  (338 shorter events, 146.7 us)
Async XLA Ops:
  7.2 14.4 %copy-start.36 = (s32[4,17]{1,0:T(4,128)S(1)}, s32[4,17]{1,0:T(4,128)}, u32[]{:S(2)}) copy-start(s32[4,17]{1,0:T(4,128)} %param.22) | copy-start | bytes 820
  7.2 18.9 %copy-start = (bf16[4,256,768]{2,1,0:T(8,128)(2,1)S(1)}, bf16[4,256,768]{2,1,0:T(8,128)(2,1)}, u32[]{:S(2)}) copy-start(bf16[4,256,768]{2,1,0:T(8,128)(2,1)} %param.21) | copy-start | bytes 4718596
  7.2 74.1 %all-gather.3.cloned.1.call-start = ((), (), s32[]{:S(2)}) async-start(), calls=%async_computation.3 | async-start | bytes 3852288 | tf_op jit(solution)/shard_map/all_gather | solution.py:216
  17.7 221.2 %all-gather.5.cloned.1.call-start = ((), (), s32[]{:S(2)}) async-start(), calls=%async_computation.4 | async-start | bytes 10948608 | tf_op jit(solution)/shard_map/all_gather | solution.py:217
  21.5 538.2 %reduce-scatter.4.cloned.1.call-start = ((), (), s32[]{:S(2)}) async-start(), calls=%async_computation.5 | async-start | bytes 4915200 | tf_op jit(solution)/shard_map/reduce_scatter | solution.py:165
  24.1 61.2 %copy-start.29 = (s32[1024]{0:T(1024)}, s32[1024]{0:T(1024)S(1)}, u32[]{:S(2)}) copy-start(s32[1024]{0:T(1024)S(1)} %pad_add_fusion.2) | copy-start | bytes 12292
  25.1 60.2 %copy-start.28 = (s32[1024]{0:T(1024)}, s32[1024]{0:T(1024)S(1)}, u32[]{:S(2)}) copy-start(s32[1024]{0:T(1024)S(1)} %pad_add_fusion.3) | copy-start | bytes 12292
  100.3 12.8 %collective-permute-start = (bf16[256,3,192]{0,2,1:T(8,128)(2,1)S(1)}, bf16[256,3,192]{0,2,1:T(8,128)(2,1)S(1)}, u32[]{:S(2)}, u32[]{:S(2)}) collective-permute-start(bf16[256,3,192]{0,2,1:T(8,128)(2,1)S(1)} %get-tuple-element.88), channel_id=1, source_target_pairs={{0,8},{8,16},{16,24},{24,0},{1,9},{9,17},{17,25},{25,1},{2,10},{10... | collective-permute-start | bytes 884744 | tf_op jit(solution)/shard_map/ppermute | solution.py:252
  101.7 20.7 %collective-permute-start.1 = (bf16[256,3,192]{0,2,1:T(8,128)(2,1)S(1)}, bf16[256,3,192]{0,2,1:T(8,128)(2,1)S(1)}, u32[]{:S(2)}, u32[]{:S(2)}) collective-permute-start(bf16[256,3,192]{0,2,1:T(8,128)(2,1)S(1)} %get-tuple-element.87), channel_id=1, source_target_pairs={{0,16},{8,24},{16,0},{24,8},{1,17},{9,25},{17,1},{25,9},{2,18},{10... | collective-permute-start | bytes 884744 | tf_op jit(solution)/shard_map/ppermute | solution.py:252
  102.4 27.4 %collective-permute-start.2 = (bf16[256,3,192]{0,2,1:T(8,128)(2,1)}, bf16[256,3,192]{0,2,1:T(8,128)(2,1)}, u32[]{:S(2)}, u32[]{:S(2)}) collective-permute-start(bf16[256,3,192]{0,2,1:T(8,128)(2,1)} %get-tuple-element.89), channel_id=1, source_target_pairs={{0,24},{8,0},{16,8},{24,16},{1,25},{9,1},{17,9},{25,17},{2,26},{10... | collective-permute-start | bytes 884744 | tf_op jit(solution)/shard_map/ppermute | solution.py:252
  106.9 26.5 %collective-permute-start.6 = (bf16[256,3,192]{0,2,1:T(8,128)(2,1)}, bf16[256,3,192]{0,2,1:T(8,128)(2,1)}, u32[]{:S(2)}, u32[]{:S(2)}) collective-permute-start(bf16[256,3,192]{0,2,1:T(8,128)(2,1)} %get-tuple-element.92), channel_id=1, source_target_pairs={{0,8},{8,16},{16,24},{24,0},{1,9},{9,17},{17,25},{25,1},{2,10},{10... | collective-permute-start | bytes 884744 | tf_op jit(solution)/shard_map/ppermute | solution.py:252
  106.9 30.0 %collective-permute-start.7 = (bf16[256,3,192]{0,2,1:T(8,128)(2,1)}, bf16[256,3,192]{0,2,1:T(8,128)(2,1)}, u32[]{:S(2)}, u32[]{:S(2)}) collective-permute-start(bf16[256,3,192]{0,2,1:T(8,128)(2,1)} %get-tuple-element.91), channel_id=1, source_target_pairs={{0,16},{8,24},{16,0},{24,8},{1,17},{9,25},{17,1},{25,9},{2,18},{10... | collective-permute-start | bytes 884744 | tf_op jit(solution)/shard_map/ppermute | solution.py:252
  113.1 26.6 %collective-permute-start.8 = (bf16[256,3,192]{0,2,1:T(8,128)(2,1)}, bf16[256,3,192]{0,2,1:T(8,128)(2,1)}, u32[]{:S(2)}, u32[]{:S(2)}) collective-permute-start(bf16[256,3,192]{0,2,1:T(8,128)(2,1)} %get-tuple-element.93), channel_id=1, source_target_pairs={{0,24},{8,0},{16,8},{24,16},{1,25},{9,1},{17,9},{25,17},{2,26},{10... | collective-permute-start | bytes 884744 | tf_op jit(solution)/shard_map/ppermute | solution.py:252
  123.2 22.9 %collective-permute-start.12 = (bf16[256,3,192]{0,2,1:T(8,128)(2,1)}, bf16[256,3,192]{0,2,1:T(8,128)(2,1)}, u32[]{:S(2)}, u32[]{:S(2)}) collective-permute-start(bf16[256,3,192]{0,2,1:T(8,128)(2,1)} %get-tuple-element.96), channel_id=1, source_target_pairs={{0,8},{8,16},{16,24},{24,0},{1,9},{9,17},{17,25},{25,1},{2,10},{10... | collective-permute-start | bytes 884744 | tf_op jit(solution)/shard_map/ppermute | solution.py:252
  129.8 32.7 %collective-permute-start.13 = (bf16[256,3,192]{0,2,1:T(8,128)(2,1)}, bf16[256,3,192]{0,2,1:T(8,128)(2,1)}, u32[]{:S(2)}, u32[]{:S(2)}) collective-permute-start(bf16[256,3,192]{0,2,1:T(8,128)(2,1)} %get-tuple-element.95), channel_id=1, source_target_pairs={{0,16},{8,24},{16,0},{24,8},{1,17},{9,25},{17,1},{25,9},{2,18},{10... | collective-permute-start | bytes 884744 | tf_op jit(solution)/shard_map/ppermute | solution.py:252
  133.4 33.6 %collective-permute-start.14 = (bf16[256,3,192]{0,2,1:T(8,128)(2,1)}, bf16[256,3,192]{0,2,1:T(8,128)(2,1)}, u32[]{:S(2)}, u32[]{:S(2)}) collective-permute-start(bf16[256,3,192]{0,2,1:T(8,128)(2,1)} %get-tuple-element.97), channel_id=1, source_target_pairs={{0,24},{8,0},{16,8},{24,16},{1,25},{9,1},{17,9},{25,17},{2,26},{10... | collective-permute-start | bytes 884744 | tf_op jit(solution)/shard_map/ppermute | solution.py:252
  136.9 33.8 %collective-permute-start.18 = (bf16[256,3,192]{0,2,1:T(8,128)(2,1)}, bf16[256,3,192]{0,2,1:T(8,128)(2,1)}, u32[]{:S(2)}, u32[]{:S(2)}) collective-permute-start(bf16[256,3,192]{0,2,1:T(8,128)(2,1)} %get-tuple-element.100), channel_id=1, source_target_pairs={{0,8},{8,16},{16,24},{24,0},{1,9},{9,17},{17,25},{25,1},{2,10},{10... | collective-permute-start | bytes 884744 | tf_op jit(solution)/shard_map/ppermute | solution.py:252
  139.7 49.2 %collective-permute-start.19 = (bf16[256,3,192]{0,2,1:T(8,128)(2,1)}, bf16[256,3,192]{0,2,1:T(8,128)(2,1)}, u32[]{:S(2)}, u32[]{:S(2)}) collective-permute-start(bf16[256,3,192]{0,2,1:T(8,128)(2,1)} %get-tuple-element.99), channel_id=1, source_target_pairs={{0,16},{8,24},{16,0},{24,8},{1,17},{9,25},{17,1},{25,9},{2,18},{10... | collective-permute-start | bytes 884744 | tf_op jit(solution)/shard_map/ppermute | solution.py:252
  146.1 45.6 %collective-permute-start.20 = (bf16[256,3,192]{0,2,1:T(8,128)(2,1)}, bf16[256,3,192]{0,2,1:T(8,128)(2,1)}, u32[]{:S(2)}, u32[]{:S(2)}) collective-permute-start(bf16[256,3,192]{0,2,1:T(8,128)(2,1)} %get-tuple-element.101), channel_id=1, source_target_pairs={{0,24},{8,0},{16,8},{24,16},{1,25},{9,1},{17,9},{25,17},{2,26},{10... | collective-permute-start | bytes 884744 | tf_op jit(solution)/shard_map/ppermute | solution.py:252
  162.5 57.7 %collective-permute-start.3 = (bf16[256,192]{1,0:T(8,128)(2,1)}, bf16[256,192]{1,0:T(8,128)(2,1)}, u32[]{:S(2)}, u32[]{:S(2)}) collective-permute-start(bf16[256,192]{1,0:T(8,128)(2,1)} %get-tuple-element.108), channel_id=1, source_target_pairs={{0,24},{8,0},{16,8},{24,16},{1,25},{9,1},{17,9},{25,17},{2,26},{10... | collective-permute-start | bytes 294920 | tf_op jit(solution)/shard_map/ppermute | solution.py:252
  167.0 54.6 %collective-permute-start.4 = (bf16[256,192]{1,0:T(8,128)(2,1)}, bf16[256,192]{1,0:T(8,128)(2,1)}, u32[]{:S(2)}, u32[]{:S(2)}) collective-permute-start(bf16[256,192]{1,0:T(8,128)(2,1)} %get-tuple-element.107), channel_id=1, source_target_pairs={{0,16},{8,24},{16,0},{24,8},{1,17},{9,25},{17,1},{25,9},{2,18},{10... | collective-permute-start | bytes 294920 | tf_op jit(solution)/shard_map/ppermute | solution.py:252
  170.7 52.8 %collective-permute-start.5 = (bf16[256,192]{1,0:T(8,128)(2,1)}, bf16[256,192]{1,0:T(8,128)(2,1)}, u32[]{:S(2)}, u32[]{:S(2)}) collective-permute-start(bf16[256,192]{1,0:T(8,128)(2,1)} %get-tuple-element.106), channel_id=1, source_target_pairs={{0,8},{8,16},{16,24},{24,0},{1,9},{9,17},{17,25},{25,1},{2,10},{10... | collective-permute-start | bytes 294920 | tf_op jit(solution)/shard_map/ppermute | solution.py:252
  176.6 18.8 %copy-start.11 = (bf16[256,576]{1,0:T(8,128)(2,1)S(1)}, bf16[256,576]{1,0:T(8,128)(2,1)}, u32[]{:S(2)}) copy-start(bf16[256,576]{1,0:T(8,128)(2,1)} %copy.253) | copy-start | bytes 884740
  176.6 18.8 %copy-start.12 = (bf16[256,576]{1,0:T(8,128)(2,1)S(1)}, bf16[256,576]{1,0:T(8,128)(2,1)}, u32[]{:S(2)}) copy-start(bf16[256,576]{1,0:T(8,128)(2,1)} %copy.254) | copy-start | bytes 884740
  188.9 36.0 %collective-permute-start.10 = (bf16[256,192]{1,0:T(8,128)(2,1)}, bf16[256,192]{1,0:T(8,128)(2,1)}, u32[]{:S(2)}, u32[]{:S(2)}) collective-permute-start(bf16[256,192]{1,0:T(8,128)(2,1)} %get-tuple-element.111), channel_id=1, source_target_pairs={{0,16},{8,24},{16,0},{24,8},{1,17},{9,25},{17,1},{25,9},{2,18},{10... | collective-permute-start | bytes 294920 | tf_op jit(solution)/shard_map/ppermute | solution.py:252
  191.7 34.5 %collective-permute-start.11 = (bf16[256,192]{1,0:T(8,128)(2,1)}, bf16[256,192]{1,0:T(8,128)(2,1)}, u32[]{:S(2)}, u32[]{:S(2)}) collective-permute-start(bf16[256,192]{1,0:T(8,128)(2,1)} %get-tuple-element.110), channel_id=1, source_target_pairs={{0,8},{8,16},{16,24},{24,0},{1,9},{9,17},{17,25},{25,1},{2,10},{10... | collective-permute-start | bytes 294920 | tf_op jit(solution)/shard_map/ppermute | solution.py:252
  220.2 7.7 %collective-permute-start.9 = (bf16[256,192]{1,0:T(8,128)(2,1)S(1)}, bf16[256,192]{1,0:T(8,128)(2,1)S(1)}, u32[]{:S(2)}, u32[]{:S(2)}) collective-permute-start(bf16[256,192]{1,0:T(8,128)(2,1)S(1)} %copy-done.25), channel_id=1, source_target_pairs={{0,24},{8,0},{16,8},{24,16},{1,25},{9,1},{17,9},{25,17},{2,26},{10... | collective-permute-start | bytes 294920 | tf_op jit(solution)/shard_map/ppermute | solution.py:252
  221.7 9.2 %collective-permute-start.15 = (bf16[256,192]{1,0:T(8,128)(2,1)S(1)}, bf16[256,192]{1,0:T(8,128)(2,1)S(1)}, u32[]{:S(2)}, u32[]{:S(2)}) collective-permute-start(bf16[256,192]{1,0:T(8,128)(2,1)S(1)} %get-tuple-element.116), channel_id=1, source_target_pairs={{0,24},{8,0},{16,8},{24,16},{1,25},{9,1},{17,9},{25,17},{2,26},{10... | collective-permute-start | bytes 294920 | tf_op jit(solution)/shard_map/ppermute | solution.py:252
  223.5 7.4 collective-permute-start.16
  224.9 7.9 %collective-permute-start.17 = (bf16[256,192]{1,0:T(8,128)(2,1)S(1)}, bf16[256,192]{1,0:T(8,128)(2,1)S(1)}, u32[]{:S(2)}, u32[]{:S(2)}) collective-permute-start(bf16[256,192]{1,0:T(8,128)(2,1)S(1)} %get-tuple-element.114), channel_id=1, source_target_pairs={{0,8},{8,16},{16,24},{24,0},{1,9},{9,17},{17,25},{25,1},{2,10},{10... | collective-permute-start | bytes 294920 | tf_op jit(solution)/shard_map/ppermute | solution.py:252
  226.2 7.4 collective-permute-start.21
  227.9 6.2 collective-permute-start.22
  230.9 5.9 collective-permute-start.23
  257.1 12.3 %copy-start.2 = (f32[1024,768]{1,0:T(8,128)S(1)}, f32[1024,768]{1,0:T(8,128)}, u32[]{:S(2)}) copy-start(f32[1024,768]{1,0:T(8,128)} %copy-done.1) | copy-start | bytes 9437188
  257.1 12.3 %copy-start.6 = (bf16[3072,768]{1,0:T(8,128)(2,1)S(1)}, bf16[3072,768]{1,0:T(8,128)(2,1)}, u32[]{:S(2)}) copy-start(bf16[3072,768]{1,0:T(8,128)(2,1)} %reshape.454) | copy-start | bytes 14155780
  297.0 13.0 %copy-start.3 = (f32[1024,768]{1,0:T(8,128)S(1)}, f32[1024,768]{1,0:T(8,128)}, u32[]{:S(2)}) copy-start(f32[1024,768]{1,0:T(8,128)} %copy-done.1) | copy-start | bytes 9437188
  358.1 7.0 collective-permute-start.24
  358.1 9.2 %collective-permute-start.25 = (bf16[256,192]{1,0:T(8,128)(2,1)S(1)}, bf16[256,192]{1,0:T(8,128)(2,1)S(1)}, u32[]{:S(2)}, u32[]{:S(2)}) collective-permute-start(bf16[256,192]{1,0:T(8,128)(2,1)S(1)} %get-tuple-element.123), channel_id=1, source_target_pairs={{0,16},{8,24},{16,0},{24,8},{1,17},{9,25},{17,1},{25,9},{2,18},{10... | collective-permute-start | bytes 294920 | tf_op jit(solution)/shard_map/ppermute | solution.py:252
  358.6 9.6 %collective-permute-start.26 = (bf16[256,192]{1,0:T(8,128)(2,1)S(1)}, bf16[256,192]{1,0:T(8,128)(2,1)S(1)}, u32[]{:S(2)}, u32[]{:S(2)}) collective-permute-start(bf16[256,192]{1,0:T(8,128)(2,1)S(1)} %get-tuple-element.122), channel_id=1, source_target_pairs={{0,24},{8,0},{16,8},{24,16},{1,25},{9,1},{17,9},{25,17},{2,26},{10... | collective-permute-start | bytes 294920 | tf_op jit(solution)/shard_map/ppermute | solution.py:252
  361.4 26.2 %collective-permute-start.30 = (bf16[256,192]{1,0:T(8,128)(2,1)S(1)}, bf16[256,192]{1,0:T(8,128)(2,1)S(1)}, u32[]{:S(2)}, u32[]{:S(2)}) collective-permute-start(bf16[256,192]{1,0:T(8,128)(2,1)S(1)} %get-tuple-element.128), channel_id=1, source_target_pairs={{0,8},{8,16},{16,24},{24,0},{1,9},{9,17},{17,25},{25,1},{2,10},{10... | collective-permute-start | bytes 294920 | tf_op jit(solution)/shard_map/ppermute | solution.py:252
  361.8 26.2 %collective-permute-start.31 = (bf16[256,192]{1,0:T(8,128)(2,1)S(1)}, bf16[256,192]{1,0:T(8,128)(2,1)S(1)}, u32[]{:S(2)}, u32[]{:S(2)}) collective-permute-start(bf16[256,192]{1,0:T(8,128)(2,1)S(1)} %get-tuple-element.127), channel_id=1, source_target_pairs={{0,16},{8,24},{16,0},{24,8},{1,17},{9,25},{17,1},{25,9},{2,18},{10... | collective-permute-start | bytes 294920 | tf_op jit(solution)/shard_map/ppermute | solution.py:252
  365.0 25.1 %collective-permute-start.32 = (bf16[256,192]{1,0:T(8,128)(2,1)S(1)}, bf16[256,192]{1,0:T(8,128)(2,1)}, u32[]{:S(2)}, u32[]{:S(2)}) collective-permute-start(bf16[256,192]{1,0:T(8,128)(2,1)S(1)} %get-tuple-element.126), channel_id=1, source_target_pairs={{0,24},{8,0},{16,8},{24,16},{1,25},{9,1},{17,9},{25,17},{2,26},{10... | collective-permute-start | bytes 294920 | tf_op jit(solution)/shard_map/ppermute | solution.py:252
  367.4 41.5 %collective-permute-start.36 = (bf16[256,192]{1,0:T(8,128)(2,1)S(1)}, bf16[256,192]{1,0:T(8,128)(2,1)S(1)}, u32[]{:S(2)}, u32[]{:S(2)}) collective-permute-start(bf16[256,192]{1,0:T(8,128)(2,1)S(1)} %get-tuple-element.132), channel_id=1, source_target_pairs={{0,8},{8,16},{16,24},{24,0},{1,9},{9,17},{17,25},{25,1},{2,10},{10... | collective-permute-start | bytes 294920 | tf_op jit(solution)/shard_map/ppermute | solution.py:252
  368.2 43.5 %collective-permute-start.37 = (bf16[256,192]{1,0:T(8,128)(2,1)S(1)}, bf16[256,192]{1,0:T(8,128)(2,1)S(1)}, u32[]{:S(2)}, u32[]{:S(2)}) collective-permute-start(bf16[256,192]{1,0:T(8,128)(2,1)S(1)} %get-tuple-element.131), channel_id=1, source_target_pairs={{0,16},{8,24},{16,0},{24,8},{1,17},{9,25},{17,1},{25,9},{2,18},{10... | collective-permute-start | bytes 294920 | tf_op jit(solution)/shard_map/ppermute | solution.py:252
  387.6 24.9 %collective-permute-start.38 = (bf16[256,192]{1,0:T(8,128)(2,1)S(1)}, bf16[256,192]{1,0:T(8,128)(2,1)S(1)}, u32[]{:S(2)}, u32[]{:S(2)}) collective-permute-start(bf16[256,192]{1,0:T(8,128)(2,1)S(1)} %get-tuple-element.130), channel_id=1, source_target_pairs={{0,24},{8,0},{16,8},{24,16},{1,25},{9,1},{17,9},{25,17},{2,26},{10... | collective-permute-start | bytes 294920 | tf_op jit(solution)/shard_map/ppermute | solution.py:252
  388.0 44.3 %collective-permute-start.42 = (bf16[256,192]{1,0:T(8,128)(2,1)S(1)}, bf16[256,192]{1,0:T(8,128)(2,1)}, u32[]{:S(2)}, u32[]{:S(2)}) collective-permute-start(bf16[256,192]{1,0:T(8,128)(2,1)S(1)} %get-tuple-element.136), channel_id=1, source_target_pairs={{0,8},{8,16},{16,24},{24,0},{1,9},{9,17},{17,25},{25,1},{2,10},{10... | collective-permute-start | bytes 294920 | tf_op jit(solution)/shard_map/ppermute | solution.py:252
  390.1 43.7 %collective-permute-start.43 = (bf16[256,192]{1,0:T(8,128)(2,1)S(1)}, bf16[256,192]{1,0:T(8,128)(2,1)}, u32[]{:S(2)}, u32[]{:S(2)}) collective-permute-start(bf16[256,192]{1,0:T(8,128)(2,1)S(1)} %get-tuple-element.135), channel_id=1, source_target_pairs={{0,16},{8,24},{16,0},{24,8},{1,17},{9,25},{17,1},{25,9},{2,18},{10... | collective-permute-start | bytes 294920 | tf_op jit(solution)/shard_map/ppermute | solution.py:252
  408.8 26.7 %collective-permute-start.44 = (bf16[256,192]{1,0:T(8,128)(2,1)}, bf16[256,192]{1,0:T(8,128)(2,1)}, u32[]{:S(2)}, u32[]{:S(2)}) collective-permute-start(bf16[256,192]{1,0:T(8,128)(2,1)} %get-tuple-element.134), channel_id=1, source_target_pairs={{0,24},{8,0},{16,8},{24,16},{1,25},{9,1},{17,9},{25,17},{2,26},{10... | collective-permute-start | bytes 294920 | tf_op jit(solution)/shard_map/ppermute | solution.py:252
  411.7 27.0 %collective-permute-start.27 = (bf16[256,576]{1,0:T(8,128)(2,1)S(1)}, bf16[256,576]{1,0:T(8,128)(2,1)S(1)}, u32[]{:S(2)}, u32[]{:S(2)}) collective-permute-start(bf16[256,576]{1,0:T(8,128)(2,1)S(1)} %get-tuple-element.73), channel_id=1, source_target_pairs={{0,24},{8,0},{16,8},{24,16},{1,25},{9,1},{17,9},{25,17},{2,26},{10... | collective-permute-start | bytes 884744 | tf_op jit(solution)/shard_map/ppermute | solution.py:252
  413.1 27.0 %collective-permute-start.28 = (bf16[256,576]{1,0:T(8,128)(2,1)S(1)}, bf16[256,576]{1,0:T(8,128)(2,1)S(1)}, u32[]{:S(2)}, u32[]{:S(2)}) collective-permute-start(bf16[256,576]{1,0:T(8,128)(2,1)S(1)} %get-tuple-element.72), channel_id=1, source_target_pairs={{0,16},{8,24},{16,0},{24,8},{1,17},{9,25},{17,1},{25,9},{2,18},{10... | collective-permute-start | bytes 884744 | tf_op jit(solution)/shard_map/ppermute | solution.py:252
  432.3 23.3 %collective-permute-start.29 = (bf16[256,576]{1,0:T(8,128)(2,1)S(1)}, bf16[256,576]{1,0:T(8,128)(2,1)}, u32[]{:S(2)}, u32[]{:S(2)}) collective-permute-start(bf16[256,576]{1,0:T(8,128)(2,1)S(1)} %get-tuple-element.71), channel_id=1, source_target_pairs={{0,8},{8,16},{16,24},{24,0},{1,9},{9,17},{17,25},{25,1},{2,10},{10... | collective-permute-start | bytes 884744 | tf_op jit(solution)/shard_map/ppermute | solution.py:252
  433.9 22.2 %collective-permute-start.35 = (bf16[256,576]{1,0:T(8,128)(2,1)S(1)}, bf16[256,576]{1,0:T(8,128)(2,1)S(1)}, u32[]{:S(2)}, u32[]{:S(2)}) collective-permute-start(bf16[256,576]{1,0:T(8,128)(2,1)S(1)} %get-tuple-element.75), channel_id=1, source_target_pairs={{0,8},{8,16},{16,24},{24,0},{1,9},{9,17},{17,25},{25,1},{2,10},{10... | collective-permute-start | bytes 884744 | tf_op jit(solution)/shard_map/ppermute | solution.py:252
  435.6 28.6 %collective-permute-start.33 = (bf16[256,576]{1,0:T(8,128)(2,1)}, bf16[256,576]{1,0:T(8,128)(2,1)}, u32[]{:S(2)}, u32[]{:S(2)}) collective-permute-start(bf16[256,576]{1,0:T(8,128)(2,1)} %get-tuple-element.77), channel_id=1, source_target_pairs={{0,24},{8,0},{16,8},{24,16},{1,25},{9,1},{17,9},{25,17},{2,26},{10... | collective-permute-start | bytes 884744 | tf_op jit(solution)/shard_map/ppermute | solution.py:252
  438.7 16.9 %copy-start.20 = (bf16[256,576]{1,0:T(8,128)(2,1)}, bf16[256,576]{1,0:T(8,128)(2,1)S(1)}, u32[]{:S(2)}) copy-start(bf16[256,576]{1,0:T(8,128)(2,1)S(1)} %collective-permute-done.27) | copy-start | bytes 884740
  438.7 27.1 %collective-permute-start.34 = (bf16[256,576]{1,0:T(8,128)(2,1)}, bf16[256,576]{1,0:T(8,128)(2,1)}, u32[]{:S(2)}, u32[]{:S(2)}) collective-permute-start(bf16[256,576]{1,0:T(8,128)(2,1)} %get-tuple-element.76), channel_id=1, source_target_pairs={{0,16},{8,24},{16,0},{24,8},{1,17},{9,25},{17,1},{25,9},{2,18},{10... | collective-permute-start | bytes 884744 | tf_op jit(solution)/shard_map/ppermute | solution.py:252
  440.2 15.4 %copy-start.22 = (bf16[256,576]{1,0:T(8,128)(2,1)}, bf16[256,576]{1,0:T(8,128)(2,1)S(1)}, u32[]{:S(2)}) copy-start(bf16[256,576]{1,0:T(8,128)(2,1)S(1)} %collective-permute-done.28) | copy-start | bytes 884740
  440.2 27.2 %collective-permute-start.39 = (bf16[256,576]{1,0:T(8,128)(2,1)}, bf16[256,576]{1,0:T(8,128)(2,1)}, u32[]{:S(2)}, u32[]{:S(2)}) collective-permute-start(bf16[256,576]{1,0:T(8,128)(2,1)} %get-tuple-element.81), channel_id=1, source_target_pairs={{0,24},{8,0},{16,8},{24,16},{1,25},{9,1},{17,9},{25,17},{2,26},{10... | collective-permute-start | bytes 884744 | tf_op jit(solution)/shard_map/ppermute | solution.py:252
  455.6 17.1 %collective-permute-start.40 = (bf16[256,576]{1,0:T(8,128)(2,1)}, bf16[256,576]{1,0:T(8,128)(2,1)}, u32[]{:S(2)}, u32[]{:S(2)}) collective-permute-start(bf16[256,576]{1,0:T(8,128)(2,1)} %get-tuple-element.80), channel_id=1, source_target_pairs={{0,16},{8,24},{16,0},{24,8},{1,17},{9,25},{17,1},{25,9},{2,18},{10... | collective-permute-start | bytes 884744 | tf_op jit(solution)/shard_map/ppermute | solution.py:252
  456.1 18.5 %collective-permute-start.41 = (bf16[256,576]{1,0:T(8,128)(2,1)}, bf16[256,576]{1,0:T(8,128)(2,1)}, u32[]{:S(2)}, u32[]{:S(2)}) collective-permute-start(bf16[256,576]{1,0:T(8,128)(2,1)} %get-tuple-element.79), channel_id=1, source_target_pairs={{0,8},{8,16},{16,24},{24,0},{1,9},{9,17},{17,25},{25,1},{2,10},{10... | collective-permute-start | bytes 884744 | tf_op jit(solution)/shard_map/ppermute | solution.py:252
  464.2 14.6 %collective-permute-start.45 = (bf16[256,576]{1,0:T(8,128)(2,1)}, bf16[256,576]{1,0:T(8,128)(2,1)}, u32[]{:S(2)}, u32[]{:S(2)}) collective-permute-start(bf16[256,576]{1,0:T(8,128)(2,1)} %get-tuple-element.85), channel_id=1, source_target_pairs={{0,24},{8,0},{16,8},{24,16},{1,25},{9,1},{17,9},{25,17},{2,26},{10... | collective-permute-start | bytes 884744 | tf_op jit(solution)/shard_map/ppermute | solution.py:252
  465.8 14.1 %collective-permute-start.46 = (bf16[256,576]{1,0:T(8,128)(2,1)}, bf16[256,576]{1,0:T(8,128)(2,1)}, u32[]{:S(2)}, u32[]{:S(2)}) collective-permute-start(bf16[256,576]{1,0:T(8,128)(2,1)} %get-tuple-element.84), channel_id=1, source_target_pairs={{0,16},{8,24},{16,0},{24,8},{1,17},{9,25},{17,1},{25,9},{2,18},{10... | collective-permute-start | bytes 884744 | tf_op jit(solution)/shard_map/ppermute | solution.py:252
  467.4 13.7 %collective-permute-start.47 = (bf16[256,576]{1,0:T(8,128)(2,1)}, bf16[256,576]{1,0:T(8,128)(2,1)}, u32[]{:S(2)}, u32[]{:S(2)}) collective-permute-start(bf16[256,576]{1,0:T(8,128)(2,1)} %get-tuple-element.83), channel_id=1, source_target_pairs={{0,8},{8,16},{16,24},{24,0},{1,9},{9,17},{17,25},{25,1},{2,10},{10... | collective-permute-start | bytes 884744 | tf_op jit(solution)/shard_map/ppermute | solution.py:252
  509.7 84.4 %reduce-scatter.6.cloned.1.call-start = ((), (), s32[]{:S(2)}) async-start(), calls=%async_computation.6 | async-start | bytes 1105920 | tf_op jit(solution)/shard_map/reduce_scatter | solution.py:166
  559.6 182.6 %reduce-scatter.8.cloned.1.call-start = ((), (), s32[]{:S(2)}) async-start(), calls=%async_computation.7 | async-start | bytes 11354112 | tf_op jit(solution)/shard_map/reduce_scatter | solution.py:324
  (33 other events, 164.3 us)
Sparse Core Ops, SparseCore 0:
  17.8 63.4 all-gather.2
  84.3 114.2 all-gather.4
  509.8 49.7 reduce-scatter.3
  561.8 32.3 reduce-scatter.5
  600.0 142.2 reduce-scatter.7
